TPU v7x, 256 devices: a whole 4x4x8 slice. The times are simulated.
256 devices in a mesh: dp: 8 (over z), tm: 32 (over x, y, core).
Axes of the slice: x: 4, y: 4, z: 8, core: 2. Of those that a mesh axis runs over, the one named last changes fastest.
Arguments:
- clips: bfloat16 [8, 128, 16, 16, 128], P('dp', 'tm'), may hold values from -6 to 6
- segment_ids: int32 [8, 128], P('dp'), may hold values from 0 to 3, never falling along the last dimension, each value on 1 to 64 neighbouring positions
- conv_weight: bfloat16 [3456, 128], replicated, may hold values from -0.109375 to 0.109375
- cotangent: bfloat16 [8, 128, 16, 16, 128], P('dp', 'tm'), may hold values from -6 to 6
Outputs:
- activated: bfloat16 [8, 128, 16, 16, 128], P('dp', 'tm')
- grad_clips: bfloat16 [8, 128, 16, 16, 128], P('dp', 'tm')
- grad_weight: float32 [3456, 128], P('tm')
Inputs may be any that keep to these rules, and one draw needn't show every extreme that they name: segment_ids never fall along a sequence; each clip has 1 to 64 frames and one has exactly that many.
All inputs are finite; a program needn't handle non-finite values.
Results may differ from a plain program's by a relative error of at most 0.013.
Values may be sent and summed in bfloat16 or wider, within the bound.
No kernel may reach another device: no remote copies, remote signals or barrier semaphores. Data moves between devices by JAX's collectives and lax.ppermute only.
A program may use at most 64 MiB of HBM per device.

v0:
```python
import jax
import jax.numpy as jnp
from jax import lax
from jax.sharding import PartitionSpec as P


def from_behind(value, axis, steps):
    count = lax.axis_size(axis)
    leading, last = (max(0, -steps), min(count, count - steps))
    return lax.ppermute(value, axis, [(source, source + steps) for source in range(leading, last)])


def per_device(clips, segment_ids, conv_weight, cotangent):
    nfr = clips.shape[1]
    hh = clips.shape[2]
    ww = clips.shape[3]
    cc = clips.shape[4]
    rows = nfr * hh * ww
    earlier = from_behind(clips[:, nfr - 2 :], "tm", 1)
    extended = jnp.concatenate([earlier, clips], axis=1)[0]
    segrow = segment_ids[0]
    segp = jnp.concatenate([jnp.full((2,), -1, jnp.int32), segrow, jnp.full((2,), -2, jnp.int32)])
    start = lax.axis_index("tm") * nfr
    seglocal = lax.dynamic_slice_in_dim(segp, start, nfr + 4, 0)
    own = seglocal[2 : 2 + nfr]
    patches = []
    pre = jnp.zeros((rows, cc), jnp.float32)
    for kt in range(3):
        moved = extended[kt : kt + nfr]
        keep = seglocal[kt : kt + nfr] == own
        moved = jnp.where(keep[:, None, None, None], moved, jnp.zeros_like(moved))
        padded = jnp.pad(moved, ((0, 0), (1, 1), (1, 1), (0, 0)))
        pieces = [padded[:, ky : ky + hh, kx : kx + ww] for ky in range(3) for kx in range(3)]
        patch = jnp.concatenate(pieces, axis=3).reshape(rows, 9 * cc)
        patches.append(patch)
        pre = pre + jnp.dot(
            patch, conv_weight[kt * 9 * cc : (kt + 1) * 9 * cc], preferred_element_type=jnp.float32
        )
    activated = jax.nn.silu(pre).astype(jnp.bfloat16).reshape(clips.shape)
    sig = jax.nn.sigmoid(pre)
    grad_pre = (
        cotangent.reshape(rows, cc).astype(jnp.float32) * sig * (1.0 + pre * (1.0 - sig))
    ).astype(jnp.bfloat16)
    count = lax.axis_size("dp") * lax.axis_size("tm") * rows
    grad_local = jnp.concatenate(
        [
            lax.dot_general(
                patch, grad_pre, (((0,), (0,)), ((), ())), preferred_element_type=jnp.float32
            )
            for patch in patches
        ],
        axis=0,
    )
    grad_local = grad_local / jnp.sqrt(jnp.float32(count))
    frames_grad = grad_pre.reshape(1, nfr, hh, ww, cc)
    later_part = from_behind(frames_grad[:, :2], "tm", -1)
    grad_ext = jnp.concatenate([frames_grad, later_part], axis=1)[0]
    summed = jnp.zeros((rows, 9 * cc), jnp.float32)
    for kt in range(3):
        d = 2 - kt
        later = grad_ext[d : d + nfr]
        keep = seglocal[2 + d : 2 + d + nfr] == own
        later = jnp.where(keep[:, None, None, None], later, jnp.zeros_like(later)).reshape(rows, cc)
        summed = summed + lax.dot_general(
            later,
            conv_weight[kt * 9 * cc : (kt + 1) * 9 * cc],
            (((1,), (1,)), ((), ())),
            preferred_element_type=jnp.float32,
        )
    summed = summed.reshape(nfr, hh, ww, 9, cc)
    canvas = jnp.zeros((nfr, hh + 2, ww + 2, cc), jnp.float32)
    for ky in range(3):
        for kx in range(3):
            canvas = canvas.at[:, ky : ky + hh, kx : kx + ww].add(summed[:, :, :, ky * 3 + kx])
    grad_clips = canvas[:, 1:-1, 1:-1].astype(jnp.bfloat16).reshape(clips.shape)
    share_rows = grad_local.shape[0] // lax.axis_size("tm")
    total = lax.psum(grad_local, ("dp", "tm"))
    grad_weight = lax.dynamic_slice_in_dim(total, lax.axis_index("tm") * share_rows, share_rows, 0)
    return (activated, grad_clips, grad_weight)


def solution(mesh):
    return jax.shard_map(
        per_device,
        mesh=mesh,
        in_specs=(
            P("dp", "tm", None, None, None),
            P("dp", None),
            P(),
            P("dp", "tm", None, None, None),
        ),
        out_specs=(P("dp", "tm", None, None, None), P("dp", "tm", None, None, None), P("tm", None)),
        check_vma=False,
    )
```

profile of v0, /device:TPU:8, one launch (start us, length us, event | category | flops | bytes accessed | tf_op | source)
XLA Modules:
  0.0 301.4 jit_solution(8584760968547292022)
XLA Ops:
  7.2 0.9 slice.482
  8.2 1.9 collective-permute-start
  10.1 0.7 pad_add_fusion
  11.0 2.5 pad_slice_fusion
  13.6 0.6 fusion.33
  14.7 0.7 and_reduce_fusion
  15.4 0.6 fusion.34
  16.5 0.1 fusion.22
  16.6 0.2 fusion.6
  16.8 0.1 fusion.16
  17.0 0.1 fusion.17
  17.1 0.1 fusion.18
  17.5 0.1 fusion.21
  17.6 0.1 fusion.8
  17.8 0.1 fusion.9
  17.9 0.1 fusion.10
  18.2 0.1 fusion.13
  18.4 0.3 copy-done.1
  18.6 0.8 fusion.30
  19.4 0.8 convolution_add_fusion.3
  20.2 0.2 copy-done.3
  20.4 1.6 fusion.3
  22.0 0.8 fusion.37
  22.8 0.8 fusion.36
  23.6 0.8 fusion.35
  24.5 3.8 %collective-permute-start.1 = (bf16[1,2,16,16,128]{4,3,2,1,0:T(8,128)(2,1)S(1)}, bf16[1,2,16,16,128]{4,3,2,1,0:T(8,128)(2,1)S(1)}, u32[]{:S(2)}, u32[]{:S(2)}) collective-permute-start(bf16[1,2,16,16,128]{4,3,2,1,0:T(8,128)(2,1)S(1)} %slice.545), channel_id=1, source_target_pairs={{1,0},{2,1},{3,2},{4,3},{5,4},{6,5},{7,6},{8,7},{9,8},{10,9},{11,1... | collective-permute-start | bytes 393224 | tf_op jit(solution)/shard_map/ppermute | solution.py:10
  28.3 1.3 maximum_multiply_fusion
  29.6 1.0 collective-permute-done.1
  30.6 0.2 bitcast_select_fusion.1
  30.9 0.8 fusion.28
  31.6 0.2 bitcast_select_fusion
  31.9 0.8 convolution_add_fusion.1
  32.6 3.0 convolution_add_fusion
  35.6 6.9 %reshape.439 = f32[4,16,16,9,128]{4,3,2,1,0:T(8,128)} reshape(f32[1024,1152]{1,0:T(8,128)} %convolution_add_fusion) | data formatting | bytes 9437184 | tf_op jit(solution)/shard_map/reshape | solution.py:70
  42.5 16.6 %fusion.32 = (f32[4,16,16,1,128]{4,3,2,1,0:T(1,128)S(1)}, f32[4,16,16,1,128]{4,3,2,1,0:T(1,128)S(1)}, f32[4,16,16,1,128]{4,3,2,1,0:T(1,128)S(1)}, f32[4,16,16,1,...) fusion(f32[4,16,16,9,128]{4,3,2,1,0:T(8,128)} %reshape.439), kind=kLoop, calls=%fused_computation.101 | loop fusion | bytes 9437184 | tf_op jit(solution)/shard_map/slice | solution.py:74
  59.1 2.2 dynamic-slice_add_fusion
  61.3 4.3 %scatter-add.31 = f32[4,18,18,128]{3,2,1,0:T(8,128)S(1)} dynamic-update-slice(f32[4,18,18,128]{3,2,1,0:T(8,128)S(1)} %scatter-add.30, f32[4,16,16,128]{3,2,1,0:T(8,128)} %dynamic-slice_add_fusion, s32[]{:T(128)} %constant.283.clone.1, s32[]{:T(128)} %bitcast.21, s32[]{:T(128)} %bitcast.22, s32[]{:T(128)} %constant.283.clone.1) | dynamic-update-slice | bytes 1048580 | tf_op jit(solution)/shard_map/scatter-add | solution.py:74
  65.6 3.8 %add_select_fusion = f32[4,16,16,128]{3,2,1,0:T(8,128)} fusion(f32[4,16,16,128]{3,2,1,0:T(8,128)} %bitcast.89, f32[4,18,18,128]{3,2,1,0:T(8,128)S(1)} %scatter-add.31, s32[]{:T(128)} %bitcast.24, s32[]{:T(128)} %bitcast.25, pred[]{:T(512)} %and_reduce_fusion), kind=kLoop, calls=%fused_computation.5 | loop fusion | flops 262144 | bytes 1572873 | tf_op jit(solution)/shard_map/select.11
  69.4 4.3 %scatter-add.34 = f32[4,18,18,128]{3,2,1,0:T(8,128)S(1)} dynamic-update-slice(f32[4,18,18,128]{3,2,1,0:T(8,128)S(1)} %scatter-add.31, f32[4,16,16,128]{3,2,1,0:T(8,128)} %add_select_fusion, s32[]{:T(128)} %constant.283.clone.1, s32[]{:T(128)} %bitcast.24, s32[]{:T(128)} %bitcast.25, s32[]{:T(128)} %constant.283.clone.1) | dynamic-update-slice | bytes 1048580 | tf_op jit(solution)/shard_map/scatter-add | solution.py:74
  73.7 1.1 fusion.1
  74.9 0.9 slice_add_fusion.4
  75.8 3.0 %scatter-add.36 = f32[4,18,18,128]{3,2,1,0:T(8,128)S(1)} dynamic-update-slice(f32[4,18,18,128]{3,2,1,0:T(8,128)S(1)} %fusion.1, f32[4,16,16,128]{3,2,1,0:T(8,128)} %slice_add_fusion.4, s32[]{:T(128)} %constant.283.clone.1, s32[]{:T(128)} %constant.292.clone.1, s32[]{:T(128)} %constant.292.clone.1, s32[]{:T(128)} %constant.283.clone.1) | dynamic-update-slice | bytes 1048580 | tf_op jit(solution)/shard_map/scatter-add | solution.py:74
  78.9 1.7 scatter-add.39
  80.7 1.7 scatter-add.41
  82.5 1.7 scatter-add.44
  84.2 0.8 fusion.5
  84.9 208.2 %all-reduce.6.cloned.1.call-done = f32[3456,128]{1,0:T(8,128)} async-done(((f32[3456,128]{1,0:T(8,128)}), f32[3456,128]{1,0:T(8,128)}) %all-reduce.6.cloned.1.call-update) | async-done | bytes 1769488 | tf_op jit(solution)/shard_map/psum | solution.py:77
  293.1 1.5 constant_dynamic-slice_fusion
  (45 shorter events, 2.2 us)
Async XLA Ops:
  7.2 7.2 %copy-start = (bf16[1,4,16,16,128]{4,3,2,1,0:T(8,128)(2,1)S(1)}, bf16[1,4,16,16,128]{4,3,2,1,0:T(8,128)(2,1)}, u32[]{:S(2)}) copy-start(bf16[1,4,16,16,128]{4,3,2,1,0:T(8,128)(2,1)} %param.22) | copy-start | bytes 786436
  7.2 285.9 %all-reduce.6.cloned.1.call-start = ((), (), s32[]{:S(2)}) async-start(), calls=%async_computation | async-start | bytes 3538944 | tf_op jit(solution)/shard_map/psum | solution.py:77
  8.2 8.3 %collective-permute-start = (bf16[1,2,16,16,128]{4,3,2,1,0:T(8,128)(2,1)S(1)}, bf16[1,2,16,16,128]{4,3,2,1,0:T(8,128)(2,1)S(1)}, u32[]{:S(2)}, u32[]{:S(2)}) collective-permute-start(bf16[1,2,16,16,128]{4,3,2,1,0:T(8,128)(2,1)S(1)} %slice.482), channel_id=1, source_target_pairs={{0,1},{1,2},{2,3},{3,4},{4,5},{5,6},{6,7},{7,8},{8,9},{9,10},{10,1... | collective-permute-start | bytes 393224 | tf_op jit(solution)/shard_map/ppermute | solution.py:10
  13.5 1.2 copy-start.2
  17.4 1.2 copy-start.1
  19.4 1.0 copy-start.3
  24.5 6.1 %collective-permute-start.1 = (bf16[1,2,16,16,128]{4,3,2,1,0:T(8,128)(2,1)S(1)}, bf16[1,2,16,16,128]{4,3,2,1,0:T(8,128)(2,1)S(1)}, u32[]{:S(2)}, u32[]{:S(2)}) collective-permute-start(bf16[1,2,16,16,128]{4,3,2,1,0:T(8,128)(2,1)S(1)} %slice.545), channel_id=1, source_target_pairs={{1,0},{2,1},{3,2},{4,3},{5,4},{6,5},{7,6},{8,7},{9,8},{10,9},{11,1... | collective-permute-start | bytes 393224 | tf_op jit(solution)/shard_map/ppermute | solution.py:10
Sparse Core Ops, SparseCore 0:
  29.8 263.2 all-reduce.5
where the time goes:
time: 302 us; the launch traced here: 301 us
  waiting for transfers between devices  209 us (69%)
  local copies, waits for them, and re-layouts  50.1 us (17%)
  between operations  14.5 us (5%)
  other arithmetic  11.7 us (4%)
  matrix products  10.2 us (3%)
  starting transfers between devices  5.78 us (2%)
    psum x1, waiting for transfers between devices, per_device(): total = lax.psum(grad_local, ('dp', 'tm'))  208 us
    scatter-add x7, local copies, waits for them, and re-layouts, per_device(): canvas.at[:, ky:ky + hh, kx:kx + ww].add(summed[:, :, :, ky * 3 + kx])  16.8 us
    slice x1, local copies, waits for them, and re-layouts, per_device(): summed[:, :, :, ky * 3 + kx]  16.6 us
    reshape x1, local copies, waits for them, and re-layouts, per_device(): summed = summed.reshape(nfr, hh, ww, 9, cc)  6.85 us
  transfers between devices with their start and end apart: 3, of which 2 were waited for; matrix products, arithmetic and copies ran while one was open for 20% of the time, Pallas kernels for 0%

commit v1 on v0

--- a/solution.py
+++ b/solution.py
@@ -8,6 +8,19 @@
     count = lax.axis_size(axis)
     leading, last = (max(0, -steps), min(count, count - steps))
     return lax.ppermute(value, axis, [(source, source + steps) for source in range(leading, last)])
+
+
+def reduce_weight_grad(grad_local):
+    tm = lax.axis_size("tm")
+    dp = lax.axis_size("dp")
+    rows, cols = grad_local.shape
+    blocks = grad_local.reshape(tm, rows // tm, cols)
+    mine = lax.all_to_all(blocks, "tm", 0, 0, tiled=True).sum(axis=0)
+    step = 1
+    while step < dp:
+        mine = mine + lax.ppermute(mine, "dp", [(i, i ^ step) for i in range(dp)])
+        step *= 2
+    return mine
 
 
 def per_device(clips, segment_ids, conv_weight, cotangent):
@@ -73,9 +86,7 @@
         for kx in range(3):
             canvas = canvas.at[:, ky : ky + hh, kx : kx + ww].add(summed[:, :, :, ky * 3 + kx])
     grad_clips = canvas[:, 1:-1, 1:-1].astype(jnp.bfloat16).reshape(clips.shape)
-    share_rows = grad_local.shape[0] // lax.axis_size("tm")
-    total = lax.psum(grad_local, ("dp", "tm"))
-    grad_weight = lax.dynamic_slice_in_dim(total, lax.axis_index("tm") * share_rows, share_rows, 0)
+    grad_weight = reduce_weight_grad(grad_local)
     return (activated, grad_clips, grad_weight)
 
 

time: 302 us -> 108 us (0.36)
  waiting for transfers between devices: 209 us -> 2.87 us
  starting transfers between devices: 5.78 us -> 24.7 us
  between operations: 14.5 us -> 1.13 us
  other arithmetic: 11.7 us -> 16.3 us
    psum x1 -> x0, waiting for transfers between devices: 208 us -> none  [per_device(): total = lax.psum(grad_local, ('dp', 'tm'))]
    ppermute x0 -> x3, starting transfers between devices: none -> 11.5 us  [reduce_weight_grad(): mine = mine + lax.ppermute(mine, 'dp', [(i, i ^ step) for i in range(dp)])]
    all_to_all x0 -> x1, starting transfers between devices: none -> 7.67 us  [reduce_weight_grad(): mine = lax.all_to_all(blocks, 'tm', 0, 0, tiled=True).sum(axis=0)]
    add x5, other arithmetic: 3.27 us -> 7.2 us  [per_device(): canvas.at[:, ky:ky + hh, kx:kx + ww].add(summed[:, :, :, ky * 3 + kx])]
  transfers between devices with their start and end apart: 3 -> 6, of which waited for: 2 -> 2; matrix products, arithmetic and copies ran while one was open for 20% -> 64% of each run, Pallas kernels for 0% -> 0%
where the time goes in v1:
time: 108 us; the launch traced here: 107 us
  local copies, waits for them, and re-layouts  51.6 us (48%)
  starting transfers between devices  24.7 us (23%)
  other arithmetic  16.3 us (15%)
  matrix products  10.2 us (9%)
  waiting for transfers between devices  2.87 us (3%)
  between operations  1.13 us (1%)
    scatter-add x7, local copies, waits for them, and re-layouts, per_device(): canvas.at[:, ky:ky + hh, kx:kx + ww].add(summed[:, :, :, ky * 3 + kx])  18.1 us
    slice x1, local copies, waits for them, and re-layouts, per_device(): summed[:, :, :, ky * 3 + kx]  16.7 us
    ppermute x3, starting transfers between devices, reduce_weight_grad(): mine = mine + lax.ppermute(mine, 'dp', [(i, i ^ step) for i in range(dp)])  11.5 us
    all_to_all x1, starting transfers between devices, reduce_weight_grad(): mine = lax.all_to_all(blocks, 'tm', 0, 0, tiled=True).sum(axis=0)  7.67 us
    add x5, other arithmetic, per_device(): canvas.at[:, ky:ky + hh, kx:kx + ww].add(summed[:, :, :, ky * 3 + kx])  7.2 us
    reshape x1, local copies, waits for them, and re-layouts, per_device(): summed = summed.reshape(nfr, hh, ww, 9, cc)  6.85 us
    ppermute x2, starting transfers between devices, from_behind(): lax.ppermute(value, axis, [(source, source + steps) for source in range(l...  5.56 us
    another operation x3, other arithmetic  4.6 us
  transfers between devices with their start and end apart: 6, of which 2 were waited for; matrix products, arithmetic and copies ran while one was open for 64% of the time, Pallas kernels for 0%

profile of v1, /device:TPU:8, one launch (start us, length us, event | category | flops | bytes accessed | tf_op | source)
XLA Modules:
  0.0 106.8 jit_solution(3710371003314020776)
XLA Ops:
  0.6 1.0 slice.482
  1.6 1.9 %collective-permute-start = (bf16[1,2,16,16,128]{4,3,2,1,0:T(8,128)(2,1)S(1)}, bf16[1,2,16,16,128]{4,3,2,1,0:T(8,128)(2,1)S(1)}, u32[]{:S(2)}, u32[]{:S(2)}) collective-permute-start(bf16[1,2,16,16,128]{4,3,2,1,0:T(8,128)(2,1)S(1)} %slice.482), channel_id=1, source_target_pairs={{0,1},{1,2},{2,3},{3,4},{4,5},{5,6},{6,7},{7,8},{8,9},{9,10},{10,1... | collective-permute-start | bytes 393224 | tf_op jit(solution)/shard_map/ppermute | solution.py:10
  3.6 0.7 pad_add_fusion
  4.5 2.5 %pad_slice_fusion = (bf16[4,16,16,128]{3,2,1,0:T(8,128)(2,1)S(1)}, bf16[4,16,16,128]{3,2,1,0:T(8,128)(2,1)S(1)}, bf16[4,16,16,128]{3,2,1,0:T(8,128)(2,1)S(1)}, b...) fusion(bf16[4,16,16,128]{3,2,1,0:T(8,128)(2,1)} %bitcast.81), kind=kLoop, calls=%fused_computation.6 | loop fusion | bytes 2359296 | tf_op jit(solution)/shard_map/slice | solution.py:46
  7.1 0.6 fusion.33
  8.2 0.7 and_reduce_fusion
  9.0 0.6 fusion.34
  10.1 0.2 fusion.6
  10.7 0.1 fusion.18
  11.9 0.3 copy-done.1
  12.1 0.8 fusion.30
  12.9 0.8 convolution_add_fusion.3
  13.7 0.2 copy-done.4
  13.9 1.6 %fusion.3 = (bf16[1024,128]{1,0:T(8,128)(2,1)S(1)}, bf16[1024,128]{1,0:T(8,128)(2,1)}) fusion(bf16[1,4,16,16,128]{4,3,2,1,0:T(8,128)(2,1)S(1)} %copy-done.4, f32[1024,128]{1,0:T(8,128)S(1)} %convolution_add_fusion.3, bf16[1024,1152]{1,0:T(8,128)(2,1)S(1)} %constant_dynamic-update-slice_fusion.4, bf16[3456,128]{1,0:T(8,128)(2,1)S(1)} %copy-done.1), kind=kOutput, calls=%fused_computation.41 | convolution fusion | flops 303693824 | bytes 3964928 | tf_op jit(solution)/shard_map/dot_general | solution.py:49
  15.5 0.8 fusion.37
  16.3 0.8 fusion.36
  17.2 0.8 fusion.35
  18.0 3.6 %collective-permute-start.1 = (bf16[1,2,16,16,128]{4,3,2,1,0:T(8,128)(2,1)S(1)}, bf16[1,2,16,16,128]{4,3,2,1,0:T(8,128)(2,1)S(1)}, u32[]{:S(2)}, u32[]{:S(2)}) collective-permute-start(bf16[1,2,16,16,128]{4,3,2,1,0:T(8,128)(2,1)S(1)} %slice.545), channel_id=1, source_target_pairs={{1,0},{2,1},{3,2},{4,3},{5,4},{6,5},{7,6},{8,7},{9,8},{10,9},{11,1... | collective-permute-start | bytes 393224 | tf_op jit(solution)/shard_map/ppermute | solution.py:10
  21.6 0.1 maximum_multiply_fusion
  21.8 1.3 %div.16 = f32[32,108,128]{2,1,0:T(8,128)} reshape(f32[3456,128]{1,0:T(8,128)S(1)} %maximum_multiply_fusion) | data formatting | bytes 3538944 | tf_op jit(solution)/shard_map/div | solution.py:67
  23.1 7.7 %all-to-all-start = ((f32[32,108,128]{2,1,0:T(8,128)}), f32[32,108,128]{2,1,0:T(8,128)S(1)}, u32[]{:S(2)}, u32[]{:S(2)}) async-start(f32[32,108,128]{2,1,0:T(8,128)} %div.16), calls=%async_computation | async-start | bytes 3670016 | tf_op jit(solution)/shard_map/all_to_all | solution.py:18
  30.8 0.2 bitcast_select_fusion.1
  31.1 0.8 fusion.28
  31.8 0.2 bitcast_select_fusion
  32.1 0.8 convolution_add_fusion.1
  32.8 3.0 %convolution_add_fusion = f32[1024,1152]{1,0:T(8,128)} fusion(f32[1024,1152]{1,0:T(8,128)S(1)} %convolution_add_fusion.1, bf16[1024,128]{1,0:T(8,128)(2,1)S(1)} %get-tuple-element.120, bf16[3456,128]{1,0:T(8,128)(2,1)S(1)} %copy-done.2), kind=kOutput, calls=%fused_computation | convolution fusion | flops 303169536 | bytes 9994240 | tf_op jit(solution)/shard_map/dot_general | solution.py:77
  35.8 6.9 %reshape.443 = f32[4,16,16,9,128]{4,3,2,1,0:T(8,128)} reshape(f32[1024,1152]{1,0:T(8,128)} %convolution_add_fusion) | data formatting | bytes 9437184 | tf_op jit(solution)/shard_map/reshape | solution.py:83
  42.7 16.7 %fusion.32 = (f32[4,16,16,1,128]{4,3,2,1,0:T(1,128)S(1)}, f32[4,16,16,1,128]{4,3,2,1,0:T(1,128)}, f32[4,16,16,1,128]{4,3,2,1,0:T(1,128)}, f32[4,16,16,1,128]{4,3...) fusion(f32[4,16,16,9,128]{4,3,2,1,0:T(8,128)} %reshape.443), kind=kLoop, calls=%fused_computation.100 | loop fusion | bytes 9437184 | tf_op jit(solution)/shard_map/slice | solution.py:87
  59.5 2.2 %dynamic-slice_add_fusion = f32[4,16,16,128]{3,2,1,0:T(8,128)} fusion(f32[4,16,16,128]{3,2,1,0:T(8,128)S(1)} %bitcast.90, s32[]{:T(128)} %bitcast.21, s32[]{:T(128)} %bitcast.22, f32[4,16,16,128]{3,2,1,0:T(8,128)S(1)} %bitcast.80), kind=kLoop, calls=%fused_computation.42 | loop fusion | flops 131072 | bytes 1572872 | tf_op jit(solution)/shard_map/add | solution.py:87
  61.6 4.3 %scatter-add.31 = f32[4,18,18,128]{3,2,1,0:T(8,128)S(1)} dynamic-update-slice(f32[4,18,18,128]{3,2,1,0:T(8,128)S(1)} %scatter-add.30, f32[4,16,16,128]{3,2,1,0:T(8,128)} %dynamic-slice_add_fusion, s32[]{:T(128)} %constant.282.clone.1, s32[]{:T(128)} %bitcast.21, s32[]{:T(128)} %bitcast.22, s32[]{:T(128)} %constant.282.clone.1) | dynamic-update-slice | bytes 1048580 | tf_op jit(solution)/shard_map/scatter-add | solution.py:87
  66.0 3.9 %add_select_fusion = f32[4,16,16,128]{3,2,1,0:T(8,128)} fusion(f32[4,16,16,128]{3,2,1,0:T(8,128)} %bitcast.89, f32[4,18,18,128]{3,2,1,0:T(8,128)S(1)} %scatter-add.31, s32[]{:T(128)} %bitcast.24, s32[]{:T(128)} %bitcast.25, pred[]{:T(512)} %and_reduce_fusion), kind=kLoop, calls=%fused_computation.5 | loop fusion | flops 262144 | bytes 1572873 | tf_op jit(solution)/shard_map/select.11
  69.8 4.3 %scatter-add.34 = f32[4,18,18,128]{3,2,1,0:T(8,128)S(1)} dynamic-update-slice(f32[4,18,18,128]{3,2,1,0:T(8,128)S(1)} %scatter-add.31, f32[4,16,16,128]{3,2,1,0:T(8,128)} %add_select_fusion, s32[]{:T(128)} %constant.282.clone.1, s32[]{:T(128)} %bitcast.24, s32[]{:T(128)} %bitcast.25, s32[]{:T(128)} %constant.282.clone.1) | dynamic-update-slice | bytes 1048580 | tf_op jit(solution)/shard_map/scatter-add | solution.py:87
  74.2 1.1 %fusion.1 = f32[4,18,18,128]{3,2,1,0:T(8,128)S(1)} fusion(f32[4,18,18,128]{3,2,1,0:T(8,128)S(1)} %scatter-add.34, f32[4,16,16,128]{3,2,1,0:T(8,128)} %bitcast.88), kind=kLoop, calls=%fused_computation.38 | loop fusion | flops 131072 | bytes 1572864 | tf_op jit(solution)/shard_map/scatter-add | solution.py:87
  75.3 1.9 %slice_add_fusion.4 = f32[4,16,16,128]{3,2,1,0:T(8,128)} fusion(f32[4,16,16,128]{3,2,1,0:T(8,128)} %bitcast.87, f32[4,18,18,128]{3,2,1,0:T(8,128)S(1)} %fusion.1), kind=kLoop, calls=%fused_computation.36 | loop fusion | flops 131072 | bytes 1572864 | tf_op jit(solution)/shard_map/add | solution.py:87
  77.2 3.0 %scatter-add.36 = f32[4,18,18,128]{3,2,1,0:T(8,128)S(1)} dynamic-update-slice(f32[4,18,18,128]{3,2,1,0:T(8,128)S(1)} %fusion.1, f32[4,16,16,128]{3,2,1,0:T(8,128)} %slice_add_fusion.4, s32[]{:T(128)} %constant.282.clone.1, s32[]{:T(128)} %constant.291.clone.1, s32[]{:T(128)} %constant.291.clone.1, s32[]{:T(128)} %constant.282.clone.1) | dynamic-update-slice | bytes 1048580 | tf_op jit(solution)/shard_map/scatter-add | solution.py:87
  80.3 1.9 %slice_add_fusion.3 = f32[4,16,16,128]{3,2,1,0:T(8,128)} fusion(f32[4,16,16,128]{3,2,1,0:T(8,128)} %bitcast.86, f32[4,18,18,128]{3,2,1,0:T(8,128)S(1)} %scatter-add.36), kind=kLoop, calls=%fused_computation.35 | loop fusion | flops 131072 | bytes 1572864 | tf_op jit(solution)/shard_map/add | solution.py:87
  82.2 3.0 %scatter-add.39 = f32[4,18,18,128]{3,2,1,0:T(8,128)S(1)} dynamic-update-slice(f32[4,18,18,128]{3,2,1,0:T(8,128)S(1)} %scatter-add.36, f32[4,16,16,128]{3,2,1,0:T(8,128)} %slice_add_fusion.3, s32[]{:T(128)} %constant.282.clone.1, s32[]{:T(128)} %constant.291.clone.1, s32[]{:T(128)} %constant.288.clone.1, s32[]{:T(128)} %constant.282.clone.1) | dynamic-update-slice | bytes 1048580 | tf_op jit(solution)/shard_map/scatter-add | solution.py:87
  85.2 1.1 %fusion = f32[4,18,18,128]{3,2,1,0:T(8,128)S(1)} fusion(f32[4,18,18,128]{3,2,1,0:T(8,128)S(1)} %scatter-add.39, f32[4,16,16,128]{3,2,1,0:T(8,128)} %bitcast.85), kind=kLoop, calls=%fused_computation.34 | loop fusion | flops 131072 | bytes 1572864 | tf_op jit(solution)/shard_map/scatter-add | solution.py:87
  86.5 2.0 %collective-permute-start.2 = (f32[108,128]{1,0:T(8,128)S(1)}, f32[108,128]{1,0:T(8,128)S(1)}, u32[]{:S(2)}, u32[]{:S(2)}) collective-permute-start(f32[108,128]{1,0:T(8,128)S(1)} %reduce_sum.9), channel_id=1, source_target_pairs={{0,32},{32,0},{64,96},{96,64},{128,160},{160,128},{192,224},{224,1... | collective-permute-start | bytes 165896 | tf_op jit(solution)/shard_map/ppermute | solution.py:21
  88.5 1.1 %slice_add_fusion.1 = f32[4,16,16,128]{3,2,1,0:T(8,128)S(1)} fusion(f32[4,16,16,128]{3,2,1,0:T(8,128)} %bitcast.84, f32[4,18,18,128]{3,2,1,0:T(8,128)S(1)} %fusion), kind=kLoop, calls=%fused_computation.32 | loop fusion | flops 131072 | bytes 1572864 | tf_op jit(solution)/shard_map/add | solution.py:87
  89.6 1.7 %scatter-add.41 = f32[4,18,18,128]{3,2,1,0:T(8,128)S(1)} dynamic-update-slice(f32[4,18,18,128]{3,2,1,0:T(8,128)S(1)} %fusion, f32[4,16,16,128]{3,2,1,0:T(8,128)S(1)} %slice_add_fusion.1, s32[]{:T(128)} %constant.282.clone.1, s32[]{:T(128)} %constant.288.clone.1, s32[]{:T(128)} %constant.291.clone.1, s32[]{:T(128)} %constant.282.clone.1) | dynamic-update-slice | bytes 1048580 | tf_op jit(solution)/shard_map/scatter-add | solution.py:87
  91.3 3.4 %collective-permute-start.3 = (f32[108,128]{1,0:T(8,128)S(1)}, f32[108,128]{1,0:T(8,128)S(1)}, u32[]{:S(2)}, u32[]{:S(2)}) collective-permute-start(f32[108,128]{1,0:T(8,128)S(1)} %add.119), channel_id=1, source_target_pairs={{0,64},{32,96},{64,0},{96,32},{128,192},{160,224},{192,128},{224,1... | collective-permute-start | bytes 165896 | tf_op jit(solution)/shard_map/ppermute | solution.py:21
  94.7 1.7 %scatter-add.44 = f32[4,18,18,128]{3,2,1,0:T(8,128)S(1)} dynamic-update-slice(f32[4,18,18,128]{3,2,1,0:T(8,128)S(1)} %scatter-add.41, f32[4,16,16,128]{3,2,1,0:T(8,128)S(1)} %slice_add_fusion, s32[]{:T(128)} %constant.282.clone.1, s32[]{:T(128)} %constant.288.clone.1, s32[]{:T(128)} %constant.288.clone.1, s32[]{:T(128)} %constant.282.clone.1) | dynamic-update-slice | bytes 1048580 | tf_op jit(solution)/shard_map/scatter-add | solution.py:87
  96.4 1.4 %collective-permute-done.3 = f32[108,128]{1,0:T(8,128)S(1)} collective-permute-done((f32[108,128]{1,0:T(8,128)S(1)}, f32[108,128]{1,0:T(8,128)S(1)}, u32[]{:S(2)}, u32[]{:S(2)}) %collective-permute-start.3) | collective-permute-done | bytes 55328 | tf_op jit(solution)/shard_map/ppermute | solution.py:21
  97.8 6.1 %collective-permute-start.4 = (f32[108,128]{1,0:T(8,128)S(1)}, f32[108,128]{1,0:T(8,128)S(1)}, u32[]{:S(2)}, u32[]{:S(2)}) collective-permute-start(f32[108,128]{1,0:T(8,128)S(1)} %add.120), channel_id=1, source_target_pairs={{0,128},{32,160},{64,192},{96,224},{128,0},{160,32},{192,64},{224,... | collective-permute-start | bytes 165896 | tf_op jit(solution)/shard_map/ppermute | solution.py:21
  103.9 0.8 fusion.5
  104.7 1.5 %collective-permute-done.4 = f32[108,128]{1,0:T(8,128)S(1)} collective-permute-done((f32[108,128]{1,0:T(8,128)S(1)}, f32[108,128]{1,0:T(8,128)S(1)}, u32[]{:S(2)}, u32[]{:S(2)}) %collective-permute-start.4) | collective-permute-done | bytes 55328 | tf_op jit(solution)/shard_map/ppermute | solution.py:21
  106.2 0.6 add.121
  (56 shorter events, 2.9 us)
Async XLA Ops:
  0.6 7.3 %copy-start = (bf16[1,4,16,16,128]{4,3,2,1,0:T(8,128)(2,1)S(1)}, bf16[1,4,16,16,128]{4,3,2,1,0:T(8,128)(2,1)}, u32[]{:S(2)}) copy-start(bf16[1,4,16,16,128]{4,3,2,1,0:T(8,128)(2,1)} %param.22) | copy-start | bytes 786436
  1.6 8.3 %collective-permute-start = (bf16[1,2,16,16,128]{4,3,2,1,0:T(8,128)(2,1)S(1)}, bf16[1,2,16,16,128]{4,3,2,1,0:T(8,128)(2,1)S(1)}, u32[]{:S(2)}, u32[]{:S(2)}) collective-permute-start(bf16[1,2,16,16,128]{4,3,2,1,0:T(8,128)(2,1)S(1)} %slice.482), channel_id=1, source_target_pairs={{0,1},{1,2},{2,3},{3,4},{4,5},{5,6},{6,7},{7,8},{8,9},{9,10},{10,1... | collective-permute-start | bytes 393224 | tf_op jit(solution)/shard_map/ppermute | solution.py:10
  7.0 1.2 %copy-start.3 = (s32[4]{0:T(128)S(1)}, s32[4]{0:T(128)}, u32[]{:S(2)}) copy-start(s32[4]{0:T(128)} %constant.289.clone.1) | copy-start | bytes 52
  11.0 1.2 %copy-start.1 = (bf16[3456,128]{1,0:T(8,128)(2,1)S(1)}, bf16[3456,128]{1,0:T(8,128)(2,1)}, u32[]{:S(2)}) copy-start(bf16[3456,128]{1,0:T(8,128)(2,1)} %param.24) | copy-start | bytes 2654212
  12.9 1.0 copy-start.4
  18.0 12.8 %collective-permute-start.1 = (bf16[1,2,16,16,128]{4,3,2,1,0:T(8,128)(2,1)S(1)}, bf16[1,2,16,16,128]{4,3,2,1,0:T(8,128)(2,1)S(1)}, u32[]{:S(2)}, u32[]{:S(2)}) collective-permute-start(bf16[1,2,16,16,128]{4,3,2,1,0:T(8,128)(2,1)S(1)} %slice.545), channel_id=1, source_target_pairs={{1,0},{2,1},{3,2},{4,3},{5,4},{6,5},{7,6},{8,7},{9,8},{10,9},{11,1... | collective-permute-start | bytes 393224 | tf_op jit(solution)/shard_map/ppermute | solution.py:10
  23.1 7.9 %copy-start.2 = (bf16[3456,128]{1,0:T(8,128)(2,1)S(1)}, bf16[3456,128]{1,0:T(8,128)(2,1)}, u32[]{:S(2)}) copy-start(bf16[3456,128]{1,0:T(8,128)(2,1)} %param.24) | copy-start | bytes 2654212
  23.1 63.3 %all-to-all-start = ((f32[32,108,128]{2,1,0:T(8,128)}), f32[32,108,128]{2,1,0:T(8,128)S(1)}, u32[]{:S(2)}, u32[]{:S(2)}) async-start(f32[32,108,128]{2,1,0:T(8,128)} %div.16), calls=%async_computation | async-start | bytes 3670016 | tf_op jit(solution)/shard_map/all_to_all | solution.py:18
  86.5 4.8 %collective-permute-start.2 = (f32[108,128]{1,0:T(8,128)S(1)}, f32[108,128]{1,0:T(8,128)S(1)}, u32[]{:S(2)}, u32[]{:S(2)}) collective-permute-start(f32[108,128]{1,0:T(8,128)S(1)} %reduce_sum.9), channel_id=1, source_target_pairs={{0,32},{32,0},{64,96},{96,64},{128,160},{160,128},{192,224},{224,1... | collective-permute-start | bytes 165896 | tf_op jit(solution)/shard_map/ppermute | solution.py:21
  91.3 6.5 %collective-permute-start.3 = (f32[108,128]{1,0:T(8,128)S(1)}, f32[108,128]{1,0:T(8,128)S(1)}, u32[]{:S(2)}, u32[]{:S(2)}) collective-permute-start(f32[108,128]{1,0:T(8,128)S(1)} %add.119), channel_id=1, source_target_pairs={{0,64},{32,96},{64,0},{96,32},{128,192},{160,224},{192,128},{224,1... | collective-permute-start | bytes 165896 | tf_op jit(solution)/shard_map/ppermute | solution.py:21
  97.8 8.4 %collective-permute-start.4 = (f32[108,128]{1,0:T(8,128)S(1)}, f32[108,128]{1,0:T(8,128)S(1)}, u32[]{:S(2)}, u32[]{:S(2)}) collective-permute-start(f32[108,128]{1,0:T(8,128)S(1)} %add.120), channel_id=1, source_target_pairs={{0,128},{32,160},{64,192},{96,224},{128,0},{160,32},{192,64},{224,... | collective-permute-start | bytes 165896 | tf_op jit(solution)/shard_map/ppermute | solution.py:21

commit v2 on v1

v2 whole, which is shorter than its diff:
```python
import jax
import jax.numpy as jnp
from jax import lax
from jax.sharding import PartitionSpec as P


def from_behind(value, axis, steps):
    count = lax.axis_size(axis)
    leading, last = (max(0, -steps), min(count, count - steps))
    return lax.ppermute(value, axis, [(source, source + steps) for source in range(leading, last)])


def reduce_weight_grad(grad_local):
    tm = lax.axis_size("tm")
    dp = lax.axis_size("dp")
    rows, cols = grad_local.shape
    blocks = grad_local.reshape(tm, rows // tm, cols)
    mine = lax.all_to_all(blocks, "tm", 0, 0, tiled=True).sum(axis=0)
    received = [mine] + [
        lax.ppermute(mine, "dp", [(i, (i + shift) % dp) for i in range(dp)]) for shift in range(1, dp)
    ]
    stacked = jnp.stack(received)
    me = lax.axis_index("dp")
    ordered = jnp.take(stacked, (me - jnp.arange(dp)) % dp, axis=0)
    while ordered.shape[0] > 1:
        ordered = ordered[0::2] + ordered[1::2]
    return ordered[0]


def im2col(frames, offset, hh, ww):
    padded = jnp.pad(frames, ((0, 0), (1, 1), (1, 1), (0, 0)))
    pieces = [
        padded[:, offset(ky) : offset(ky) + hh, offset(kx) : offset(kx) + ww]
        for ky in range(3)
        for kx in range(3)
    ]
    return jnp.concatenate(pieces, axis=3).reshape(-1, 9 * frames.shape[-1])


def per_device(clips, segment_ids, conv_weight, cotangent):
    nfr = clips.shape[1]
    hh = clips.shape[2]
    ww = clips.shape[3]
    cc = clips.shape[4]
    rows = nfr * hh * ww
    earlier = from_behind(clips[:, nfr - 2 :], "tm", 1)[0]
    ahead = from_behind(jnp.concatenate([clips[:, :2], cotangent[:, :2]], axis=1), "tm", -1)[0]
    frames = jnp.concatenate([earlier, clips[0], ahead[:2]], axis=0)
    cot_ext = jnp.concatenate([cotangent[0], ahead[2:]], axis=0)
    segrow = segment_ids[0]
    segp = jnp.concatenate([jnp.full((2,), -1, jnp.int32), segrow, jnp.full((2,), -2, jnp.int32)])
    start = lax.axis_index("tm") * nfr
    seglocal = lax.dynamic_slice_in_dim(segp, start, nfr + 4, 0)
    nout = nfr + 2
    centre = seglocal[2 : 2 + nout]
    pre = jnp.zeros((nout * hh * ww, cc), jnp.float32)
    patches = []
    for kt in range(3):
        moved = frames[kt : kt + nout]
        keep = seglocal[kt : kt + nout] == centre
        moved = jnp.where(keep[:, None, None, None], moved, jnp.zeros_like(moved))
        patch = im2col(moved, lambda k: k, hh, ww)
        patches.append(patch[:rows])
        pre = pre + jnp.dot(
            patch, conv_weight[kt * 9 * cc : (kt + 1) * 9 * cc], preferred_element_type=jnp.float32
        )
    sig = jax.nn.sigmoid(pre)
    activated = jax.nn.silu(pre[:rows]).astype(jnp.bfloat16).reshape(clips.shape)
    grad_pre = (
        cot_ext.reshape(nout * hh * ww, cc).astype(jnp.float32) * sig * (1.0 + pre * (1.0 - sig))
    ).astype(jnp.bfloat16)
    own_grad = grad_pre[:rows]
    count = lax.axis_size("dp") * lax.axis_size("tm") * rows
    grad_local = jnp.concatenate(
        [
            lax.dot_general(
                patch, own_grad, (((0,), (0,)), ((), ())), preferred_element_type=jnp.float32
            )
            for patch in patches
        ],
        axis=0,
    )
    grad_local = grad_local / jnp.sqrt(jnp.float32(count))
    grad_ext = grad_pre.reshape(nout, hh, ww, cc)
    own = seglocal[2 : 2 + nfr]
    summed = jnp.zeros((rows, cc), jnp.float32)
    for kt in range(3):
        d = 2 - kt
        later = grad_ext[d : d + nfr]
        keep = seglocal[2 + d : 2 + d + nfr] == own
        later = jnp.where(keep[:, None, None, None], later, jnp.zeros_like(later))
        patch = im2col(later, lambda k: 2 - k, hh, ww)
        block = conv_weight[kt * 9 * cc : (kt + 1) * 9 * cc].reshape(9, cc, cc)
        flipped = jnp.swapaxes(block, 1, 2).reshape(9 * cc, cc)
        summed = summed + jnp.dot(patch, flipped, preferred_element_type=jnp.float32)
    grad_clips = summed.astype(jnp.bfloat16).reshape(clips.shape)
    grad_weight = reduce_weight_grad(grad_local)
    return (activated, grad_clips, grad_weight)


def solution(mesh):
    return jax.shard_map(
        per_device,
        mesh=mesh,
        in_specs=(
            P("dp", "tm", None, None, None),
            P("dp", None),
            P(),
            P("dp", "tm", None, None, None),
        ),
        out_specs=(P("dp", "tm", None, None, None), P("dp", "tm", None, None, None), P("tm", None)),
        check_vma=False,
    )
```

time: 108 us -> 85.5 us (0.79)
  the two profiles are of different devices: /device:TPU:8 before, /device:TPU:1 now
where the time goes in v2:
time: 85.5 us; the launch traced here: 85.1 us
  starting transfers between devices  32.2 us (38%)
  waiting for transfers between devices  23.9 us (28%)
  local copies, waits for them, and re-layouts  14 us (16%)
  matrix products  9.84 us (12%)
  other arithmetic  3.68 us (4%)
  between operations  1.31 us (2%)
    all_to_all x1, waiting for transfers between devices, reduce_weight_grad(): mine = lax.all_to_all(blocks, 'tm', 0, 0, tiled=True).sum(axis=0)  18.2 us
    ppermute x7, starting transfers between devices, reduce_weight_grad(): lax.ppermute(mine, 'dp', [(i, (i + shift) % dp) for i in range(dp)])  16.6 us
    all_to_all x1, starting transfers between devices, reduce_weight_grad(): mine = lax.all_to_all(blocks, 'tm', 0, 0, tiled=True).sum(axis=0)  8.45 us
    ppermute x2, starting transfers between devices, from_behind(): lax.ppermute(value, axis, [(source, source + steps) for source in range(l...  7.2 us
    unnamed x60, local copies, waits for them, and re-layouts  6.51 us
    ppermute x7, waiting for transfers between devices, reduce_weight_grad(): lax.ppermute(mine, 'dp', [(i, (i + shift) % dp) for i in range(dp)])  5.77 us
    dot_general x3, matrix products, per_device(): jnp.dot(patch, conv_weight[kt * 9 * cc:(kt + 1) * 9 * cc], preferred_elem...  4.35 us
    dot_general x3, matrix products, per_device(): jnp.dot(patch, flipped, preferred_element_type=jnp.float32)  3.04 us
  transfers between devices with their start and end apart: 10, of which 2 were waited for; matrix products, arithmetic and copies ran while one was open for 12% of the time, Pallas kernels for 0%

profile of v2, /device:TPU:1, one launch (start us, length us, event | category | flops | bytes accessed | tf_op | source)
XLA Modules:
  0.0 85.1 jit_solution(1661052609490763106)
XLA Ops:
  0.6 1.0 %fusion.59 = (bf16[1,2,16,16,128]{4,3,2,1,0:T(8,128)(2,1)S(1)}, bf16[1,2,16,16,128]{4,3,2,1,0:T(8,128)(2,1)S(1)}) fusion(bf16[1,4,16,16,128]{4,3,2,1,0:T(8,128)(2,1)} %param.4), kind=kLoop, calls=%fused_computation.166 | loop fusion | bytes 524288 | tf_op jit(solution)/shard_map/slice | solution.py:47
  1.6 0.9 %slice.284 = bf16[1,2,16,16,128]{4,3,2,1,0:T(8,128)(2,1)S(1)} slice(bf16[1,4,16,16,128]{4,3,2,1,0:T(8,128)(2,1)} %param.7), slice={[0:1], [0:2], [0:16], [0:16], [0:128]} | slice | bytes 262144 | tf_op jit(solution)/shard_map/slice | solution.py:47
  2.6 5.3 %collective-permute-start.1 = (bf16[1,4,16,16,128]{4,3,2,1,0:T(8,128)(2,1)S(1)}, bf16[1,4,16,16,128]{4,3,2,1,0:T(8,128)(2,1)S(1)}, u32[]{:S(2)}, u32[]{:S(2)}) collective-permute-start(bf16[1,4,16,16,128]{4,3,2,1,0:T(8,128)(2,1)S(1)} %pad_maximum_fusion.4), channel_id=1, source_target_pairs={{1,0},{2,1},{3,2},{4,3},{5,4},{6,5},{7,6},{8,7},{9,8},{10,9},{11,1... | collective-permute-start | bytes 786440 | tf_op jit(solution)/shard_map/ppermute | solution.py:10
  7.9 1.9 %collective-permute-start = (bf16[1,2,16,16,128]{4,3,2,1,0:T(8,128)(2,1)S(1)}, bf16[1,2,16,16,128]{4,3,2,1,0:T(8,128)(2,1)S(1)}, u32[]{:S(2)}, u32[]{:S(2)}) collective-permute-start(bf16[1,2,16,16,128]{4,3,2,1,0:T(8,128)(2,1)S(1)} %get-tuple-element.23), channel_id=1, source_target_pairs={{0,1},{1,2},{2,3},{3,4},{4,5},{5,6},{6,7},{7,8},{8,9},{9,10},{10,1... | collective-permute-start | bytes 393224 | tf_op jit(solution)/shard_map/ppermute | solution.py:10
  9.8 0.7 pad_add_fusion
  10.7 1.2 %fusion.58 = (bf16[1152,128]{1,0:T(8,128)(2,1)S(1)}, bf16[1152,128]{1,0:T(8,128)(2,1)S(1)}, bf16[1152,128]{1,0:T(8,128)(2,1)S(1)}) fusion(bf16[3456,128]{1,0:T(8,128)(2,1)} %param.6), kind=kLoop, calls=%fused_computation.165 | loop fusion | bytes 1769472 | tf_op jit(solution)/shard_map/slice | solution.py:65
  12.0 0.2 copy.7
  12.2 0.2 copy.8
  12.4 0.2 copy.9
  13.0 0.2 fusion.21
  13.4 0.2 copy-done.2
  13.6 0.4 constant_dynamic-update-slice_fusion.2
  14.2 0.2 fusion.13
  14.7 0.2 fusion.15
  15.1 0.2 fusion.18
  15.5 0.2 fusion.5
  16.4 0.2 fusion.10
  16.6 0.2 slice.362
  16.8 1.0 %copy-done = bf16[3456,128]{1,0:T(8,128)(2,1)S(1)} copy-done((bf16[3456,128]{1,0:T(8,128)(2,1)S(1)}, bf16[3456,128]{1,0:T(8,128)(2,1)}, u32[]{:S(2)}) %copy-start) | copy-done | bytes 884760
  17.8 1.1 %fusion.50 = f32[1536,128]{1,0:T(8,128)S(1)} fusion(bf16[1536,1152]{1,0:T(8,128)(2,1)S(1)} %bitcast.77, bf16[3456,128]{1,0:T(8,128)(2,1)S(1)} %copy-done), kind=kOutput, calls=%fused_computation.157 | convolution fusion | flops 452984832 | bytes 4620288 | tf_op jit(solution)/shard_map/dot_general | solution.py:64
  18.9 0.2 fusion.23
  19.3 0.2 fusion.26
  19.5 0.2 slice.363
  19.7 0.2 slice.364
  19.9 1.1 %convolution_add_fusion.1 = f32[1536,128]{1,0:T(8,128)S(1)} fusion(f32[1536,128]{1,0:T(8,128)S(1)} %fusion.50, bf16[1536,1152]{1,0:T(8,128)(2,1)S(1)} %bitcast.76, bf16[3456,128]{1,0:T(8,128)(2,1)S(1)} %copy-done), kind=kOutput, calls=%fused_computation.2 | convolution fusion | flops 453181440 | bytes 5406720 | tf_op jit(solution)/shard_map/dot_general | solution.py:64
  21.0 2.2 %fusion.2 = (bf16[1536,128]{1,0:T(8,128)(2,1)S(1)}, f32[1536,128]{1,0:T(8,128)}) fusion(bf16[6,16,16,128]{3,2,1,0:T(8,128)(2,1)S(1)} %get-tuple-element.30, f32[1536,128]{1,0:T(8,128)S(1)} %convolution_add_fusion.1, bf16[1536,1152]{1,0:T(8,128)(2,1)S(1)} %bitcast.89, bf16[3456,128]{1,0:T(8,128)(2,1)S(1)} %copy-done), kind=kOutput, calls=%fused_computation.33 | convolution fusion | flops 455147520 | bytes 6193152 | tf_op jit(solution)/shard_map/dot_general | solution.py:64
  23.2 0.8 fusion.54
  24.0 0.8 fusion.56
  24.8 0.8 fusion.52
  25.8 1.4 %div.19 = f32[32,108,128]{2,1,0:T(8,128)} reshape(f32[3456,128]{1,0:T(8,128)S(1)} %maximum_multiply_fusion) | data formatting | bytes 3538944 | tf_op jit(solution)/shard_map/div | solution.py:83
  27.2 8.4 %all-to-all-start = ((f32[32,108,128]{2,1,0:T(8,128)}), f32[32,108,128]{2,1,0:T(8,128)S(1)}, u32[]{:S(2)}, u32[]{:S(2)}) async-start(f32[32,108,128]{2,1,0:T(8,128)} %div.19), calls=%async_computation | async-start | bytes 3670016 | tf_op jit(solution)/shard_map/all_to_all | solution.py:18
  35.6 0.3 pad_slice_fusion.24
  38.8 0.3 copy-done.3
  39.0 0.8 multiply_convert_fusion
  39.9 0.8 fusion.60
  40.7 0.8 convolution_add_fusion.3
  41.5 1.5 %fusion = bf16[1024,128]{1,0:T(8,128)(2,1)} fusion(f32[1024,128]{1,0:T(8,128)S(1)} %convolution_add_fusion.3, bf16[1024,1152]{1,0:T(8,128)(2,1)S(1)} %constant_dynamic-update-slice_fusion.5, bf16[1152,128]{1,0:T(8,128)(2,1)S(1)} %bitcast.90), kind=kOutput, calls=%fused_computation.6 | convolution fusion | flops 302252032 | bytes 3440640 | tf_op jit(solution)/shard_map/dot_general | solution.py:95
  42.9 18.2 %all-to-all-done = f32[32,108,128]{2,1,0:T(8,128)S(1)} async-done(((f32[32,108,128]{2,1,0:T(8,128)}), f32[32,108,128]{2,1,0:T(8,128)S(1)}, u32[]{:S(2)}, u32[]{:S(2)}) %all-to-all-start) | async-done | bytes 1769504 | tf_op jit(solution)/shard_map/all_to_all | solution.py:18
  61.2 1.7 %collective-permute-start.2 = (f32[108,128]{1,0:T(8,128)S(1)}, f32[108,128]{1,0:T(8,128)S(1)}, u32[]{:S(2)}, u32[]{:S(2)}) collective-permute-start(f32[108,128]{1,0:T(8,128)S(1)} %reduce_sum.9), channel_id=1, source_target_pairs={{0,32},{32,64},{64,96},{96,128},{128,160},{160,192},{192,224},{224... | collective-permute-start | bytes 165896 | tf_op jit(solution)/shard_map/ppermute | solution.py:20
  62.9 3.0 %collective-permute-start.3 = (f32[108,128]{1,0:T(8,128)S(1)}, f32[108,128]{1,0:T(8,128)S(1)}, u32[]{:S(2)}, u32[]{:S(2)}) collective-permute-start(f32[108,128]{1,0:T(8,128)S(1)} %reduce_sum.9), channel_id=1, source_target_pairs={{0,64},{32,96},{64,128},{96,160},{128,192},{160,224},{192,0},{224,... | collective-permute-start | bytes 165896 | tf_op jit(solution)/shard_map/ppermute | solution.py:20
  65.9 3.8 %collective-permute-start.4 = (f32[108,128]{1,0:T(8,128)S(1)}, f32[108,128]{1,0:T(8,128)S(1)}, u32[]{:S(2)}, u32[]{:S(2)}) collective-permute-start(f32[108,128]{1,0:T(8,128)S(1)} %reduce_sum.9), channel_id=1, source_target_pairs={{0,96},{32,128},{64,160},{96,192},{128,224},{160,0},{192,32},{224,... | collective-permute-start | bytes 165896 | tf_op jit(solution)/shard_map/ppermute | solution.py:20
  69.7 0.5 collective-permute-start.5
  70.1 4.5 %collective-permute-start.6 = (f32[108,128]{1,0:T(8,128)S(1)}, f32[108,128]{1,0:T(8,128)S(1)}, u32[]{:S(2)}, u32[]{:S(2)}) collective-permute-start(f32[108,128]{1,0:T(8,128)S(1)} %reduce_sum.9), channel_id=1, source_target_pairs={{0,160},{32,192},{64,224},{96,0},{128,32},{160,64},{192,96},{224,1... | collective-permute-start | bytes 165896 | tf_op jit(solution)/shard_map/ppermute | solution.py:20
  74.6 2.4 %collective-permute-start.7 = (f32[108,128]{1,0:T(8,128)S(1)}, f32[108,128]{1,0:T(8,128)S(1)}, u32[]{:S(2)}, u32[]{:S(2)}) collective-permute-start(f32[108,128]{1,0:T(8,128)S(1)} %reduce_sum.9), channel_id=1, source_target_pairs={{0,192},{32,224},{64,0},{96,32},{128,64},{160,96},{192,128},{224,1... | collective-permute-start | bytes 165896 | tf_op jit(solution)/shard_map/ppermute | solution.py:20
  77.0 0.8 collective-permute-start.8
  77.9 5.8 %collective-permute-done.7 = f32[108,128]{1,0:T(8,128)S(1)} collective-permute-done((f32[108,128]{1,0:T(8,128)S(1)}, f32[108,128]{1,0:T(8,128)S(1)}, u32[]{:S(2)}, u32[]{:S(2)}) %collective-permute-start.7) | collective-permute-done | bytes 55328 | tf_op jit(solution)/shard_map/ppermute | solution.py:20
  83.7 0.6 gather_fusion
  84.4 0.6 fusion.44
  (85 shorter events, 5.7 us)
Async XLA Ops:
  2.5 10.2 %copy-start.1 = (bf16[1,4,16,16,128]{4,3,2,1,0:T(8,128)(2,1)S(1)}, bf16[1,4,16,16,128]{4,3,2,1,0:T(8,128)(2,1)}, u32[]{:S(2)}) copy-start(bf16[1,4,16,16,128]{4,3,2,1,0:T(8,128)(2,1)} %param.4) | copy-start | bytes 786436
  2.6 10.1 %collective-permute-start.1 = (bf16[1,4,16,16,128]{4,3,2,1,0:T(8,128)(2,1)S(1)}, bf16[1,4,16,16,128]{4,3,2,1,0:T(8,128)(2,1)S(1)}, u32[]{:S(2)}, u32[]{:S(2)}) collective-permute-start(bf16[1,4,16,16,128]{4,3,2,1,0:T(8,128)(2,1)S(1)} %pad_maximum_fusion.4), channel_id=1, source_target_pairs={{1,0},{2,1},{3,2},{4,3},{5,4},{6,5},{7,6},{8,7},{9,8},{10,9},{11,1... | collective-permute-start | bytes 786440 | tf_op jit(solution)/shard_map/ppermute | solution.py:10
  7.9 5.5 %collective-permute-start = (bf16[1,2,16,16,128]{4,3,2,1,0:T(8,128)(2,1)S(1)}, bf16[1,2,16,16,128]{4,3,2,1,0:T(8,128)(2,1)S(1)}, u32[]{:S(2)}, u32[]{:S(2)}) collective-permute-start(bf16[1,2,16,16,128]{4,3,2,1,0:T(8,128)(2,1)S(1)} %get-tuple-element.23), channel_id=1, source_target_pairs={{0,1},{1,2},{2,3},{3,4},{4,5},{5,6},{6,7},{7,8},{8,9},{9,10},{10,1... | collective-permute-start | bytes 393224 | tf_op jit(solution)/shard_map/ppermute | solution.py:10
  12.6 1.0 %copy-start.2 = (bf16[1,4,16,16,128]{4,3,2,1,0:T(8,128)(2,1)S(1)}, bf16[1,4,16,16,128]{4,3,2,1,0:T(8,128)(2,1)}, u32[]{:S(2)}) copy-start(bf16[1,4,16,16,128]{4,3,2,1,0:T(8,128)(2,1)} %param.7) | copy-start | bytes 786436
  16.6 1.2 %copy-start = (bf16[3456,128]{1,0:T(8,128)(2,1)S(1)}, bf16[3456,128]{1,0:T(8,128)(2,1)}, u32[]{:S(2)}) copy-start(bf16[3456,128]{1,0:T(8,128)(2,1)} %param.6) | copy-start | bytes 2654212
  27.2 33.9 %all-to-all-start = ((f32[32,108,128]{2,1,0:T(8,128)}), f32[32,108,128]{2,1,0:T(8,128)S(1)}, u32[]{:S(2)}, u32[]{:S(2)}) async-start(f32[32,108,128]{2,1,0:T(8,128)} %div.19), calls=%async_computation | async-start | bytes 3670016 | tf_op jit(solution)/shard_map/all_to_all | solution.py:18
  37.9 1.1 %copy-start.3 = (f32[1536,128]{1,0:T(8,128)S(1)}, f32[1536,128]{1,0:T(8,128)}, u32[]{:S(2)}) copy-start(f32[1536,128]{1,0:T(8,128)} %get-tuple-element.29) | copy-start | bytes 2359300
  61.2 13.4 %collective-permute-start.2 = (f32[108,128]{1,0:T(8,128)S(1)}, f32[108,128]{1,0:T(8,128)S(1)}, u32[]{:S(2)}, u32[]{:S(2)}) collective-permute-start(f32[108,128]{1,0:T(8,128)S(1)} %reduce_sum.9), channel_id=1, source_target_pairs={{0,32},{32,64},{64,96},{96,128},{128,160},{160,192},{192,224},{224... | collective-permute-start | bytes 165896 | tf_op jit(solution)/shard_map/ppermute | solution.py:20
  62.9 14.1 %collective-permute-start.3 = (f32[108,128]{1,0:T(8,128)S(1)}, f32[108,128]{1,0:T(8,128)S(1)}, u32[]{:S(2)}, u32[]{:S(2)}) collective-permute-start(f32[108,128]{1,0:T(8,128)S(1)} %reduce_sum.9), channel_id=1, source_target_pairs={{0,64},{32,96},{64,128},{96,160},{128,192},{160,224},{192,0},{224,... | collective-permute-start | bytes 165896 | tf_op jit(solution)/shard_map/ppermute | solution.py:20
  65.9 11.9 %collective-permute-start.4 = (f32[108,128]{1,0:T(8,128)S(1)}, f32[108,128]{1,0:T(8,128)S(1)}, u32[]{:S(2)}, u32[]{:S(2)}) collective-permute-start(f32[108,128]{1,0:T(8,128)S(1)} %reduce_sum.9), channel_id=1, source_target_pairs={{0,96},{32,128},{64,160},{96,192},{128,224},{160,0},{192,32},{224,... | collective-permute-start | bytes 165896 | tf_op jit(solution)/shard_map/ppermute | solution.py:20
  69.7 8.2 %collective-permute-start.5 = (f32[108,128]{1,0:T(8,128)S(1)}, f32[108,128]{1,0:T(8,128)S(1)}, u32[]{:S(2)}, u32[]{:S(2)}) collective-permute-start(f32[108,128]{1,0:T(8,128)S(1)} %reduce_sum.9), channel_id=1, source_target_pairs={{0,128},{32,160},{64,192},{96,224},{128,0},{160,32},{192,64},{224,... | collective-permute-start | bytes 165896 | tf_op jit(solution)/shard_map/ppermute | solution.py:20
  70.1 7.7 %collective-permute-start.6 = (f32[108,128]{1,0:T(8,128)S(1)}, f32[108,128]{1,0:T(8,128)S(1)}, u32[]{:S(2)}, u32[]{:S(2)}) collective-permute-start(f32[108,128]{1,0:T(8,128)S(1)} %reduce_sum.9), channel_id=1, source_target_pairs={{0,160},{32,192},{64,224},{96,0},{128,32},{160,64},{192,96},{224,1... | collective-permute-start | bytes 165896 | tf_op jit(solution)/shard_map/ppermute | solution.py:20
  74.6 9.0 %collective-permute-start.7 = (f32[108,128]{1,0:T(8,128)S(1)}, f32[108,128]{1,0:T(8,128)S(1)}, u32[]{:S(2)}, u32[]{:S(2)}) collective-permute-start(f32[108,128]{1,0:T(8,128)S(1)} %reduce_sum.9), channel_id=1, source_target_pairs={{0,192},{32,224},{64,0},{96,32},{128,64},{160,96},{192,128},{224,1... | collective-permute-start | bytes 165896 | tf_op jit(solution)/shard_map/ppermute | solution.py:20
  77.0 6.6 %collective-permute-start.8 = (f32[108,128]{1,0:T(8,128)S(1)}, f32[108,128]{1,0:T(8,128)S(1)}, u32[]{:S(2)}, u32[]{:S(2)}) collective-permute-start(f32[108,128]{1,0:T(8,128)S(1)} %reduce_sum.9), channel_id=1, source_target_pairs={{0,224},{32,0},{64,32},{96,64},{128,96},{160,128},{192,160},{224,1... | collective-permute-start | bytes 165896 | tf_op jit(solution)/shard_map/ppermute | solution.py:20

commit v3 on v2

--- a/solution.py
+++ b/solution.py
@@ -1,7 +1,9 @@
 import jax
 import jax.numpy as jnp
 from jax import lax
-from jax.sharding import PartitionSpec as P
+from jax.sharding import Mesh, PartitionSpec as P
+
+TM = ("chip", "core")
 
 
 def from_behind(value, axis, steps):
@@ -11,20 +13,21 @@
 
 
 def reduce_weight_grad(grad_local):
-    tm = lax.axis_size("tm")
+    chips = lax.axis_size("chip")
+    cores = lax.axis_size("core")
     dp = lax.axis_size("dp")
     rows, cols = grad_local.shape
-    blocks = grad_local.reshape(tm, rows // tm, cols)
-    mine = lax.all_to_all(blocks, "tm", 0, 0, tiled=True).sum(axis=0)
-    received = [mine] + [
-        lax.ppermute(mine, "dp", [(i, (i + shift) % dp) for i in range(dp)]) for shift in range(1, dp)
-    ]
-    stacked = jnp.stack(received)
-    me = lax.axis_index("dp")
-    ordered = jnp.take(stacked, (me - jnp.arange(dp)) % dp, axis=0)
-    while ordered.shape[0] > 1:
-        ordered = ordered[0::2] + ordered[1::2]
-    return ordered[0]
+    blocks = grad_local.reshape(chips, cores, rows // (chips * cores), cols)
+    core = lax.axis_index("core")
+    mine = jnp.where(core == 0, blocks[:, 0], blocks[:, 1])
+    other = jnp.where(core == 0, blocks[:, 1], blocks[:, 0])
+    mine = mine + lax.ppermute(other, "core", [(0, 1), (1, 0)])
+    mine = lax.all_to_all(mine, "chip", 0, 0, tiled=True).sum(axis=0)
+    step = 1
+    while step < dp:
+        mine = mine + lax.ppermute(mine, "dp", [(i, i ^ step) for i in range(dp)])
+        step *= 2
+    return mine
 
 
 def im2col(frames, offset, hh, ww):
@@ -43,13 +46,13 @@
     ww = clips.shape[3]
     cc = clips.shape[4]
     rows = nfr * hh * ww
-    earlier = from_behind(clips[:, nfr - 2 :], "tm", 1)[0]
-    ahead = from_behind(jnp.concatenate([clips[:, :2], cotangent[:, :2]], axis=1), "tm", -1)[0]
+    earlier = from_behind(clips[:, nfr - 2 :], TM, 1)[0]
+    ahead = from_behind(jnp.concatenate([clips[:, :2], cotangent[:, :2]], axis=1), TM, -1)[0]
     frames = jnp.concatenate([earlier, clips[0], ahead[:2]], axis=0)
     cot_ext = jnp.concatenate([cotangent[0], ahead[2:]], axis=0)
     segrow = segment_ids[0]
     segp = jnp.concatenate([jnp.full((2,), -1, jnp.int32), segrow, jnp.full((2,), -2, jnp.int32)])
-    start = lax.axis_index("tm") * nfr
+    start = (lax.axis_index("chip") * lax.axis_size("core") + lax.axis_index("core")) * nfr
     seglocal = lax.dynamic_slice_in_dim(segp, start, nfr + 4, 0)
     nout = nfr + 2
     centre = seglocal[2 : 2 + nout]
@@ -70,7 +73,7 @@
         cot_ext.reshape(nout * hh * ww, cc).astype(jnp.float32) * sig * (1.0 + pre * (1.0 - sig))
     ).astype(jnp.bfloat16)
     own_grad = grad_pre[:rows]
-    count = lax.axis_size("dp") * lax.axis_size("tm") * rows
+    count = lax.axis_size("dp") * (lax.axis_size("chip") * lax.axis_size("core")) * rows
     grad_local = jnp.concatenate(
         [
             lax.dot_general(
@@ -80,7 +83,6 @@
         ],
         axis=0,
     )
-    grad_local = grad_local / jnp.sqrt(jnp.float32(count))
     grad_ext = grad_pre.reshape(nout, hh, ww, cc)
     own = seglocal[2 : 2 + nfr]
     summed = jnp.zeros((rows, cc), jnp.float32)
@@ -94,20 +96,23 @@
         flipped = jnp.swapaxes(block, 1, 2).reshape(9 * cc, cc)
         summed = summed + jnp.dot(patch, flipped, preferred_element_type=jnp.float32)
     grad_clips = summed.astype(jnp.bfloat16).reshape(clips.shape)
-    grad_weight = reduce_weight_grad(grad_local)
+    grad_weight = reduce_weight_grad(grad_local) / jnp.sqrt(jnp.float32(count))
     return (activated, grad_clips, grad_weight)
 
 
 def solution(mesh):
+    dp, tm = mesh.devices.shape
+    cores = 2 if tm % 2 == 0 else 1
+    split = Mesh(mesh.devices.reshape(dp, tm // cores, cores), ("dp", "chip", "core"))
     return jax.shard_map(
         per_device,
-        mesh=mesh,
+        mesh=split,
         in_specs=(
-            P("dp", "tm", None, None, None),
+            P("dp", TM, None, None, None),
             P("dp", None),
             P(),
-            P("dp", "tm", None, None, None),
+            P("dp", TM, None, None, None),
         ),
-        out_specs=(P("dp", "tm", None, None, None), P("dp", "tm", None, None, None), P("tm", None)),
+        out_specs=(P("dp", TM, None, None, None), P("dp", TM, None, None, None), P(TM, None)),
         check_vma=False,
     )

time: 85.5 us -> 84.4 us (0.987)
  the two profiles are of different devices: /device:TPU:1 before, /device:TPU:8 now
where the time goes in v3:
time: 84.4 us; the launch traced here: 83.9 us
  starting transfers between devices  26 us (31%)
  local copies, waits for them, and re-layouts  23.2 us (27%)
  waiting for transfers between devices  14.7 us (17%)
  matrix products  13.4 us (16%)
  other arithmetic  5.41 us (6%)
  between operations  1.2 us (1%)
    unnamed x67, local copies, waits for them, and re-layouts  13.7 us
    ppermute x3, starting transfers between devices, reduce_weight_grad(): mine = mine + lax.ppermute(mine, 'dp', [(i, i ^ step) for i in range(dp)])  12.4 us
    all_to_all x1, waiting for transfers between devices, reduce_weight_grad(): mine = lax.all_to_all(mine, 'chip', 0, 0, tiled=True).sum(axis=0)  10.4 us
    all_to_all x1, starting transfers between devices, reduce_weight_grad(): mine = lax.all_to_all(mine, 'chip', 0, 0, tiled=True).sum(axis=0)  8.79 us
    dot_general x3, matrix products, per_device(): jnp.dot(patch, flipped, preferred_element_type=jnp.float32)  6.59 us
    ppermute x2, starting transfers between devices, from_behind(): lax.ppermute(value, axis, [(source, source + steps) for source in range(l...  4.46 us
    dot_general x3, matrix products, per_device(): jnp.dot(patch, conv_weight[kt * 9 * cc:(kt + 1) * 9 * cc], preferred_elem...  4.41 us
    ppermute x3, waiting for transfers between devices, reduce_weight_grad(): mine = mine + lax.ppermute(mine, 'dp', [(i, i ^ step) for i in range(dp)])  2.84 us
  transfers between devices with their start and end apart: 7, of which 4 were waited for; matrix products, arithmetic and copies ran while one was open for 24% of the time, Pallas kernels for 0%

profile of v3, /device:TPU:8, one launch (start us, length us, event | category | flops | bytes accessed | tf_op | source)
XLA Modules:
  0.0 83.9 jit_solution(13774542428686360831)
XLA Ops:
  0.6 1.0 %fusion.55 = (bf16[1,2,16,16,128]{4,3,2,1,0:T(8,128)(2,1)S(1)}, bf16[1,2,16,16,128]{4,3,2,1,0:T(8,128)(2,1)S(1)}) fusion(bf16[1,4,16,16,128]{4,3,2,1,0:T(8,128)(2,1)} %param.4), kind=kLoop, calls=%fused_computation.142 | loop fusion | bytes 524288 | tf_op jit(solution)/shard_map/slice | solution.py:50
  1.6 0.9 %slice.272 = bf16[1,2,16,16,128]{4,3,2,1,0:T(8,128)(2,1)S(1)} slice(bf16[1,4,16,16,128]{4,3,2,1,0:T(8,128)(2,1)} %param.7), slice={[0:1], [0:2], [0:16], [0:16], [0:128]} | slice | bytes 262144 | tf_op jit(solution)/shard_map/slice | solution.py:50
  2.6 2.1 %collective-permute-start.1 = (bf16[1,4,16,16,128]{4,3,2,1,0:T(8,128)(2,1)S(1)}, bf16[1,4,16,16,128]{4,3,2,1,0:T(8,128)(2,1)S(1)}, u32[]{:S(2)}, u32[]{:S(2)}) collective-permute-start(bf16[1,4,16,16,128]{4,3,2,1,0:T(8,128)(2,1)S(1)} %pad_maximum_fusion.5), channel_id=1, source_target_pairs={{1,0},{2,1},{3,2},{4,3},{5,4},{6,5},{7,6},{8,7},{9,8},{10,9},{11,1... | collective-permute-start | bytes 786440 | tf_op jit(solution)/shard_map/ppermute | solution.py:12
  4.7 2.4 %collective-permute-start = (bf16[1,2,16,16,128]{4,3,2,1,0:T(8,128)(2,1)S(1)}, bf16[1,2,16,16,128]{4,3,2,1,0:T(8,128)(2,1)S(1)}, u32[]{:S(2)}, u32[]{:S(2)}) collective-permute-start(bf16[1,2,16,16,128]{4,3,2,1,0:T(8,128)(2,1)S(1)} %get-tuple-element.23), channel_id=1, source_target_pairs={{0,1},{1,2},{2,3},{3,4},{4,5},{5,6},{6,7},{7,8},{8,9},{9,10},{10,1... | collective-permute-start | bytes 393224 | tf_op jit(solution)/shard_map/ppermute | solution.py:12
  7.1 1.2 %fusion.54 = (bf16[1152,128]{1,0:T(8,128)(2,1)S(1)}, bf16[1152,128]{1,0:T(8,128)(2,1)S(1)}, bf16[1152,128]{1,0:T(8,128)(2,1)S(1)}) fusion(bf16[3456,128]{1,0:T(8,128)(2,1)} %param.6), kind=kLoop, calls=%fused_computation.141 | loop fusion | bytes 1769472 | tf_op jit(solution)/shard_map/slice | solution.py:68
  8.5 0.2 copy.22
  8.8 0.2 copy.23
  9.0 0.2 copy.24
  10.0 1.5 %collective-permute-done = bf16[1,2,16,16,128]{4,3,2,1,0:T(8,128)(2,1)S(1)} collective-permute-done((bf16[1,2,16,16,128]{4,3,2,1,0:T(8,128)(2,1)S(1)}, bf16[1,2,16,16,128]{4,3,2,1,0:T(8,128)(2,1)S(1)}, u32[]{:S(2)}, u32[]{:S(2)}) %collective-permute-start) | collective-permute-done | bytes 131104 | tf_op jit(solution)/shard_map/ppermute | solution.py:12
  11.5 0.4 constant_dynamic-update-slice_fusion.2
  14.7 1.0 %copy-done.3 = bf16[3456,128]{1,0:T(8,128)(2,1)S(1)} copy-done((bf16[3456,128]{1,0:T(8,128)(2,1)S(1)}, bf16[3456,128]{1,0:T(8,128)(2,1)}, u32[]{:S(2)}) %copy-start.3) | copy-done | bytes 884760
  15.7 1.1 %fusion.46 = f32[1536,128]{1,0:T(8,128)S(1)} fusion(bf16[1536,1152]{1,0:T(8,128)(2,1)S(1)} %bitcast.61, bf16[3456,128]{1,0:T(8,128)(2,1)S(1)} %copy-done.3), kind=kOutput, calls=%fused_computation.133 | convolution fusion | flops 452984832 | bytes 4620288 | tf_op jit(solution)/shard_map/dot_general | solution.py:67
  17.8 1.1 %convolution_add_fusion.1 = f32[1536,128]{1,0:T(8,128)S(1)} fusion(f32[1536,128]{1,0:T(8,128)S(1)} %fusion.46, bf16[1536,1152]{1,0:T(8,128)(2,1)S(1)} %bitcast.60, bf16[3456,128]{1,0:T(8,128)(2,1)S(1)} %copy-done.3), kind=kOutput, calls=%fused_computation.1 | convolution fusion | flops 453181440 | bytes 5406720 | tf_op jit(solution)/shard_map/dot_general | solution.py:67
  19.0 2.2 %fusion.2 = (bf16[1536,128]{1,0:T(8,128)(2,1)S(1)}, f32[1536,128]{1,0:T(8,128)}) fusion(bf16[6,16,16,128]{3,2,1,0:T(8,128)(2,1)S(1)} %get-tuple-element.30, f32[1536,128]{1,0:T(8,128)S(1)} %convolution_add_fusion.1, bf16[1536,1152]{1,0:T(8,128)(2,1)S(1)} %bitcast.73, bf16[3456,128]{1,0:T(8,128)(2,1)S(1)} %copy-done.3), kind=kOutput, calls=%fused_computation.34 | convolution fusion | flops 455147520 | bytes 6193152 | tf_op jit(solution)/shard_map/dot_general | solution.py:67
  21.2 0.7 slice.343
  21.9 0.8 fusion.50
  22.7 0.8 fusion.52
  23.5 0.8 fusion.48
  24.3 1.4 %pad_maximum_fusion = f32[3456,128]{1,0:T(8,128)} fusion(f32[1152,128]{1,0:T(8,128)S(1)} %fusion.48, f32[1152,128]{1,0:T(8,128)S(1)} %fusion.50, f32[1152,128]{1,0:T(8,128)S(1)} %fusion.52), kind=kLoop, calls=%fused_computation.2 | loop fusion | flops 884736 | bytes 3538944 | tf_op jit(solution)/shard_map/concatenate | solution.py:77
  25.7 1.5 %reshape.92 = f32[16,2,108,128]{3,2,1,0:T(8,128)S(1)} reshape(f32[3456,128]{1,0:T(8,128)} %pad_maximum_fusion) | data formatting | bytes 3538944 | tf_op jit(solution)/shard_map/reshape | solution.py:20
  27.3 0.3 copy.25
  27.6 0.3 collective-permute-start.2
  27.9 0.3 copy-done.7
  28.1 1.1 %pad_slice_fusion.24 = (bf16[4,16,16,128]{3,2,1,0:T(8,128)(2,1)S(1)}, bf16[4,16,16,128]{3,2,1,0:T(8,128)(2,1)S(1)}, bf16[4,16,16,128]{3,2,1,0:T(8,128)(2,1)S(1)}...) fusion(bf16[4,16,16,128]{3,2,1,0:T(8,128)(2,1)S(1)} %bitcast.84), kind=kLoop, calls=%fused_computation.35 | loop fusion | bytes 2359296 | tf_op jit(solution)/shard_map/slice | solution.py:36
  29.2 0.8 constant_dynamic-update-slice_fusion.13
  30.0 0.7 constant_dynamic-update-slice_fusion.12
  30.7 0.7 constant_dynamic-update-slice_fusion.11
  31.4 0.7 constant_dynamic-update-slice_fusion.10
  32.2 0.8 %constant_dynamic-update-slice_fusion.9 = (bf16[1024,1152]{1,0:T(8,128)(2,1)}, bf16[1024,128]{1,0:T(8,128)(2,1)S(1)}, bf16[1024,128]{1,0:T(8,128)(2,1)S(1)}) fusion(bf16[1024,1152]{1,0:T(8,128)(2,1)} %constant_dynamic-update-slice_fusion.10, bf16[1536,128]{1,0:T(8,128)(2,1)S(1)} %get-tuple-element.28), kind=kLoop, calls=%fused_computation.120 | loop fusion | bytes 1572864
  35.0 0.5 copy-done
  35.6 1.4 %copy-done.2 = bf16[4,16,16,1152]{3,2,1,0:T(8,128)(2,1)} copy-done((bf16[4,16,16,1152]{3,2,1,0:T(8,128)(2,1)}, bf16[4,16,16,1152]{3,2,1,0:T(8,128)(2,1)S(1)}, u32[]{:S(2)}) %copy-start.2) | copy-done | bytes 2359320
  37.1 0.7 constant_dynamic-update-slice_fusion.8
  37.8 1.3 %bitcast_add_fusion = f32[16,108,128]{2,1,0:T(8,128)} fusion(f32[16,108,128]{2,0,1:T(8,128)S(1)} %collective-permute-done.2, f32[16,2,108,128]{3,2,1,0:T(8,128)S(1)} %reshape.92, pred[]{:T(512)S(6)} %eq.22), kind=kLoop, calls=%fused_computation.30 | loop fusion | flops 442368 | bytes 3538945 | tf_op jit(solution)/shard_map/add | solution.py:24
  39.1 8.8 %all-to-all-start = ((f32[16,108,128]{2,1,0:T(8,128)}), f32[16,108,128]{2,1,0:T(8,128)S(1)}, u32[]{:S(2)}, u32[]{:S(2)}) async-start(f32[16,108,128]{2,1,0:T(8,128)} %bitcast_add_fusion), calls=%async_computation | async-start | bytes 1835008 | tf_op jit(solution)/shard_map/all_to_all | solution.py:25
  47.9 0.8 constant_dynamic-update-slice_fusion.7
  48.6 0.8 constant_dynamic-update-slice_fusion.6
  49.4 2.6 %fusion.56 = f32[1024,128]{1,0:T(8,128)S(1)} fusion(bf16[1024,1152]{1,0:T(8,128)(2,1)} %bitcast.66, bf16[1152,128]{1,0:T(8,128)(2,1)S(1)} %bitcast.79), kind=kOutput, calls=%fused_computation.143 | convolution fusion | flops 301989888 | bytes 3178496 | tf_op jit(solution)/shard_map/dot_general | solution.py:97
  52.0 0.8 convolution_add_fusion.3
  52.8 10.4 %all-to-all-done = f32[16,108,128]{2,1,0:T(8,128)S(1)} async-done(((f32[16,108,128]{2,1,0:T(8,128)}), f32[16,108,128]{2,1,0:T(8,128)S(1)}, u32[]{:S(2)}, u32[]{:S(2)}) %all-to-all-start) | async-done | bytes 884768 | tf_op jit(solution)/shard_map/all_to_all | solution.py:25
  63.2 2.0 %collective-permute-start.3 = (f32[108,128]{1,0:T(8,128)S(1)}, f32[108,128]{1,0:T(8,128)S(1)}, u32[]{:S(2)}, u32[]{:S(2)}) collective-permute-start(f32[108,128]{1,0:T(8,128)S(1)} %reduce_sum.9), channel_id=1, source_target_pairs={{0,32},{32,0},{64,96},{96,64},{128,160},{160,128},{192,224},{224,1... | collective-permute-start | bytes 165896 | tf_op jit(solution)/shard_map/ppermute | solution.py:28
  65.2 0.7 constant_dynamic-update-slice_fusion.5
  65.9 1.5 %collective-permute-done.3 = f32[108,128]{1,0:T(8,128)S(1)} collective-permute-done((f32[108,128]{1,0:T(8,128)S(1)}, f32[108,128]{1,0:T(8,128)S(1)}, u32[]{:S(2)}, u32[]{:S(2)}) %collective-permute-start.3) | collective-permute-done | bytes 55328 | tf_op jit(solution)/shard_map/ppermute | solution.py:28
  67.5 3.6 %collective-permute-start.4 = (f32[108,128]{1,0:T(8,128)S(1)}, f32[108,128]{1,0:T(8,128)S(1)}, u32[]{:S(2)}, u32[]{:S(2)}) collective-permute-start(f32[108,128]{1,0:T(8,128)S(1)} %add.62), channel_id=1, source_target_pairs={{0,64},{32,96},{64,0},{96,32},{128,192},{160,224},{192,128},{224,1... | collective-permute-start | bytes 165896 | tf_op jit(solution)/shard_map/ppermute | solution.py:28
  71.1 3.2 %fusion = bf16[1024,128]{1,0:T(8,128)(2,1)} fusion(f32[1024,128]{1,0:T(8,128)S(1)} %convolution_add_fusion.3, bf16[1024,1152]{1,0:T(8,128)(2,1)} %constant_dynamic-update-slice_fusion.5, bf16[1152,128]{1,0:T(8,128)(2,1)S(1)} %bitcast.74), kind=kOutput, calls=%fused_computation.5 | convolution fusion | flops 302252032 | bytes 3440640 | tf_op jit(solution)/shard_map/dot_general | solution.py:97
  74.3 6.8 %collective-permute-start.5 = (f32[108,128]{1,0:T(8,128)S(1)}, f32[108,128]{1,0:T(8,128)S(1)}, u32[]{:S(2)}, u32[]{:S(2)}) collective-permute-start(f32[108,128]{1,0:T(8,128)S(1)} %add.63), channel_id=1, source_target_pairs={{0,128},{32,160},{64,192},{96,224},{128,0},{160,32},{192,64},{224,... | collective-permute-start | bytes 165896 | tf_op jit(solution)/shard_map/ppermute | solution.py:28
  81.2 0.8 %multiply_convert_fusion = bf16[1024,128]{1,0:T(8,128)(2,1)} fusion(f32[1536,128]{1,0:T(8,128)S(1)} %copy-done.9), kind=kLoop, calls=%fused_computation.59 | loop fusion | flops 655360 | bytes 786432 | tf_op jit(solution)/shard_map/convert_element_type | solution.py:71
  82.0 1.3 %collective-permute-done.5 = f32[108,128]{1,0:T(8,128)S(1)} collective-permute-done((f32[108,128]{1,0:T(8,128)S(1)}, f32[108,128]{1,0:T(8,128)S(1)}, u32[]{:S(2)}, u32[]{:S(2)}) %collective-permute-start.5) | collective-permute-done | bytes 55328 | tf_op jit(solution)/shard_map/ppermute | solution.py:28
  83.3 0.6 add_multiply_fusion
  (83 shorter events, 6.8 us)
Async XLA Ops:
  0.6 7.7 %copy-start.10 = (s32[1,128]{1,0:T(1,128)S(1)}, s32[1,128]{1,0:T(1,128)}, u32[]{:S(2)}) copy-start(s32[1,128]{1,0:T(1,128)} %param.5) | copy-start | bytes 1540
  2.6 6.8 %copy-start.4 = (bf16[1,4,16,16,128]{4,3,2,1,0:T(8,128)(2,1)S(1)}, bf16[1,4,16,16,128]{4,3,2,1,0:T(8,128)(2,1)}, u32[]{:S(2)}) copy-start(bf16[1,4,16,16,128]{4,3,2,1,0:T(8,128)(2,1)} %param.4) | copy-start | bytes 786436
  2.6 6.7 %collective-permute-start.1 = (bf16[1,4,16,16,128]{4,3,2,1,0:T(8,128)(2,1)S(1)}, bf16[1,4,16,16,128]{4,3,2,1,0:T(8,128)(2,1)S(1)}, u32[]{:S(2)}, u32[]{:S(2)}) collective-permute-start(bf16[1,4,16,16,128]{4,3,2,1,0:T(8,128)(2,1)S(1)} %pad_maximum_fusion.5), channel_id=1, source_target_pairs={{1,0},{2,1},{3,2},{4,3},{5,4},{6,5},{7,6},{8,7},{9,8},{10,9},{11,1... | collective-permute-start | bytes 786440 | tf_op jit(solution)/shard_map/ppermute | solution.py:12
  4.7 6.8 %collective-permute-start = (bf16[1,2,16,16,128]{4,3,2,1,0:T(8,128)(2,1)S(1)}, bf16[1,2,16,16,128]{4,3,2,1,0:T(8,128)(2,1)S(1)}, u32[]{:S(2)}, u32[]{:S(2)}) collective-permute-start(bf16[1,2,16,16,128]{4,3,2,1,0:T(8,128)(2,1)S(1)} %get-tuple-element.23), channel_id=1, source_target_pairs={{0,1},{1,2},{2,3},{3,4},{4,5},{5,6},{6,7},{7,8},{8,9},{9,10},{10,1... | collective-permute-start | bytes 393224 | tf_op jit(solution)/shard_map/ppermute | solution.py:12
  9.2 2.3 %copy-start.8 = (bf16[1,4,16,16,128]{4,3,2,1,0:T(8,128)(2,1)S(1)}, bf16[1,4,16,16,128]{4,3,2,1,0:T(8,128)(2,1)}, u32[]{:S(2)}) copy-start(bf16[1,4,16,16,128]{4,3,2,1,0:T(8,128)(2,1)} %param.7) | copy-start | bytes 786436
  14.5 1.2 %copy-start.3 = (bf16[3456,128]{1,0:T(8,128)(2,1)S(1)}, bf16[3456,128]{1,0:T(8,128)(2,1)}, u32[]{:S(2)}) copy-start(bf16[3456,128]{1,0:T(8,128)(2,1)} %param.6) | copy-start | bytes 2654212
  27.2 1.0 %copy-start.7 = (bf16[1024,128]{1,0:T(8,128)(2,1)S(1)}, bf16[1024,128]{1,0:T(8,128)(2,1)}, u32[]{:S(2)}) copy-start(bf16[1024,128]{1,0:T(8,128)(2,1)} %slice.343) | copy-start | bytes 786436
  27.6 10.2 %collective-permute-start.2 = (f32[16,108,128]{2,0,1:T(8,128)S(1)}, f32[16,108,128]{2,0,1:T(8,128)S(1)}, u32[]{:S(2)}, u32[]{:S(2)}) collective-permute-start(f32[16,108,128]{2,0,1:T(8,128)S(1)} %copy.25), channel_id=1, source_target_pairs={{0,1},{1,0},{2,3},{3,2},{4,5},{5,4},{6,7},{7,6},{8,9},{9,8},{10,11... | collective-permute-start | bytes 2654216 | tf_op jit(solution)/shard_map/ppermute | solution.py:24
  34.1 1.4 %copy-start = (bf16[4,16,16,1152]{3,2,1,0:T(8,128)(2,1)}, bf16[4,16,16,1152]{3,2,1,0:T(8,128)(2,1)S(1)}, u32[]{:S(2)}) copy-start(bf16[4,16,16,1152]{3,2,1,0:T(8,128)(2,1)S(1)} %fusion.43) | copy-start | bytes 7077892
  35.6 1.4 %copy-start.2 = (bf16[4,16,16,1152]{3,2,1,0:T(8,128)(2,1)}, bf16[4,16,16,1152]{3,2,1,0:T(8,128)(2,1)S(1)}, u32[]{:S(2)}) copy-start(bf16[4,16,16,1152]{3,2,1,0:T(8,128)(2,1)S(1)} %fusion.35) | copy-start | bytes 7077892
  37.8 10.1 %copy-start.6 = (bf16[4,16,16,128]{3,2,1,0:T(8,128)(2,1)S(1)}, bf16[4,16,16,128]{3,2,1,0:T(8,128)(2,1)}, u32[]{:S(2)}) copy-start(bf16[4,16,16,128]{3,2,1,0:T(8,128)(2,1)} %get-tuple-element.17) | copy-start | bytes 786436
  37.8 10.8 %copy-start.5 = (bf16[4,16,16,128]{3,2,1,0:T(8,128)(2,1)S(1)}, bf16[4,16,16,128]{3,2,1,0:T(8,128)(2,1)}, u32[]{:S(2)}) copy-start(bf16[4,16,16,128]{3,2,1,0:T(8,128)(2,1)} %get-tuple-element.18) | copy-start | bytes 786436
  39.1 24.1 %all-to-all-start = ((f32[16,108,128]{2,1,0:T(8,128)}), f32[16,108,128]{2,1,0:T(8,128)S(1)}, u32[]{:S(2)}, u32[]{:S(2)}) async-start(f32[16,108,128]{2,1,0:T(8,128)} %bitcast_add_fusion), calls=%async_computation | async-start | bytes 1835008 | tf_op jit(solution)/shard_map/all_to_all | solution.py:25
  49.4 2.6 %copy-start.1 = (bf16[4,16,16,1152]{3,2,1,0:T(8,128)(2,1)S(1)}, bf16[4,16,16,1152]{3,2,1,0:T(8,128)(2,1)}, u32[]{:S(2)}) copy-start(bf16[4,16,16,1152]{3,2,1,0:T(8,128)(2,1)} %copy-done) | copy-start | bytes 7077892
  63.2 4.3 %collective-permute-start.3 = (f32[108,128]{1,0:T(8,128)S(1)}, f32[108,128]{1,0:T(8,128)S(1)}, u32[]{:S(2)}, u32[]{:S(2)}) collective-permute-start(f32[108,128]{1,0:T(8,128)S(1)} %reduce_sum.9), channel_id=1, source_target_pairs={{0,32},{32,0},{64,96},{96,64},{128,160},{160,128},{192,224},{224,1... | collective-permute-start | bytes 165896 | tf_op jit(solution)/shard_map/ppermute | solution.py:28
  67.5 6.8 %collective-permute-start.4 = (f32[108,128]{1,0:T(8,128)S(1)}, f32[108,128]{1,0:T(8,128)S(1)}, u32[]{:S(2)}, u32[]{:S(2)}) collective-permute-start(f32[108,128]{1,0:T(8,128)S(1)} %add.62), channel_id=1, source_target_pairs={{0,64},{32,96},{64,0},{96,32},{128,192},{160,224},{192,128},{224,1... | collective-permute-start | bytes 165896 | tf_op jit(solution)/shard_map/ppermute | solution.py:28
  71.1 10.1 %copy-start.9 = (f32[1536,128]{1,0:T(8,128)S(1)}, f32[1536,128]{1,0:T(8,128)}, u32[]{:S(2)}) copy-start(f32[1536,128]{1,0:T(8,128)} %get-tuple-element.29) | copy-start | bytes 2359300
  74.3 9.0 %collective-permute-start.5 = (f32[108,128]{1,0:T(8,128)S(1)}, f32[108,128]{1,0:T(8,128)S(1)}, u32[]{:S(2)}, u32[]{:S(2)}) collective-permute-start(f32[108,128]{1,0:T(8,128)S(1)} %add.63), channel_id=1, source_target_pairs={{0,128},{32,160},{64,192},{96,224},{128,0},{160,32},{192,64},{224,... | collective-permute-start | bytes 165896 | tf_op jit(solution)/shard_map/ppermute | solution.py:28

commit v4 on v3

--- a/solution.py
+++ b/solution.py
@@ -13,16 +13,11 @@
 
 
 def reduce_weight_grad(grad_local):
-    chips = lax.axis_size("chip")
-    cores = lax.axis_size("core")
+    tm = lax.axis_size("chip") * lax.axis_size("core")
     dp = lax.axis_size("dp")
     rows, cols = grad_local.shape
-    blocks = grad_local.reshape(chips, cores, rows // (chips * cores), cols)
-    core = lax.axis_index("core")
-    mine = jnp.where(core == 0, blocks[:, 0], blocks[:, 1])
-    other = jnp.where(core == 0, blocks[:, 1], blocks[:, 0])
-    mine = mine + lax.ppermute(other, "core", [(0, 1), (1, 0)])
-    mine = lax.all_to_all(mine, "chip", 0, 0, tiled=True).sum(axis=0)
+    blocks = grad_local.reshape(tm, rows // tm, cols)
+    mine = lax.all_to_all(blocks, TM, 0, 0, tiled=True).sum(axis=0)
     step = 1
     while step < dp:
         mine = mine + lax.ppermute(mine, "dp", [(i, i ^ step) for i in range(dp)])
@@ -48,15 +43,17 @@
     rows = nfr * hh * ww
     earlier = from_behind(clips[:, nfr - 2 :], TM, 1)[0]
     ahead = from_behind(jnp.concatenate([clips[:, :2], cotangent[:, :2]], axis=1), TM, -1)[0]
-    frames = jnp.concatenate([earlier, clips[0], ahead[:2]], axis=0)
+    blank = jnp.zeros((2, hh, ww, cc), clips.dtype)
+    frames = jnp.concatenate([blank, clips[0], blank], axis=0)
     cot_ext = jnp.concatenate([cotangent[0], ahead[2:]], axis=0)
     segrow = segment_ids[0]
     segp = jnp.concatenate([jnp.full((2,), -1, jnp.int32), segrow, jnp.full((2,), -2, jnp.int32)])
     start = (lax.axis_index("chip") * lax.axis_size("core") + lax.axis_index("core")) * nfr
     seglocal = lax.dynamic_slice_in_dim(segp, start, nfr + 4, 0)
     nout = nfr + 2
+    frame_rows = hh * ww
     centre = seglocal[2 : 2 + nout]
-    pre = jnp.zeros((nout * hh * ww, cc), jnp.float32)
+    pre = jnp.zeros((nout * frame_rows, cc), jnp.float32)
     patches = []
     for kt in range(3):
         moved = frames[kt : kt + nout]
@@ -67,6 +64,17 @@
         pre = pre + jnp.dot(
             patch, conv_weight[kt * 9 * cc : (kt + 1) * 9 * cc], preferred_element_type=jnp.float32
         )
+    halo = jnp.concatenate([earlier, ahead[:2]], axis=0)
+    halo_patch = im2col(halo, lambda k: k, hh, ww).reshape(4, frame_rows, 9 * cc)
+    terms = ((0, 0, 0), (0, 1, 1), (1, 1, 0), (nfr, 2, 2), (nfr + 1, 2, 1), (nfr + 1, 3, 2))
+    fixes = [jnp.zeros((frame_rows, cc), jnp.float32) for _ in range(nout)]
+    for t, h, kt in terms:
+        keep = (seglocal[t + kt] == seglocal[t + 2]).astype(jnp.float32)
+        part = jnp.dot(
+            halo_patch[h], conv_weight[kt * 9 * cc : (kt + 1) * 9 * cc], preferred_element_type=jnp.float32
+        )
+        fixes[t] = fixes[t] + keep * part
+    pre = pre + jnp.concatenate(fixes, axis=0)
     sig = jax.nn.sigmoid(pre)
     activated = jax.nn.silu(pre[:rows]).astype(jnp.bfloat16).reshape(clips.shape)
     grad_pre = (
@@ -74,15 +82,20 @@
     ).astype(jnp.bfloat16)
     own_grad = grad_pre[:rows]
     count = lax.axis_size("dp") * (lax.axis_size("chip") * lax.axis_size("core")) * rows
-    grad_local = jnp.concatenate(
-        [
-            lax.dot_general(
-                patch, own_grad, (((0,), (0,)), ((), ())), preferred_element_type=jnp.float32
+    per_tap = [
+        lax.dot_general(patch, own_grad, (((0,), (0,)), ((), ())), preferred_element_type=jnp.float32)
+        for patch in patches
+    ]
+    for t, h, kt in terms:
+        if t < nfr:
+            keep = (seglocal[t + kt] == seglocal[t + 2]).astype(jnp.float32)
+            per_tap[kt] = per_tap[kt] + keep * lax.dot_general(
+                halo_patch[h],
+                own_grad[t * frame_rows : (t + 1) * frame_rows],
+                (((0,), (0,)), ((), ())),
+                preferred_element_type=jnp.float32,
             )
-            for patch in patches
-        ],
-        axis=0,
-    )
+    grad_local = jnp.concatenate(per_tap, axis=0)
     grad_ext = grad_pre.reshape(nout, hh, ww, cc)
     own = seglocal[2 : 2 + nfr]
     summed = jnp.zeros((rows, cc), jnp.float32)

time: 84.4 us -> 105 us (1.24)
  waiting for transfers between devices: 14.7 us -> 23.4 us
  between operations: 1.2 us -> 5.99 us
  other arithmetic: 5.41 us -> 8.99 us
  starting transfers between devices: 26 us -> 27.6 us
    all_to_all x1, waiting for transfers between devices: 10.4 us -> 18.6 us  [reduce_weight_grad(): mine = lax.all_to_all(blocks, TM, 0, 0, tiled=True).sum(axis=0)]
    unnamed x67 -> x78, local copies, waits for them, and re-layouts: 13.7 us -> 7.73 us
    dot_general x3, matrix products: 6.59 us -> 3.04 us  [per_device(): jnp.dot(patch, flipped, preferred_element_type=jnp.float32)]
    transpose x3, local copies, waits for them, and re-layouts: 0.67 us -> 3.96 us  [per_device(): flipped = jnp.swapaxes(block, 1, 2).reshape(9 * cc, cc)]
    dot_general x0 -> x9, matrix products: none -> 3.16 us  [the longest x6 1.84 us: per_device(): jnp.dot(halo_patch[h], conv_weight[kt * 9 * cc:(kt + 1) * 9 * cc], prefer...]
    slice x3, local copies, waits for them, and re-layouts: 0.54 us -> 3.45 us  [per_device(): patches.append(patch[:rows])]
    ppermute x3, waiting for transfers between devices: 2.84 us -> 4.78 us  [reduce_weight_grad(): mine = mine + lax.ppermute(mine, 'dp', [(i, i ^ step) for i in range(dp)])]
    reduce_sum x1, other arithmetic: 0.05 us -> 1.6 us  [reduce_weight_grad(): mine = lax.all_to_all(blocks, TM, 0, 0, tiled=True).sum(axis=0)]
  transfers between devices with their start and end apart: 7 -> 6, of which waited for: 4 -> 4; matrix products, arithmetic and copies ran while one was open for 24% -> 25% of each run, Pallas kernels for 0% -> 0%
where the time goes in v4:
time: 105 us; the launch traced here: 104 us
  starting transfers between devices  27.6 us (26%)
  local copies, waits for them, and re-layouts  23.9 us (23%)
  waiting for transfers between devices  23.4 us (22%)
  matrix products  14 us (13%)
  other arithmetic  8.99 us (9%)
  between operations  5.99 us (6%)
    all_to_all x1, waiting for transfers between devices, reduce_weight_grad(): mine = lax.all_to_all(blocks, TM, 0, 0, tiled=True).sum(axis=0)  18.6 us
    ppermute x3, starting transfers between devices, reduce_weight_grad(): mine = mine + lax.ppermute(mine, 'dp', [(i, i ^ step) for i in range(dp)])  12.9 us
    all_to_all x1, starting transfers between devices, reduce_weight_grad(): mine = lax.all_to_all(blocks, TM, 0, 0, tiled=True).sum(axis=0)  10.3 us
    unnamed x78, local copies, waits for them, and re-layouts  7.73 us
    dot_general x3, matrix products, per_device(): jnp.dot(patch, conv_weight[kt * 9 * cc:(kt + 1) * 9 * cc], preferred_elem...  5.38 us
    ppermute x3, waiting for transfers between devices, reduce_weight_grad(): mine = mine + lax.ppermute(mine, 'dp', [(i, i ^ step) for i in range(dp)])  4.78 us
    ppermute x2, starting transfers between devices, from_behind(): lax.ppermute(value, axis, [(source, source + steps) for source in range(l...  4.32 us
    transpose x3, local copies, waits for them, and re-layouts, per_device(): flipped = jnp.swapaxes(block, 1, 2).reshape(9 * cc, cc)  3.96 us
  transfers between devices with their start and end apart: 6, of which 4 were waited for; matrix products, arithmetic and copies ran while one was open for 25% of the time, Pallas kernels for 0%

profile of v4, /device:TPU:8, one launch (start us, length us, event | category | flops | bytes accessed | tf_op | source)
XLA Modules:
  0.0 103.9 jit_solution(10535216617670180138)
XLA Ops:
  0.6 1.6 %fusion.82 = (bf16[1,2,16,16,128]{4,3,2,1,0:T(8,128)(2,1)}, bf16[1,2,16,16,128]{4,3,2,1,0:T(8,128)(2,1)S(1)}) fusion(bf16[1,4,16,16,128]{4,3,2,1,0:T(8,128)(2,1)} %param.4), kind=kLoop, calls=%fused_computation.186 | loop fusion | bytes 524288 | tf_op jit(solution)/shard_map/slice | solution.py:44
  2.3 0.9 slice.376
  3.2 0.7 pad_maximum_fusion.4
  3.9 1.9 %collective-permute-start.1 = (bf16[1,4,16,16,128]{4,3,2,1,0:T(8,128)(2,1)}, bf16[1,4,16,16,128]{4,3,2,1,0:T(8,128)(2,1)}, u32[]{:S(2)}, u32[]{:S(2)}) collective-permute-start(bf16[1,4,16,16,128]{4,3,2,1,0:T(8,128)(2,1)} %pad_maximum_fusion.4), channel_id=1, source_target_pairs={{1,0},{2,1},{3,2},{4,3},{5,4},{6,5},{7,6},{8,7},{9,8},{10,9},{11,1... | collective-permute-start | bytes 786440 | tf_op jit(solution)/shard_map/ppermute | solution.py:12
  5.8 2.4 %collective-permute-start = (bf16[1,2,16,16,128]{4,3,2,1,0:T(8,128)(2,1)}, bf16[1,2,16,16,128]{4,3,2,1,0:T(8,128)(2,1)}, u32[]{:S(2)}, u32[]{:S(2)}) collective-permute-start(bf16[1,2,16,16,128]{4,3,2,1,0:T(8,128)(2,1)} %get-tuple-element.29), channel_id=1, source_target_pairs={{0,1},{1,2},{2,3},{3,4},{4,5},{5,6},{6,7},{7,8},{8,9},{9,10},{10,1... | collective-permute-start | bytes 393224 | tf_op jit(solution)/shard_map/ppermute | solution.py:12
  8.3 0.7 pad_add_fusion
  9.2 1.3 %fusion.81 = (bf16[6,16,16,128]{3,2,1,0:T(8,128)(2,1)S(1)}, bf16[6,16,16,128]{3,2,1,0:T(8,128)(2,1)S(1)}, bf16[6,16,16,128]{3,2,1,0:T(8,128)(2,1)S(1)}) fusion(bf16[4,16,16,128]{3,2,1,0:T(8,128)(2,1)} %bitcast.93, bf16[2,16,16,128]{3,2,1,0:T(8,128)(2,1)S(1)} %broadcast_in_dim.43, pred[6]{0:T(512)(128)(4,1)S(1)} %get-tuple-element.33, ...), kind=kLoop, calls=%fused_computation.185 | loop fusion | flops 786432 | bytes 1572876 | tf_op jit(solution)/shard_map/concatenate | solution.py:47
  12.3 0.4 constant_dynamic-update-slice_fusion.2
  13.5 0.9 fusion.80
  14.4 1.1 %fusion.71 = f32[1536,128]{1,0:T(8,128)S(1)} fusion(bf16[1536,1152]{1,0:T(8,128)(2,1)S(1)} %bitcast.74, bf16[3456,128]{1,0:T(8,128)(2,1)S(1)} %copy-done.2), kind=kOutput, calls=%fused_computation.175 | convolution fusion | flops 452984832 | bytes 4620288 | tf_op jit(solution)/shard_map/dot_general | solution.py:64
  16.8 2.0 %convolution_add_fusion.1 = f32[1536,128]{1,0:T(8,128)} fusion(f32[1536,128]{1,0:T(8,128)S(1)} %fusion.71, bf16[1536,1152]{1,0:T(8,128)(2,1)S(1)} %bitcast.73, bf16[3456,128]{1,0:T(8,128)(2,1)S(1)} %copy-done.2), kind=kOutput, calls=%fused_computation.8 | convolution fusion | flops 453181440 | bytes 5406720 | tf_op jit(solution)/shard_map/dot_general | solution.py:64
  18.8 0.6 fusion.83
  19.4 1.6 %slice.449 = bf16[4,16,16,1152]{3,2,1,0:T(8,128)(2,1)} slice(bf16[6,16,16,1152]{3,2,1,0:T(8,128)(2,1)S(1)} %fusion.18), slice={[0:4], [0:16], [0:16], [0:1152]} | slice | bytes 4718592 | tf_op jit(solution)/shard_map/slice | solution.py:63
  25.8 1.7 %slice.453 = bf16[4,16,16,1152]{3,2,1,0:T(8,128)(2,1)} slice(bf16[6,16,16,1152]{3,2,1,0:T(8,128)(2,1)S(1)} %fusion.34), slice={[0:4], [0:16], [0:16], [0:1152]} | slice | bytes 4718592 | tf_op jit(solution)/shard_map/slice | solution.py:63
  27.5 1.9 %copy.7 = bf16[9,128,128]{2,1,0:T(8,128)(2,1)} copy(bf16[9,128,128]{1,2,0:T(8,128)(2,1)} %bitcast.100) | data formatting | bytes 589824 | tf_op jit(solution)/shard_map/transpose | solution.py:109
  29.4 0.9 copy.8
  30.3 1.2 %copy.9 = bf16[9,128,128]{2,1,0:T(8,128)(2,1)S(1)} copy(bf16[9,128,128]{1,2,0:T(8,128)(2,1)} %bitcast.98) | data formatting | bytes 589824 | tf_op jit(solution)/shard_map/transpose | solution.py:109
  31.5 1.0 slice_bitcast_fusion
  32.6 0.9 pad_maximum_fusion.5
  33.9 1.0 constant_dynamic-update-slice_fusion.3
  35.8 0.3 fusion.8
  37.5 1.0 %copy-done.7 = bf16[6,16,16,1152]{3,2,1,0:T(8,128)(2,1)S(1)} copy-done((bf16[6,16,16,1152]{3,2,1,0:T(8,128)(2,1)S(1)}, bf16[6,16,16,1152]{3,2,1,0:T(8,128)(2,1)}, u32[]{:S(2)}) %copy-start.7) | copy-done | bytes 3538968
  38.5 2.2 %fusion.10 = (bf16[1536,128]{1,0:T(8,128)(2,1)S(1)}, f32[1536,128]{1,0:T(8,128)}) fusion(bf16[6,16,16,128]{3,2,1,0:T(8,128)(2,1)S(1)} %pad_maximum_fusion.3, f32[1536,128]{1,0:T(8,128)S(1)} %fusion.5, f32[1536,128]{1,0:T(8,128)S(1)} %copy-done.8, bf16[1536,1152]{1,0:T(8,128)(2,1)S(1)} %bitcast.95, bf16[3456,128]{1,0:T(8,128)(2,1)S(1)} %copy-done.2), kind=kOutput, calls=%fused_computation.49 | convolution fusion | flops 455344128 | bytes 6979584 | tf_op jit(solution)/shard_map/dot_general | solution.py:64
  40.8 0.8 slice.448
  41.5 0.8 fusion.77
  42.4 0.6 fusion.2
  42.9 0.4 fusion.1
  43.3 0.8 fusion.75
  44.1 0.4 fusion
  44.5 0.4 copy-done.1
  45.0 0.8 fusion.73
  45.9 1.4 %reshape.108 = f32[32,108,128]{2,1,0:T(8,128)} reshape(f32[3456,128]{1,0:T(8,128)S(1)} %pad_maximum_fusion) | data formatting | bytes 3538944 | tf_op jit(solution)/shard_map/reshape | solution.py:19
  47.3 10.3 %all-to-all-start = ((f32[32,108,128]{2,1,0:T(8,128)}), f32[32,108,128]{2,1,0:T(8,128)}, u32[]{:S(2)}, u32[]{:S(2)}) async-start(f32[32,108,128]{2,1,0:T(8,128)} %reshape.108), calls=%async_computation | async-start | bytes 3670016 | tf_op jit(solution)/shard_map/all_to_all | solution.py:20
  57.6 0.4 pad_slice_fusion.24
  58.3 0.3 copy-done.4
  61.1 0.8 fusion.84
  62.1 0.8 convolution_add_fusion.3
  62.9 18.6 %all-to-all-done = f32[32,108,128]{2,1,0:T(8,128)} async-done(((f32[32,108,128]{2,1,0:T(8,128)}), f32[32,108,128]{2,1,0:T(8,128)}, u32[]{:S(2)}, u32[]{:S(2)}) %all-to-all-start) | async-done | bytes 1769504 | tf_op jit(solution)/shard_map/all_to_all | solution.py:20
  81.5 1.6 %reduce_sum.9 = f32[108,128]{1,0:T(8,128)S(1)} reduce(f32[32,108,128]{2,1,0:T(8,128)} %all-to-all-done, f32[]{:T(128)} %constant.38.clone.1), dimensions={0}, to_apply=%region_0.1 | reduce | flops 428544 | bytes 1824772 | tf_op jit(solution)/shard_map/reduce_sum | solution.py:20
  83.1 2.0 %collective-permute-start.2 = (f32[108,128]{1,0:T(8,128)S(1)}, f32[108,128]{1,0:T(8,128)S(1)}, u32[]{:S(2)}, u32[]{:S(2)}) collective-permute-start(f32[108,128]{1,0:T(8,128)S(1)} %reduce_sum.9), channel_id=1, source_target_pairs={{0,32},{32,0},{64,96},{96,64},{128,160},{160,128},{192,224},{224,1... | collective-permute-start | bytes 165896 | tf_op jit(solution)/shard_map/ppermute | solution.py:23
  85.2 2.2 %collective-permute-done.2 = f32[108,128]{1,0:T(8,128)S(1)} collective-permute-done((f32[108,128]{1,0:T(8,128)S(1)}, f32[108,128]{1,0:T(8,128)S(1)}, u32[]{:S(2)}, u32[]{:S(2)}) %collective-permute-start.2) | collective-permute-done | bytes 55328 | tf_op jit(solution)/shard_map/ppermute | solution.py:23
  87.4 3.4 %collective-permute-start.3 = (f32[108,128]{1,0:T(8,128)S(1)}, f32[108,128]{1,0:T(8,128)S(1)}, u32[]{:S(2)}, u32[]{:S(2)}) collective-permute-start(f32[108,128]{1,0:T(8,128)S(1)} %add.88), channel_id=1, source_target_pairs={{0,64},{32,96},{64,0},{96,32},{128,192},{160,224},{192,128},{224,1... | collective-permute-start | bytes 165896 | tf_op jit(solution)/shard_map/ppermute | solution.py:23
  90.8 1.5 %fusion.4 = bf16[1024,128]{1,0:T(8,128)(2,1)} fusion(f32[1024,128]{1,0:T(8,128)S(1)} %convolution_add_fusion.3, bf16[1024,1152]{1,0:T(8,128)(2,1)S(1)} %constant_dynamic-update-slice_fusion.7, bf16[1152,128]{1,0:T(8,128)(2,1)S(1)} %bitcast.96), kind=kOutput, calls=%fused_computation.12 | convolution fusion | flops 302252032 | bytes 3440640 | tf_op jit(solution)/shard_map/dot_general | solution.py:110
  92.2 0.7 collective-permute-done.3
  92.9 7.5 %collective-permute-start.4 = (f32[108,128]{1,0:T(8,128)S(1)}, f32[108,128]{1,0:T(8,128)S(1)}, u32[]{:S(2)}, u32[]{:S(2)}) collective-permute-start(f32[108,128]{1,0:T(8,128)S(1)} %add.89), channel_id=1, source_target_pairs={{0,128},{32,160},{64,192},{96,224},{128,0},{160,32},{192,64},{224,... | collective-permute-start | bytes 165896 | tf_op jit(solution)/shard_map/ppermute | solution.py:23
  100.5 0.8 multiply_convert_fusion
  101.3 1.9 %collective-permute-done.4 = f32[108,128]{1,0:T(8,128)S(1)} collective-permute-done((f32[108,128]{1,0:T(8,128)S(1)}, f32[108,128]{1,0:T(8,128)S(1)}, u32[]{:S(2)}, u32[]{:S(2)}) %collective-permute-start.4) | collective-permute-done | bytes 55328 | tf_op jit(solution)/shard_map/ppermute | solution.py:23
  103.2 0.6 add_multiply_fusion
  (105 shorter events, 9.6 us)
Async XLA Ops:
  3.9 27.6 %collective-permute-start.1 = (bf16[1,4,16,16,128]{4,3,2,1,0:T(8,128)(2,1)}, bf16[1,4,16,16,128]{4,3,2,1,0:T(8,128)(2,1)}, u32[]{:S(2)}, u32[]{:S(2)}) collective-permute-start(bf16[1,4,16,16,128]{4,3,2,1,0:T(8,128)(2,1)} %pad_maximum_fusion.4), channel_id=1, source_target_pairs={{1,0},{2,1},{3,2},{4,3},{5,4},{6,5},{7,6},{8,7},{9,8},{10,9},{11,1... | collective-permute-start | bytes 786440 | tf_op jit(solution)/shard_map/ppermute | solution.py:12
  5.8 26.7 %collective-permute-start = (bf16[1,2,16,16,128]{4,3,2,1,0:T(8,128)(2,1)}, bf16[1,2,16,16,128]{4,3,2,1,0:T(8,128)(2,1)}, u32[]{:S(2)}, u32[]{:S(2)}) collective-permute-start(bf16[1,2,16,16,128]{4,3,2,1,0:T(8,128)(2,1)} %get-tuple-element.29), channel_id=1, source_target_pairs={{0,1},{1,2},{2,3},{3,4},{4,5},{5,6},{6,7},{7,8},{8,9},{9,10},{10,1... | collective-permute-start | bytes 393224 | tf_op jit(solution)/shard_map/ppermute | solution.py:12
  11.3 1.0 copy-start.5
  12.3 1.2 %copy-start.2 = (bf16[3456,128]{1,0:T(8,128)(2,1)S(1)}, bf16[3456,128]{1,0:T(8,128)(2,1)}, u32[]{:S(2)}) copy-start(bf16[3456,128]{1,0:T(8,128)(2,1)} %param.6) | copy-start | bytes 2654212
  16.8 9.0 %copy-start.6 = (bf16[6,16,16,1152]{3,2,1,0:T(8,128)(2,1)}, bf16[6,16,16,1152]{3,2,1,0:T(8,128)(2,1)S(1)}, u32[]{:S(2)}) copy-start(bf16[6,16,16,1152]{3,2,1,0:T(8,128)(2,1)S(1)} %fusion.34) | copy-start | bytes 10616836
  35.8 1.3 %copy-start.12 = (bf16[1,4,16,16,128]{4,3,2,1,0:T(8,128)(2,1)S(1)}, bf16[1,4,16,16,128]{4,3,2,1,0:T(8,128)(2,1)}, u32[]{:S(2)}) copy-start(bf16[1,4,16,16,128]{4,3,2,1,0:T(8,128)(2,1)} %param.7) | copy-start | bytes 786436
  36.1 1.4 %copy-start.8 = (f32[1536,128]{1,0:T(8,128)S(1)}, f32[1536,128]{1,0:T(8,128)}, u32[]{:S(2)}) copy-start(f32[1536,128]{1,0:T(8,128)} %convolution_add_fusion.1) | copy-start | bytes 2359300
  36.4 2.1 %copy-start.7 = (bf16[6,16,16,1152]{3,2,1,0:T(8,128)(2,1)S(1)}, bf16[6,16,16,1152]{3,2,1,0:T(8,128)(2,1)}, u32[]{:S(2)}) copy-start(bf16[6,16,16,1152]{3,2,1,0:T(8,128)(2,1)} %copy-done.6) | copy-start | bytes 10616836
  38.5 3.0 %copy-start = (bf16[4,16,16,1152]{3,2,1,0:T(8,128)(2,1)S(1)}, bf16[4,16,16,1152]{3,2,1,0:T(8,128)(2,1)}, u32[]{:S(2)}) copy-start(bf16[4,16,16,1152]{3,2,1,0:T(8,128)(2,1)} %slice.449) | copy-start | bytes 7077892
  40.8 3.8 %copy-start.3 = (bf16[1536,128]{1,0:T(8,128)(2,1)}, bf16[1536,128]{1,0:T(8,128)(2,1)S(1)}, u32[]{:S(2)}) copy-start(bf16[1536,128]{1,0:T(8,128)(2,1)S(1)} %get-tuple-element.41) | copy-start | bytes 1179652
  43.3 1.7 %copy-start.1 = (bf16[4,16,16,1152]{3,2,1,0:T(8,128)(2,1)S(1)}, bf16[4,16,16,1152]{3,2,1,0:T(8,128)(2,1)}, u32[]{:S(2)}) copy-start(bf16[4,16,16,1152]{3,2,1,0:T(8,128)(2,1)} %slice.453) | copy-start | bytes 7077892
  47.3 10.3 %copy-start.11 = (bf16[1024,128]{1,0:T(8,128)(2,1)S(1)}, bf16[1024,128]{1,0:T(8,128)(2,1)}, u32[]{:S(2)}) copy-start(bf16[1024,128]{1,0:T(8,128)(2,1)} %slice.448) | copy-start | bytes 786436
  47.3 34.2 %all-to-all-start = ((f32[32,108,128]{2,1,0:T(8,128)}), f32[32,108,128]{2,1,0:T(8,128)}, u32[]{:S(2)}, u32[]{:S(2)}) async-start(f32[32,108,128]{2,1,0:T(8,128)} %reshape.108), calls=%async_computation | async-start | bytes 3670016 | tf_op jit(solution)/shard_map/all_to_all | solution.py:20
  57.6 1.0 copy-start.4
  60.2 1.0 copy-start.10
  61.1 1.0 copy-start.9
  83.1 4.3 %collective-permute-start.2 = (f32[108,128]{1,0:T(8,128)S(1)}, f32[108,128]{1,0:T(8,128)S(1)}, u32[]{:S(2)}, u32[]{:S(2)}) collective-permute-start(f32[108,128]{1,0:T(8,128)S(1)} %reduce_sum.9), channel_id=1, source_target_pairs={{0,32},{32,0},{64,96},{96,64},{128,160},{160,128},{192,224},{224,1... | collective-permute-start | bytes 165896 | tf_op jit(solution)/shard_map/ppermute | solution.py:23
  87.4 5.5 %collective-permute-start.3 = (f32[108,128]{1,0:T(8,128)S(1)}, f32[108,128]{1,0:T(8,128)S(1)}, u32[]{:S(2)}, u32[]{:S(2)}) collective-permute-start(f32[108,128]{1,0:T(8,128)S(1)} %add.88), channel_id=1, source_target_pairs={{0,64},{32,96},{64,0},{96,32},{128,192},{160,224},{192,128},{224,1... | collective-permute-start | bytes 165896 | tf_op jit(solution)/shard_map/ppermute | solution.py:23
  90.8 9.7 %copy-start.13 = (f32[1536,128]{1,0:T(8,128)S(1)}, f32[1536,128]{1,0:T(8,128)}, u32[]{:S(2)}) copy-start(f32[1536,128]{1,0:T(8,128)} %get-tuple-element.42) | copy-start | bytes 2359300
  92.9 10.3 %collective-permute-start.4 = (f32[108,128]{1,0:T(8,128)S(1)}, f32[108,128]{1,0:T(8,128)S(1)}, u32[]{:S(2)}, u32[]{:S(2)}) collective-permute-start(f32[108,128]{1,0:T(8,128)S(1)} %add.89), channel_id=1, source_target_pairs={{0,128},{32,160},{64,192},{96,224},{128,0},{160,32},{192,64},{224,... | collective-permute-start | bytes 165896 | tf_op jit(solution)/shard_map/ppermute | solution.py:23

commit v5 on v3

--- a/solution.py
+++ b/solution.py
@@ -13,16 +13,11 @@
 
 
 def reduce_weight_grad(grad_local):
-    chips = lax.axis_size("chip")
-    cores = lax.axis_size("core")
+    tm = lax.axis_size("chip") * lax.axis_size("core")
     dp = lax.axis_size("dp")
     rows, cols = grad_local.shape
-    blocks = grad_local.reshape(chips, cores, rows // (chips * cores), cols)
-    core = lax.axis_index("core")
-    mine = jnp.where(core == 0, blocks[:, 0], blocks[:, 1])
-    other = jnp.where(core == 0, blocks[:, 1], blocks[:, 0])
-    mine = mine + lax.ppermute(other, "core", [(0, 1), (1, 0)])
-    mine = lax.all_to_all(mine, "chip", 0, 0, tiled=True).sum(axis=0)
+    blocks = grad_local.reshape(tm, rows // tm, cols)
+    mine = lax.all_to_all(blocks, TM, 0, 0, tiled=True).sum(axis=0)
     step = 1
     while step < dp:
         mine = mine + lax.ppermute(mine, "dp", [(i, i ^ step) for i in range(dp)])

time: 84.4 us -> 82.2 us (0.974)
  waiting for transfers between devices: 14.7 us -> 24 us
  local copies, waits for them, and re-layouts: 23.2 us -> 14.5 us
  matrix products: 13.4 us -> 9.84 us
  starting transfers between devices: 26 us -> 27.5 us
  other arithmetic: 5.41 us -> 4.37 us
    all_to_all x1, waiting for transfers between devices: 10.4 us -> 19.1 us  [reduce_weight_grad(): mine = lax.all_to_all(blocks, TM, 0, 0, tiled=True).sum(axis=0)]
    unnamed x67 -> x59, local copies, waits for them, and re-layouts: 13.7 us -> 6.25 us
    dot_general x3, matrix products: 6.59 us -> 3.04 us  [per_device(): jnp.dot(patch, flipped, preferred_element_type=jnp.float32)]
    ppermute x3, waiting for transfers between devices: 2.84 us -> 4.78 us  [reduce_weight_grad(): mine = mine + lax.ppermute(mine, 'dp', [(i, i ^ step) for i in range(dp)])]
    reduce_sum x1, other arithmetic: 0.05 us -> 1.6 us  [reduce_weight_grad(): mine = lax.all_to_all(blocks, TM, 0, 0, tiled=True).sum(axis=0)]
    all_to_all x1, starting transfers between devices: 8.79 us -> 10.2 us  [reduce_weight_grad(): mine = lax.all_to_all(blocks, TM, 0, 0, tiled=True).sum(axis=0)]
    transpose x3, local copies, waits for them, and re-layouts: 0.67 us -> 2.05 us  [per_device(): flipped = jnp.swapaxes(block, 1, 2).reshape(9 * cc, cc)]
    ppermute x2, waiting for transfers between devices: 1.52 us -> 0.15 us  [from_behind(): lax.ppermute(value, axis, [(source, source + steps) for source in range(l...]
  transfers between devices with their start and end apart: 7 -> 6, of which waited for: 4 -> 5; matrix products, arithmetic and copies ran while one was open for 24% -> 14% of each run, Pallas kernels for 0% -> 0%
where the time goes in v5:
time: 82.2 us; the launch traced here: 81.5 us
  starting transfers between devices  27.5 us (33%)
  waiting for transfers between devices  24 us (29%)
  local copies, waits for them, and re-layouts  14.5 us (18%)
  matrix products  9.84 us (12%)
  other arithmetic  4.37 us (5%)
  between operations  1.22 us (1%)
    all_to_all x1, waiting for transfers between devices, reduce_weight_grad(): mine = lax.all_to_all(blocks, TM, 0, 0, tiled=True).sum(axis=0)  19.1 us
    ppermute x3, starting transfers between devices, reduce_weight_grad(): mine = mine + lax.ppermute(mine, 'dp', [(i, i ^ step) for i in range(dp)])  12.9 us
    all_to_all x1, starting transfers between devices, reduce_weight_grad(): mine = lax.all_to_all(blocks, TM, 0, 0, tiled=True).sum(axis=0)  10.2 us
    unnamed x59, local copies, waits for them, and re-layouts  6.25 us
    ppermute x3, waiting for transfers between devices, reduce_weight_grad(): mine = mine + lax.ppermute(mine, 'dp', [(i, i ^ step) for i in range(dp)])  4.78 us
    ppermute x2, starting transfers between devices, from_behind(): lax.ppermute(value, axis, [(source, source + steps) for source in range(l...  4.46 us
    dot_general x3, matrix products, per_device(): jnp.dot(patch, conv_weight[kt * 9 * cc:(kt + 1) * 9 * cc], preferred_elem...  4.35 us
    dot_general x3, matrix products, per_device(): jnp.dot(patch, flipped, preferred_element_type=jnp.float32)  3.04 us
  transfers between devices with their start and end apart: 6, of which 5 were waited for; matrix products, arithmetic and copies ran while one was open for 14% of the time, Pallas kernels for 0%

profile of v5, /device:TPU:8, one launch (start us, length us, event | category | flops | bytes accessed | tf_op | source)
XLA Modules:
  0.0 81.5 jit_solution(12652781407693786697)
XLA Ops:
  0.6 1.0 %fusion.55 = (bf16[1,2,16,16,128]{4,3,2,1,0:T(8,128)(2,1)S(1)}, bf16[1,2,16,16,128]{4,3,2,1,0:T(8,128)(2,1)S(1)}) fusion(bf16[1,4,16,16,128]{4,3,2,1,0:T(8,128)(2,1)} %param.4), kind=kLoop, calls=%fused_computation.140 | loop fusion | bytes 524288 | tf_op jit(solution)/shard_map/slice | solution.py:45
  1.6 0.9 %slice.264 = bf16[1,2,16,16,128]{4,3,2,1,0:T(8,128)(2,1)S(1)} slice(bf16[1,4,16,16,128]{4,3,2,1,0:T(8,128)(2,1)} %param.7), slice={[0:1], [0:2], [0:16], [0:16], [0:128]} | slice | bytes 262144 | tf_op jit(solution)/shard_map/slice | solution.py:45
  2.6 2.1 %collective-permute-start.1 = (bf16[1,4,16,16,128]{4,3,2,1,0:T(8,128)(2,1)S(1)}, bf16[1,4,16,16,128]{4,3,2,1,0:T(8,128)(2,1)S(1)}, u32[]{:S(2)}, u32[]{:S(2)}) collective-permute-start(bf16[1,4,16,16,128]{4,3,2,1,0:T(8,128)(2,1)S(1)} %pad_maximum_fusion.5), channel_id=1, source_target_pairs={{1,0},{2,1},{3,2},{4,3},{5,4},{6,5},{7,6},{8,7},{9,8},{10,9},{11,1... | collective-permute-start | bytes 786440 | tf_op jit(solution)/shard_map/ppermute | solution.py:12
  4.7 2.4 %collective-permute-start = (bf16[1,2,16,16,128]{4,3,2,1,0:T(8,128)(2,1)S(1)}, bf16[1,2,16,16,128]{4,3,2,1,0:T(8,128)(2,1)S(1)}, u32[]{:S(2)}, u32[]{:S(2)}) collective-permute-start(bf16[1,2,16,16,128]{4,3,2,1,0:T(8,128)(2,1)S(1)} %get-tuple-element.23), channel_id=1, source_target_pairs={{0,1},{1,2},{2,3},{3,4},{4,5},{5,6},{6,7},{7,8},{8,9},{9,10},{10,1... | collective-permute-start | bytes 393224 | tf_op jit(solution)/shard_map/ppermute | solution.py:12
  7.1 1.2 %fusion.54 = (bf16[1152,128]{1,0:T(8,128)(2,1)S(1)}, bf16[1152,128]{1,0:T(8,128)(2,1)S(1)}, bf16[1152,128]{1,0:T(8,128)(2,1)S(1)}) fusion(bf16[3456,128]{1,0:T(8,128)(2,1)} %param.6), kind=kLoop, calls=%fused_computation.139 | loop fusion | bytes 1769472 | tf_op jit(solution)/shard_map/slice | solution.py:63
  8.5 0.2 copy.7
  8.8 0.9 %copy.8 = bf16[9,128,128]{2,1,0:T(8,128)(2,1)} copy(bf16[9,128,128]{1,2,0:T(8,128)(2,1)S(1)} %bitcast.73) | data formatting | bytes 589824 | tf_op jit(solution)/shard_map/transpose | solution.py:91
  9.7 0.9 %copy.9 = bf16[9,128,128]{2,1,0:T(8,128)(2,1)} copy(bf16[9,128,128]{1,2,0:T(8,128)(2,1)S(1)} %bitcast.72) | data formatting | bytes 589824 | tf_op jit(solution)/shard_map/transpose | solution.py:91
  11.0 0.2 fusion.21
  11.2 0.2 fusion.22
  11.5 0.4 constant_dynamic-update-slice_fusion.2
  12.2 0.2 fusion.13
  12.4 0.2 fusion.14
  12.6 0.2 fusion.15
  13.1 0.2 fusion.18
  13.5 0.2 fusion.5
  13.7 0.2 fusion.6
  14.0 0.2 fusion.7
  14.4 0.2 fusion.10
  14.6 0.2 slice.334
  14.8 1.0 %copy-done = bf16[3456,128]{1,0:T(8,128)(2,1)S(1)} copy-done((bf16[3456,128]{1,0:T(8,128)(2,1)S(1)}, bf16[3456,128]{1,0:T(8,128)(2,1)}, u32[]{:S(2)}) %copy-start) | copy-done | bytes 884760
  15.7 1.1 %fusion.46 = f32[1536,128]{1,0:T(8,128)S(1)} fusion(bf16[1536,1152]{1,0:T(8,128)(2,1)S(1)} %bitcast.57, bf16[3456,128]{1,0:T(8,128)(2,1)S(1)} %copy-done), kind=kOutput, calls=%fused_computation.131 | convolution fusion | flops 452984832 | bytes 4620288 | tf_op jit(solution)/shard_map/dot_general | solution.py:62
  16.8 0.2 fusion.23
  17.3 0.2 fusion.26
  17.5 0.2 slice.335
  17.7 0.2 slice.336
  17.9 1.1 %convolution_add_fusion.1 = f32[1536,128]{1,0:T(8,128)S(1)} fusion(f32[1536,128]{1,0:T(8,128)S(1)} %fusion.46, bf16[1536,1152]{1,0:T(8,128)(2,1)S(1)} %bitcast.56, bf16[3456,128]{1,0:T(8,128)(2,1)S(1)} %copy-done), kind=kOutput, calls=%fused_computation.1 | convolution fusion | flops 453181440 | bytes 5406720 | tf_op jit(solution)/shard_map/dot_general | solution.py:62
  19.0 2.2 %fusion.2 = (bf16[1536,128]{1,0:T(8,128)(2,1)S(1)}, f32[1536,128]{1,0:T(8,128)}) fusion(bf16[6,16,16,128]{3,2,1,0:T(8,128)(2,1)S(1)} %get-tuple-element.30, f32[1536,128]{1,0:T(8,128)S(1)} %convolution_add_fusion.1, bf16[1536,1152]{1,0:T(8,128)(2,1)S(1)} %bitcast.69, bf16[3456,128]{1,0:T(8,128)(2,1)S(1)} %copy-done), kind=kOutput, calls=%fused_computation.32 | convolution fusion | flops 455147520 | bytes 6193152 | tf_op jit(solution)/shard_map/dot_general | solution.py:62
  21.2 0.8 fusion.50
  22.0 0.8 fusion.52
  22.8 0.8 %fusion.48 = f32[1152,128]{1,0:T(8,128)S(1)} fusion(bf16[1024,1152]{1,0:T(8,128)(2,1)S(1)} %bitcast.59, bf16[1536,128]{1,0:T(8,128)(2,1)S(1)} %get-tuple-element.28), kind=kOutput, calls=%fused_computation.133 | convolution fusion | flops 301989888 | bytes 3211264 | tf_op jit(solution)/shard_map/dot_general | solution.py:74
  23.7 1.3 %reshape.88 = f32[32,108,128]{2,1,0:T(8,128)} reshape(f32[3456,128]{1,0:T(8,128)S(1)} %pad_maximum_fusion) | data formatting | bytes 3538944 | tf_op jit(solution)/shard_map/reshape | solution.py:19
  25.1 10.2 %all-to-all-start = ((f32[32,108,128]{2,1,0:T(8,128)}), f32[32,108,128]{2,1,0:T(8,128)}, u32[]{:S(2)}, u32[]{:S(2)}) async-start(f32[32,108,128]{2,1,0:T(8,128)} %reshape.88), calls=%async_computation | async-start | bytes 3670016 | tf_op jit(solution)/shard_map/all_to_all | solution.py:20
  35.3 0.3 pad_slice_fusion.24
  38.3 0.8 fusion.56
  39.1 0.2 copy-done.3
  39.3 0.8 convolution_add_fusion.3
  40.1 19.1 %all-to-all-done = f32[32,108,128]{2,1,0:T(8,128)} async-done(((f32[32,108,128]{2,1,0:T(8,128)}), f32[32,108,128]{2,1,0:T(8,128)}, u32[]{:S(2)}, u32[]{:S(2)}) %all-to-all-start) | async-done | bytes 1769504 | tf_op jit(solution)/shard_map/all_to_all | solution.py:20
  59.2 1.6 %reduce_sum.9 = f32[108,128]{1,0:T(8,128)S(1)} reduce(f32[32,108,128]{2,1,0:T(8,128)} %all-to-all-done, f32[]{:T(128)} %constant.33.clone.1), dimensions={0}, to_apply=%region_0.1 | reduce | flops 428544 | bytes 1824772 | tf_op jit(solution)/shard_map/reduce_sum | solution.py:20
  60.8 2.0 %collective-permute-start.2 = (f32[108,128]{1,0:T(8,128)S(1)}, f32[108,128]{1,0:T(8,128)S(1)}, u32[]{:S(2)}, u32[]{:S(2)}) collective-permute-start(f32[108,128]{1,0:T(8,128)S(1)} %reduce_sum.9), channel_id=1, source_target_pairs={{0,32},{32,0},{64,96},{96,64},{128,160},{160,128},{192,224},{224,1... | collective-permute-start | bytes 165896 | tf_op jit(solution)/shard_map/ppermute | solution.py:23
  62.8 2.2 %collective-permute-done.2 = f32[108,128]{1,0:T(8,128)S(1)} collective-permute-done((f32[108,128]{1,0:T(8,128)S(1)}, f32[108,128]{1,0:T(8,128)S(1)}, u32[]{:S(2)}, u32[]{:S(2)}) %collective-permute-start.2) | collective-permute-done | bytes 55328 | tf_op jit(solution)/shard_map/ppermute | solution.py:23
  65.0 3.4 %collective-permute-start.3 = (f32[108,128]{1,0:T(8,128)S(1)}, f32[108,128]{1,0:T(8,128)S(1)}, u32[]{:S(2)}, u32[]{:S(2)}) collective-permute-start(f32[108,128]{1,0:T(8,128)S(1)} %add.58), channel_id=1, source_target_pairs={{0,64},{32,96},{64,0},{96,32},{128,192},{160,224},{192,128},{224,1... | collective-permute-start | bytes 165896 | tf_op jit(solution)/shard_map/ppermute | solution.py:23
  68.4 1.5 %fusion = bf16[1024,128]{1,0:T(8,128)(2,1)} fusion(f32[1024,128]{1,0:T(8,128)S(1)} %convolution_add_fusion.3, bf16[1024,1152]{1,0:T(8,128)(2,1)S(1)} %constant_dynamic-update-slice_fusion.5, bf16[1152,128]{1,0:T(8,128)(2,1)S(1)} %bitcast.70), kind=kOutput, calls=%fused_computation.5 | convolution fusion | flops 302252032 | bytes 3440640 | tf_op jit(solution)/shard_map/dot_general | solution.py:92
  69.9 0.7 collective-permute-done.3
  70.6 7.5 %collective-permute-start.4 = (f32[108,128]{1,0:T(8,128)S(1)}, f32[108,128]{1,0:T(8,128)S(1)}, u32[]{:S(2)}, u32[]{:S(2)}) collective-permute-start(f32[108,128]{1,0:T(8,128)S(1)} %add.59), channel_id=1, source_target_pairs={{0,128},{32,160},{64,192},{96,224},{128,0},{160,32},{192,64},{224,... | collective-permute-start | bytes 165896 | tf_op jit(solution)/shard_map/ppermute | solution.py:23
  78.1 0.8 %multiply_convert_fusion = bf16[1024,128]{1,0:T(8,128)(2,1)} fusion(f32[1536,128]{1,0:T(8,128)S(1)} %copy-done.5), kind=kLoop, calls=%fused_computation.57 | loop fusion | flops 655360 | bytes 786432 | tf_op jit(solution)/shard_map/convert_element_type | solution.py:66
  79.0 1.9 %collective-permute-done.4 = f32[108,128]{1,0:T(8,128)S(1)} collective-permute-done((f32[108,128]{1,0:T(8,128)S(1)}, f32[108,128]{1,0:T(8,128)S(1)}, u32[]{:S(2)}, u32[]{:S(2)}) %collective-permute-start.4) | collective-permute-done | bytes 55328 | tf_op jit(solution)/shard_map/ppermute | solution.py:23
  80.9 0.6 add_multiply_fusion
  (70 shorter events, 5.0 us)
Async XLA Ops:
  0.6 7.7 %copy-start.6 = (s32[1,128]{1,0:T(1,128)S(1)}, s32[1,128]{1,0:T(1,128)}, u32[]{:S(2)}) copy-start(s32[1,128]{1,0:T(1,128)} %param.5) | copy-start | bytes 1540
  2.6 8.2 %copy-start.1 = (bf16[1,4,16,16,128]{4,3,2,1,0:T(8,128)(2,1)S(1)}, bf16[1,4,16,16,128]{4,3,2,1,0:T(8,128)(2,1)}, u32[]{:S(2)}) copy-start(bf16[1,4,16,16,128]{4,3,2,1,0:T(8,128)(2,1)} %param.4) | copy-start | bytes 786436
  2.6 8.1 %collective-permute-start.1 = (bf16[1,4,16,16,128]{4,3,2,1,0:T(8,128)(2,1)S(1)}, bf16[1,4,16,16,128]{4,3,2,1,0:T(8,128)(2,1)S(1)}, u32[]{:S(2)}, u32[]{:S(2)}) collective-permute-start(bf16[1,4,16,16,128]{4,3,2,1,0:T(8,128)(2,1)S(1)} %pad_maximum_fusion.5), channel_id=1, source_target_pairs={{1,0},{2,1},{3,2},{4,3},{5,4},{6,5},{7,6},{8,7},{9,8},{10,9},{11,1... | collective-permute-start | bytes 786440 | tf_op jit(solution)/shard_map/ppermute | solution.py:12
  4.7 6.8 %collective-permute-start = (bf16[1,2,16,16,128]{4,3,2,1,0:T(8,128)(2,1)S(1)}, bf16[1,2,16,16,128]{4,3,2,1,0:T(8,128)(2,1)S(1)}, u32[]{:S(2)}, u32[]{:S(2)}) collective-permute-start(bf16[1,2,16,16,128]{4,3,2,1,0:T(8,128)(2,1)S(1)} %get-tuple-element.23), channel_id=1, source_target_pairs={{0,1},{1,2},{2,3},{3,4},{4,5},{5,6},{6,7},{7,8},{8,9},{9,10},{10,1... | collective-permute-start | bytes 393224 | tf_op jit(solution)/shard_map/ppermute | solution.py:12
  10.6 0.9 %copy-start.4 = (bf16[1,4,16,16,128]{4,3,2,1,0:T(8,128)(2,1)S(1)}, bf16[1,4,16,16,128]{4,3,2,1,0:T(8,128)(2,1)}, u32[]{:S(2)}) copy-start(bf16[1,4,16,16,128]{4,3,2,1,0:T(8,128)(2,1)} %param.7) | copy-start | bytes 786436
  14.6 1.2 %copy-start = (bf16[3456,128]{1,0:T(8,128)(2,1)S(1)}, bf16[3456,128]{1,0:T(8,128)(2,1)}, u32[]{:S(2)}) copy-start(bf16[3456,128]{1,0:T(8,128)(2,1)} %param.6) | copy-start | bytes 2654212
  25.1 34.1 %all-to-all-start = ((f32[32,108,128]{2,1,0:T(8,128)}), f32[32,108,128]{2,1,0:T(8,128)}, u32[]{:S(2)}, u32[]{:S(2)}) async-start(f32[32,108,128]{2,1,0:T(8,128)} %reshape.88), calls=%async_computation | async-start | bytes 3670016 | tf_op jit(solution)/shard_map/all_to_all | solution.py:20
  38.3 1.0 %copy-start.3 = (bf16[9,128,128]{2,1,0:T(8,128)(2,1)S(1)}, bf16[9,128,128]{2,1,0:T(8,128)(2,1)}, u32[]{:S(2)}) copy-start(bf16[9,128,128]{2,1,0:T(8,128)(2,1)} %copy.8) | copy-start | bytes 884740
  40.1 28.3 %copy-start.2 = (bf16[9,128,128]{2,1,0:T(8,128)(2,1)S(1)}, bf16[9,128,128]{2,1,0:T(8,128)(2,1)}, u32[]{:S(2)}) copy-start(bf16[9,128,128]{2,1,0:T(8,128)(2,1)} %copy.9) | copy-start | bytes 884740
  60.8 4.3 %collective-permute-start.2 = (f32[108,128]{1,0:T(8,128)S(1)}, f32[108,128]{1,0:T(8,128)S(1)}, u32[]{:S(2)}, u32[]{:S(2)}) collective-permute-start(f32[108,128]{1,0:T(8,128)S(1)} %reduce_sum.9), channel_id=1, source_target_pairs={{0,32},{32,0},{64,96},{96,64},{128,160},{160,128},{192,224},{224,1... | collective-permute-start | bytes 165896 | tf_op jit(solution)/shard_map/ppermute | solution.py:23
  65.0 5.5 %collective-permute-start.3 = (f32[108,128]{1,0:T(8,128)S(1)}, f32[108,128]{1,0:T(8,128)S(1)}, u32[]{:S(2)}, u32[]{:S(2)}) collective-permute-start(f32[108,128]{1,0:T(8,128)S(1)} %add.58), channel_id=1, source_target_pairs={{0,64},{32,96},{64,0},{96,32},{128,192},{160,224},{192,128},{224,1... | collective-permute-start | bytes 165896 | tf_op jit(solution)/shard_map/ppermute | solution.py:23
  68.4 9.7 %copy-start.5 = (f32[1536,128]{1,0:T(8,128)S(1)}, f32[1536,128]{1,0:T(8,128)}, u32[]{:S(2)}) copy-start(f32[1536,128]{1,0:T(8,128)} %get-tuple-element.29) | copy-start | bytes 2359300
  70.6 10.3 %collective-permute-start.4 = (f32[108,128]{1,0:T(8,128)S(1)}, f32[108,128]{1,0:T(8,128)S(1)}, u32[]{:S(2)}, u32[]{:S(2)}) collective-permute-start(f32[108,128]{1,0:T(8,128)S(1)} %add.59), channel_id=1, source_target_pairs={{0,128},{32,160},{64,192},{96,224},{128,0},{160,32},{192,64},{224,... | collective-permute-start | bytes 165896 | tf_op jit(solution)/shard_map/ppermute | solution.py:23

commit v6 on v5

--- a/solution.py
+++ b/solution.py
@@ -1,6 +1,10 @@
+import functools
+
 import jax
 import jax.numpy as jnp
 from jax import lax
+from jax.experimental import pallas as pl
+from jax.experimental.pallas import tpu as pltpu
 from jax.sharding import Mesh, PartitionSpec as P
 
 TM = ("chip", "core")
@@ -35,6 +39,72 @@
     return jnp.concatenate(pieces, axis=3).reshape(-1, 9 * frames.shape[-1])
 
 
+def forward_kernel(hh, ww, nout, nfr, mask_ref, xe_ref, ce_ref, w_ref, act_ref, gp_ref, gw_ref, col_ref, pad_ref, acc_ref):
+    frame = hh * ww
+    cc = xe_ref.shape[1]
+    taps = 9 * cc
+    lead = 2 * ww
+    r = lax.broadcasted_iota(jnp.int32, (frame, cc), 0)
+    i = r // ww
+    j = r % ww
+    pad_ref[...] = jnp.zeros_like(pad_ref)
+    for f in range(nout + 2):
+        pad_ref[pl.ds(lead, frame), :] = xe_ref[pl.ds(f * frame, frame), :].astype(jnp.float32)
+        for ky in range(3):
+            for kx in range(3):
+                dy, dx = ky - 1, kx - 1
+                s = pad_ref[pl.ds(lead + dy * ww + dx, frame), :]
+                valid = (i + dy >= 0) & (i + dy < hh) & (j + dx >= 0) & (j + dx < ww)
+                s = jnp.where(valid, s, 0.0)
+                col_ref[f, :, pl.ds((ky * 3 + kx) * cc, cc)] = s.astype(col_ref.dtype)
+    for t in range(nout):
+        pre = jnp.zeros((frame, cc), jnp.float32)
+        for kt in range(3):
+            part = jnp.dot(col_ref[t + kt], w_ref[pl.ds(kt * taps, taps), :], preferred_element_type=jnp.float32)
+            pre = pre + mask_ref[kt, t] * part
+        sig = 1.0 / (1.0 + jnp.exp(-pre))
+        if t < nfr:
+            act_ref[pl.ds(t * frame, frame), :] = (pre * sig).astype(act_ref.dtype)
+        cot = ce_ref[pl.ds(t * frame, frame), :].astype(jnp.float32)
+        gp_ref[pl.ds(t * frame, frame), :] = (cot * sig * (1.0 + pre * (1.0 - sig))).astype(gp_ref.dtype)
+    acc_ref[...] = jnp.zeros_like(acc_ref)
+    for t in range(nfr):
+        g = gp_ref[pl.ds(t * frame, frame), :].astype(jnp.float32)
+        gt = jnp.transpose(g).astype(col_ref.dtype)
+        for kt in range(3):
+            part = jnp.dot(gt, col_ref[t + kt], preferred_element_type=jnp.float32)
+            acc_ref[kt] = acc_ref[kt] + mask_ref[kt, t] * part
+    for kt in range(3):
+        gw_ref[pl.ds(kt * taps, taps), :] = jnp.transpose(acc_ref[kt])
+
+
+def forward_call(mask, xe, ce, w, hh, ww, nout, nfr):
+    frame = hh * ww
+    cc = xe.shape[1]
+    krows = w.shape[0]
+    vmem = pl.BlockSpec(memory_space=pltpu.VMEM)
+    flops = 2 * 3 * frame * 9 * cc * cc * (nout + nfr)
+    return pl.pallas_call(
+        functools.partial(forward_kernel, hh, ww, nout, nfr),
+        out_shape=(
+            jax.ShapeDtypeStruct((nfr * frame, cc), jnp.bfloat16),
+            jax.ShapeDtypeStruct((nout * frame, cc), jnp.bfloat16),
+            jax.ShapeDtypeStruct((krows, cc), jnp.float32),
+        ),
+        in_specs=[pl.BlockSpec(memory_space=pltpu.SMEM), vmem, vmem, vmem],
+        out_specs=(vmem, vmem, vmem),
+        scratch_shapes=[
+            pltpu.VMEM((nout + 2, frame, 9 * cc), jnp.bfloat16),
+            pltpu.VMEM((frame + 4 * ww, cc), jnp.float32),
+            pltpu.VMEM((3, cc, 9 * cc), jnp.float32),
+        ],
+        compiler_params=pltpu.CompilerParams(vmem_limit_bytes=48 * 1024 * 1024),
+        cost_estimate=pl.CostEstimate(
+            flops=flops, transcendentals=nout * frame * cc, bytes_accessed=2 * (xe.size + ce.size + w.size) + 4 * krows * cc
+        ),
+    )(mask, xe, ce, w)
+
+
 def per_device(clips, segment_ids, conv_weight, cotangent):
     nfr = clips.shape[1]
     hh = clips.shape[2]
@@ -51,33 +121,12 @@
     seglocal = lax.dynamic_slice_in_dim(segp, start, nfr + 4, 0)
     nout = nfr + 2
     centre = seglocal[2 : 2 + nout]
-    pre = jnp.zeros((nout * hh * ww, cc), jnp.float32)
-    patches = []
-    for kt in range(3):
-        moved = frames[kt : kt + nout]
-        keep = seglocal[kt : kt + nout] == centre
-        moved = jnp.where(keep[:, None, None, None], moved, jnp.zeros_like(moved))
-        patch = im2col(moved, lambda k: k, hh, ww)
-        patches.append(patch[:rows])
-        pre = pre + jnp.dot(
-            patch, conv_weight[kt * 9 * cc : (kt + 1) * 9 * cc], preferred_element_type=jnp.float32
-        )
-    sig = jax.nn.sigmoid(pre)
-    activated = jax.nn.silu(pre[:rows]).astype(jnp.bfloat16).reshape(clips.shape)
-    grad_pre = (
-        cot_ext.reshape(nout * hh * ww, cc).astype(jnp.float32) * sig * (1.0 + pre * (1.0 - sig))
-    ).astype(jnp.bfloat16)
-    own_grad = grad_pre[:rows]
+    mask = jnp.stack([(seglocal[kt : kt + nout] == centre) for kt in range(3)]).astype(jnp.float32)
+    act, grad_pre, grad_local = forward_call(
+        mask, frames.reshape(-1, cc), cot_ext.reshape(-1, cc), conv_weight, hh, ww, nout, nfr
+    )
+    activated = act.reshape(clips.shape)
     count = lax.axis_size("dp") * (lax.axis_size("chip") * lax.axis_size("core")) * rows
-    grad_local = jnp.concatenate(
-        [
-            lax.dot_general(
-                patch, own_grad, (((0,), (0,)), ((), ())), preferred_element_type=jnp.float32
-            )
-            for patch in patches
-        ],
-        axis=0,
-    )
     grad_ext = grad_pre.reshape(nout, hh, ww, cc)
     own = seglocal[2 : 2 + nfr]
     summed = jnp.zeros((rows, cc), jnp.float32)

time: 82.2 us -> 77.8 us (0.946)
  matrix products: 9.84 us -> 3.04 us
  Pallas kernels: 0 us -> 5.28 us
  local copies, waits for them, and re-layouts: 14.5 us -> 11.2 us
    dot_general x6 -> x0, matrix products: 6.8 us -> none  [the longest x3 4.35 us: per_device(): jnp.dot(patch, conv_weight[kt * 9 * cc:(kt + 1) * 9 * cc], preferred_elem...]
    pallas_call x0 -> x1, Pallas kernels: none -> 5.28 us  [forward_call(): pl.pallas_call(functools.partial(forward_kernel, hh, ww, nout, nfr), out_...]
    unnamed x59 -> x38, local copies, waits for them, and re-layouts: 6.25 us -> 3.13 us
    ppermute x2, starting transfers between devices: 4.46 us -> 5.7 us  [from_behind(): lax.ppermute(value, axis, [(source, source + steps) for source in range(l...]
    concatenate x1, other arithmetic: 0.04 us -> 0.97 us  [per_device(): frames = jnp.concatenate([earlier, clips[0], ahead[:2]], axis=0)]
    slice x5 -> x2, local copies, waits for them, and re-layouts: 2.74 us -> 2.23 us  [the longest x1 1.24 us: per_device(): block = conv_weight[kt * 9 * cc:(kt + 1) * 9 * cc].reshape(9, cc, cc)]
  transfers between devices with their start and end apart: 6 -> 6, of which waited for: 5 -> 4; matrix products, arithmetic and copies ran while one was open for 14% -> 17% of each run, Pallas kernels for 0% -> 0%
where the time goes in v6:
time: 77.8 us; the launch traced here: 77.1 us
  starting transfers between devices  28.2 us (36%)
  waiting for transfers between devices  23.3 us (30%)
  local copies, waits for them, and re-layouts  11.2 us (14%)
  Pallas kernels  5.28 us (7%)
  other arithmetic  5.17 us (7%)
  matrix products  3.04 us (4%)
  between operations  1 us (1%)
    all_to_all x1, waiting for transfers between devices, reduce_weight_grad(): mine = lax.all_to_all(blocks, TM, 0, 0, tiled=True).sum(axis=0)  18.7 us
    ppermute x3, starting transfers between devices, reduce_weight_grad(): mine = mine + lax.ppermute(mine, 'dp', [(i, i ^ step) for i in range(dp)])  12.8 us
    all_to_all x1, starting transfers between devices, reduce_weight_grad(): mine = lax.all_to_all(blocks, TM, 0, 0, tiled=True).sum(axis=0)  9.7 us
    ppermute x2, starting transfers between devices, from_behind(): lax.ppermute(value, axis, [(source, source + steps) for source in range(l...  5.7 us
    pallas_call x1, Pallas kernels, forward_call(): pl.pallas_call(functools.partial(forward_kernel, hh, ww, nout, nfr), out_...  5.28 us
    ppermute x3, waiting for transfers between devices, reduce_weight_grad(): mine = mine + lax.ppermute(mine, 'dp', [(i, i ^ step) for i in range(dp)])  4.61 us
    unnamed x38, local copies, waits for them, and re-layouts  3.13 us
    dot_general x3, matrix products, per_device(): jnp.dot(patch, flipped, preferred_element_type=jnp.float32)  3.04 us
  transfers between devices with their start and end apart: 6, of which 4 were waited for; matrix products, arithmetic and copies ran while one was open for 17% of the time, Pallas kernels for 0%

profile of v6, /device:TPU:8, one launch (start us, length us, event | category | flops | bytes accessed | tf_op | source)
XLA Modules:
  0.0 77.1 jit_solution(17056617354610098463)
XLA Ops:
  0.6 1.0 %fusion.18 = (bf16[1,2,16,16,128]{4,3,2,1,0:T(8,128)(2,1)S(1)}, bf16[1,2,16,16,128]{4,3,2,1,0:T(8,128)(2,1)S(1)}) fusion(bf16[1,4,16,16,128]{4,3,2,1,0:T(8,128)(2,1)} %param.4), kind=kLoop, calls=%fused_computation.69 | loop fusion | bytes 524288 | tf_op jit(solution)/shard_map/slice | solution.py:114
  1.6 1.9 %collective-permute-start = (bf16[1,2,16,16,128]{4,3,2,1,0:T(8,128)(2,1)S(1)}, bf16[1,2,16,16,128]{4,3,2,1,0:T(8,128)(2,1)}, u32[]{:S(2)}, u32[]{:S(2)}) collective-permute-start(bf16[1,2,16,16,128]{4,3,2,1,0:T(8,128)(2,1)S(1)} %get-tuple-element.25), channel_id=1, source_target_pairs={{0,1},{1,2},{2,3},{3,4},{4,5},{5,6},{6,7},{7,8},{8,9},{9,10},{10,1... | collective-permute-start | bytes 393224 | tf_op jit(solution)/shard_map/ppermute | solution.py:16
  3.6 0.9 %slice.148 = bf16[1,2,16,16,128]{4,3,2,1,0:T(8,128)(2,1)S(1)} slice(bf16[1,4,16,16,128]{4,3,2,1,0:T(8,128)(2,1)} %param.7), slice={[0:1], [0:2], [0:16], [0:16], [0:128]} | slice | bytes 262144 | tf_op jit(solution)/shard_map/slice | solution.py:115
  4.5 3.8 %collective-permute-start.1 = (bf16[1,4,16,16,128]{4,3,2,1,0:T(8,128)(2,1)S(1)}, bf16[1,4,16,16,128]{4,3,2,1,0:T(8,128)(2,1)S(1)}, u32[]{:S(2)}, u32[]{:S(2)}) collective-permute-start(bf16[1,4,16,16,128]{4,3,2,1,0:T(8,128)(2,1)S(1)} %pad_maximum_fusion.2), channel_id=1, source_target_pairs={{1,0},{2,1},{3,2},{4,3},{5,4},{6,5},{7,6},{8,7},{9,8},{10,9},{11,1... | collective-permute-start | bytes 786440 | tf_op jit(solution)/shard_map/ppermute | solution.py:16
  8.3 0.7 pad_add_fusion
  9.1 0.1 dynamic_slice.3
  9.1 0.1 slice_compare_fusion
  9.2 1.2 %fusion.17 = (bf16[1152,128]{1,0:T(8,128)(2,1)S(1)}, bf16[1152,128]{1,0:T(8,128)(2,1)S(1)}, bf16[1152,128]{1,0:T(8,128)(2,1)S(1)}) fusion(bf16[3456,128]{1,0:T(8,128)(2,1)} %w_ref.1), kind=kLoop, calls=%fused_computation.68 | loop fusion | bytes 1769472 | tf_op jit(solution)/shard_map/slice | solution.py:139
  10.5 0.1 compare_bitcast_fusion.1
  10.6 0.9 %copy.9 = bf16[9,128,128]{2,1,0:T(8,128)(2,1)} copy(bf16[9,128,128]{1,2,0:T(8,128)(2,1)S(1)} %bitcast.56) | data formatting | bytes 589824 | tf_op jit(solution)/shard_map/transpose | solution.py:140
  11.4 0.2 copy.7
  11.7 0.9 %copy.8 = bf16[9,128,128]{2,1,0:T(8,128)(2,1)} copy(bf16[9,128,128]{1,2,0:T(8,128)(2,1)S(1)} %bitcast.54) | data formatting | bytes 589824 | tf_op jit(solution)/shard_map/transpose | solution.py:140
  12.6 0.1 pad.22.clone
  12.6 0.1 add_convert_fusion.mask_ref
  12.8 1.0 %pad_maximum_fusion = bf16[8,16,16,128]{3,2,1,0:T(8,128)(2,1)S(1)} fusion(bf16[2,16,16,128]{3,2,1,0:T(8,128)(2,1)S(1)} %get-tuple-element.24, bf16[4,16,16,128]{3,2,1,0:T(8,128)(2,1)S(1)} %bitcast.69, bf16[2,16,16,128]{3,2,1,0:T(8,128)(2,1)} %bitcast.3), kind=kLoop, calls=%fused_computation.27 | loop fusion | flops 524288 | bytes 1048576 | tf_op jit(solution)/shard_map/concatenate | solution.py:116
  13.8 5.3 %shard_map.67 = (bf16[1024,128]{1,0:T(8,128)(2,1)}, bf16[1536,128]{1,0:T(8,128)(2,1)S(1)}, f32[3456,128]{1,0:T(8,128)S(1)}) custom-call(f32[3,6]{1,0:T(4,128)S(1)} %add_convert_fusion.mask_ref, bf16[2048,128]{1,0:T(8,128)(2,1)S(1)} %bitcast.48, bf16[1536,128]{1,0:T(8,128)(2,1)S(1)} %bitcast.49, bf16[3456,128]{1,0:T(8,128)(2,1)S(1)} %copy-done), custom_call_target="tpu_custom_call" | custom-call | flops 2264924160 | bytes 3571712 | tf_op jit(solution)/shard_map/pallas_call | solution.py:87
  19.1 1.3 %reshape.76 = f32[32,108,128]{2,1,0:T(8,128)} reshape(f32[3456,128]{1,0:T(8,128)S(1)} %get-tuple-element.8) | data formatting | bytes 3538944 | tf_op jit(solution)/shard_map/reshape | solution.py:23
  20.4 9.7 %all-to-all-start = ((f32[32,108,128]{2,1,0:T(8,128)}), f32[32,108,128]{2,1,0:T(8,128)}, u32[]{:S(2)}, u32[]{:S(2)}) async-start(f32[32,108,128]{2,1,0:T(8,128)} %reshape.76), calls=%async_computation | async-start | bytes 3670016 | tf_op jit(solution)/shard_map/all_to_all | solution.py:24
  30.1 1.1 %pad_slice_fusion = (bf16[4,16,16,128]{3,2,1,0:T(8,128)(2,1)}, bf16[4,16,16,128]{3,2,1,0:T(8,128)(2,1)S(1)}, bf16[4,16,16,128]{3,2,1,0:T(8,128)(2,1)S(1)}, bf16[...) fusion(bf16[4,16,16,128]{3,2,1,0:T(8,128)(2,1)S(1)} %bitcast.62), kind=kLoop, calls=%fused_computation.3 | loop fusion | bytes 2359296 | tf_op jit(solution)/shard_map/slice | solution.py:35
  31.5 0.1 constant_dynamic-update-slice_fusion.6
  31.6 0.1 broadcast_select_fusion
  31.7 0.1 fusion.9
  31.9 0.1 fusion.11
  32.0 0.1 fusion.12
  32.2 0.1 fusion.13
  32.3 0.1 fusion.14
  32.5 0.1 fusion.16
  32.6 0.1 fusion.1
  32.8 0.1 fusion.3
  32.9 0.1 fusion.4
  33.1 0.1 fusion.5
  33.2 0.1 fusion.6
  33.4 0.1 fusion.8
  33.6 0.8 %fusion.19 = f32[1024,128]{1,0:T(8,128)S(1)} fusion(bf16[1024,1152]{1,0:T(8,128)(2,1)S(1)} %bitcast.51, bf16[1152,128]{1,0:T(8,128)(2,1)S(1)} %bitcast.57), kind=kOutput, calls=%fused_computation.70 | convolution fusion | flops 301989888 | bytes 3178496 | tf_op jit(solution)/shard_map/dot_general | solution.py:141
  34.4 0.2 copy-done.2
  34.6 0.8 %convolution_add_fusion.1 = f32[1024,128]{1,0:T(8,128)S(1)} fusion(f32[1024,128]{1,0:T(8,128)S(1)} %fusion.19, bf16[1024,1152]{1,0:T(8,128)(2,1)S(1)} %bitcast.50, bf16[1152,128]{1,0:T(8,128)(2,1)S(1)} %bitcast.53), kind=kOutput, calls=%fused_computation.1 | convolution fusion | flops 302120960 | bytes 3702784 | tf_op jit(solution)/shard_map/dot_general | solution.py:141
  35.4 18.7 %all-to-all-done = f32[32,108,128]{2,1,0:T(8,128)} async-done(((f32[32,108,128]{2,1,0:T(8,128)}), f32[32,108,128]{2,1,0:T(8,128)}, u32[]{:S(2)}, u32[]{:S(2)}) %all-to-all-start) | async-done | bytes 1769504 | tf_op jit(solution)/shard_map/all_to_all | solution.py:24
  54.0 1.6 %reduce_sum.9 = f32[108,128]{1,0:T(8,128)S(1)} reduce(f32[32,108,128]{2,1,0:T(8,128)} %all-to-all-done, f32[]{:T(128)} %constant.29.clone.1), dimensions={0}, to_apply=%region_0.1 | reduce | flops 428544 | bytes 1824772 | tf_op jit(solution)/shard_map/reduce_sum | solution.py:24
  55.7 2.0 %collective-permute-start.2 = (f32[108,128]{1,0:T(8,128)S(1)}, f32[108,128]{1,0:T(8,128)S(1)}, u32[]{:S(2)}, u32[]{:S(2)}) collective-permute-start(f32[108,128]{1,0:T(8,128)S(1)} %reduce_sum.9), channel_id=1, source_target_pairs={{0,32},{32,0},{64,96},{96,64},{128,160},{160,128},{192,224},{224,1... | collective-permute-start | bytes 165896 | tf_op jit(solution)/shard_map/ppermute | solution.py:27
  57.7 1.0 %constant_dynamic-update-slice_fusion.3 = bf16[1024,1152]{1,0:T(8,128)(2,1)S(1)} fusion(bf16[1024,1152]{1,0:T(8,128)(2,1)S(1)} %constant_dynamic-update-slice_fusion.4, bf16[1024,128]{1,0:T(8,128)(2,1)} %bitcast.59), kind=kLoop, calls=%fused_computation.53 | loop fusion | bytes 524288
  58.7 1.2 %collective-permute-done.2 = f32[108,128]{1,0:T(8,128)S(1)} collective-permute-done((f32[108,128]{1,0:T(8,128)S(1)}, f32[108,128]{1,0:T(8,128)S(1)}, u32[]{:S(2)}, u32[]{:S(2)}) %collective-permute-start.2) | collective-permute-done | bytes 55328 | tf_op jit(solution)/shard_map/ppermute | solution.py:27
  59.9 0.8 %add.31 = f32[108,128]{1,0:T(8,128)S(1)} add(f32[108,128]{1,0:T(8,128)} %copy-done.6, f32[108,128]{1,0:T(8,128)S(1)} %collective-permute-done.2) | non-fusion elementwise | flops 13824 | bytes 165888 | tf_op jit(solution)/shard_map/add | solution.py:27
  60.7 3.3 %collective-permute-start.3 = (f32[108,128]{1,0:T(8,128)S(1)}, f32[108,128]{1,0:T(8,128)S(1)}, u32[]{:S(2)}, u32[]{:S(2)}) collective-permute-start(f32[108,128]{1,0:T(8,128)S(1)} %add.31), channel_id=1, source_target_pairs={{0,64},{32,96},{64,0},{96,32},{128,192},{160,224},{192,128},{224,1... | collective-permute-start | bytes 165896 | tf_op jit(solution)/shard_map/ppermute | solution.py:27
  64.1 2.1 %collective-permute-done.3 = f32[108,128]{1,0:T(8,128)S(1)} collective-permute-done((f32[108,128]{1,0:T(8,128)S(1)}, f32[108,128]{1,0:T(8,128)S(1)}, u32[]{:S(2)}, u32[]{:S(2)}) %collective-permute-start.3) | collective-permute-done | bytes 55328 | tf_op jit(solution)/shard_map/ppermute | solution.py:27
  66.2 7.5 %collective-permute-start.4 = (f32[108,128]{1,0:T(8,128)S(1)}, f32[108,128]{1,0:T(8,128)S(1)}, u32[]{:S(2)}, u32[]{:S(2)}) collective-permute-start(f32[108,128]{1,0:T(8,128)S(1)} %add.32), channel_id=1, source_target_pairs={{0,128},{32,160},{64,192},{96,224},{128,0},{160,32},{192,64},{224,... | collective-permute-start | bytes 165896 | tf_op jit(solution)/shard_map/ppermute | solution.py:27
  73.7 1.5 %fusion = bf16[1024,128]{1,0:T(8,128)(2,1)} fusion(f32[1024,128]{1,0:T(8,128)S(1)} %convolution_add_fusion.1, bf16[1024,1152]{1,0:T(8,128)(2,1)S(1)} %constant_dynamic-update-slice_fusion.2, bf16[1152,128]{1,0:T(8,128)(2,1)S(1)} %bitcast.52), kind=kOutput, calls=%fused_computation.2 | convolution fusion | flops 302252032 | bytes 3440640 | tf_op jit(solution)/shard_map/dot_general | solution.py:141
  75.2 1.3 %collective-permute-done.4 = f32[108,128]{1,0:T(8,128)S(1)} collective-permute-done((f32[108,128]{1,0:T(8,128)S(1)}, f32[108,128]{1,0:T(8,128)S(1)}, u32[]{:S(2)}, u32[]{:S(2)}) %collective-permute-start.4) | collective-permute-done | bytes 55328 | tf_op jit(solution)/shard_map/ppermute | solution.py:27
  76.5 0.6 add_multiply_fusion
  (35 shorter events, 1.0 us)
Async XLA Ops:
  1.6 11.2 %collective-permute-start = (bf16[1,2,16,16,128]{4,3,2,1,0:T(8,128)(2,1)S(1)}, bf16[1,2,16,16,128]{4,3,2,1,0:T(8,128)(2,1)}, u32[]{:S(2)}, u32[]{:S(2)}) collective-permute-start(bf16[1,2,16,16,128]{4,3,2,1,0:T(8,128)(2,1)S(1)} %get-tuple-element.25), channel_id=1, source_target_pairs={{0,1},{1,2},{2,3},{3,4},{4,5},{5,6},{6,7},{7,8},{8,9},{9,10},{10,1... | collective-permute-start | bytes 393224 | tf_op jit(solution)/shard_map/ppermute | solution.py:16
  4.5 8.3 %copy-start.5 = (bf16[1,4,16,16,128]{4,3,2,1,0:T(8,128)(2,1)S(1)}, bf16[1,4,16,16,128]{4,3,2,1,0:T(8,128)(2,1)}, u32[]{:S(2)}) copy-start(bf16[1,4,16,16,128]{4,3,2,1,0:T(8,128)(2,1)} %param.7) | copy-start | bytes 786436
  4.5 8.2 %collective-permute-start.1 = (bf16[1,4,16,16,128]{4,3,2,1,0:T(8,128)(2,1)S(1)}, bf16[1,4,16,16,128]{4,3,2,1,0:T(8,128)(2,1)S(1)}, u32[]{:S(2)}, u32[]{:S(2)}) collective-permute-start(bf16[1,4,16,16,128]{4,3,2,1,0:T(8,128)(2,1)S(1)} %pad_maximum_fusion.2), channel_id=1, source_target_pairs={{1,0},{2,1},{3,2},{4,3},{5,4},{6,5},{7,6},{8,7},{9,8},{10,9},{11,1... | collective-permute-start | bytes 786440 | tf_op jit(solution)/shard_map/ppermute | solution.py:16
  9.2 3.6 %copy-start.4 = (bf16[1,4,16,16,128]{4,3,2,1,0:T(8,128)(2,1)S(1)}, bf16[1,4,16,16,128]{4,3,2,1,0:T(8,128)(2,1)}, u32[]{:S(2)}) copy-start(bf16[1,4,16,16,128]{4,3,2,1,0:T(8,128)(2,1)} %param.4) | copy-start | bytes 786436
  10.5 3.3 %copy-start = (bf16[3456,128]{1,0:T(8,128)(2,1)S(1)}, bf16[3456,128]{1,0:T(8,128)(2,1)}, u32[]{:S(2)}) copy-start(bf16[3456,128]{1,0:T(8,128)(2,1)} %w_ref.1) | copy-start | bytes 2654212
  20.4 33.6 %all-to-all-start = ((f32[32,108,128]{2,1,0:T(8,128)}), f32[32,108,128]{2,1,0:T(8,128)}, u32[]{:S(2)}, u32[]{:S(2)}) async-start(f32[32,108,128]{2,1,0:T(8,128)} %reshape.76), calls=%async_computation | async-start | bytes 3670016 | tf_op jit(solution)/shard_map/all_to_all | solution.py:24
  33.6 1.0 %copy-start.2 = (bf16[9,128,128]{2,1,0:T(8,128)(2,1)S(1)}, bf16[9,128,128]{2,1,0:T(8,128)(2,1)}, u32[]{:S(2)}) copy-start(bf16[9,128,128]{2,1,0:T(8,128)(2,1)} %copy.8) | copy-start | bytes 884740
  35.4 28.7 %copy-start.3 = (bf16[4,16,16,128]{3,2,1,0:T(8,128)(2,1)S(1)}, bf16[4,16,16,128]{3,2,1,0:T(8,128)(2,1)}, u32[]{:S(2)}) copy-start(bf16[4,16,16,128]{3,2,1,0:T(8,128)(2,1)} %get-tuple-element.15) | copy-start | bytes 786436
  35.4 38.4 %copy-start.1 = (bf16[9,128,128]{2,1,0:T(8,128)(2,1)S(1)}, bf16[9,128,128]{2,1,0:T(8,128)(2,1)}, u32[]{:S(2)}) copy-start(bf16[9,128,128]{2,1,0:T(8,128)(2,1)} %copy.9) | copy-start | bytes 884740
  55.6 3.0 %copy-start.6 = (f32[108,128]{1,0:T(8,128)}, f32[108,128]{1,0:T(8,128)S(1)}, u32[]{:S(2)}) copy-start(f32[108,128]{1,0:T(8,128)S(1)} %reduce_sum.9) | copy-start | bytes 165892
  55.7 4.3 %collective-permute-start.2 = (f32[108,128]{1,0:T(8,128)S(1)}, f32[108,128]{1,0:T(8,128)S(1)}, u32[]{:S(2)}, u32[]{:S(2)}) collective-permute-start(f32[108,128]{1,0:T(8,128)S(1)} %reduce_sum.9), channel_id=1, source_target_pairs={{0,32},{32,0},{64,96},{96,64},{128,160},{160,128},{192,224},{224,1... | collective-permute-start | bytes 165896 | tf_op jit(solution)/shard_map/ppermute | solution.py:27
  60.7 5.4 %collective-permute-start.3 = (f32[108,128]{1,0:T(8,128)S(1)}, f32[108,128]{1,0:T(8,128)S(1)}, u32[]{:S(2)}, u32[]{:S(2)}) collective-permute-start(f32[108,128]{1,0:T(8,128)S(1)} %add.31), channel_id=1, source_target_pairs={{0,64},{32,96},{64,0},{96,32},{128,192},{160,224},{192,128},{224,1... | collective-permute-start | bytes 165896 | tf_op jit(solution)/shard_map/ppermute | solution.py:27
  66.2 10.3 %collective-permute-start.4 = (f32[108,128]{1,0:T(8,128)S(1)}, f32[108,128]{1,0:T(8,128)S(1)}, u32[]{:S(2)}, u32[]{:S(2)}) collective-permute-start(f32[108,128]{1,0:T(8,128)S(1)} %add.32), channel_id=1, source_target_pairs={{0,128},{32,160},{64,192},{96,224},{128,0},{160,32},{192,64},{224,... | collective-permute-start | bytes 165896 | tf_op jit(solution)/shard_map/ppermute | solution.py:27

commit v7 on v6

--- a/solution.py
+++ b/solution.py
@@ -19,9 +19,7 @@
 def reduce_weight_grad(grad_local):
     tm = lax.axis_size("chip") * lax.axis_size("core")
     dp = lax.axis_size("dp")
-    rows, cols = grad_local.shape
-    blocks = grad_local.reshape(tm, rows // tm, cols)
-    mine = lax.all_to_all(blocks, TM, 0, 0, tiled=True).sum(axis=0)
+    mine = lax.all_to_all(grad_local, TM, 0, 0, tiled=True).sum(axis=0)
     step = 1
     while step < dp:
         mine = mine + lax.ppermute(mine, "dp", [(i, i ^ step) for i in range(dp)])
@@ -39,9 +37,9 @@
     return jnp.concatenate(pieces, axis=3).reshape(-1, 9 * frames.shape[-1])
 
 
-def forward_kernel(hh, ww, nout, nfr, mask_ref, xe_ref, ce_ref, w_ref, act_ref, gp_ref, gw_ref, col_ref, pad_ref, acc_ref):
+def forward_kernel(hh, ww, nout, nfr, mask_ref, early_ref, own_ref, ahead_ref, cot_ref, w_ref, act_ref, gp_ref, gw_ref, col_ref, pad_ref, acc_ref, flat_ref):
     frame = hh * ww
-    cc = xe_ref.shape[1]
+    cc = own_ref.shape[1]
     taps = 9 * cc
     lead = 2 * ww
     r = lax.broadcasted_iota(jnp.int32, (frame, cc), 0)
@@ -49,7 +47,13 @@
     j = r % ww
     pad_ref[...] = jnp.zeros_like(pad_ref)
     for f in range(nout + 2):
-        pad_ref[pl.ds(lead, frame), :] = xe_ref[pl.ds(f * frame, frame), :].astype(jnp.float32)
+        if f < 2:
+            source = early_ref[pl.ds(f * frame, frame), :]
+        elif f < nfr + 2:
+            source = own_ref[pl.ds((f - 2) * frame, frame), :]
+        else:
+            source = ahead_ref[pl.ds((f - nfr - 2) * frame, frame), :]
+        pad_ref[pl.ds(lead, frame), :] = source.astype(jnp.float32)
         for ky in range(3):
             for kx in range(3):
                 dy, dx = ky - 1, kx - 1
@@ -65,7 +69,10 @@
         sig = 1.0 / (1.0 + jnp.exp(-pre))
         if t < nfr:
             act_ref[pl.ds(t * frame, frame), :] = (pre * sig).astype(act_ref.dtype)
-        cot = ce_ref[pl.ds(t * frame, frame), :].astype(jnp.float32)
+        if t < nfr:
+            cot = cot_ref[pl.ds(t * frame, frame), :].astype(jnp.float32)
+        else:
+            cot = ahead_ref[pl.ds((t - nfr + 2) * frame, frame), :].astype(jnp.float32)
         gp_ref[pl.ds(t * frame, frame), :] = (cot * sig * (1.0 + pre * (1.0 - sig))).astype(gp_ref.dtype)
     acc_ref[...] = jnp.zeros_like(acc_ref)
     for t in range(nfr):
@@ -75,12 +82,15 @@
             part = jnp.dot(gt, col_ref[t + kt], preferred_element_type=jnp.float32)
             acc_ref[kt] = acc_ref[kt] + mask_ref[kt, t] * part
     for kt in range(3):
-        gw_ref[pl.ds(kt * taps, taps), :] = jnp.transpose(acc_ref[kt])
+        flat_ref[pl.ds(kt * taps, taps), :] = jnp.transpose(acc_ref[kt])
+    blocks, share = gw_ref.shape[0], gw_ref.shape[1]
+    for b in range(blocks):
+        gw_ref[b] = flat_ref[pl.ds(b * share, share), :]
 
 
-def forward_call(mask, xe, ce, w, hh, ww, nout, nfr):
+def forward_call(mask, early, own, ahead, cot, w, hh, ww, nout, nfr, blocks):
     frame = hh * ww
-    cc = xe.shape[1]
+    cc = own.shape[1]
     krows = w.shape[0]
     vmem = pl.BlockSpec(memory_space=pltpu.VMEM)
     flops = 2 * 3 * frame * 9 * cc * cc * (nout + nfr)
@@ -89,20 +99,23 @@
         out_shape=(
             jax.ShapeDtypeStruct((nfr * frame, cc), jnp.bfloat16),
             jax.ShapeDtypeStruct((nout * frame, cc), jnp.bfloat16),
-            jax.ShapeDtypeStruct((krows, cc), jnp.float32),
+            jax.ShapeDtypeStruct((blocks, krows // blocks, cc), jnp.float32),
         ),
-        in_specs=[pl.BlockSpec(memory_space=pltpu.SMEM), vmem, vmem, vmem],
+        in_specs=[pl.BlockSpec(memory_space=pltpu.SMEM), vmem, vmem, vmem, vmem, vmem],
         out_specs=(vmem, vmem, vmem),
         scratch_shapes=[
             pltpu.VMEM((nout + 2, frame, 9 * cc), jnp.bfloat16),
             pltpu.VMEM((frame + 4 * ww, cc), jnp.float32),
             pltpu.VMEM((3, cc, 9 * cc), jnp.float32),
+            pltpu.VMEM((krows, cc), jnp.float32),
         ],
         compiler_params=pltpu.CompilerParams(vmem_limit_bytes=48 * 1024 * 1024),
         cost_estimate=pl.CostEstimate(
-            flops=flops, transcendentals=nout * frame * cc, bytes_accessed=2 * (xe.size + ce.size + w.size) + 4 * krows * cc
+            flops=flops,
+            transcendentals=nout * frame * cc,
+            bytes_accessed=2 * (early.size + own.size + ahead.size + cot.size + w.size) + 4 * krows * cc,
         ),
-    )(mask, xe, ce, w)
+    )(mask, early, own, ahead, cot, w)
 
 
 def per_device(clips, segment_ids, conv_weight, cotangent):
@@ -113,8 +126,6 @@
     rows = nfr * hh * ww
     earlier = from_behind(clips[:, nfr - 2 :], TM, 1)[0]
     ahead = from_behind(jnp.concatenate([clips[:, :2], cotangent[:, :2]], axis=1), TM, -1)[0]
-    frames = jnp.concatenate([earlier, clips[0], ahead[:2]], axis=0)
-    cot_ext = jnp.concatenate([cotangent[0], ahead[2:]], axis=0)
     segrow = segment_ids[0]
     segp = jnp.concatenate([jnp.full((2,), -1, jnp.int32), segrow, jnp.full((2,), -2, jnp.int32)])
     start = (lax.axis_index("chip") * lax.axis_size("core") + lax.axis_index("core")) * nfr
@@ -122,8 +133,19 @@
     nout = nfr + 2
     centre = seglocal[2 : 2 + nout]
     mask = jnp.stack([(seglocal[kt : kt + nout] == centre) for kt in range(3)]).astype(jnp.float32)
+    tm = lax.axis_size("chip") * lax.axis_size("core")
     act, grad_pre, grad_local = forward_call(
-        mask, frames.reshape(-1, cc), cot_ext.reshape(-1, cc), conv_weight, hh, ww, nout, nfr
+        mask,
+        earlier.reshape(-1, cc),
+        clips.reshape(-1, cc),
+        ahead.reshape(-1, cc),
+        cotangent.reshape(-1, cc),
+        conv_weight,
+        hh,
+        ww,
+        nout,
+        nfr,
+        tm,
     )
     activated = act.reshape(clips.shape)
     count = lax.axis_size("dp") * (lax.axis_size("chip") * lax.axis_size("core")) * rows

time: 77.8 us -> 75.7 us (0.973)
  other arithmetic: 5.17 us -> 3.34 us
  local copies, waits for them, and re-layouts: 11.2 us -> 9.71 us
  Pallas kernels: 5.28 us -> 6.41 us
    reshape x1 -> x0, local copies, waits for them, and re-layouts: 1.34 us -> none  [reduce_weight_grad(): blocks = grad_local.reshape(tm, rows // tm, cols)]
    pallas_call x1, Pallas kernels: 5.28 us -> 6.41 us  [forward_call(): pl.pallas_call(functools.partial(forward_kernel, hh, ww, nout, nfr), out_...]
    concatenate x2 -> x0, other arithmetic: 1 us -> none  [the longest x1 0.97 us: per_device(): frames = jnp.concatenate([earlier, clips[0], ahead[:2]], axis=0)]
    add x2, other arithmetic: 0.84 us -> 0.02 us  [reduce_weight_grad(): mine = mine + lax.ppermute(mine, 'dp', [(i, i ^ step) for i in range(dp)])]
    unnamed x38 -> x34, local copies, waits for them, and re-layouts: 3.13 us -> 3.12 us
where the time goes in v7:
time: 75.7 us; the launch traced here: 75.1 us
  starting transfers between devices  28.2 us (37%)
  waiting for transfers between devices  23.4 us (31%)
  local copies, waits for them, and re-layouts  9.71 us (13%)
  Pallas kernels  6.41 us (8%)
  other arithmetic  3.34 us (4%)
  matrix products  3.04 us (4%)
  between operations  0.97 us (1%)
    all_to_all x1, waiting for transfers between devices, reduce_weight_grad(): mine = lax.all_to_all(grad_local, TM, 0, 0, tiled=True).sum(axis=0)  18.8 us
    ppermute x3, starting transfers between devices, reduce_weight_grad(): mine = mine + lax.ppermute(mine, 'dp', [(i, i ^ step) for i in range(dp)])  12.9 us
    all_to_all x1, starting transfers between devices, reduce_weight_grad(): mine = lax.all_to_all(grad_local, TM, 0, 0, tiled=True).sum(axis=0)  9.73 us
    pallas_call x1, Pallas kernels, forward_call(): pl.pallas_call(functools.partial(forward_kernel, hh, ww, nout, nfr), out_...  6.41 us
    ppermute x2, starting transfers between devices, from_behind(): lax.ppermute(value, axis, [(source, source + steps) for source in range(l...  5.56 us
    ppermute x3, waiting for transfers between devices, reduce_weight_grad(): mine = mine + lax.ppermute(mine, 'dp', [(i, i ^ step) for i in range(dp)])  4.62 us
    unnamed x34, local copies, waits for them, and re-layouts  3.12 us
    dot_general x3, matrix products, per_device(): jnp.dot(patch, flipped, preferred_element_type=jnp.float32)  3.04 us
  transfers between devices with their start and end apart: 6, of which 4 were waited for; matrix products, arithmetic and copies ran while one was open for 17% of the time, Pallas kernels for 0%

profile of v7, /device:TPU:8, one launch (start us, length us, event | category | flops | bytes accessed | tf_op | source)
XLA Modules:
  0.0 75.1 jit_solution(15831359228062284026)
XLA Ops:
  0.7 1.1 %fusion.18 = (bf16[1,2,16,16,128]{4,3,2,1,0:T(8,128)(2,1)S(1)}, bf16[1,2,16,16,128]{4,3,2,1,0:T(8,128)(2,1)S(1)}) fusion(bf16[1,4,16,16,128]{4,3,2,1,0:T(8,128)(2,1)} %param.4), kind=kLoop, calls=%fused_computation.65 | loop fusion | bytes 524288 | tf_op jit(solution)/shard_map/slice | solution.py:128
  1.8 1.9 %collective-permute-start = (bf16[1,2,16,16,128]{4,3,2,1,0:T(8,128)(2,1)S(1)}, bf16[1,2,16,16,128]{4,3,2,1,0:T(8,128)(2,1)S(1)}, u32[]{:S(2)}, u32[]{:S(2)}) collective-permute-start(bf16[1,2,16,16,128]{4,3,2,1,0:T(8,128)(2,1)S(1)} %get-tuple-element.24), channel_id=1, source_target_pairs={{0,1},{1,2},{2,3},{3,4},{4,5},{5,6},{6,7},{7,8},{8,9},{9,10},{10,1... | collective-permute-start | bytes 393224 | tf_op jit(solution)/shard_map/ppermute | solution.py:16
  3.7 0.9 %slice.136 = bf16[1,2,16,16,128]{4,3,2,1,0:T(8,128)(2,1)S(1)} slice(bf16[1,4,16,16,128]{4,3,2,1,0:T(8,128)(2,1)} %param.7), slice={[0:1], [0:2], [0:16], [0:16], [0:128]} | slice | bytes 262144 | tf_op jit(solution)/shard_map/slice | solution.py:128
  4.6 3.6 %collective-permute-start.1 = (bf16[1,4,16,16,128]{4,3,2,1,0:T(8,128)(2,1)S(1)}, bf16[1,4,16,16,128]{4,3,2,1,0:T(8,128)(2,1)S(1)}, u32[]{:S(2)}, u32[]{:S(2)}) collective-permute-start(bf16[1,4,16,16,128]{4,3,2,1,0:T(8,128)(2,1)S(1)} %pad_maximum_fusion), channel_id=1, source_target_pairs={{1,0},{2,1},{3,2},{4,3},{5,4},{6,5},{7,6},{8,7},{9,8},{10,9},{11,1... | collective-permute-start | bytes 786440 | tf_op jit(solution)/shard_map/ppermute | solution.py:16
  8.3 0.7 pad_add_fusion
  9.1 0.1 dynamic_slice.3
  9.1 0.1 compare_bitcast_fusion.1
  9.2 1.2 %fusion.17 = (bf16[1152,128]{1,0:T(8,128)(2,1)S(1)}, bf16[1152,128]{1,0:T(8,128)(2,1)S(1)}, bf16[1152,128]{1,0:T(8,128)(2,1)S(1)}) fusion(bf16[3456,128]{1,0:T(8,128)(2,1)} %w_ref.1), kind=kLoop, calls=%fused_computation.64 | loop fusion | bytes 1769472 | tf_op jit(solution)/shard_map/slice | solution.py:161
  10.4 0.1 pad.17.clone
  10.5 0.1 add_convert_fusion.mask_ref
  10.6 0.9 %copy.9 = bf16[9,128,128]{2,1,0:T(8,128)(2,1)} copy(bf16[9,128,128]{1,2,0:T(8,128)(2,1)S(1)} %bitcast.53) | data formatting | bytes 589824 | tf_op jit(solution)/shard_map/transpose | solution.py:162
  11.5 0.2 copy.7
  11.7 0.9 %copy.8 = bf16[9,128,128]{2,1,0:T(8,128)(2,1)} copy(bf16[9,128,128]{1,2,0:T(8,128)(2,1)S(1)} %bitcast.51) | data formatting | bytes 589824 | tf_op jit(solution)/shard_map/transpose | solution.py:162
  12.6 0.1 slice_compare_fusion
  12.7 6.4 %shard_map.67 = (bf16[1024,128]{1,0:T(8,128)(2,1)}, bf16[1536,128]{1,0:T(8,128)(2,1)S(1)}, f32[32,108,128]{2,1,0:T(8,128)}) custom-call(f32[3,6]{1,0:T(4,128)S(1)} %add_convert_fusion.mask_ref, bf16[512,128]{1,0:T(8,128)(2,1)S(1)} %bitcast.46, bf16[1024,128]{1,0:T(8,128)(2,1)S(1)} %bitcast.43, bf16[1024,128]{1,0:T(8,128)(2,1)S(1)} %bitcast.45, ...), custom_call_target="tpu_custom_call" | custom-call | flops 2264924160 | bytes 3571712 | tf_op jit(solution)/shard_map/pallas_call | solution.py:97
  19.1 9.7 %all-to-all-start = ((f32[32,108,128]{2,1,0:T(8,128)}), f32[32,108,128]{2,1,0:T(8,128)}, u32[]{:S(2)}, u32[]{:S(2)}) async-start(f32[32,108,128]{2,1,0:T(8,128)} %get-tuple-element.8), calls=%async_computation | async-start | bytes 3670016 | tf_op jit(solution)/shard_map/all_to_all | solution.py:22
  28.9 0.9 %pad_slice_fusion = (bf16[4,16,16,128]{3,2,1,0:T(8,128)(2,1)S(1)}, bf16[4,16,16,128]{3,2,1,0:T(8,128)(2,1)S(1)}, bf16[4,16,16,128]{3,2,1,0:T(8,128)(2,1)S(1)}, b...) fusion(bf16[4,16,16,128]{3,2,1,0:T(8,128)(2,1)S(1)} %bitcast.63), kind=kLoop, calls=%fused_computation.3 | loop fusion | bytes 2359296 | tf_op jit(solution)/shard_map/slice | solution.py:33
  30.1 0.1 constant_dynamic-update-slice_fusion.6
  30.2 0.1 broadcast_select_fusion
  30.3 0.1 fusion.9
  30.4 0.1 fusion.10
  30.5 0.1 fusion.11
  30.6 0.1 fusion.12
  30.7 0.1 constant_dynamic-update-slice_fusion.1
  30.8 0.1 fusion.13
  30.9 0.1 fusion.14
  31.1 0.1 fusion.16
  31.2 0.1 fusion.1
  31.3 0.1 fusion.2
  31.3 0.1 fusion.3
  31.4 0.1 fusion.4
  31.6 0.1 fusion.5
  31.7 0.1 fusion.6
  31.9 0.1 fusion.8
  32.2 0.8 %fusion.19 = f32[1024,128]{1,0:T(8,128)S(1)} fusion(bf16[1024,1152]{1,0:T(8,128)(2,1)S(1)} %bitcast.48, bf16[1152,128]{1,0:T(8,128)(2,1)S(1)} %bitcast.54), kind=kOutput, calls=%fused_computation.66 | convolution fusion | flops 301989888 | bytes 3178496 | tf_op jit(solution)/shard_map/dot_general | solution.py:163
  33.0 0.2 copy-done.4
  33.2 0.8 %convolution_add_fusion.1 = f32[1024,128]{1,0:T(8,128)S(1)} fusion(f32[1024,128]{1,0:T(8,128)S(1)} %fusion.19, bf16[1024,1152]{1,0:T(8,128)(2,1)S(1)} %bitcast.47, bf16[1152,128]{1,0:T(8,128)(2,1)S(1)} %bitcast.50), kind=kOutput, calls=%fused_computation.1 | convolution fusion | flops 302120960 | bytes 3702784 | tf_op jit(solution)/shard_map/dot_general | solution.py:163
  33.9 18.8 %all-to-all-done = f32[32,108,128]{2,1,0:T(8,128)} async-done(((f32[32,108,128]{2,1,0:T(8,128)}), f32[32,108,128]{2,1,0:T(8,128)}, u32[]{:S(2)}, u32[]{:S(2)}) %all-to-all-start) | async-done | bytes 1769504 | tf_op jit(solution)/shard_map/all_to_all | solution.py:22
  52.7 1.6 %reduce_sum.9 = f32[108,128]{1,0:T(8,128)S(1)} reduce(f32[32,108,128]{2,1,0:T(8,128)} %all-to-all-done, f32[]{:T(128)} %constant.29.clone.1), dimensions={0}, to_apply=%region_0.1 | reduce | flops 428544 | bytes 1824772 | tf_op jit(solution)/shard_map/reduce_sum | solution.py:22
  54.3 2.0 %collective-permute-start.2 = (f32[108,128]{1,0:T(8,128)S(1)}, f32[108,128]{1,0:T(8,128)S(1)}, u32[]{:S(2)}, u32[]{:S(2)}) collective-permute-start(f32[108,128]{1,0:T(8,128)S(1)} %reduce_sum.9), channel_id=1, source_target_pairs={{0,32},{32,0},{64,96},{96,64},{128,160},{160,128},{192,224},{224,1... | collective-permute-start | bytes 165896 | tf_op jit(solution)/shard_map/ppermute | solution.py:25
  56.3 1.0 %constant_dynamic-update-slice_fusion.3 = bf16[1024,1152]{1,0:T(8,128)(2,1)S(1)} fusion(bf16[1024,1152]{1,0:T(8,128)(2,1)S(1)} %constant_dynamic-update-slice_fusion.4, bf16[1024,128]{1,0:T(8,128)(2,1)} %bitcast.56), kind=kLoop, calls=%fused_computation.49 | loop fusion | bytes 524288
  57.4 1.2 %collective-permute-done.2 = f32[108,128]{1,0:T(8,128)S(1)} collective-permute-done((f32[108,128]{1,0:T(8,128)S(1)}, f32[108,128]{1,0:T(8,128)S(1)}, u32[]{:S(2)}, u32[]{:S(2)}) %collective-permute-start.2) | collective-permute-done | bytes 55328 | tf_op jit(solution)/shard_map/ppermute | solution.py:25
  58.6 3.4 %collective-permute-start.3 = (f32[108,128]{1,0:T(8,128)S(1)}, f32[108,128]{1,0:T(8,128)S(1)}, u32[]{:S(2)}, u32[]{:S(2)}) collective-permute-start(f32[108,128]{1,0:T(8,128)S(1)} %add.31), channel_id=1, source_target_pairs={{0,64},{32,96},{64,0},{96,32},{128,192},{160,224},{192,128},{224,1... | collective-permute-start | bytes 165896 | tf_op jit(solution)/shard_map/ppermute | solution.py:25
  62.0 2.1 %collective-permute-done.3 = f32[108,128]{1,0:T(8,128)S(1)} collective-permute-done((f32[108,128]{1,0:T(8,128)S(1)}, f32[108,128]{1,0:T(8,128)S(1)}, u32[]{:S(2)}, u32[]{:S(2)}) %collective-permute-start.3) | collective-permute-done | bytes 55328 | tf_op jit(solution)/shard_map/ppermute | solution.py:25
  64.1 7.5 %collective-permute-start.4 = (f32[108,128]{1,0:T(8,128)S(1)}, f32[108,128]{1,0:T(8,128)S(1)}, u32[]{:S(2)}, u32[]{:S(2)}) collective-permute-start(f32[108,128]{1,0:T(8,128)S(1)} %add.32), channel_id=1, source_target_pairs={{0,128},{32,160},{64,192},{96,224},{128,0},{160,32},{192,64},{224,... | collective-permute-start | bytes 165896 | tf_op jit(solution)/shard_map/ppermute | solution.py:25
  71.7 1.5 %fusion = bf16[1024,128]{1,0:T(8,128)(2,1)} fusion(f32[1024,128]{1,0:T(8,128)S(1)} %convolution_add_fusion.1, bf16[1024,1152]{1,0:T(8,128)(2,1)S(1)} %constant_dynamic-update-slice_fusion.2, bf16[1152,128]{1,0:T(8,128)(2,1)S(1)} %bitcast.49), kind=kOutput, calls=%fused_computation.2 | convolution fusion | flops 302252032 | bytes 3440640 | tf_op jit(solution)/shard_map/dot_general | solution.py:163
  73.2 1.3 %collective-permute-done.4 = f32[108,128]{1,0:T(8,128)S(1)} collective-permute-done((f32[108,128]{1,0:T(8,128)S(1)}, f32[108,128]{1,0:T(8,128)S(1)}, u32[]{:S(2)}, u32[]{:S(2)}) %collective-permute-start.4) | collective-permute-done | bytes 55328 | tf_op jit(solution)/shard_map/ppermute | solution.py:25
  74.4 0.6 add_multiply_fusion
  (27 shorter events, 0.7 us)
Async XLA Ops:
  0.6 12.0 %copy-start.1 = (bf16[1,4,16,16,128]{4,3,2,1,0:T(8,128)(2,1)S(1)}, bf16[1,4,16,16,128]{4,3,2,1,0:T(8,128)(2,1)}, u32[]{:S(2)}) copy-start(bf16[1,4,16,16,128]{4,3,2,1,0:T(8,128)(2,1)} %param.4) | copy-start | bytes 786436
  0.6 12.0 %copy-start.2 = (bf16[1,4,16,16,128]{4,3,2,1,0:T(8,128)(2,1)S(1)}, bf16[1,4,16,16,128]{4,3,2,1,0:T(8,128)(2,1)}, u32[]{:S(2)}) copy-start(bf16[1,4,16,16,128]{4,3,2,1,0:T(8,128)(2,1)} %param.7) | copy-start | bytes 786436
  0.7 12.0 %copy-start = (bf16[3456,128]{1,0:T(8,128)(2,1)S(1)}, bf16[3456,128]{1,0:T(8,128)(2,1)}, u32[]{:S(2)}) copy-start(bf16[3456,128]{1,0:T(8,128)(2,1)} %w_ref.1) | copy-start | bytes 2654212
  1.8 10.9 %collective-permute-start = (bf16[1,2,16,16,128]{4,3,2,1,0:T(8,128)(2,1)S(1)}, bf16[1,2,16,16,128]{4,3,2,1,0:T(8,128)(2,1)S(1)}, u32[]{:S(2)}, u32[]{:S(2)}) collective-permute-start(bf16[1,2,16,16,128]{4,3,2,1,0:T(8,128)(2,1)S(1)} %get-tuple-element.24), channel_id=1, source_target_pairs={{0,1},{1,2},{2,3},{3,4},{4,5},{5,6},{6,7},{7,8},{8,9},{9,10},{10,1... | collective-permute-start | bytes 393224 | tf_op jit(solution)/shard_map/ppermute | solution.py:16
  4.6 8.0 %collective-permute-start.1 = (bf16[1,4,16,16,128]{4,3,2,1,0:T(8,128)(2,1)S(1)}, bf16[1,4,16,16,128]{4,3,2,1,0:T(8,128)(2,1)S(1)}, u32[]{:S(2)}, u32[]{:S(2)}) collective-permute-start(bf16[1,4,16,16,128]{4,3,2,1,0:T(8,128)(2,1)S(1)} %pad_maximum_fusion), channel_id=1, source_target_pairs={{1,0},{2,1},{3,2},{4,3},{5,4},{6,5},{7,6},{8,7},{9,8},{10,9},{11,1... | collective-permute-start | bytes 786440 | tf_op jit(solution)/shard_map/ppermute | solution.py:16
  19.1 33.6 %all-to-all-start = ((f32[32,108,128]{2,1,0:T(8,128)}), f32[32,108,128]{2,1,0:T(8,128)}, u32[]{:S(2)}, u32[]{:S(2)}) async-start(f32[32,108,128]{2,1,0:T(8,128)} %get-tuple-element.8), calls=%async_computation | async-start | bytes 3670016 | tf_op jit(solution)/shard_map/all_to_all | solution.py:22
  32.2 1.0 %copy-start.4 = (bf16[9,128,128]{2,1,0:T(8,128)(2,1)S(1)}, bf16[9,128,128]{2,1,0:T(8,128)(2,1)}, u32[]{:S(2)}) copy-start(bf16[9,128,128]{2,1,0:T(8,128)(2,1)} %copy.8) | copy-start | bytes 884740
  33.9 37.7 %copy-start.3 = (bf16[9,128,128]{2,1,0:T(8,128)(2,1)S(1)}, bf16[9,128,128]{2,1,0:T(8,128)(2,1)}, u32[]{:S(2)}) copy-start(bf16[9,128,128]{2,1,0:T(8,128)(2,1)} %copy.9) | copy-start | bytes 884740
  54.3 4.3 %collective-permute-start.2 = (f32[108,128]{1,0:T(8,128)S(1)}, f32[108,128]{1,0:T(8,128)S(1)}, u32[]{:S(2)}, u32[]{:S(2)}) collective-permute-start(f32[108,128]{1,0:T(8,128)S(1)} %reduce_sum.9), channel_id=1, source_target_pairs={{0,32},{32,0},{64,96},{96,64},{128,160},{160,128},{192,224},{224,1... | collective-permute-start | bytes 165896 | tf_op jit(solution)/shard_map/ppermute | solution.py:25
  58.6 5.5 %collective-permute-start.3 = (f32[108,128]{1,0:T(8,128)S(1)}, f32[108,128]{1,0:T(8,128)S(1)}, u32[]{:S(2)}, u32[]{:S(2)}) collective-permute-start(f32[108,128]{1,0:T(8,128)S(1)} %add.31), channel_id=1, source_target_pairs={{0,64},{32,96},{64,0},{96,32},{128,192},{160,224},{192,128},{224,1... | collective-permute-start | bytes 165896 | tf_op jit(solution)/shard_map/ppermute | solution.py:25
  64.1 10.3 %collective-permute-start.4 = (f32[108,128]{1,0:T(8,128)S(1)}, f32[108,128]{1,0:T(8,128)S(1)}, u32[]{:S(2)}, u32[]{:S(2)}) collective-permute-start(f32[108,128]{1,0:T(8,128)S(1)} %add.32), channel_id=1, source_target_pairs={{0,128},{32,160},{64,192},{96,224},{128,0},{160,32},{192,64},{224,... | collective-permute-start | bytes 165896 | tf_op jit(solution)/shard_map/ppermute | solution.py:25

commit v8 on v7

--- a/solution.py
+++ b/solution.py
@@ -60,27 +60,22 @@
                 s = pad_ref[pl.ds(lead + dy * ww + dx, frame), :]
                 valid = (i + dy >= 0) & (i + dy < hh) & (j + dx >= 0) & (j + dx < ww)
                 s = jnp.where(valid, s, 0.0)
-                col_ref[f, :, pl.ds((ky * 3 + kx) * cc, cc)] = s.astype(col_ref.dtype)
-    for t in range(nout):
-        pre = jnp.zeros((frame, cc), jnp.float32)
-        for kt in range(3):
-            part = jnp.dot(col_ref[t + kt], w_ref[pl.ds(kt * taps, taps), :], preferred_element_type=jnp.float32)
-            pre = pre + mask_ref[kt, t] * part
-        sig = 1.0 / (1.0 + jnp.exp(-pre))
-        if t < nfr:
-            act_ref[pl.ds(t * frame, frame), :] = (pre * sig).astype(act_ref.dtype)
-        if t < nfr:
-            cot = cot_ref[pl.ds(t * frame, frame), :].astype(jnp.float32)
-        else:
-            cot = ahead_ref[pl.ds((t - nfr + 2) * frame, frame), :].astype(jnp.float32)
-        gp_ref[pl.ds(t * frame, frame), :] = (cot * sig * (1.0 + pre * (1.0 - sig))).astype(gp_ref.dtype)
-    acc_ref[...] = jnp.zeros_like(acc_ref)
-    for t in range(nfr):
-        g = gp_ref[pl.ds(t * frame, frame), :].astype(jnp.float32)
-        gt = jnp.transpose(g).astype(col_ref.dtype)
-        for kt in range(3):
-            part = jnp.dot(gt, col_ref[t + kt], preferred_element_type=jnp.float32)
-            acc_ref[kt] = acc_ref[kt] + mask_ref[kt, t] * part
+                col_ref[pl.ds(f * frame, frame), pl.ds((ky * 3 + kx) * cc, cc)] = s.astype(col_ref.dtype)
+    pre = None
+    for kt in range(3):
+        part = jnp.dot(col_ref[pl.ds(kt * frame, nout * frame), :], w_ref[pl.ds(kt * taps, taps), :], preferred_element_type=jnp.float32)
+        part = jnp.concatenate([mask_ref[kt, t] * part[t * frame : (t + 1) * frame] for t in range(nout)], axis=0)
+        pre = part if pre is None else pre + part
+    sig = 1.0 / (1.0 + jnp.exp(-pre))
+    act_ref[...] = (pre[: nfr * frame] * sig[: nfr * frame]).astype(act_ref.dtype)
+    cot = jnp.concatenate([cot_ref[...], ahead_ref[pl.ds(2 * frame, (nout - nfr) * frame), :]], axis=0).astype(jnp.float32)
+    grad = (cot * sig * (1.0 + pre * (1.0 - sig))).astype(gp_ref.dtype)
+    gp_ref[...] = grad
+    own_grad = grad[: nfr * frame].astype(jnp.float32)
+    for kt in range(3):
+        scaled = jnp.concatenate([mask_ref[kt, t] * own_grad[t * frame : (t + 1) * frame] for t in range(nfr)], axis=0)
+        lhs = jnp.transpose(scaled).astype(col_ref.dtype)
+        acc_ref[kt] = jnp.dot(lhs, col_ref[pl.ds(kt * frame, nfr * frame), :], preferred_element_type=jnp.float32)
     for kt in range(3):
         flat_ref[pl.ds(kt * taps, taps), :] = jnp.transpose(acc_ref[kt])
     blocks, share = gw_ref.shape[0], gw_ref.shape[1]
@@ -104,7 +99,7 @@
         in_specs=[pl.BlockSpec(memory_space=pltpu.SMEM), vmem, vmem, vmem, vmem, vmem],
         out_specs=(vmem, vmem, vmem),
         scratch_shapes=[
-            pltpu.VMEM((nout + 2, frame, 9 * cc), jnp.bfloat16),
+            pltpu.VMEM(((nout + 2) * frame, 9 * cc), jnp.bfloat16),
             pltpu.VMEM((frame + 4 * ww, cc), jnp.float32),
             pltpu.VMEM((3, cc, 9 * cc), jnp.float32),
             pltpu.VMEM((krows, cc), jnp.float32),

time: 75.7 us -> 77.1 us (1.018)
  Pallas kernels: 6.41 us -> 7.78 us
    pallas_call x1, Pallas kernels: 6.41 us -> 7.78 us  [forward_call(): pl.pallas_call(functools.partial(forward_kernel, hh, ww, nout, nfr), out_...]
  transfers between devices with their start and end apart: 6 -> 6, of which waited for: 4 -> 4; matrix products, arithmetic and copies ran while one was open for 17% -> 16% of each run, Pallas kernels for 0% -> 0%
where the time goes in v8:
time: 77.1 us; the launch traced here: 76.4 us
  starting transfers between devices  28.2 us (37%)
  waiting for transfers between devices  23.4 us (30%)
  local copies, waits for them, and re-layouts  9.71 us (13%)
  Pallas kernels  7.78 us (10%)
  other arithmetic  3.34 us (4%)
  matrix products  3.04 us (4%)
  between operations  0.97 us (1%)
    all_to_all x1, waiting for transfers between devices, reduce_weight_grad(): mine = lax.all_to_all(grad_local, TM, 0, 0, tiled=True).sum(axis=0)  18.8 us
    ppermute x3, starting transfers between devices, reduce_weight_grad(): mine = mine + lax.ppermute(mine, 'dp', [(i, i ^ step) for i in range(dp)])  12.9 us
    all_to_all x1, starting transfers between devices, reduce_weight_grad(): mine = lax.all_to_all(grad_local, TM, 0, 0, tiled=True).sum(axis=0)  9.73 us
    pallas_call x1, Pallas kernels, forward_call(): pl.pallas_call(functools.partial(forward_kernel, hh, ww, nout, nfr), out_...  7.78 us
    ppermute x2, starting transfers between devices, from_behind(): lax.ppermute(value, axis, [(source, source + steps) for source in range(l...  5.56 us
    ppermute x3, waiting for transfers between devices, reduce_weight_grad(): mine = mine + lax.ppermute(mine, 'dp', [(i, i ^ step) for i in range(dp)])  4.62 us
    unnamed x34, local copies, waits for them, and re-layouts  3.12 us
    dot_general x3, matrix products, per_device(): jnp.dot(patch, flipped, preferred_element_type=jnp.float32)  3.04 us
  transfers between devices with their start and end apart: 6, of which 4 were waited for; matrix products, arithmetic and copies ran while one was open for 16% of the time, Pallas kernels for 0%

profile of v8, /device:TPU:8, one launch (start us, length us, event | category | flops | bytes accessed | tf_op | source)
XLA Modules:
  0.0 76.4 jit_solution(7297618797505859085)
XLA Ops:
  0.7 1.1 %fusion.18 = (bf16[1,2,16,16,128]{4,3,2,1,0:T(8,128)(2,1)S(1)}, bf16[1,2,16,16,128]{4,3,2,1,0:T(8,128)(2,1)S(1)}) fusion(bf16[1,4,16,16,128]{4,3,2,1,0:T(8,128)(2,1)} %param.4), kind=kLoop, calls=%fused_computation.65 | loop fusion | bytes 524288 | tf_op jit(solution)/shard_map/slice | solution.py:123
  1.8 1.9 %collective-permute-start = (bf16[1,2,16,16,128]{4,3,2,1,0:T(8,128)(2,1)S(1)}, bf16[1,2,16,16,128]{4,3,2,1,0:T(8,128)(2,1)S(1)}, u32[]{:S(2)}, u32[]{:S(2)}) collective-permute-start(bf16[1,2,16,16,128]{4,3,2,1,0:T(8,128)(2,1)S(1)} %get-tuple-element.24), channel_id=1, source_target_pairs={{0,1},{1,2},{2,3},{3,4},{4,5},{5,6},{6,7},{7,8},{8,9},{9,10},{10,1... | collective-permute-start | bytes 393224 | tf_op jit(solution)/shard_map/ppermute | solution.py:16
  3.7 0.9 %slice.136 = bf16[1,2,16,16,128]{4,3,2,1,0:T(8,128)(2,1)S(1)} slice(bf16[1,4,16,16,128]{4,3,2,1,0:T(8,128)(2,1)} %param.7), slice={[0:1], [0:2], [0:16], [0:16], [0:128]} | slice | bytes 262144 | tf_op jit(solution)/shard_map/slice | solution.py:123
  4.6 3.6 %collective-permute-start.1 = (bf16[1,4,16,16,128]{4,3,2,1,0:T(8,128)(2,1)S(1)}, bf16[1,4,16,16,128]{4,3,2,1,0:T(8,128)(2,1)S(1)}, u32[]{:S(2)}, u32[]{:S(2)}) collective-permute-start(bf16[1,4,16,16,128]{4,3,2,1,0:T(8,128)(2,1)S(1)} %pad_maximum_fusion), channel_id=1, source_target_pairs={{1,0},{2,1},{3,2},{4,3},{5,4},{6,5},{7,6},{8,7},{9,8},{10,9},{11,1... | collective-permute-start | bytes 786440 | tf_op jit(solution)/shard_map/ppermute | solution.py:16
  8.3 0.7 pad_add_fusion
  9.1 0.1 dynamic_slice.3
  9.1 0.1 compare_bitcast_fusion.1
  9.2 1.2 %fusion.17 = (bf16[1152,128]{1,0:T(8,128)(2,1)S(1)}, bf16[1152,128]{1,0:T(8,128)(2,1)S(1)}, bf16[1152,128]{1,0:T(8,128)(2,1)S(1)}) fusion(bf16[3456,128]{1,0:T(8,128)(2,1)} %w_ref.1), kind=kLoop, calls=%fused_computation.64 | loop fusion | bytes 1769472 | tf_op jit(solution)/shard_map/slice | solution.py:156
  10.4 0.1 pad.17.clone
  10.5 0.1 add_convert_fusion.mask_ref
  10.6 0.9 %copy.9 = bf16[9,128,128]{2,1,0:T(8,128)(2,1)} copy(bf16[9,128,128]{1,2,0:T(8,128)(2,1)S(1)} %bitcast.53) | data formatting | bytes 589824 | tf_op jit(solution)/shard_map/transpose | solution.py:157
  11.5 0.2 copy.7
  11.7 0.9 %copy.8 = bf16[9,128,128]{2,1,0:T(8,128)(2,1)} copy(bf16[9,128,128]{1,2,0:T(8,128)(2,1)S(1)} %bitcast.51) | data formatting | bytes 589824 | tf_op jit(solution)/shard_map/transpose | solution.py:157
  12.6 0.1 slice_compare_fusion
  12.7 7.8 %shard_map.67 = (bf16[1024,128]{1,0:T(8,128)(2,1)}, bf16[1536,128]{1,0:T(8,128)(2,1)S(1)}, f32[32,108,128]{2,1,0:T(8,128)}) custom-call(f32[3,6]{1,0:T(4,128)S(1)} %add_convert_fusion.mask_ref, bf16[512,128]{1,0:T(8,128)(2,1)S(1)} %bitcast.46, bf16[1024,128]{1,0:T(8,128)(2,1)S(1)} %bitcast.43, bf16[1024,128]{1,0:T(8,128)(2,1)S(1)} %bitcast.45, ...), custom_call_target="tpu_custom_call" | custom-call | flops 2264924160 | bytes 3571712 | tf_op jit(solution)/shard_map/pallas_call | solution.py:92
  20.5 9.7 %all-to-all-start = ((f32[32,108,128]{2,1,0:T(8,128)}), f32[32,108,128]{2,1,0:T(8,128)}, u32[]{:S(2)}, u32[]{:S(2)}) async-start(f32[32,108,128]{2,1,0:T(8,128)} %get-tuple-element.8), calls=%async_computation | async-start | bytes 3670016 | tf_op jit(solution)/shard_map/all_to_all | solution.py:22
  30.2 0.9 %pad_slice_fusion = (bf16[4,16,16,128]{3,2,1,0:T(8,128)(2,1)S(1)}, bf16[4,16,16,128]{3,2,1,0:T(8,128)(2,1)S(1)}, bf16[4,16,16,128]{3,2,1,0:T(8,128)(2,1)S(1)}, b...) fusion(bf16[4,16,16,128]{3,2,1,0:T(8,128)(2,1)S(1)} %bitcast.63), kind=kLoop, calls=%fused_computation.3 | loop fusion | bytes 2359296 | tf_op jit(solution)/shard_map/slice | solution.py:33
  31.4 0.1 constant_dynamic-update-slice_fusion.6
  31.6 0.1 broadcast_select_fusion
  31.7 0.1 fusion.9
  31.8 0.1 fusion.10
  31.8 0.1 fusion.11
  31.9 0.1 fusion.12
  32.1 0.1 constant_dynamic-update-slice_fusion.1
  32.1 0.1 fusion.13
  32.2 0.1 fusion.14
  32.4 0.1 fusion.16
  32.5 0.1 fusion.1
  32.6 0.1 fusion.2
  32.7 0.1 fusion.3
  32.8 0.1 fusion.4
  33.0 0.1 fusion.5
  33.1 0.1 fusion.6
  33.3 0.1 fusion.8
  33.6 0.8 %fusion.19 = f32[1024,128]{1,0:T(8,128)S(1)} fusion(bf16[1024,1152]{1,0:T(8,128)(2,1)S(1)} %bitcast.48, bf16[1152,128]{1,0:T(8,128)(2,1)S(1)} %bitcast.54), kind=kOutput, calls=%fused_computation.66 | convolution fusion | flops 301989888 | bytes 3178496 | tf_op jit(solution)/shard_map/dot_general | solution.py:158
  34.4 0.2 copy-done.4
  34.5 0.8 %convolution_add_fusion.1 = f32[1024,128]{1,0:T(8,128)S(1)} fusion(f32[1024,128]{1,0:T(8,128)S(1)} %fusion.19, bf16[1024,1152]{1,0:T(8,128)(2,1)S(1)} %bitcast.47, bf16[1152,128]{1,0:T(8,128)(2,1)S(1)} %bitcast.50), kind=kOutput, calls=%fused_computation.1 | convolution fusion | flops 302120960 | bytes 3702784 | tf_op jit(solution)/shard_map/dot_general | solution.py:158
  35.3 18.8 %all-to-all-done = f32[32,108,128]{2,1,0:T(8,128)} async-done(((f32[32,108,128]{2,1,0:T(8,128)}), f32[32,108,128]{2,1,0:T(8,128)}, u32[]{:S(2)}, u32[]{:S(2)}) %all-to-all-start) | async-done | bytes 1769504 | tf_op jit(solution)/shard_map/all_to_all | solution.py:22
  54.1 1.6 %reduce_sum.9 = f32[108,128]{1,0:T(8,128)S(1)} reduce(f32[32,108,128]{2,1,0:T(8,128)} %all-to-all-done, f32[]{:T(128)} %constant.29.clone.1), dimensions={0}, to_apply=%region_0.1 | reduce | flops 428544 | bytes 1824772 | tf_op jit(solution)/shard_map/reduce_sum | solution.py:22
  55.7 2.0 %collective-permute-start.2 = (f32[108,128]{1,0:T(8,128)S(1)}, f32[108,128]{1,0:T(8,128)S(1)}, u32[]{:S(2)}, u32[]{:S(2)}) collective-permute-start(f32[108,128]{1,0:T(8,128)S(1)} %reduce_sum.9), channel_id=1, source_target_pairs={{0,32},{32,0},{64,96},{96,64},{128,160},{160,128},{192,224},{224,1... | collective-permute-start | bytes 165896 | tf_op jit(solution)/shard_map/ppermute | solution.py:25
  57.7 1.0 %constant_dynamic-update-slice_fusion.3 = bf16[1024,1152]{1,0:T(8,128)(2,1)S(1)} fusion(bf16[1024,1152]{1,0:T(8,128)(2,1)S(1)} %constant_dynamic-update-slice_fusion.4, bf16[1024,128]{1,0:T(8,128)(2,1)} %bitcast.56), kind=kLoop, calls=%fused_computation.49 | loop fusion | bytes 524288
  58.7 1.2 %collective-permute-done.2 = f32[108,128]{1,0:T(8,128)S(1)} collective-permute-done((f32[108,128]{1,0:T(8,128)S(1)}, f32[108,128]{1,0:T(8,128)S(1)}, u32[]{:S(2)}, u32[]{:S(2)}) %collective-permute-start.2) | collective-permute-done | bytes 55328 | tf_op jit(solution)/shard_map/ppermute | solution.py:25
  60.0 3.4 %collective-permute-start.3 = (f32[108,128]{1,0:T(8,128)S(1)}, f32[108,128]{1,0:T(8,128)S(1)}, u32[]{:S(2)}, u32[]{:S(2)}) collective-permute-start(f32[108,128]{1,0:T(8,128)S(1)} %add.31), channel_id=1, source_target_pairs={{0,64},{32,96},{64,0},{96,32},{128,192},{160,224},{192,128},{224,1... | collective-permute-start | bytes 165896 | tf_op jit(solution)/shard_map/ppermute | solution.py:25
  63.4 2.1 %collective-permute-done.3 = f32[108,128]{1,0:T(8,128)S(1)} collective-permute-done((f32[108,128]{1,0:T(8,128)S(1)}, f32[108,128]{1,0:T(8,128)S(1)}, u32[]{:S(2)}, u32[]{:S(2)}) %collective-permute-start.3) | collective-permute-done | bytes 55328 | tf_op jit(solution)/shard_map/ppermute | solution.py:25
  65.5 7.5 %collective-permute-start.4 = (f32[108,128]{1,0:T(8,128)S(1)}, f32[108,128]{1,0:T(8,128)S(1)}, u32[]{:S(2)}, u32[]{:S(2)}) collective-permute-start(f32[108,128]{1,0:T(8,128)S(1)} %add.32), channel_id=1, source_target_pairs={{0,128},{32,160},{64,192},{96,224},{128,0},{160,32},{192,64},{224,... | collective-permute-start | bytes 165896 | tf_op jit(solution)/shard_map/ppermute | solution.py:25
  73.0 1.5 %fusion = bf16[1024,128]{1,0:T(8,128)(2,1)} fusion(f32[1024,128]{1,0:T(8,128)S(1)} %convolution_add_fusion.1, bf16[1024,1152]{1,0:T(8,128)(2,1)S(1)} %constant_dynamic-update-slice_fusion.2, bf16[1152,128]{1,0:T(8,128)(2,1)S(1)} %bitcast.49), kind=kOutput, calls=%fused_computation.2 | convolution fusion | flops 302252032 | bytes 3440640 | tf_op jit(solution)/shard_map/dot_general | solution.py:158
  74.5 1.3 %collective-permute-done.4 = f32[108,128]{1,0:T(8,128)S(1)} collective-permute-done((f32[108,128]{1,0:T(8,128)S(1)}, f32[108,128]{1,0:T(8,128)S(1)}, u32[]{:S(2)}, u32[]{:S(2)}) %collective-permute-start.4) | collective-permute-done | bytes 55328 | tf_op jit(solution)/shard_map/ppermute | solution.py:25
  75.8 0.6 add_multiply_fusion
  (27 shorter events, 0.7 us)
Async XLA Ops:
  0.6 12.0 %copy-start.1 = (bf16[1,4,16,16,128]{4,3,2,1,0:T(8,128)(2,1)S(1)}, bf16[1,4,16,16,128]{4,3,2,1,0:T(8,128)(2,1)}, u32[]{:S(2)}) copy-start(bf16[1,4,16,16,128]{4,3,2,1,0:T(8,128)(2,1)} %param.4) | copy-start | bytes 786436
  0.6 12.0 %copy-start.2 = (bf16[1,4,16,16,128]{4,3,2,1,0:T(8,128)(2,1)S(1)}, bf16[1,4,16,16,128]{4,3,2,1,0:T(8,128)(2,1)}, u32[]{:S(2)}) copy-start(bf16[1,4,16,16,128]{4,3,2,1,0:T(8,128)(2,1)} %param.7) | copy-start | bytes 786436
  0.7 12.0 %copy-start = (bf16[3456,128]{1,0:T(8,128)(2,1)S(1)}, bf16[3456,128]{1,0:T(8,128)(2,1)}, u32[]{:S(2)}) copy-start(bf16[3456,128]{1,0:T(8,128)(2,1)} %w_ref.1) | copy-start | bytes 2654212
  1.8 10.9 %collective-permute-start = (bf16[1,2,16,16,128]{4,3,2,1,0:T(8,128)(2,1)S(1)}, bf16[1,2,16,16,128]{4,3,2,1,0:T(8,128)(2,1)S(1)}, u32[]{:S(2)}, u32[]{:S(2)}) collective-permute-start(bf16[1,2,16,16,128]{4,3,2,1,0:T(8,128)(2,1)S(1)} %get-tuple-element.24), channel_id=1, source_target_pairs={{0,1},{1,2},{2,3},{3,4},{4,5},{5,6},{6,7},{7,8},{8,9},{9,10},{10,1... | collective-permute-start | bytes 393224 | tf_op jit(solution)/shard_map/ppermute | solution.py:16
  4.6 8.0 %collective-permute-start.1 = (bf16[1,4,16,16,128]{4,3,2,1,0:T(8,128)(2,1)S(1)}, bf16[1,4,16,16,128]{4,3,2,1,0:T(8,128)(2,1)S(1)}, u32[]{:S(2)}, u32[]{:S(2)}) collective-permute-start(bf16[1,4,16,16,128]{4,3,2,1,0:T(8,128)(2,1)S(1)} %pad_maximum_fusion), channel_id=1, source_target_pairs={{1,0},{2,1},{3,2},{4,3},{5,4},{6,5},{7,6},{8,7},{9,8},{10,9},{11,1... | collective-permute-start | bytes 786440 | tf_op jit(solution)/shard_map/ppermute | solution.py:16
  20.5 33.6 %all-to-all-start = ((f32[32,108,128]{2,1,0:T(8,128)}), f32[32,108,128]{2,1,0:T(8,128)}, u32[]{:S(2)}, u32[]{:S(2)}) async-start(f32[32,108,128]{2,1,0:T(8,128)} %get-tuple-element.8), calls=%async_computation | async-start | bytes 3670016 | tf_op jit(solution)/shard_map/all_to_all | solution.py:22
  33.6 1.0 %copy-start.4 = (bf16[9,128,128]{2,1,0:T(8,128)(2,1)S(1)}, bf16[9,128,128]{2,1,0:T(8,128)(2,1)}, u32[]{:S(2)}) copy-start(bf16[9,128,128]{2,1,0:T(8,128)(2,1)} %copy.8) | copy-start | bytes 884740
  35.3 37.7 %copy-start.3 = (bf16[9,128,128]{2,1,0:T(8,128)(2,1)S(1)}, bf16[9,128,128]{2,1,0:T(8,128)(2,1)}, u32[]{:S(2)}) copy-start(bf16[9,128,128]{2,1,0:T(8,128)(2,1)} %copy.9) | copy-start | bytes 884740
  55.7 4.3 %collective-permute-start.2 = (f32[108,128]{1,0:T(8,128)S(1)}, f32[108,128]{1,0:T(8,128)S(1)}, u32[]{:S(2)}, u32[]{:S(2)}) collective-permute-start(f32[108,128]{1,0:T(8,128)S(1)} %reduce_sum.9), channel_id=1, source_target_pairs={{0,32},{32,0},{64,96},{96,64},{128,160},{160,128},{192,224},{224,1... | collective-permute-start | bytes 165896 | tf_op jit(solution)/shard_map/ppermute | solution.py:25
  60.0 5.5 %collective-permute-start.3 = (f32[108,128]{1,0:T(8,128)S(1)}, f32[108,128]{1,0:T(8,128)S(1)}, u32[]{:S(2)}, u32[]{:S(2)}) collective-permute-start(f32[108,128]{1,0:T(8,128)S(1)} %add.31), channel_id=1, source_target_pairs={{0,64},{32,96},{64,0},{96,32},{128,192},{160,224},{192,128},{224,1... | collective-permute-start | bytes 165896 | tf_op jit(solution)/shard_map/ppermute | solution.py:25
  65.5 10.3 %collective-permute-start.4 = (f32[108,128]{1,0:T(8,128)S(1)}, f32[108,128]{1,0:T(8,128)S(1)}, u32[]{:S(2)}, u32[]{:S(2)}) collective-permute-start(f32[108,128]{1,0:T(8,128)S(1)} %add.32), channel_id=1, source_target_pairs={{0,128},{32,160},{64,192},{96,224},{128,0},{160,32},{192,64},{224,... | collective-permute-start | bytes 165896 | tf_op jit(solution)/shard_map/ppermute | solution.py:25

commit v9 on v7

--- a/solution.py
+++ b/solution.py
@@ -16,10 +16,11 @@
     return lax.ppermute(value, axis, [(source, source + steps) for source in range(leading, last)])
 
 
-def reduce_weight_grad(grad_local):
-    tm = lax.axis_size("chip") * lax.axis_size("core")
+def reduce_weight_grad(mine, other):
     dp = lax.axis_size("dp")
-    mine = lax.all_to_all(grad_local, TM, 0, 0, tiled=True).sum(axis=0)
+    cores = lax.axis_size("core")
+    mine = mine + lax.ppermute(other, "core", [(i, (i + 1) % cores) for i in range(cores)])
+    mine = lax.all_to_all(mine, "chip", 0, 0, tiled=True).sum(axis=0)
     step = 1
     while step < dp:
         mine = mine + lax.ppermute(mine, "dp", [(i, i ^ step) for i in range(dp)])
@@ -37,7 +38,7 @@
     return jnp.concatenate(pieces, axis=3).reshape(-1, 9 * frames.shape[-1])
 
 
-def forward_kernel(hh, ww, nout, nfr, mask_ref, early_ref, own_ref, ahead_ref, cot_ref, w_ref, act_ref, gp_ref, gw_ref, col_ref, pad_ref, acc_ref, flat_ref):
+def forward_kernel(hh, ww, nout, nfr, core_ref, mask_ref, early_ref, own_ref, ahead_ref, cot_ref, w_ref, act_ref, gp_ref, mine_ref, other_ref, col_ref, pad_ref, acc_ref, flat_ref):
     frame = hh * ww
     cc = own_ref.shape[1]
     taps = 9 * cc
@@ -83,12 +84,16 @@
             acc_ref[kt] = acc_ref[kt] + mask_ref[kt, t] * part
     for kt in range(3):
         flat_ref[pl.ds(kt * taps, taps), :] = jnp.transpose(acc_ref[kt])
-    blocks, share = gw_ref.shape[0], gw_ref.shape[1]
-    for b in range(blocks):
-        gw_ref[b] = flat_ref[pl.ds(b * share, share), :]
+    chips, share = mine_ref.shape[0], mine_ref.shape[1]
+    first = core_ref[0] == 0
+    for c in range(chips):
+        even = flat_ref[pl.ds(2 * c * share, share), :]
+        odd = flat_ref[pl.ds((2 * c + 1) * share, share), :]
+        mine_ref[c] = jnp.where(first, even, odd)
+        other_ref[c] = jnp.where(first, odd, even)
 
 
-def forward_call(mask, early, own, ahead, cot, w, hh, ww, nout, nfr, blocks):
+def forward_call(core, mask, early, own, ahead, cot, w, hh, ww, nout, nfr, blocks):
     frame = hh * ww
     cc = own.shape[1]
     krows = w.shape[0]
@@ -99,10 +104,11 @@
         out_shape=(
             jax.ShapeDtypeStruct((nfr * frame, cc), jnp.bfloat16),
             jax.ShapeDtypeStruct((nout * frame, cc), jnp.bfloat16),
-            jax.ShapeDtypeStruct((blocks, krows // blocks, cc), jnp.float32),
+            jax.ShapeDtypeStruct((blocks // 2, krows // blocks, cc), jnp.float32),
+            jax.ShapeDtypeStruct((blocks // 2, krows // blocks, cc), jnp.float32),
         ),
-        in_specs=[pl.BlockSpec(memory_space=pltpu.SMEM), vmem, vmem, vmem, vmem, vmem],
-        out_specs=(vmem, vmem, vmem),
+        in_specs=[pl.BlockSpec(memory_space=pltpu.SMEM), pl.BlockSpec(memory_space=pltpu.SMEM), vmem, vmem, vmem, vmem, vmem],
+        out_specs=(vmem, vmem, vmem, vmem),
         scratch_shapes=[
             pltpu.VMEM((nout + 2, frame, 9 * cc), jnp.bfloat16),
             pltpu.VMEM((frame + 4 * ww, cc), jnp.float32),
@@ -115,7 +121,7 @@
             transcendentals=nout * frame * cc,
             bytes_accessed=2 * (early.size + own.size + ahead.size + cot.size + w.size) + 4 * krows * cc,
         ),
-    )(mask, early, own, ahead, cot, w)
+    )(core, mask, early, own, ahead, cot, w)
 
 
 def per_device(clips, segment_ids, conv_weight, cotangent):
@@ -134,7 +140,9 @@
     centre = seglocal[2 : 2 + nout]
     mask = jnp.stack([(seglocal[kt : kt + nout] == centre) for kt in range(3)]).astype(jnp.float32)
     tm = lax.axis_size("chip") * lax.axis_size("core")
-    act, grad_pre, grad_local = forward_call(
+    core = lax.axis_index("core").astype(jnp.int32).reshape(1)
+    act, grad_pre, mine, other = forward_call(
+        core,
         mask,
         earlier.reshape(-1, cc),
         clips.reshape(-1, cc),
@@ -162,7 +170,7 @@
         flipped = jnp.swapaxes(block, 1, 2).reshape(9 * cc, cc)
         summed = summed + jnp.dot(patch, flipped, preferred_element_type=jnp.float32)
     grad_clips = summed.astype(jnp.bfloat16).reshape(clips.shape)
-    grad_weight = reduce_weight_grad(grad_local) / jnp.sqrt(jnp.float32(count))
+    grad_weight = reduce_weight_grad(mine, other) / jnp.sqrt(jnp.float32(count))
     return (activated, grad_clips, grad_weight)
 
 

time: 75.7 us -> 72.2 us (0.954)
  waiting for transfers between devices: 23.4 us -> 13.8 us
  local copies, waits for them, and re-layouts: 9.71 us -> 13.1 us
  matrix products: 3.04 us -> 4.86 us
  starting transfers between devices: 28.2 us -> 29.6 us
  Pallas kernels: 6.41 us -> 5.17 us
  other arithmetic: 3.34 us -> 4.23 us
    all_to_all x1, waiting for transfers between devices: 18.8 us -> 10.6 us  [reduce_weight_grad(): mine = lax.all_to_all(mine, 'chip', 0, 0, tiled=True).sum(axis=0)]
    unnamed x34 -> x38, local copies, waits for them, and re-layouts: 3.12 us -> 5.85 us
    ppermute x0 -> x1, starting transfers between devices: none -> 1.94 us  [reduce_weight_grad(): lax.ppermute(other, 'core', [(i, (i + 1) % cores) for i in range(cores)])]
    dot_general x3, matrix products: 3.04 us -> 4.86 us  [per_device(): jnp.dot(patch, flipped, preferred_element_type=jnp.float32)]
    ppermute x3, waiting for transfers between devices: 4.62 us -> 3.06 us  [reduce_weight_grad(): mine = mine + lax.ppermute(mine, 'dp', [(i, i ^ step) for i in range(dp)])]
    add x0 -> x1, other arithmetic: none -> 1.25 us  [reduce_weight_grad(): mine + lax.ppermute(other, 'core', [(i, (i + 1) % cores) for i in range(c...]
    pallas_call x1, Pallas kernels: 6.41 us -> 5.17 us  [forward_call(): pl.pallas_call(functools.partial(forward_kernel, hh, ww, nout, nfr), out_...]
    all_to_all x1, starting transfers between devices: 9.73 us -> 8.6 us  [reduce_weight_grad(): mine = lax.all_to_all(mine, 'chip', 0, 0, tiled=True).sum(axis=0)]
  transfers between devices with their start and end apart: 6 -> 7, of which waited for: 4 -> 5; matrix products, arithmetic and copies ran while one was open for 17% -> 22% of each run, Pallas kernels for 0% -> 0%
where the time goes in v9:
time: 72.2 us; the launch traced here: 71.8 us
  starting transfers between devices  29.6 us (41%)
  waiting for transfers between devices  13.8 us (19%)
  local copies, waits for them, and re-layouts  13.1 us (18%)
  Pallas kernels  5.17 us (7%)
  matrix products  4.86 us (7%)
  other arithmetic  4.23 us (6%)
  between operations  0.96 us (1%)
    ppermute x3, starting transfers between devices, reduce_weight_grad(): mine = mine + lax.ppermute(mine, 'dp', [(i, i ^ step) for i in range(dp)])  13.5 us
    all_to_all x1, waiting for transfers between devices, reduce_weight_grad(): mine = lax.all_to_all(mine, 'chip', 0, 0, tiled=True).sum(axis=0)  10.6 us
    all_to_all x1, starting transfers between devices, reduce_weight_grad(): mine = lax.all_to_all(mine, 'chip', 0, 0, tiled=True).sum(axis=0)  8.6 us
    unnamed x38, local copies, waits for them, and re-layouts  5.85 us
    ppermute x2, starting transfers between devices, from_behind(): lax.ppermute(value, axis, [(source, source + steps) for source in range(l...  5.56 us
    pallas_call x1, Pallas kernels, forward_call(): pl.pallas_call(functools.partial(forward_kernel, hh, ww, nout, nfr), out_...  5.17 us
    dot_general x3, matrix products, per_device(): jnp.dot(patch, flipped, preferred_element_type=jnp.float32)  4.86 us
    ppermute x3, waiting for transfers between devices, reduce_weight_grad(): mine = mine + lax.ppermute(mine, 'dp', [(i, i ^ step) for i in range(dp)])  3.06 us
  transfers between devices with their start and end apart: 7, of which 5 were waited for; matrix products, arithmetic and copies ran while one was open for 22% of the time, Pallas kernels for 0%

profile of v9, /device:TPU:8, one launch (start us, length us, event | category | flops | bytes accessed | tf_op | source)
XLA Modules:
  0.0 71.8 jit_solution(12853368939194113228)
XLA Ops:
  0.7 1.1 %fusion.18 = (bf16[1,2,16,16,128]{4,3,2,1,0:T(8,128)(2,1)S(1)}, bf16[1,2,16,16,128]{4,3,2,1,0:T(8,128)(2,1)S(1)}) fusion(bf16[1,4,16,16,128]{4,3,2,1,0:T(8,128)(2,1)} %param.4), kind=kLoop, calls=%fused_computation.66 | loop fusion | bytes 524288 | tf_op jit(solution)/shard_map/slice | solution.py:134
  1.8 1.9 %collective-permute-start = (bf16[1,2,16,16,128]{4,3,2,1,0:T(8,128)(2,1)S(1)}, bf16[1,2,16,16,128]{4,3,2,1,0:T(8,128)(2,1)S(1)}, u32[]{:S(2)}, u32[]{:S(2)}) collective-permute-start(bf16[1,2,16,16,128]{4,3,2,1,0:T(8,128)(2,1)S(1)} %get-tuple-element.26), channel_id=1, source_target_pairs={{0,1},{1,2},{2,3},{3,4},{4,5},{5,6},{6,7},{7,8},{8,9},{9,10},{10,1... | collective-permute-start | bytes 393224 | tf_op jit(solution)/shard_map/ppermute | solution.py:16
  3.7 0.9 %slice.136 = bf16[1,2,16,16,128]{4,3,2,1,0:T(8,128)(2,1)S(1)} slice(bf16[1,4,16,16,128]{4,3,2,1,0:T(8,128)(2,1)} %param.7), slice={[0:1], [0:2], [0:16], [0:16], [0:128]} | slice | bytes 262144 | tf_op jit(solution)/shard_map/slice | solution.py:134
  4.6 3.6 %collective-permute-start.1 = (bf16[1,4,16,16,128]{4,3,2,1,0:T(8,128)(2,1)S(1)}, bf16[1,4,16,16,128]{4,3,2,1,0:T(8,128)(2,1)S(1)}, u32[]{:S(2)}, u32[]{:S(2)}) collective-permute-start(bf16[1,4,16,16,128]{4,3,2,1,0:T(8,128)(2,1)S(1)} %pad_maximum_fusion), channel_id=1, source_target_pairs={{1,0},{2,1},{3,2},{4,3},{5,4},{6,5},{7,6},{8,7},{9,8},{10,9},{11,1... | collective-permute-start | bytes 786440 | tf_op jit(solution)/shard_map/ppermute | solution.py:16
  8.3 0.7 %pad_add_fusion = s32[132]{0:T(256)S(1)} fusion(s32[2]{0:T(128)S(1)} %broadcast.26, s32[128]{0:T(128)} %bitcast.68, s32[2]{0:T(128)S(1)} %broadcast.25), kind=kLoop, calls=%fused_computation.62 | loop fusion | flops 264 | bytes 1056 | tf_op jit(solution)/shard_map/concatenate | solution.py:136
  9.1 0.1 dynamic_slice.3
  9.1 0.1 compare_bitcast_fusion.1
  9.2 1.2 %fusion.17 = (bf16[1152,128]{1,0:T(8,128)(2,1)S(1)}, bf16[1152,128]{1,0:T(8,128)(2,1)S(1)}, bf16[1152,128]{1,0:T(8,128)(2,1)S(1)}) fusion(bf16[3456,128]{1,0:T(8,128)(2,1)} %w_ref.1), kind=kLoop, calls=%fused_computation.65 | loop fusion | bytes 1769472 | tf_op jit(solution)/shard_map/slice | solution.py:169
  10.4 0.1 pad.17.clone
  10.6 0.2 copy.12
  10.8 0.9 %copy.10 = bf16[9,128,128]{2,1,0:T(8,128)(2,1)} copy(bf16[9,128,128]{1,2,0:T(8,128)(2,1)S(1)} %bitcast.53) | data formatting | bytes 589824 | tf_op jit(solution)/shard_map/transpose | solution.py:170
  11.7 0.2 copy.11
  12.0 0.2 collective-permute-done.1
  12.2 5.2 %shard_map.67 = (bf16[1024,128]{1,0:T(8,128)(2,1)}, bf16[1536,128]{1,0:T(8,128)(2,1)S(1)}, f32[16,108,128]{2,1,0:T(8,128)S(1)}, f32[16,108,128]{2,1,0:T(8,128)S(1)}) custom-call(s32[1]{0:T(128)} %bitcast.core_ref, f32[3,6]{1,0:T(4,128)S(1)} %add_convert_fusion.mask_ref, bf16[512,128]{1,0:T(8,128)(2,1)S(1)} %bitcast.47, bf16[1024,128]{1,0:T(8,128)(2,1)S(1)} %bitcast.44, ...), custom_call_target="tpu_custom_call" | custom-call | flops 2264924160 | bytes 3571712 | tf_op jit(solution)/shard_map/pallas_call | solution.py:102
  17.4 0.3 copy.13
  17.7 1.9 %collective-permute-start.2 = (f32[16,108,128]{2,0,1:T(8,128)S(1)}, f32[16,108,128]{2,0,1:T(8,128)S(1)}, u32[]{:S(2)}, u32[]{:S(2)}) collective-permute-start(f32[16,108,128]{2,0,1:T(8,128)S(1)} %copy.13), channel_id=1, source_target_pairs={{0,1},{1,0},{2,3},{3,2},{4,5},{5,4},{6,7},{7,6},{8,9},{9,8},{10,11... | collective-permute-start | bytes 2654216 | tf_op jit(solution)/shard_map/ppermute | solution.py:22
  19.6 1.1 %pad_slice_fusion = (bf16[4,16,16,128]{3,2,1,0:T(8,128)(2,1)}, bf16[4,16,16,128]{3,2,1,0:T(8,128)(2,1)S(1)}, bf16[4,16,16,128]{3,2,1,0:T(8,128)(2,1)S(1)}, bf16[...) fusion(bf16[4,16,16,128]{3,2,1,0:T(8,128)(2,1)S(1)} %bitcast.60), kind=kLoop, calls=%fused_computation.4 | loop fusion | bytes 2359296 | tf_op jit(solution)/shard_map/slice | solution.py:34
  20.9 0.1 constant_dynamic-update-slice_fusion.6
  21.1 0.1 broadcast_select_fusion
  21.3 0.1 fusion.11
  21.4 0.1 fusion.12
  21.6 0.1 fusion.13
  21.8 0.1 fusion.14
  21.9 0.1 fusion.16
  22.2 0.1 fusion.3
  22.3 0.1 fusion.4
  22.5 0.1 fusion.5
  22.6 0.1 fusion.6
  22.8 0.1 fusion.8
  22.9 0.6 copy-done.3
  23.5 1.4 %copy-done.5 = bf16[4,16,16,1152]{3,2,1,0:T(8,128)(2,1)} copy-done((bf16[4,16,16,1152]{3,2,1,0:T(8,128)(2,1)}, bf16[4,16,16,1152]{3,2,1,0:T(8,128)(2,1)S(1)}, u32[]{:S(2)}) %copy-start.5) | copy-done | bytes 2359320
  24.9 1.3 %copy_add_fusion = f32[16,108,128]{2,1,0:T(8,128)} fusion(f32[16,108,128]{2,1,0:T(8,128)S(1)} %get-tuple-element.9, f32[16,108,128]{2,0,1:T(8,128)S(1)} %collective-permute-done.2), kind=kLoop, calls=%fused_computation.3 | loop fusion | flops 221184 | bytes 2654208 | tf_op jit(solution)/shard_map/add | solution.py:22
  26.1 8.6 %all-to-all-start = ((f32[16,108,128]{2,1,0:T(8,128)}), f32[16,108,128]{2,1,0:T(8,128)}, u32[]{:S(2)}, u32[]{:S(2)}) async-start(f32[16,108,128]{2,1,0:T(8,128)} %copy_add_fusion), calls=%async_computation | async-start | bytes 1835008 | tf_op jit(solution)/shard_map/all_to_all | solution.py:23
  34.7 1.0 %constant_dynamic-update-slice_fusion.5 = bf16[1024,1152]{1,0:T(8,128)(2,1)S(1)} fusion(bf16[1024,1152]{1,0:T(8,128)(2,1)S(1)} %get-tuple-element.14, bf16[1024,128]{1,0:T(8,128)(2,1)} %bitcast.59), kind=kLoop, calls=%fused_computation.52 | loop fusion | bytes 524288
  35.8 2.6 %fusion.19 = f32[1024,128]{1,0:T(8,128)S(1)} fusion(bf16[1024,1152]{1,0:T(8,128)(2,1)} %bitcast.49, bf16[1152,128]{1,0:T(8,128)(2,1)S(1)} %bitcast.55), kind=kOutput, calls=%fused_computation.67 | convolution fusion | flops 301989888 | bytes 3178496 | tf_op jit(solution)/shard_map/dot_general | solution.py:171
  38.5 0.8 %convolution_add_fusion.1 = f32[1024,128]{1,0:T(8,128)S(1)} fusion(f32[1024,128]{1,0:T(8,128)S(1)} %fusion.19, bf16[1024,1152]{1,0:T(8,128)(2,1)S(1)} %bitcast.48, bf16[1152,128]{1,0:T(8,128)(2,1)S(1)} %bitcast.51), kind=kOutput, calls=%fused_computation.1 | convolution fusion | flops 302120960 | bytes 3702784 | tf_op jit(solution)/shard_map/dot_general | solution.py:171
  39.2 10.6 %all-to-all-done = f32[16,108,128]{2,1,0:T(8,128)} async-done(((f32[16,108,128]{2,1,0:T(8,128)}), f32[16,108,128]{2,1,0:T(8,128)}, u32[]{:S(2)}, u32[]{:S(2)}) %all-to-all-start) | async-done | bytes 884768 | tf_op jit(solution)/shard_map/all_to_all | solution.py:23
  49.8 1.2 %reduce_sum.9 = f32[108,128]{1,0:T(8,128)S(1)} reduce(f32[16,108,128]{2,1,0:T(8,128)} %all-to-all-done, f32[]{:T(128)} %constant.29.clone.1), dimensions={0}, to_apply=%region_0.1 | reduce | flops 207360 | bytes 940036 | tf_op jit(solution)/shard_map/reduce_sum | solution.py:23
  51.0 2.0 %collective-permute-start.3 = (f32[108,128]{1,0:T(8,128)S(1)}, f32[108,128]{1,0:T(8,128)S(1)}, u32[]{:S(2)}, u32[]{:S(2)}) collective-permute-start(f32[108,128]{1,0:T(8,128)S(1)} %reduce_sum.9), channel_id=1, source_target_pairs={{0,32},{32,0},{64,96},{96,64},{128,160},{160,128},{192,224},{224,1... | collective-permute-start | bytes 165896 | tf_op jit(solution)/shard_map/ppermute | solution.py:26
  53.0 1.0 %constant_dynamic-update-slice_fusion.3 = bf16[1024,1152]{1,0:T(8,128)(2,1)S(1)} fusion(bf16[1024,1152]{1,0:T(8,128)(2,1)S(1)} %constant_dynamic-update-slice_fusion.4, bf16[1024,128]{1,0:T(8,128)(2,1)} %bitcast.57), kind=kLoop, calls=%fused_computation.50 | loop fusion | bytes 524288
  54.1 1.2 %collective-permute-done.3 = f32[108,128]{1,0:T(8,128)S(1)} collective-permute-done((f32[108,128]{1,0:T(8,128)S(1)}, f32[108,128]{1,0:T(8,128)S(1)}, u32[]{:S(2)}, u32[]{:S(2)}) %collective-permute-start.3) | collective-permute-done | bytes 55328 | tf_op jit(solution)/shard_map/ppermute | solution.py:26
  55.3 3.8 %collective-permute-start.4 = (f32[108,128]{1,0:T(8,128)S(1)}, f32[108,128]{1,0:T(8,128)S(1)}, u32[]{:S(2)}, u32[]{:S(2)}) collective-permute-start(f32[108,128]{1,0:T(8,128)S(1)} %add.35), channel_id=1, source_target_pairs={{0,64},{32,96},{64,0},{96,32},{128,192},{160,224},{192,128},{224,1... | collective-permute-start | bytes 165896 | tf_op jit(solution)/shard_map/ppermute | solution.py:26
  59.1 1.0 %constant_dynamic-update-slice_fusion.2 = bf16[1024,1152]{1,0:T(8,128)(2,1)S(1)} fusion(bf16[1024,1152]{1,0:T(8,128)(2,1)S(1)} %constant_dynamic-update-slice_fusion.3, bf16[1024,128]{1,0:T(8,128)(2,1)} %bitcast.56), kind=kLoop, calls=%fused_computation.49 | loop fusion | bytes 524288 | tf_op jit(solution)/shard_map/concatenate | solution.py:38
  60.1 1.1 %collective-permute-done.4 = f32[108,128]{1,0:T(8,128)S(1)} collective-permute-done((f32[108,128]{1,0:T(8,128)S(1)}, f32[108,128]{1,0:T(8,128)S(1)}, u32[]{:S(2)}, u32[]{:S(2)}) %collective-permute-start.4) | collective-permute-done | bytes 55328 | tf_op jit(solution)/shard_map/ppermute | solution.py:26
  61.3 7.7 %collective-permute-start.5 = (f32[108,128]{1,0:T(8,128)S(1)}, f32[108,128]{1,0:T(8,128)S(1)}, u32[]{:S(2)}, u32[]{:S(2)}) collective-permute-start(f32[108,128]{1,0:T(8,128)S(1)} %add.36), channel_id=1, source_target_pairs={{0,128},{32,160},{64,192},{96,224},{128,0},{160,32},{192,64},{224,... | collective-permute-start | bytes 165896 | tf_op jit(solution)/shard_map/ppermute | solution.py:26
  69.0 1.5 %fusion = bf16[1024,128]{1,0:T(8,128)(2,1)} fusion(f32[1024,128]{1,0:T(8,128)S(1)} %convolution_add_fusion.1, bf16[1024,1152]{1,0:T(8,128)(2,1)S(1)} %constant_dynamic-update-slice_fusion.2, bf16[1152,128]{1,0:T(8,128)(2,1)S(1)} %bitcast.50), kind=kOutput, calls=%fused_computation.2 | convolution fusion | flops 302252032 | bytes 3440640 | tf_op jit(solution)/shard_map/dot_general | solution.py:171
  70.5 0.7 collective-permute-done.5
  71.2 0.6 add_multiply_fusion
  (35 shorter events, 1.1 us)
Async XLA Ops:
  0.6 11.5 %copy-start.1 = (bf16[1,4,16,16,128]{4,3,2,1,0:T(8,128)(2,1)S(1)}, bf16[1,4,16,16,128]{4,3,2,1,0:T(8,128)(2,1)}, u32[]{:S(2)}) copy-start(bf16[1,4,16,16,128]{4,3,2,1,0:T(8,128)(2,1)} %param.4) | copy-start | bytes 786436
  0.6 11.5 %copy-start.2 = (bf16[1,4,16,16,128]{4,3,2,1,0:T(8,128)(2,1)S(1)}, bf16[1,4,16,16,128]{4,3,2,1,0:T(8,128)(2,1)}, u32[]{:S(2)}) copy-start(bf16[1,4,16,16,128]{4,3,2,1,0:T(8,128)(2,1)} %param.7) | copy-start | bytes 786436
  0.7 11.5 %copy-start = (bf16[3456,128]{1,0:T(8,128)(2,1)S(1)}, bf16[3456,128]{1,0:T(8,128)(2,1)}, u32[]{:S(2)}) copy-start(bf16[3456,128]{1,0:T(8,128)(2,1)} %w_ref.1) | copy-start | bytes 2654212
  1.8 10.2 %collective-permute-start = (bf16[1,2,16,16,128]{4,3,2,1,0:T(8,128)(2,1)S(1)}, bf16[1,2,16,16,128]{4,3,2,1,0:T(8,128)(2,1)S(1)}, u32[]{:S(2)}, u32[]{:S(2)}) collective-permute-start(bf16[1,2,16,16,128]{4,3,2,1,0:T(8,128)(2,1)S(1)} %get-tuple-element.26), channel_id=1, source_target_pairs={{0,1},{1,2},{2,3},{3,4},{4,5},{5,6},{6,7},{7,8},{8,9},{9,10},{10,1... | collective-permute-start | bytes 393224 | tf_op jit(solution)/shard_map/ppermute | solution.py:16
  4.6 7.5 %collective-permute-start.1 = (bf16[1,4,16,16,128]{4,3,2,1,0:T(8,128)(2,1)S(1)}, bf16[1,4,16,16,128]{4,3,2,1,0:T(8,128)(2,1)S(1)}, u32[]{:S(2)}, u32[]{:S(2)}) collective-permute-start(bf16[1,4,16,16,128]{4,3,2,1,0:T(8,128)(2,1)S(1)} %pad_maximum_fusion), channel_id=1, source_target_pairs={{1,0},{2,1},{3,2},{4,3},{5,4},{6,5},{7,6},{8,7},{9,8},{10,9},{11,1... | collective-permute-start | bytes 786440 | tf_op jit(solution)/shard_map/ppermute | solution.py:16
  17.7 5.8 %collective-permute-start.2 = (f32[16,108,128]{2,0,1:T(8,128)S(1)}, f32[16,108,128]{2,0,1:T(8,128)S(1)}, u32[]{:S(2)}, u32[]{:S(2)}) collective-permute-start(f32[16,108,128]{2,0,1:T(8,128)S(1)} %copy.13), channel_id=1, source_target_pairs={{0,1},{1,0},{2,3},{3,2},{4,5},{5,4},{6,7},{7,6},{8,9},{9,8},{10,11... | collective-permute-start | bytes 2654216 | tf_op jit(solution)/shard_map/ppermute | solution.py:22
  22.0 1.4 %copy-start.3 = (bf16[4,16,16,1152]{3,2,1,0:T(8,128)(2,1)}, bf16[4,16,16,1152]{3,2,1,0:T(8,128)(2,1)S(1)}, u32[]{:S(2)}) copy-start(bf16[4,16,16,1152]{3,2,1,0:T(8,128)(2,1)S(1)} %fusion.16) | copy-start | bytes 7077892
  23.5 1.4 %copy-start.5 = (bf16[4,16,16,1152]{3,2,1,0:T(8,128)(2,1)}, bf16[4,16,16,1152]{3,2,1,0:T(8,128)(2,1)S(1)}, u32[]{:S(2)}) copy-start(bf16[4,16,16,1152]{3,2,1,0:T(8,128)(2,1)S(1)} %fusion.8) | copy-start | bytes 7077892
  24.9 10.9 %copy-start.6 = (bf16[9,128,128]{2,1,0:T(8,128)(2,1)S(1)}, bf16[9,128,128]{2,1,0:T(8,128)(2,1)}, u32[]{:S(2)}) copy-start(bf16[9,128,128]{2,1,0:T(8,128)(2,1)} %copy.10) | copy-start | bytes 884740
  26.1 23.7 %all-to-all-start = ((f32[16,108,128]{2,1,0:T(8,128)}), f32[16,108,128]{2,1,0:T(8,128)}, u32[]{:S(2)}, u32[]{:S(2)}) async-start(f32[16,108,128]{2,1,0:T(8,128)} %copy_add_fusion), calls=%async_computation | async-start | bytes 1835008 | tf_op jit(solution)/shard_map/all_to_all | solution.py:23
  35.8 2.6 %copy-start.4 = (bf16[4,16,16,1152]{3,2,1,0:T(8,128)(2,1)S(1)}, bf16[4,16,16,1152]{3,2,1,0:T(8,128)(2,1)}, u32[]{:S(2)}) copy-start(bf16[4,16,16,1152]{3,2,1,0:T(8,128)(2,1)} %copy-done.3) | copy-start | bytes 7077892
  51.0 4.3 %collective-permute-start.3 = (f32[108,128]{1,0:T(8,128)S(1)}, f32[108,128]{1,0:T(8,128)S(1)}, u32[]{:S(2)}, u32[]{:S(2)}) collective-permute-start(f32[108,128]{1,0:T(8,128)S(1)} %reduce_sum.9), channel_id=1, source_target_pairs={{0,32},{32,0},{64,96},{96,64},{128,160},{160,128},{192,224},{224,1... | collective-permute-start | bytes 165896 | tf_op jit(solution)/shard_map/ppermute | solution.py:26
  55.3 5.9 %collective-permute-start.4 = (f32[108,128]{1,0:T(8,128)S(1)}, f32[108,128]{1,0:T(8,128)S(1)}, u32[]{:S(2)}, u32[]{:S(2)}) collective-permute-start(f32[108,128]{1,0:T(8,128)S(1)} %add.35), channel_id=1, source_target_pairs={{0,64},{32,96},{64,0},{96,32},{128,192},{160,224},{192,128},{224,1... | collective-permute-start | bytes 165896 | tf_op jit(solution)/shard_map/ppermute | solution.py:26
  61.3 9.9 %collective-permute-start.5 = (f32[108,128]{1,0:T(8,128)S(1)}, f32[108,128]{1,0:T(8,128)S(1)}, u32[]{:S(2)}, u32[]{:S(2)}) collective-permute-start(f32[108,128]{1,0:T(8,128)S(1)} %add.36), channel_id=1, source_target_pairs={{0,128},{32,160},{64,192},{96,224},{128,0},{160,32},{192,64},{224,... | collective-permute-start | bytes 165896 | tf_op jit(solution)/shard_map/ppermute | solution.py:26

commit v10 on v9

--- a/solution.py
+++ b/solution.py
@@ -21,10 +21,10 @@
     cores = lax.axis_size("core")
     mine = mine + lax.ppermute(other, "core", [(i, (i + 1) % cores) for i in range(cores)])
     mine = lax.all_to_all(mine, "chip", 0, 0, tiled=True).sum(axis=0)
-    step = 1
-    while step < dp:
+    step = dp // 2
+    while step >= 1:
         mine = mine + lax.ppermute(mine, "dp", [(i, i ^ step) for i in range(dp)])
-        step *= 2
+        step //= 2
     return mine
 
 

time: 72.2 us -> 71.9 us (level)
  starting transfers between devices: 29.6 us -> 27 us
  waiting for transfers between devices: 13.8 us -> 15.8 us
    ppermute x3, starting transfers between devices: 13.5 us -> 10.9 us  [reduce_weight_grad(): mine = mine + lax.ppermute(mine, 'dp', [(i, i ^ step) for i in range(dp)])]
    ppermute x3, waiting for transfers between devices: 3.06 us -> 5.05 us  [reduce_weight_grad(): mine = mine + lax.ppermute(mine, 'dp', [(i, i ^ step) for i in range(dp)])]
where the time goes in v10:
time: 71.9 us; the launch traced here: 71.2 us
  starting transfers between devices  27 us (38%)
  waiting for transfers between devices  15.8 us (22%)
  local copies, waits for them, and re-layouts  13.1 us (18%)
  Pallas kernels  5.17 us (7%)
  matrix products  4.86 us (7%)
  other arithmetic  4.23 us (6%)
  between operations  0.96 us (1%)
    ppermute x3, starting transfers between devices, reduce_weight_grad(): mine = mine + lax.ppermute(mine, 'dp', [(i, i ^ step) for i in range(dp)])  10.9 us
    all_to_all x1, waiting for transfers between devices, reduce_weight_grad(): mine = lax.all_to_all(mine, 'chip', 0, 0, tiled=True).sum(axis=0)  10.6 us
    all_to_all x1, starting transfers between devices, reduce_weight_grad(): mine = lax.all_to_all(mine, 'chip', 0, 0, tiled=True).sum(axis=0)  8.6 us
    unnamed x38, local copies, waits for them, and re-layouts  5.85 us
    ppermute x2, starting transfers between devices, from_behind(): lax.ppermute(value, axis, [(source, source + steps) for source in range(l...  5.56 us
    pallas_call x1, Pallas kernels, forward_call(): pl.pallas_call(functools.partial(forward_kernel, hh, ww, nout, nfr), out_...  5.17 us
    ppermute x3, waiting for transfers between devices, reduce_weight_grad(): mine = mine + lax.ppermute(mine, 'dp', [(i, i ^ step) for i in range(dp)])  5.05 us
    dot_general x3, matrix products, per_device(): jnp.dot(patch, flipped, preferred_element_type=jnp.float32)  4.86 us
  transfers between devices with their start and end apart: 7, of which 5 were waited for; matrix products, arithmetic and copies ran while one was open for 22% of the time, Pallas kernels for 0%

profile of v10, /device:TPU:8, one launch (start us, length us, event | category | flops | bytes accessed | tf_op | source)
XLA Modules:
  0.0 71.2 jit_solution(13061736618146676340)
XLA Ops:
  0.7 1.1 %fusion.18 = (bf16[1,2,16,16,128]{4,3,2,1,0:T(8,128)(2,1)S(1)}, bf16[1,2,16,16,128]{4,3,2,1,0:T(8,128)(2,1)S(1)}) fusion(bf16[1,4,16,16,128]{4,3,2,1,0:T(8,128)(2,1)} %param.4), kind=kLoop, calls=%fused_computation.66 | loop fusion | bytes 524288 | tf_op jit(solution)/shard_map/slice | solution.py:134
  1.8 1.9 %collective-permute-start = (bf16[1,2,16,16,128]{4,3,2,1,0:T(8,128)(2,1)S(1)}, bf16[1,2,16,16,128]{4,3,2,1,0:T(8,128)(2,1)S(1)}, u32[]{:S(2)}, u32[]{:S(2)}) collective-permute-start(bf16[1,2,16,16,128]{4,3,2,1,0:T(8,128)(2,1)S(1)} %get-tuple-element.26), channel_id=1, source_target_pairs={{0,1},{1,2},{2,3},{3,4},{4,5},{5,6},{6,7},{7,8},{8,9},{9,10},{10,1... | collective-permute-start | bytes 393224 | tf_op jit(solution)/shard_map/ppermute | solution.py:16
  3.7 0.9 %slice.136 = bf16[1,2,16,16,128]{4,3,2,1,0:T(8,128)(2,1)S(1)} slice(bf16[1,4,16,16,128]{4,3,2,1,0:T(8,128)(2,1)} %param.7), slice={[0:1], [0:2], [0:16], [0:16], [0:128]} | slice | bytes 262144 | tf_op jit(solution)/shard_map/slice | solution.py:134
  4.6 3.6 %collective-permute-start.1 = (bf16[1,4,16,16,128]{4,3,2,1,0:T(8,128)(2,1)S(1)}, bf16[1,4,16,16,128]{4,3,2,1,0:T(8,128)(2,1)S(1)}, u32[]{:S(2)}, u32[]{:S(2)}) collective-permute-start(bf16[1,4,16,16,128]{4,3,2,1,0:T(8,128)(2,1)S(1)} %pad_maximum_fusion), channel_id=1, source_target_pairs={{1,0},{2,1},{3,2},{4,3},{5,4},{6,5},{7,6},{8,7},{9,8},{10,9},{11,1... | collective-permute-start | bytes 786440 | tf_op jit(solution)/shard_map/ppermute | solution.py:16
  8.3 0.7 %pad_add_fusion = s32[132]{0:T(256)S(1)} fusion(s32[2]{0:T(128)S(1)} %broadcast.26, s32[128]{0:T(128)} %bitcast.68, s32[2]{0:T(128)S(1)} %broadcast.25), kind=kLoop, calls=%fused_computation.62 | loop fusion | flops 264 | bytes 1056 | tf_op jit(solution)/shard_map/concatenate | solution.py:136
  9.1 0.1 dynamic_slice.3
  9.1 0.1 compare_bitcast_fusion.1
  9.2 1.2 %fusion.17 = (bf16[1152,128]{1,0:T(8,128)(2,1)S(1)}, bf16[1152,128]{1,0:T(8,128)(2,1)S(1)}, bf16[1152,128]{1,0:T(8,128)(2,1)S(1)}) fusion(bf16[3456,128]{1,0:T(8,128)(2,1)} %w_ref.1), kind=kLoop, calls=%fused_computation.65 | loop fusion | bytes 1769472 | tf_op jit(solution)/shard_map/slice | solution.py:169
  10.4 0.1 pad.17.clone
  10.6 0.2 copy.12
  10.8 0.9 %copy.10 = bf16[9,128,128]{2,1,0:T(8,128)(2,1)} copy(bf16[9,128,128]{1,2,0:T(8,128)(2,1)S(1)} %bitcast.53) | data formatting | bytes 589824 | tf_op jit(solution)/shard_map/transpose | solution.py:170
  11.7 0.2 copy.11
  12.0 0.2 collective-permute-done.1
  12.2 5.2 %shard_map.67 = (bf16[1024,128]{1,0:T(8,128)(2,1)}, bf16[1536,128]{1,0:T(8,128)(2,1)S(1)}, f32[16,108,128]{2,1,0:T(8,128)S(1)}, f32[16,108,128]{2,1,0:T(8,128)S(1)}) custom-call(s32[1]{0:T(128)} %bitcast.core_ref, f32[3,6]{1,0:T(4,128)S(1)} %add_convert_fusion.mask_ref, bf16[512,128]{1,0:T(8,128)(2,1)S(1)} %bitcast.47, bf16[1024,128]{1,0:T(8,128)(2,1)S(1)} %bitcast.44, ...), custom_call_target="tpu_custom_call" | custom-call | flops 2264924160 | bytes 3571712 | tf_op jit(solution)/shard_map/pallas_call | solution.py:102
  17.4 0.3 copy.13
  17.7 1.9 %collective-permute-start.2 = (f32[16,108,128]{2,0,1:T(8,128)S(1)}, f32[16,108,128]{2,0,1:T(8,128)S(1)}, u32[]{:S(2)}, u32[]{:S(2)}) collective-permute-start(f32[16,108,128]{2,0,1:T(8,128)S(1)} %copy.13), channel_id=1, source_target_pairs={{0,1},{1,0},{2,3},{3,2},{4,5},{5,4},{6,7},{7,6},{8,9},{9,8},{10,11... | collective-permute-start | bytes 2654216 | tf_op jit(solution)/shard_map/ppermute | solution.py:22
  19.6 1.1 %pad_slice_fusion = (bf16[4,16,16,128]{3,2,1,0:T(8,128)(2,1)}, bf16[4,16,16,128]{3,2,1,0:T(8,128)(2,1)S(1)}, bf16[4,16,16,128]{3,2,1,0:T(8,128)(2,1)S(1)}, bf16[...) fusion(bf16[4,16,16,128]{3,2,1,0:T(8,128)(2,1)S(1)} %bitcast.60), kind=kLoop, calls=%fused_computation.4 | loop fusion | bytes 2359296 | tf_op jit(solution)/shard_map/slice | solution.py:34
  20.9 0.1 constant_dynamic-update-slice_fusion.6
  21.1 0.1 broadcast_select_fusion
  21.3 0.1 fusion.11
  21.4 0.1 fusion.12
  21.6 0.1 fusion.13
  21.8 0.1 fusion.14
  21.9 0.1 fusion.16
  22.2 0.1 fusion.3
  22.3 0.1 fusion.4
  22.5 0.1 fusion.5
  22.6 0.1 fusion.6
  22.8 0.1 fusion.8
  22.9 0.6 copy-done.3
  23.5 1.4 %copy-done.5 = bf16[4,16,16,1152]{3,2,1,0:T(8,128)(2,1)} copy-done((bf16[4,16,16,1152]{3,2,1,0:T(8,128)(2,1)}, bf16[4,16,16,1152]{3,2,1,0:T(8,128)(2,1)S(1)}, u32[]{:S(2)}) %copy-start.5) | copy-done | bytes 2359320
  24.9 1.3 %copy_add_fusion = f32[16,108,128]{2,1,0:T(8,128)} fusion(f32[16,108,128]{2,1,0:T(8,128)S(1)} %get-tuple-element.9, f32[16,108,128]{2,0,1:T(8,128)S(1)} %collective-permute-done.2), kind=kLoop, calls=%fused_computation.3 | loop fusion | flops 221184 | bytes 2654208 | tf_op jit(solution)/shard_map/add | solution.py:22
  26.1 8.6 %all-to-all-start = ((f32[16,108,128]{2,1,0:T(8,128)}), f32[16,108,128]{2,1,0:T(8,128)}, u32[]{:S(2)}, u32[]{:S(2)}) async-start(f32[16,108,128]{2,1,0:T(8,128)} %copy_add_fusion), calls=%async_computation | async-start | bytes 1835008 | tf_op jit(solution)/shard_map/all_to_all | solution.py:23
  34.7 1.0 %constant_dynamic-update-slice_fusion.5 = bf16[1024,1152]{1,0:T(8,128)(2,1)S(1)} fusion(bf16[1024,1152]{1,0:T(8,128)(2,1)S(1)} %get-tuple-element.14, bf16[1024,128]{1,0:T(8,128)(2,1)} %bitcast.59), kind=kLoop, calls=%fused_computation.52 | loop fusion | bytes 524288
  35.8 2.6 %fusion.19 = f32[1024,128]{1,0:T(8,128)S(1)} fusion(bf16[1024,1152]{1,0:T(8,128)(2,1)} %bitcast.49, bf16[1152,128]{1,0:T(8,128)(2,1)S(1)} %bitcast.55), kind=kOutput, calls=%fused_computation.67 | convolution fusion | flops 301989888 | bytes 3178496 | tf_op jit(solution)/shard_map/dot_general | solution.py:171
  38.5 0.8 %convolution_add_fusion.1 = f32[1024,128]{1,0:T(8,128)S(1)} fusion(f32[1024,128]{1,0:T(8,128)S(1)} %fusion.19, bf16[1024,1152]{1,0:T(8,128)(2,1)S(1)} %bitcast.48, bf16[1152,128]{1,0:T(8,128)(2,1)S(1)} %bitcast.51), kind=kOutput, calls=%fused_computation.1 | convolution fusion | flops 302120960 | bytes 3702784 | tf_op jit(solution)/shard_map/dot_general | solution.py:171
  39.2 10.6 %all-to-all-done = f32[16,108,128]{2,1,0:T(8,128)} async-done(((f32[16,108,128]{2,1,0:T(8,128)}), f32[16,108,128]{2,1,0:T(8,128)}, u32[]{:S(2)}, u32[]{:S(2)}) %all-to-all-start) | async-done | bytes 884768 | tf_op jit(solution)/shard_map/all_to_all | solution.py:23
  49.8 1.2 %reduce_sum.9 = f32[108,128]{1,0:T(8,128)S(1)} reduce(f32[16,108,128]{2,1,0:T(8,128)} %all-to-all-done, f32[]{:T(128)} %constant.29.clone.1), dimensions={0}, to_apply=%region_0.1 | reduce | flops 207360 | bytes 940036 | tf_op jit(solution)/shard_map/reduce_sum | solution.py:23
  51.0 7.3 %collective-permute-start.3 = (f32[108,128]{1,0:T(8,128)S(1)}, f32[108,128]{1,0:T(8,128)S(1)}, u32[]{:S(2)}, u32[]{:S(2)}) collective-permute-start(f32[108,128]{1,0:T(8,128)S(1)} %reduce_sum.9), channel_id=1, source_target_pairs={{0,128},{32,160},{64,192},{96,224},{128,0},{160,32},{192,64},{224,... | collective-permute-start | bytes 165896 | tf_op jit(solution)/shard_map/ppermute | solution.py:26
  58.3 1.0 %constant_dynamic-update-slice_fusion.3 = bf16[1024,1152]{1,0:T(8,128)(2,1)S(1)} fusion(bf16[1024,1152]{1,0:T(8,128)(2,1)S(1)} %constant_dynamic-update-slice_fusion.4, bf16[1024,128]{1,0:T(8,128)(2,1)} %bitcast.57), kind=kLoop, calls=%fused_computation.50 | loop fusion | bytes 524288
  59.3 1.2 %collective-permute-done.3 = f32[108,128]{1,0:T(8,128)S(1)} collective-permute-done((f32[108,128]{1,0:T(8,128)S(1)}, f32[108,128]{1,0:T(8,128)S(1)}, u32[]{:S(2)}, u32[]{:S(2)}) %collective-permute-start.3) | collective-permute-done | bytes 55328 | tf_op jit(solution)/shard_map/ppermute | solution.py:26
  60.6 2.7 %collective-permute-start.4 = (f32[108,128]{1,0:T(8,128)S(1)}, f32[108,128]{1,0:T(8,128)S(1)}, u32[]{:S(2)}, u32[]{:S(2)}) collective-permute-start(f32[108,128]{1,0:T(8,128)S(1)} %add.35), channel_id=1, source_target_pairs={{0,64},{32,96},{64,0},{96,32},{128,192},{160,224},{192,128},{224,1... | collective-permute-start | bytes 165896 | tf_op jit(solution)/shard_map/ppermute | solution.py:26
  63.3 1.0 %constant_dynamic-update-slice_fusion.2 = bf16[1024,1152]{1,0:T(8,128)(2,1)S(1)} fusion(bf16[1024,1152]{1,0:T(8,128)(2,1)S(1)} %constant_dynamic-update-slice_fusion.3, bf16[1024,128]{1,0:T(8,128)(2,1)} %bitcast.56), kind=kLoop, calls=%fused_computation.49 | loop fusion | bytes 524288 | tf_op jit(solution)/shard_map/concatenate | solution.py:38
  64.3 1.9 %collective-permute-done.4 = f32[108,128]{1,0:T(8,128)S(1)} collective-permute-done((f32[108,128]{1,0:T(8,128)S(1)}, f32[108,128]{1,0:T(8,128)S(1)}, u32[]{:S(2)}, u32[]{:S(2)}) %collective-permute-start.4) | collective-permute-done | bytes 55328 | tf_op jit(solution)/shard_map/ppermute | solution.py:26
  66.3 0.9 %collective-permute-start.5 = (f32[108,128]{1,0:T(8,128)S(1)}, f32[108,128]{1,0:T(8,128)S(1)}, u32[]{:S(2)}, u32[]{:S(2)}) collective-permute-start(f32[108,128]{1,0:T(8,128)S(1)} %add.36), channel_id=1, source_target_pairs={{0,32},{32,0},{64,96},{96,64},{128,160},{160,128},{192,224},{224,1... | collective-permute-start | bytes 165896 | tf_op jit(solution)/shard_map/ppermute | solution.py:26
  67.1 1.5 %fusion = bf16[1024,128]{1,0:T(8,128)(2,1)} fusion(f32[1024,128]{1,0:T(8,128)S(1)} %convolution_add_fusion.1, bf16[1024,1152]{1,0:T(8,128)(2,1)S(1)} %constant_dynamic-update-slice_fusion.2, bf16[1152,128]{1,0:T(8,128)(2,1)S(1)} %bitcast.50), kind=kOutput, calls=%fused_computation.2 | convolution fusion | flops 302252032 | bytes 3440640 | tf_op jit(solution)/shard_map/dot_general | solution.py:171
  68.6 1.9 %collective-permute-done.5 = f32[108,128]{1,0:T(8,128)S(1)} collective-permute-done((f32[108,128]{1,0:T(8,128)S(1)}, f32[108,128]{1,0:T(8,128)S(1)}, u32[]{:S(2)}, u32[]{:S(2)}) %collective-permute-start.5) | collective-permute-done | bytes 55328 | tf_op jit(solution)/shard_map/ppermute | solution.py:26
  70.5 0.6 add_multiply_fusion
  (35 shorter events, 1.1 us)
Async XLA Ops:
  0.6 11.5 %copy-start.1 = (bf16[1,4,16,16,128]{4,3,2,1,0:T(8,128)(2,1)S(1)}, bf16[1,4,16,16,128]{4,3,2,1,0:T(8,128)(2,1)}, u32[]{:S(2)}) copy-start(bf16[1,4,16,16,128]{4,3,2,1,0:T(8,128)(2,1)} %param.4) | copy-start | bytes 786436
  0.6 11.5 %copy-start.2 = (bf16[1,4,16,16,128]{4,3,2,1,0:T(8,128)(2,1)S(1)}, bf16[1,4,16,16,128]{4,3,2,1,0:T(8,128)(2,1)}, u32[]{:S(2)}) copy-start(bf16[1,4,16,16,128]{4,3,2,1,0:T(8,128)(2,1)} %param.7) | copy-start | bytes 786436
  0.7 11.5 %copy-start = (bf16[3456,128]{1,0:T(8,128)(2,1)S(1)}, bf16[3456,128]{1,0:T(8,128)(2,1)}, u32[]{:S(2)}) copy-start(bf16[3456,128]{1,0:T(8,128)(2,1)} %w_ref.1) | copy-start | bytes 2654212
  1.8 10.2 %collective-permute-start = (bf16[1,2,16,16,128]{4,3,2,1,0:T(8,128)(2,1)S(1)}, bf16[1,2,16,16,128]{4,3,2,1,0:T(8,128)(2,1)S(1)}, u32[]{:S(2)}, u32[]{:S(2)}) collective-permute-start(bf16[1,2,16,16,128]{4,3,2,1,0:T(8,128)(2,1)S(1)} %get-tuple-element.26), channel_id=1, source_target_pairs={{0,1},{1,2},{2,3},{3,4},{4,5},{5,6},{6,7},{7,8},{8,9},{9,10},{10,1... | collective-permute-start | bytes 393224 | tf_op jit(solution)/shard_map/ppermute | solution.py:16
  4.6 7.5 %collective-permute-start.1 = (bf16[1,4,16,16,128]{4,3,2,1,0:T(8,128)(2,1)S(1)}, bf16[1,4,16,16,128]{4,3,2,1,0:T(8,128)(2,1)S(1)}, u32[]{:S(2)}, u32[]{:S(2)}) collective-permute-start(bf16[1,4,16,16,128]{4,3,2,1,0:T(8,128)(2,1)S(1)} %pad_maximum_fusion), channel_id=1, source_target_pairs={{1,0},{2,1},{3,2},{4,3},{5,4},{6,5},{7,6},{8,7},{9,8},{10,9},{11,1... | collective-permute-start | bytes 786440 | tf_op jit(solution)/shard_map/ppermute | solution.py:16
  17.7 5.8 %collective-permute-start.2 = (f32[16,108,128]{2,0,1:T(8,128)S(1)}, f32[16,108,128]{2,0,1:T(8,128)S(1)}, u32[]{:S(2)}, u32[]{:S(2)}) collective-permute-start(f32[16,108,128]{2,0,1:T(8,128)S(1)} %copy.13), channel_id=1, source_target_pairs={{0,1},{1,0},{2,3},{3,2},{4,5},{5,4},{6,7},{7,6},{8,9},{9,8},{10,11... | collective-permute-start | bytes 2654216 | tf_op jit(solution)/shard_map/ppermute | solution.py:22
  22.0 1.4 %copy-start.3 = (bf16[4,16,16,1152]{3,2,1,0:T(8,128)(2,1)}, bf16[4,16,16,1152]{3,2,1,0:T(8,128)(2,1)S(1)}, u32[]{:S(2)}) copy-start(bf16[4,16,16,1152]{3,2,1,0:T(8,128)(2,1)S(1)} %fusion.16) | copy-start | bytes 7077892
  23.5 1.4 %copy-start.5 = (bf16[4,16,16,1152]{3,2,1,0:T(8,128)(2,1)}, bf16[4,16,16,1152]{3,2,1,0:T(8,128)(2,1)S(1)}, u32[]{:S(2)}) copy-start(bf16[4,16,16,1152]{3,2,1,0:T(8,128)(2,1)S(1)} %fusion.8) | copy-start | bytes 7077892
  24.9 10.9 %copy-start.6 = (bf16[9,128,128]{2,1,0:T(8,128)(2,1)S(1)}, bf16[9,128,128]{2,1,0:T(8,128)(2,1)}, u32[]{:S(2)}) copy-start(bf16[9,128,128]{2,1,0:T(8,128)(2,1)} %copy.10) | copy-start | bytes 884740
  26.1 23.7 %all-to-all-start = ((f32[16,108,128]{2,1,0:T(8,128)}), f32[16,108,128]{2,1,0:T(8,128)}, u32[]{:S(2)}, u32[]{:S(2)}) async-start(f32[16,108,128]{2,1,0:T(8,128)} %copy_add_fusion), calls=%async_computation | async-start | bytes 1835008 | tf_op jit(solution)/shard_map/all_to_all | solution.py:23
  35.8 2.6 %copy-start.4 = (bf16[4,16,16,1152]{3,2,1,0:T(8,128)(2,1)S(1)}, bf16[4,16,16,1152]{3,2,1,0:T(8,128)(2,1)}, u32[]{:S(2)}) copy-start(bf16[4,16,16,1152]{3,2,1,0:T(8,128)(2,1)} %copy-done.3) | copy-start | bytes 7077892
  51.0 9.5 %collective-permute-start.3 = (f32[108,128]{1,0:T(8,128)S(1)}, f32[108,128]{1,0:T(8,128)S(1)}, u32[]{:S(2)}, u32[]{:S(2)}) collective-permute-start(f32[108,128]{1,0:T(8,128)S(1)} %reduce_sum.9), channel_id=1, source_target_pairs={{0,128},{32,160},{64,192},{96,224},{128,0},{160,32},{192,64},{224,... | collective-permute-start | bytes 165896 | tf_op jit(solution)/shard_map/ppermute | solution.py:26
  60.6 5.7 %collective-permute-start.4 = (f32[108,128]{1,0:T(8,128)S(1)}, f32[108,128]{1,0:T(8,128)S(1)}, u32[]{:S(2)}, u32[]{:S(2)}) collective-permute-start(f32[108,128]{1,0:T(8,128)S(1)} %add.35), channel_id=1, source_target_pairs={{0,64},{32,96},{64,0},{96,32},{128,192},{160,224},{192,128},{224,1... | collective-permute-start | bytes 165896 | tf_op jit(solution)/shard_map/ppermute | solution.py:26
  66.3 4.3 %collective-permute-start.5 = (f32[108,128]{1,0:T(8,128)S(1)}, f32[108,128]{1,0:T(8,128)S(1)}, u32[]{:S(2)}, u32[]{:S(2)}) collective-permute-start(f32[108,128]{1,0:T(8,128)S(1)} %add.36), channel_id=1, source_target_pairs={{0,32},{32,0},{64,96},{96,64},{128,160},{160,128},{192,224},{224,1... | collective-permute-start | bytes 165896 | tf_op jit(solution)/shard_map/ppermute | solution.py:26

commit v11 on v9

--- a/solution.py
+++ b/solution.py
@@ -49,7 +49,7 @@
     pad_ref[...] = jnp.zeros_like(pad_ref)
     for f in range(nout + 2):
         if f < 2:
-            source = early_ref[pl.ds(f * frame, frame), :]
+            source = early_ref[pl.ds((f + nfr - 2) * frame, frame), :]
         elif f < nfr + 2:
             source = own_ref[pl.ds((f - 2) * frame, frame), :]
         else:
@@ -130,7 +130,7 @@
     ww = clips.shape[3]
     cc = clips.shape[4]
     rows = nfr * hh * ww
-    earlier = from_behind(clips[:, nfr - 2 :], TM, 1)[0]
+    earlier = from_behind(clips, TM, 1)[0]
     ahead = from_behind(jnp.concatenate([clips[:, :2], cotangent[:, :2]], axis=1), TM, -1)[0]
     segrow = segment_ids[0]
     segp = jnp.concatenate([jnp.full((2,), -1, jnp.int32), segrow, jnp.full((2,), -2, jnp.int32)])

time: 72.2 us -> 73.2 us (1.014)
    ppermute x2, waiting for transfers between devices: 0.19 us -> 1.17 us  [from_behind(): lax.ppermute(value, axis, [(source, source + steps) for source in range(l...]
    unnamed x38 -> x36, local copies, waits for them, and re-layouts: 5.85 us -> 6.8 us
    all_to_all x1, waiting for transfers between devices: 10.6 us -> 9.63 us  [reduce_weight_grad(): mine = lax.all_to_all(mine, 'chip', 0, 0, tiled=True).sum(axis=0)]
  transfers between devices with their start and end apart: 7 -> 7, of which waited for: 5 -> 5; matrix products, arithmetic and copies ran while one was open for 22% -> 24% of each run, Pallas kernels for 0% -> 0%
where the time goes in v11:
time: 73.2 us; the launch traced here: 72.7 us
  starting transfers between devices  29.7 us (41%)
  waiting for transfers between devices  13.9 us (19%)
  local copies, waits for them, and re-layouts  13.3 us (18%)
  Pallas kernels  5.17 us (7%)
  other arithmetic  4.93 us (7%)
  matrix products  4.86 us (7%)
  between operations  0.94 us (1%)
    ppermute x3, starting transfers between devices, reduce_weight_grad(): mine = mine + lax.ppermute(mine, 'dp', [(i, i ^ step) for i in range(dp)])  13.5 us
    all_to_all x1, waiting for transfers between devices, reduce_weight_grad(): mine = lax.all_to_all(mine, 'chip', 0, 0, tiled=True).sum(axis=0)  9.63 us
    all_to_all x1, starting transfers between devices, reduce_weight_grad(): mine = lax.all_to_all(mine, 'chip', 0, 0, tiled=True).sum(axis=0)  8.6 us
    unnamed x36, local copies, waits for them, and re-layouts  6.8 us
    ppermute x2, starting transfers between devices, from_behind(): lax.ppermute(value, axis, [(source, source + steps) for source in range(l...  5.69 us
    pallas_call x1, Pallas kernels, forward_call(): pl.pallas_call(functools.partial(forward_kernel, hh, ww, nout, nfr), out_...  5.17 us
    dot_general x3, matrix products, per_device(): jnp.dot(patch, flipped, preferred_element_type=jnp.float32)  4.86 us
    ppermute x3, waiting for transfers between devices, reduce_weight_grad(): mine = mine + lax.ppermute(mine, 'dp', [(i, i ^ step) for i in range(dp)])  3.06 us
  transfers between devices with their start and end apart: 7, of which 5 were waited for; matrix products, arithmetic and copies ran while one was open for 24% of the time, Pallas kernels for 0%

profile of v11, /device:TPU:8, one launch (start us, length us, event | category | flops | bytes accessed | tf_op | source)
XLA Modules:
  0.0 72.7 jit_solution(1583379735022937671)
XLA Ops:
  0.7 2.1 %collective-permute-start = (bf16[1,4,16,16,128]{4,3,2,1,0:T(8,128)(2,1)}, bf16[1,4,16,16,128]{4,3,2,1,0:T(8,128)(2,1)S(1)}, u32[]{:S(2)}, u32[]{:S(2)}) collective-permute-start(bf16[1,4,16,16,128]{4,3,2,1,0:T(8,128)(2,1)} %param.4), channel_id=1, source_target_pairs={{0,1},{1,2},{2,3},{3,4},{4,5},{5,6},{6,7},{7,8},{8,9},{9,10},{10,1... | collective-permute-start | bytes 786440 | tf_op jit(solution)/shard_map/ppermute | solution.py:16
  2.7 0.9 %slice.131 = bf16[1,2,16,16,128]{4,3,2,1,0:T(8,128)(2,1)S(1)} slice(bf16[1,4,16,16,128]{4,3,2,1,0:T(8,128)(2,1)} %param.4), slice={[0:1], [0:2], [0:16], [0:16], [0:128]} | slice | bytes 262144 | tf_op jit(solution)/shard_map/slice | solution.py:134
  3.6 0.9 %slice.132 = bf16[1,2,16,16,128]{4,3,2,1,0:T(8,128)(2,1)S(1)} slice(bf16[1,4,16,16,128]{4,3,2,1,0:T(8,128)(2,1)} %param.7), slice={[0:1], [0:2], [0:16], [0:16], [0:128]} | slice | bytes 262144 | tf_op jit(solution)/shard_map/slice | solution.py:134
  4.6 0.7 %pad_maximum_fusion = bf16[1,4,16,16,128]{4,3,2,1,0:T(8,128)(2,1)} fusion(bf16[1,2,16,16,128]{4,3,2,1,0:T(8,128)(2,1)S(1)} %slice.132, bf16[1,2,16,16,128]{4,3,2,1,0:T(8,128)(2,1)S(1)} %slice.131), kind=kLoop, calls=%fused_computation.44 | loop fusion | flops 131072 | bytes 524288 | tf_op jit(solution)/shard_map/concatenate | solution.py:134
  5.3 3.6 %collective-permute-start.1 = (bf16[1,4,16,16,128]{4,3,2,1,0:T(8,128)(2,1)}, bf16[1,4,16,16,128]{4,3,2,1,0:T(8,128)(2,1)S(1)}, u32[]{:S(2)}, u32[]{:S(2)}) collective-permute-start(bf16[1,4,16,16,128]{4,3,2,1,0:T(8,128)(2,1)} %pad_maximum_fusion), channel_id=1, source_target_pairs={{1,0},{2,1},{3,2},{4,3},{5,4},{6,5},{7,6},{8,7},{9,8},{10,9},{11,1... | collective-permute-start | bytes 786440 | tf_op jit(solution)/shard_map/ppermute | solution.py:16
  9.0 0.7 %pad_add_fusion = s32[132]{0:T(256)S(1)} fusion(s32[2]{0:T(128)S(1)} %broadcast.26, s32[128]{0:T(128)} %bitcast.68, s32[2]{0:T(128)S(1)} %broadcast.25), kind=kLoop, calls=%fused_computation.62 | loop fusion | flops 264 | bytes 1056 | tf_op jit(solution)/shard_map/concatenate | solution.py:136
  9.7 0.1 dynamic_slice.3
  9.9 1.2 %fusion.17 = (bf16[1152,128]{1,0:T(8,128)(2,1)S(1)}, bf16[1152,128]{1,0:T(8,128)(2,1)S(1)}, bf16[1152,128]{1,0:T(8,128)(2,1)S(1)}) fusion(bf16[3456,128]{1,0:T(8,128)(2,1)} %w_ref.1), kind=kLoop, calls=%fused_computation.65 | loop fusion | bytes 1769472 | tf_op jit(solution)/shard_map/slice | solution.py:169
  11.1 0.2 copy.12
  11.4 0.2 copy.10
  11.6 0.2 copy.11
  12.0 1.2 %collective-permute-done.1 = bf16[1,4,16,16,128]{4,3,2,1,0:T(8,128)(2,1)S(1)} collective-permute-done((bf16[1,4,16,16,128]{4,3,2,1,0:T(8,128)(2,1)}, bf16[1,4,16,16,128]{4,3,2,1,0:T(8,128)(2,1)S(1)}, u32[]{:S(2)}, u32[]{:S(2)}) %collective-permute-start.1) | collective-permute-done | bytes 262176 | tf_op jit(solution)/shard_map/ppermute | solution.py:16
  13.1 5.2 %shard_map.67 = (bf16[1024,128]{1,0:T(8,128)(2,1)}, bf16[1536,128]{1,0:T(8,128)(2,1)S(1)}, f32[16,108,128]{2,1,0:T(8,128)S(1)}, f32[16,108,128]{2,1,0:T(8,128)S(1)}) custom-call(s32[1]{0:T(128)} %bitcast.core_ref, f32[3,6]{1,0:T(4,128)S(1)} %add_convert_fusion.mask_ref, bf16[1024,128]{1,0:T(8,128)(2,1)S(1)} %bitcast.46, bf16[1024,128]{1,0:T(8,128)(2,1)S(1)} %bitcast.44, ...), custom_call_target="tpu_custom_call" | custom-call | flops 2264924160 | bytes 3702784 | tf_op jit(solution)/shard_map/pallas_call | solution.py:102
  18.3 0.3 copy.13
  18.6 1.8 %collective-permute-start.2 = (f32[16,108,128]{2,0,1:T(8,128)S(1)}, f32[16,108,128]{2,0,1:T(8,128)S(1)}, u32[]{:S(2)}, u32[]{:S(2)}) collective-permute-start(f32[16,108,128]{2,0,1:T(8,128)S(1)} %copy.13), channel_id=1, source_target_pairs={{0,1},{1,0},{2,3},{3,2},{4,5},{5,4},{6,7},{7,6},{8,9},{9,8},{10,11... | collective-permute-start | bytes 2654216 | tf_op jit(solution)/shard_map/ppermute | solution.py:22
  20.5 1.1 %pad_slice_fusion = (bf16[4,16,16,128]{3,2,1,0:T(8,128)(2,1)}, bf16[4,16,16,128]{3,2,1,0:T(8,128)(2,1)S(1)}, bf16[4,16,16,128]{3,2,1,0:T(8,128)(2,1)S(1)}, bf16[...) fusion(bf16[4,16,16,128]{3,2,1,0:T(8,128)(2,1)S(1)} %bitcast.60), kind=kLoop, calls=%fused_computation.4 | loop fusion | bytes 2359296 | tf_op jit(solution)/shard_map/slice | solution.py:34
  21.9 0.1 constant_dynamic-update-slice_fusion.6
  22.0 0.1 broadcast_select_fusion
  22.3 0.1 fusion.11
  22.4 0.1 fusion.12
  22.6 0.1 fusion.13
  22.7 0.1 fusion.14
  22.9 0.1 fusion.16
  23.2 0.1 fusion.3
  23.3 0.1 fusion.4
  23.5 0.1 fusion.5
  23.6 0.1 fusion.6
  23.8 0.1 fusion.8
  23.9 0.6 copy-done.3
  24.4 1.4 %copy-done.5 = bf16[4,16,16,1152]{3,2,1,0:T(8,128)(2,1)} copy-done((bf16[4,16,16,1152]{3,2,1,0:T(8,128)(2,1)}, bf16[4,16,16,1152]{3,2,1,0:T(8,128)(2,1)S(1)}, u32[]{:S(2)}) %copy-start.5) | copy-done | bytes 2359320
  25.8 1.3 %copy_add_fusion = f32[16,108,128]{2,1,0:T(8,128)} fusion(f32[16,108,128]{2,1,0:T(8,128)S(1)} %get-tuple-element.9, f32[16,108,128]{2,0,1:T(8,128)S(1)} %collective-permute-done.2), kind=kLoop, calls=%fused_computation.3 | loop fusion | flops 221184 | bytes 2654208 | tf_op jit(solution)/shard_map/add | solution.py:22
  27.1 8.6 %all-to-all-start = ((f32[16,108,128]{2,1,0:T(8,128)}), f32[16,108,128]{2,1,0:T(8,128)}, u32[]{:S(2)}, u32[]{:S(2)}) async-start(f32[16,108,128]{2,1,0:T(8,128)} %copy_add_fusion), calls=%async_computation | async-start | bytes 1835008 | tf_op jit(solution)/shard_map/all_to_all | solution.py:23
  35.7 1.0 %constant_dynamic-update-slice_fusion.5 = bf16[1024,1152]{1,0:T(8,128)(2,1)S(1)} fusion(bf16[1024,1152]{1,0:T(8,128)(2,1)S(1)} %get-tuple-element.14, bf16[1024,128]{1,0:T(8,128)(2,1)} %bitcast.59), kind=kLoop, calls=%fused_computation.52 | loop fusion | bytes 524288
  36.7 1.0 %constant_dynamic-update-slice_fusion.4 = bf16[1024,1152]{1,0:T(8,128)(2,1)S(1)} fusion(bf16[1024,1152]{1,0:T(8,128)(2,1)S(1)} %constant_dynamic-update-slice_fusion.5, bf16[1024,128]{1,0:T(8,128)(2,1)} %bitcast.58), kind=kLoop, calls=%fused_computation.51 | loop fusion | bytes 524288
  37.7 2.6 %fusion.18 = f32[1024,128]{1,0:T(8,128)S(1)} fusion(bf16[1024,1152]{1,0:T(8,128)(2,1)} %bitcast.49, bf16[1152,128]{1,0:T(8,128)(2,1)S(1)} %bitcast.55), kind=kOutput, calls=%fused_computation.66 | convolution fusion | flops 301989888 | bytes 3178496 | tf_op jit(solution)/shard_map/dot_general | solution.py:171
  40.3 0.8 %convolution_add_fusion.1 = f32[1024,128]{1,0:T(8,128)S(1)} fusion(f32[1024,128]{1,0:T(8,128)S(1)} %fusion.18, bf16[1024,1152]{1,0:T(8,128)(2,1)S(1)} %bitcast.48, bf16[1152,128]{1,0:T(8,128)(2,1)S(1)} %bitcast.51), kind=kOutput, calls=%fused_computation.1 | convolution fusion | flops 302120960 | bytes 3702784 | tf_op jit(solution)/shard_map/dot_general | solution.py:171
  41.1 9.6 %all-to-all-done = f32[16,108,128]{2,1,0:T(8,128)} async-done(((f32[16,108,128]{2,1,0:T(8,128)}), f32[16,108,128]{2,1,0:T(8,128)}, u32[]{:S(2)}, u32[]{:S(2)}) %all-to-all-start) | async-done | bytes 884768 | tf_op jit(solution)/shard_map/all_to_all | solution.py:23
  50.8 1.2 %reduce_sum.9 = f32[108,128]{1,0:T(8,128)S(1)} reduce(f32[16,108,128]{2,1,0:T(8,128)} %all-to-all-done, f32[]{:T(128)} %constant.29.clone.1), dimensions={0}, to_apply=%region_0.1 | reduce | flops 207360 | bytes 940036 | tf_op jit(solution)/shard_map/reduce_sum | solution.py:23
  52.0 2.0 %collective-permute-start.3 = (f32[108,128]{1,0:T(8,128)S(1)}, f32[108,128]{1,0:T(8,128)S(1)}, u32[]{:S(2)}, u32[]{:S(2)}) collective-permute-start(f32[108,128]{1,0:T(8,128)S(1)} %reduce_sum.9), channel_id=1, source_target_pairs={{0,32},{32,0},{64,96},{96,64},{128,160},{160,128},{192,224},{224,1... | collective-permute-start | bytes 165896 | tf_op jit(solution)/shard_map/ppermute | solution.py:26
  54.0 1.0 %constant_dynamic-update-slice_fusion.3 = bf16[1024,1152]{1,0:T(8,128)(2,1)S(1)} fusion(bf16[1024,1152]{1,0:T(8,128)(2,1)S(1)} %constant_dynamic-update-slice_fusion.4, bf16[1024,128]{1,0:T(8,128)(2,1)} %bitcast.57), kind=kLoop, calls=%fused_computation.50 | loop fusion | bytes 524288
  55.0 1.2 %collective-permute-done.3 = f32[108,128]{1,0:T(8,128)S(1)} collective-permute-done((f32[108,128]{1,0:T(8,128)S(1)}, f32[108,128]{1,0:T(8,128)S(1)}, u32[]{:S(2)}, u32[]{:S(2)}) %collective-permute-start.3) | collective-permute-done | bytes 55328 | tf_op jit(solution)/shard_map/ppermute | solution.py:26
  56.3 3.8 %collective-permute-start.4 = (f32[108,128]{1,0:T(8,128)S(1)}, f32[108,128]{1,0:T(8,128)S(1)}, u32[]{:S(2)}, u32[]{:S(2)}) collective-permute-start(f32[108,128]{1,0:T(8,128)S(1)} %add.35), channel_id=1, source_target_pairs={{0,64},{32,96},{64,0},{96,32},{128,192},{160,224},{192,128},{224,1... | collective-permute-start | bytes 165896 | tf_op jit(solution)/shard_map/ppermute | solution.py:26
  60.1 1.0 %constant_dynamic-update-slice_fusion.2 = bf16[1024,1152]{1,0:T(8,128)(2,1)S(1)} fusion(bf16[1024,1152]{1,0:T(8,128)(2,1)S(1)} %constant_dynamic-update-slice_fusion.3, bf16[1024,128]{1,0:T(8,128)(2,1)} %bitcast.56), kind=kLoop, calls=%fused_computation.49 | loop fusion | bytes 524288 | tf_op jit(solution)/shard_map/concatenate | solution.py:38
  61.1 1.1 %collective-permute-done.4 = f32[108,128]{1,0:T(8,128)S(1)} collective-permute-done((f32[108,128]{1,0:T(8,128)S(1)}, f32[108,128]{1,0:T(8,128)S(1)}, u32[]{:S(2)}, u32[]{:S(2)}) %collective-permute-start.4) | collective-permute-done | bytes 55328 | tf_op jit(solution)/shard_map/ppermute | solution.py:26
  62.2 7.7 %collective-permute-start.5 = (f32[108,128]{1,0:T(8,128)S(1)}, f32[108,128]{1,0:T(8,128)S(1)}, u32[]{:S(2)}, u32[]{:S(2)}) collective-permute-start(f32[108,128]{1,0:T(8,128)S(1)} %add.36), channel_id=1, source_target_pairs={{0,128},{32,160},{64,192},{96,224},{128,0},{160,32},{192,64},{224,... | collective-permute-start | bytes 165896 | tf_op jit(solution)/shard_map/ppermute | solution.py:26
  70.0 1.5 %fusion = bf16[1024,128]{1,0:T(8,128)(2,1)} fusion(f32[1024,128]{1,0:T(8,128)S(1)} %convolution_add_fusion.1, bf16[1024,1152]{1,0:T(8,128)(2,1)S(1)} %constant_dynamic-update-slice_fusion.2, bf16[1152,128]{1,0:T(8,128)(2,1)S(1)} %bitcast.50), kind=kOutput, calls=%fused_computation.2 | convolution fusion | flops 302252032 | bytes 3440640 | tf_op jit(solution)/shard_map/dot_general | solution.py:171
  71.4 0.7 collective-permute-done.5
  72.1 0.6 add_multiply_fusion
  (33 shorter events, 1.1 us)
Async XLA Ops:
  0.6 12.5 %copy-start.1 = (bf16[1,4,16,16,128]{4,3,2,1,0:T(8,128)(2,1)S(1)}, bf16[1,4,16,16,128]{4,3,2,1,0:T(8,128)(2,1)}, u32[]{:S(2)}) copy-start(bf16[1,4,16,16,128]{4,3,2,1,0:T(8,128)(2,1)} %param.4) | copy-start | bytes 786436
  0.6 12.5 %copy-start.2 = (bf16[1,4,16,16,128]{4,3,2,1,0:T(8,128)(2,1)S(1)}, bf16[1,4,16,16,128]{4,3,2,1,0:T(8,128)(2,1)}, u32[]{:S(2)}) copy-start(bf16[1,4,16,16,128]{4,3,2,1,0:T(8,128)(2,1)} %param.7) | copy-start | bytes 786436
  0.7 12.5 %copy-start = (bf16[3456,128]{1,0:T(8,128)(2,1)S(1)}, bf16[3456,128]{1,0:T(8,128)(2,1)}, u32[]{:S(2)}) copy-start(bf16[3456,128]{1,0:T(8,128)(2,1)} %w_ref.1) | copy-start | bytes 2654212
  0.7 12.5 %collective-permute-start = (bf16[1,4,16,16,128]{4,3,2,1,0:T(8,128)(2,1)}, bf16[1,4,16,16,128]{4,3,2,1,0:T(8,128)(2,1)S(1)}, u32[]{:S(2)}, u32[]{:S(2)}) collective-permute-start(bf16[1,4,16,16,128]{4,3,2,1,0:T(8,128)(2,1)} %param.4), channel_id=1, source_target_pairs={{0,1},{1,2},{2,3},{3,4},{4,5},{5,6},{6,7},{7,8},{8,9},{9,10},{10,1... | collective-permute-start | bytes 786440 | tf_op jit(solution)/shard_map/ppermute | solution.py:16
  5.3 7.8 %collective-permute-start.1 = (bf16[1,4,16,16,128]{4,3,2,1,0:T(8,128)(2,1)}, bf16[1,4,16,16,128]{4,3,2,1,0:T(8,128)(2,1)S(1)}, u32[]{:S(2)}, u32[]{:S(2)}) collective-permute-start(bf16[1,4,16,16,128]{4,3,2,1,0:T(8,128)(2,1)} %pad_maximum_fusion), channel_id=1, source_target_pairs={{1,0},{2,1},{3,2},{4,3},{5,4},{6,5},{7,6},{8,7},{9,8},{10,9},{11,1... | collective-permute-start | bytes 786440 | tf_op jit(solution)/shard_map/ppermute | solution.py:16
  18.6 5.8 %collective-permute-start.2 = (f32[16,108,128]{2,0,1:T(8,128)S(1)}, f32[16,108,128]{2,0,1:T(8,128)S(1)}, u32[]{:S(2)}, u32[]{:S(2)}) collective-permute-start(f32[16,108,128]{2,0,1:T(8,128)S(1)} %copy.13), channel_id=1, source_target_pairs={{0,1},{1,0},{2,3},{3,2},{4,5},{5,4},{6,7},{7,6},{8,9},{9,8},{10,11... | collective-permute-start | bytes 2654216 | tf_op jit(solution)/shard_map/ppermute | solution.py:22
  23.0 1.4 %copy-start.3 = (bf16[4,16,16,1152]{3,2,1,0:T(8,128)(2,1)}, bf16[4,16,16,1152]{3,2,1,0:T(8,128)(2,1)S(1)}, u32[]{:S(2)}) copy-start(bf16[4,16,16,1152]{3,2,1,0:T(8,128)(2,1)S(1)} %fusion.16) | copy-start | bytes 7077892
  24.4 1.4 %copy-start.5 = (bf16[4,16,16,1152]{3,2,1,0:T(8,128)(2,1)}, bf16[4,16,16,1152]{3,2,1,0:T(8,128)(2,1)S(1)}, u32[]{:S(2)}) copy-start(bf16[4,16,16,1152]{3,2,1,0:T(8,128)(2,1)S(1)} %fusion.8) | copy-start | bytes 7077892
  27.1 23.7 %all-to-all-start = ((f32[16,108,128]{2,1,0:T(8,128)}), f32[16,108,128]{2,1,0:T(8,128)}, u32[]{:S(2)}, u32[]{:S(2)}) async-start(f32[16,108,128]{2,1,0:T(8,128)} %copy_add_fusion), calls=%async_computation | async-start | bytes 1835008 | tf_op jit(solution)/shard_map/all_to_all | solution.py:23
  37.7 2.6 %copy-start.4 = (bf16[4,16,16,1152]{3,2,1,0:T(8,128)(2,1)S(1)}, bf16[4,16,16,1152]{3,2,1,0:T(8,128)(2,1)}, u32[]{:S(2)}) copy-start(bf16[4,16,16,1152]{3,2,1,0:T(8,128)(2,1)} %copy-done.3) | copy-start | bytes 7077892
  52.0 4.3 %collective-permute-start.3 = (f32[108,128]{1,0:T(8,128)S(1)}, f32[108,128]{1,0:T(8,128)S(1)}, u32[]{:S(2)}, u32[]{:S(2)}) collective-permute-start(f32[108,128]{1,0:T(8,128)S(1)} %reduce_sum.9), channel_id=1, source_target_pairs={{0,32},{32,0},{64,96},{96,64},{128,160},{160,128},{192,224},{224,1... | collective-permute-start | bytes 165896 | tf_op jit(solution)/shard_map/ppermute | solution.py:26
  56.3 5.9 %collective-permute-start.4 = (f32[108,128]{1,0:T(8,128)S(1)}, f32[108,128]{1,0:T(8,128)S(1)}, u32[]{:S(2)}, u32[]{:S(2)}) collective-permute-start(f32[108,128]{1,0:T(8,128)S(1)} %add.35), channel_id=1, source_target_pairs={{0,64},{32,96},{64,0},{96,32},{128,192},{160,224},{192,128},{224,1... | collective-permute-start | bytes 165896 | tf_op jit(solution)/shard_map/ppermute | solution.py:26
  62.2 9.9 %collective-permute-start.5 = (f32[108,128]{1,0:T(8,128)S(1)}, f32[108,128]{1,0:T(8,128)S(1)}, u32[]{:S(2)}, u32[]{:S(2)}) collective-permute-start(f32[108,128]{1,0:T(8,128)S(1)} %add.36), channel_id=1, source_target_pairs={{0,128},{32,160},{64,192},{96,224},{128,0},{160,32},{192,64},{224,... | collective-permute-start | bytes 165896 | tf_op jit(solution)/shard_map/ppermute | solution.py:26

commit v12 on v9

--- a/solution.py
+++ b/solution.py
@@ -124,6 +124,52 @@
     )(core, mask, early, own, ahead, cot, w)
 
 
+def input_grad_kernel(hh, ww, nfr, mask_ref, gp_ref, w_ref, out_ref, col_ref, pad_ref):
+    frame = hh * ww
+    cc = gp_ref.shape[1]
+    lead = 2 * ww
+    r = lax.broadcasted_iota(jnp.int32, (frame, cc), 0)
+    i = r // ww
+    j = r % ww
+    pad_ref[...] = jnp.zeros_like(pad_ref)
+    for f in range(nfr + 2):
+        pad_ref[pl.ds(lead, frame), :] = gp_ref[pl.ds(f * frame, frame), :].astype(jnp.float32)
+        for ky in range(3):
+            for kx in range(3):
+                dy, dx = 1 - ky, 1 - kx
+                s = pad_ref[pl.ds(lead + dy * ww + dx, frame), :]
+                valid = (i + dy >= 0) & (i + dy < hh) & (j + dx >= 0) & (j + dx < ww)
+                s = jnp.where(valid, s, 0.0)
+                col_ref[f, :, pl.ds((ky * 3 + kx) * cc, cc)] = s.astype(col_ref.dtype)
+    taps = 9 * cc
+    for t in range(nfr):
+        acc = jnp.zeros((frame, cc), jnp.float32)
+        for kt in range(3):
+            part = jnp.dot(col_ref[t + 2 - kt], w_ref[pl.ds(kt * taps, taps), :], preferred_element_type=jnp.float32)
+            acc = acc + mask_ref[kt, t] * part
+        out_ref[pl.ds(t * frame, frame), :] = acc.astype(out_ref.dtype)
+
+
+def input_grad_call(mask, gp, w, hh, ww, nfr):
+    frame = hh * ww
+    cc = gp.shape[1]
+    vmem = pl.BlockSpec(memory_space=pltpu.VMEM)
+    return pl.pallas_call(
+        functools.partial(input_grad_kernel, hh, ww, nfr),
+        out_shape=jax.ShapeDtypeStruct((nfr * frame, cc), jnp.bfloat16),
+        in_specs=[pl.BlockSpec(memory_space=pltpu.SMEM), vmem, vmem],
+        out_specs=vmem,
+        scratch_shapes=[
+            pltpu.VMEM((nfr + 2, frame, 9 * cc), jnp.bfloat16),
+            pltpu.VMEM((frame + 4 * ww, cc), jnp.float32),
+        ],
+        compiler_params=pltpu.CompilerParams(vmem_limit_bytes=32 * 1024 * 1024),
+        cost_estimate=pl.CostEstimate(
+            flops=2 * 3 * frame * 9 * cc * cc * nfr, transcendentals=0, bytes_accessed=2 * (gp.size + w.size) + 2 * nfr * frame * cc
+        ),
+    )(mask, gp, w)
+
+
 def per_device(clips, segment_ids, conv_weight, cotangent):
     nfr = clips.shape[1]
     hh = clips.shape[2]
@@ -157,19 +203,13 @@
     )
     activated = act.reshape(clips.shape)
     count = lax.axis_size("dp") * (lax.axis_size("chip") * lax.axis_size("core")) * rows
-    grad_ext = grad_pre.reshape(nout, hh, ww, cc)
     own = seglocal[2 : 2 + nfr]
-    summed = jnp.zeros((rows, cc), jnp.float32)
-    for kt in range(3):
-        d = 2 - kt
-        later = grad_ext[d : d + nfr]
-        keep = seglocal[2 + d : 2 + d + nfr] == own
-        later = jnp.where(keep[:, None, None, None], later, jnp.zeros_like(later))
-        patch = im2col(later, lambda k: 2 - k, hh, ww)
-        block = conv_weight[kt * 9 * cc : (kt + 1) * 9 * cc].reshape(9, cc, cc)
-        flipped = jnp.swapaxes(block, 1, 2).reshape(9 * cc, cc)
-        summed = summed + jnp.dot(patch, flipped, preferred_element_type=jnp.float32)
-    grad_clips = summed.astype(jnp.bfloat16).reshape(clips.shape)
+    later_mask = jnp.stack([(seglocal[4 - kt : 4 - kt + nfr] == own) for kt in range(3)]).astype(jnp.float32)
+    flipped = jnp.concatenate(
+        [jnp.swapaxes(conv_weight[kt * 9 * cc : (kt + 1) * 9 * cc].reshape(9, cc, cc), 1, 2).reshape(9 * cc, cc) for kt in range(3)],
+        axis=0,
+    )
+    grad_clips = input_grad_call(later_mask, grad_pre, flipped, hh, ww, nfr).reshape(clips.shape)
     grad_weight = reduce_weight_grad(mine, other) / jnp.sqrt(jnp.float32(count))
     return (activated, grad_clips, grad_weight)
 

time: 72.2 us -> 68 us (0.942)
  waiting for transfers between devices: 13.8 us -> 21.7 us
  local copies, waits for them, and re-layouts: 13.1 us -> 6.49 us
  matrix products: 4.86 us -> 0 us
  Pallas kernels: 5.17 us -> 8.6 us
  starting transfers between devices: 29.6 us -> 26.7 us
  other arithmetic: 4.23 us -> 3.34 us
    unnamed x38 -> x8, local copies, waits for them, and re-layouts: 5.85 us -> 0.96 us
    dot_general x3 -> x0, matrix products: 4.86 us -> none  [per_device(): jnp.dot(patch, flipped, preferred_element_type=jnp.float32)]
    ppermute x2, waiting for transfers between devices: 0.19 us -> 4.01 us  [from_behind(): lax.ppermute(value, axis, [(source, source + steps) for source in range(l...]
    pallas_call x0 -> x1, Pallas kernels: none -> 3.43 us  [input_grad_call(): pl.pallas_call(functools.partial(input_grad_kernel, hh, ww, nfr), out_sha...]
    ppermute x1, waiting for transfers between devices: 0.01 us -> 2.41 us  [reduce_weight_grad(): lax.ppermute(other, 'core', [(i, (i + 1) % cores) for i in range(cores)])]
    reshape x0 -> x3, local copies, waits for them, and re-layouts: none -> 2.31 us  [per_device(): conv_weight[kt * 9 * cc:(kt + 1) * 9 * cc].reshape(9, cc, cc)]
    ppermute x1, starting transfers between devices: 1.94 us -> 0.09 us  [reduce_weight_grad(): lax.ppermute(other, 'core', [(i, (i + 1) % cores) for i in range(cores)])]
    slice x3 -> x1, local copies, waits for them, and re-layouts: 2.27 us -> 0.78 us  [per_device(): conv_weight[kt * 9 * cc:(kt + 1) * 9 * cc].reshape(9, cc, cc)]
  transfers between devices with their start and end apart: 7 -> 7, of which waited for: 5 -> 5; matrix products, arithmetic and copies ran while one was open for 22% -> 7% of each run, Pallas kernels for 0% -> 5%
where the time goes in v12:
time: 68 us; the launch traced here: 67.7 us
  starting transfers between devices  26.7 us (39%)
  waiting for transfers between devices  21.7 us (32%)
  Pallas kernels  8.6 us (13%)
  local copies, waits for them, and re-layouts  6.49 us (10%)
  other arithmetic  3.34 us (5%)
  between operations  0.77 us (1%)
    ppermute x3, starting transfers between devices, reduce_weight_grad(): mine = mine + lax.ppermute(mine, 'dp', [(i, i ^ step) for i in range(dp)])  13.6 us
    all_to_all x1, waiting for transfers between devices, reduce_weight_grad(): mine = lax.all_to_all(mine, 'chip', 0, 0, tiled=True).sum(axis=0)  11 us
    all_to_all x1, starting transfers between devices, reduce_weight_grad(): mine = lax.all_to_all(mine, 'chip', 0, 0, tiled=True).sum(axis=0)  8.76 us
    pallas_call x1, Pallas kernels, forward_call(): pl.pallas_call(functools.partial(forward_kernel, hh, ww, nout, nfr), out_...  5.17 us
    ppermute x2, starting transfers between devices, from_behind(): lax.ppermute(value, axis, [(source, source + steps) for source in range(l...  4.33 us
    ppermute x3, waiting for transfers between devices, reduce_weight_grad(): mine = mine + lax.ppermute(mine, 'dp', [(i, i ^ step) for i in range(dp)])  4.27 us
    ppermute x2, waiting for transfers between devices, from_behind(): lax.ppermute(value, axis, [(source, source + steps) for source in range(l...  4.01 us
    pallas_call x1, Pallas kernels, input_grad_call(): pl.pallas_call(functools.partial(input_grad_kernel, hh, ww, nfr), out_sha...  3.43 us
  transfers between devices with their start and end apart: 7, of which 5 were waited for; matrix products, arithmetic and copies ran while one was open for 7% of the time, Pallas kernels for 5%

profile of v12, /device:TPU:8, one launch (start us, length us, event | category | flops | bytes accessed | tf_op | source)
XLA Modules:
  0.0 67.7 jit_solution(17239883577666852306)
XLA Ops:
  0.6 0.0 copy-start.1
  0.6 0.0 copy-start.3
  0.7 0.0 copy-start
  0.7 1.1 %fusion.1 = (bf16[1,2,16,16,128]{4,3,2,1,0:T(8,128)(2,1)S(1)}, bf16[1,2,16,16,128]{4,3,2,1,0:T(8,128)(2,1)S(1)}) fusion(bf16[1,4,16,16,128]{4,3,2,1,0:T(8,128)(2,1)} %param.4), kind=kLoop, calls=%fused_computation.12 | loop fusion | bytes 524288 | tf_op jit(solution)/shard_map/slice | solution.py:180
  1.7 0.9 %slice.43 = bf16[1,2,16,16,128]{4,3,2,1,0:T(8,128)(2,1)S(1)} slice(bf16[1,4,16,16,128]{4,3,2,1,0:T(8,128)(2,1)} %param.7), slice={[0:1], [0:2], [0:16], [0:16], [0:128]} | slice | bytes 262144 | tf_op jit(solution)/shard_map/slice | solution.py:180
  2.7 1.9 %collective-permute-start.1 = (bf16[1,4,16,16,128]{4,3,2,1,0:T(8,128)(2,1)S(1)}, bf16[1,4,16,16,128]{4,3,2,1,0:T(8,128)(2,1)S(1)}, u32[]{:S(2)}, u32[]{:S(2)}) collective-permute-start(bf16[1,4,16,16,128]{4,3,2,1,0:T(8,128)(2,1)S(1)} %pad_maximum_fusion.1), channel_id=1, source_target_pairs={{1,0},{2,1},{3,2},{4,3},{5,4},{6,5},{7,6},{8,7},{9,8},{10,9},{11,1... | collective-permute-start | bytes 786440 | tf_op jit(solution)/shard_map/ppermute | solution.py:16
  4.6 2.4 %collective-permute-start = (bf16[1,2,16,16,128]{4,3,2,1,0:T(8,128)(2,1)S(1)}, bf16[1,2,16,16,128]{4,3,2,1,0:T(8,128)(2,1)S(1)}, u32[]{:S(2)}, u32[]{:S(2)}) collective-permute-start(bf16[1,2,16,16,128]{4,3,2,1,0:T(8,128)(2,1)S(1)} %get-tuple-element.15), channel_id=1, source_target_pairs={{0,1},{1,2},{2,3},{3,4},{4,5},{5,6},{6,7},{7,8},{8,9},{9,10},{10,1... | collective-permute-start | bytes 393224 | tf_op jit(solution)/shard_map/ppermute | solution.py:16
  7.1 0.0 copy-done.3
  7.1 0.1 pad_add_fusion
  7.2 0.1 dynamic_slice.3
  7.2 0.1 compare_bitcast_fusion.3
  7.3 0.1 pad.10.clone
  7.4 0.1 add_convert_fusion.mask_ref
  7.5 4.0 %collective-permute-done = bf16[1,2,16,16,128]{4,3,2,1,0:T(8,128)(2,1)S(1)} collective-permute-done((bf16[1,2,16,16,128]{4,3,2,1,0:T(8,128)(2,1)S(1)}, bf16[1,2,16,16,128]{4,3,2,1,0:T(8,128)(2,1)S(1)}, u32[]{:S(2)}, u32[]{:S(2)}) %collective-permute-start) | collective-permute-done | bytes 131104 | tf_op jit(solution)/shard_map/ppermute | solution.py:16
  11.5 0.0 collective-permute-done.1
  11.5 0.0 copy-done.1
  11.5 0.0 copy-done
  11.5 0.0 copy-start.2
  11.5 0.9 %copy-done.2 = bf16[1,4,16,16,128]{4,3,2,1,0:T(8,128)(2,1)S(1)} copy-done((bf16[1,4,16,16,128]{4,3,2,1,0:T(8,128)(2,1)S(1)}, bf16[1,4,16,16,128]{4,3,2,1,0:T(8,128)(2,1)}, u32[]{:S(2)}) %copy-start.2) | copy-done | bytes 262168
  12.4 5.2 %shard_map.67 = (bf16[1024,128]{1,0:T(8,128)(2,1)}, bf16[1536,128]{1,0:T(8,128)(2,1)S(1)}, f32[16,108,128]{2,1,0:T(8,128)S(1)}, f32[16,108,128]{2,1,0:T(8,128)S(1)}) custom-call(s32[1]{0:T(128)} %bitcast.core_ref, f32[3,6]{1,0:T(4,128)S(1)} %add_convert_fusion.mask_ref, bf16[512,128]{1,0:T(8,128)(2,1)S(1)} %bitcast.33, bf16[1024,128]{1,0:T(8,128)(2,1)S(1)} %bitcast.30, ...), custom_call_target="tpu_custom_call" | custom-call | flops 2264924160 | bytes 3571712 | tf_op jit(solution)/shard_map/pallas_call | solution.py:102
  17.6 0.3 copy.13
  17.9 0.1 collective-permute-start.2
  18.0 2.4 %collective-permute-done.2 = f32[16,108,128]{2,0,1:T(8,128)S(1)} collective-permute-done((f32[16,108,128]{2,0,1:T(8,128)S(1)}, f32[16,108,128]{2,0,1:T(8,128)S(1)}, u32[]{:S(2)}, u32[]{:S(2)}) %collective-permute-start.2) | collective-permute-done | bytes 884768 | tf_op jit(solution)/shard_map/ppermute | solution.py:22
  20.4 1.2 %copy_add_fusion = f32[16,108,128]{2,1,0:T(8,128)} fusion(f32[16,108,128]{2,1,0:T(8,128)S(1)} %get-tuple-element.9, f32[16,108,128]{2,0,1:T(8,128)S(1)} %collective-permute-done.2), kind=kLoop, calls=%fused_computation | loop fusion | flops 221184 | bytes 2654208 | tf_op jit(solution)/shard_map/add | solution.py:22
  21.6 8.8 %all-to-all-start = ((f32[16,108,128]{2,1,0:T(8,128)}), f32[16,108,128]{2,1,0:T(8,128)S(1)}, u32[]{:S(2)}, u32[]{:S(2)}) async-start(f32[16,108,128]{2,1,0:T(8,128)} %copy_add_fusion), calls=%async_computation | async-start | bytes 1835008 | tf_op jit(solution)/shard_map/all_to_all | solution.py:23
  30.4 0.8 %fusion = (bf16[1152,128]{1,0:T(8,128)(2,1)S(1)}, bf16[1152,128]{1,0:T(8,128)(2,1)S(1)}, bf16[1152,128]{1,0:T(8,128)(2,1)}) fusion(bf16[3456,128]{1,0:T(8,128)(2,1)S(1)} %copy-done), kind=kLoop, calls=%fused_computation.11 | loop fusion | bytes 1769472 | tf_op jit(solution)/shard_map/slice | solution.py:209
  31.2 0.2 copy.10
  31.4 1.2 %copy.11 = bf16[9,128,128]{1,2,0:T(8,128)(2,1)S(1)} copy(bf16[9,128,128]{2,1,0:T(8,128)(2,1)} %bitcast.37) | data formatting | bytes 589824 | tf_op jit(solution)/shard_map/reshape | solution.py:209
  32.6 0.9 %copy.12 = bf16[9,128,128]{1,2,0:T(8,128)(2,1)} copy(bf16[9,128,128]{2,1,0:T(8,128)(2,1)S(1)} %bitcast.35) | data formatting | bytes 589824 | tf_op jit(solution)/shard_map/reshape | solution.py:209
  33.5 1.0 %pad_maximum_fusion.w_ref = bf16[3456,128]{1,0:T(8,128)(2,1)S(1)} fusion(bf16[1152,128]{1,0:T(8,128)(2,1)} %bitcast.39, bf16[1152,128]{1,0:T(8,128)(2,1)S(1)} %bitcast.36, bf16[1152,128]{1,0:T(8,128)(2,1)S(1)} %bitcast.34), kind=kLoop, calls=%fused_computation.1 | loop fusion | flops 2654208 | bytes 1769472 | tf_op jit(solution)/shard_map/concatenate | solution.py:208
  34.5 11.0 %all-to-all-done = f32[16,108,128]{2,1,0:T(8,128)S(1)} async-done(((f32[16,108,128]{2,1,0:T(8,128)}), f32[16,108,128]{2,1,0:T(8,128)S(1)}, u32[]{:S(2)}, u32[]{:S(2)}) %all-to-all-start) | async-done | bytes 884768 | tf_op jit(solution)/shard_map/all_to_all | solution.py:23
  45.6 0.1 reduce_sum.9
  45.6 2.0 %collective-permute-start.3 = (f32[108,128]{1,0:T(8,128)S(1)}, f32[108,128]{1,0:T(8,128)S(1)}, u32[]{:S(2)}, u32[]{:S(2)}) collective-permute-start(f32[108,128]{1,0:T(8,128)S(1)} %reduce_sum.9), channel_id=1, source_target_pairs={{0,32},{32,0},{64,96},{96,64},{128,160},{160,128},{192,224},{224,1... | collective-permute-start | bytes 165896 | tf_op jit(solution)/shard_map/ppermute | solution.py:26
  47.6 0.1 compare_bitcast_fusion.1
  47.7 2.2 %collective-permute-done.3 = f32[108,128]{1,0:T(8,128)S(1)} collective-permute-done((f32[108,128]{1,0:T(8,128)S(1)}, f32[108,128]{1,0:T(8,128)S(1)}, u32[]{:S(2)}, u32[]{:S(2)}) %collective-permute-start.3) | collective-permute-done | bytes 55328 | tf_op jit(solution)/shard_map/ppermute | solution.py:26
  49.9 3.7 %collective-permute-start.4 = (f32[108,128]{1,0:T(8,128)S(1)}, f32[108,128]{1,0:T(8,128)S(1)}, u32[]{:S(2)}, u32[]{:S(2)}) collective-permute-start(f32[108,128]{1,0:T(8,128)S(1)} %add.21), channel_id=1, source_target_pairs={{0,64},{32,96},{64,0},{96,32},{128,192},{160,224},{192,128},{224,1... | collective-permute-start | bytes 165896 | tf_op jit(solution)/shard_map/ppermute | solution.py:26
  53.6 0.1 add_convert_fusion.1.mask_ref
  53.6 2.1 %collective-permute-done.4 = f32[108,128]{1,0:T(8,128)S(1)} collective-permute-done((f32[108,128]{1,0:T(8,128)S(1)}, f32[108,128]{1,0:T(8,128)S(1)}, u32[]{:S(2)}, u32[]{:S(2)}) %collective-permute-start.4) | collective-permute-done | bytes 55328 | tf_op jit(solution)/shard_map/ppermute | solution.py:26
  55.7 7.9 %collective-permute-start.5 = (f32[108,128]{1,0:T(8,128)S(1)}, f32[108,128]{1,0:T(8,128)S(1)}, u32[]{:S(2)}, u32[]{:S(2)}) collective-permute-start(f32[108,128]{1,0:T(8,128)S(1)} %add.22), channel_id=1, source_target_pairs={{0,128},{32,160},{64,192},{96,224},{128,0},{160,32},{192,64},{224,... | collective-permute-start | bytes 165896 | tf_op jit(solution)/shard_map/ppermute | solution.py:26
  63.6 3.4 %shard_map.68 = bf16[1024,128]{1,0:T(8,128)(2,1)} custom-call(f32[3,4]{1,0:T(4,128)S(1)} %add_convert_fusion.1.mask_ref, bf16[1536,128]{1,0:T(8,128)(2,1)S(1)} %get-tuple-element.8.gp_ref, bf16[3456,128]{1,0:T(8,128)(2,1)S(1)} %pad_maximum_fusion.w_ref), custom_call_target="tpu_custom_call" | custom-call | flops 905969664 | bytes 1540096 | tf_op jit(solution)/shard_map/pallas_call | solution.py:157
  67.1 0.0 collective-permute-done.5
  67.1 0.6 add_multiply_fusion
  (5 shorter events, 0.0 us)
Async XLA Ops:
  0.6 10.8 %copy-start.1 = (bf16[1,4,16,16,128]{4,3,2,1,0:T(8,128)(2,1)S(1)}, bf16[1,4,16,16,128]{4,3,2,1,0:T(8,128)(2,1)}, u32[]{:S(2)}) copy-start(bf16[1,4,16,16,128]{4,3,2,1,0:T(8,128)(2,1)} %param.4) | copy-start | bytes 786436
  0.6 6.4 %copy-start.3 = (s32[1,128]{1,0:T(1,128)S(1)}, s32[1,128]{1,0:T(1,128)}, u32[]{:S(2)}) copy-start(s32[1,128]{1,0:T(1,128)} %param.5) | copy-start | bytes 1540
  0.7 10.8 %copy-start = (bf16[3456,128]{1,0:T(8,128)(2,1)S(1)}, bf16[3456,128]{1,0:T(8,128)(2,1)}, u32[]{:S(2)}) copy-start(bf16[3456,128]{1,0:T(8,128)(2,1)} %w_ref.1) | copy-start | bytes 2654212
  2.7 8.8 %collective-permute-start.1 = (bf16[1,4,16,16,128]{4,3,2,1,0:T(8,128)(2,1)S(1)}, bf16[1,4,16,16,128]{4,3,2,1,0:T(8,128)(2,1)S(1)}, u32[]{:S(2)}, u32[]{:S(2)}) collective-permute-start(bf16[1,4,16,16,128]{4,3,2,1,0:T(8,128)(2,1)S(1)} %pad_maximum_fusion.1), channel_id=1, source_target_pairs={{1,0},{2,1},{3,2},{4,3},{5,4},{6,5},{7,6},{8,7},{9,8},{10,9},{11,1... | collective-permute-start | bytes 786440 | tf_op jit(solution)/shard_map/ppermute | solution.py:16
  4.6 6.8 %collective-permute-start = (bf16[1,2,16,16,128]{4,3,2,1,0:T(8,128)(2,1)S(1)}, bf16[1,2,16,16,128]{4,3,2,1,0:T(8,128)(2,1)S(1)}, u32[]{:S(2)}, u32[]{:S(2)}) collective-permute-start(bf16[1,2,16,16,128]{4,3,2,1,0:T(8,128)(2,1)S(1)} %get-tuple-element.15), channel_id=1, source_target_pairs={{0,1},{1,2},{2,3},{3,4},{4,5},{5,6},{6,7},{7,8},{8,9},{9,10},{10,1... | collective-permute-start | bytes 393224 | tf_op jit(solution)/shard_map/ppermute | solution.py:16
  11.5 1.0 %copy-start.2 = (bf16[1,4,16,16,128]{4,3,2,1,0:T(8,128)(2,1)S(1)}, bf16[1,4,16,16,128]{4,3,2,1,0:T(8,128)(2,1)}, u32[]{:S(2)}) copy-start(bf16[1,4,16,16,128]{4,3,2,1,0:T(8,128)(2,1)} %param.7) | copy-start | bytes 786436
  17.9 2.5 %collective-permute-start.2 = (f32[16,108,128]{2,0,1:T(8,128)S(1)}, f32[16,108,128]{2,0,1:T(8,128)S(1)}, u32[]{:S(2)}, u32[]{:S(2)}) collective-permute-start(f32[16,108,128]{2,0,1:T(8,128)S(1)} %copy.13), channel_id=1, source_target_pairs={{0,1},{1,0},{2,3},{3,2},{4,5},{5,4},{6,7},{7,6},{8,9},{9,8},{10,11... | collective-permute-start | bytes 2654216 | tf_op jit(solution)/shard_map/ppermute | solution.py:22
  21.6 23.9 %all-to-all-start = ((f32[16,108,128]{2,1,0:T(8,128)}), f32[16,108,128]{2,1,0:T(8,128)S(1)}, u32[]{:S(2)}, u32[]{:S(2)}) async-start(f32[16,108,128]{2,1,0:T(8,128)} %copy_add_fusion), calls=%async_computation | async-start | bytes 1835008 | tf_op jit(solution)/shard_map/all_to_all | solution.py:23
  45.6 4.3 %collective-permute-start.3 = (f32[108,128]{1,0:T(8,128)S(1)}, f32[108,128]{1,0:T(8,128)S(1)}, u32[]{:S(2)}, u32[]{:S(2)}) collective-permute-start(f32[108,128]{1,0:T(8,128)S(1)} %reduce_sum.9), channel_id=1, source_target_pairs={{0,32},{32,0},{64,96},{96,64},{128,160},{160,128},{192,224},{224,1... | collective-permute-start | bytes 165896 | tf_op jit(solution)/shard_map/ppermute | solution.py:26
  49.9 5.8 %collective-permute-start.4 = (f32[108,128]{1,0:T(8,128)S(1)}, f32[108,128]{1,0:T(8,128)S(1)}, u32[]{:S(2)}, u32[]{:S(2)}) collective-permute-start(f32[108,128]{1,0:T(8,128)S(1)} %add.21), channel_id=1, source_target_pairs={{0,64},{32,96},{64,0},{96,32},{128,192},{160,224},{192,128},{224,1... | collective-permute-start | bytes 165896 | tf_op jit(solution)/shard_map/ppermute | solution.py:26
  55.7 11.3 %collective-permute-start.5 = (f32[108,128]{1,0:T(8,128)S(1)}, f32[108,128]{1,0:T(8,128)S(1)}, u32[]{:S(2)}, u32[]{:S(2)}) collective-permute-start(f32[108,128]{1,0:T(8,128)S(1)} %add.22), channel_id=1, source_target_pairs={{0,128},{32,160},{64,192},{96,224},{128,0},{160,32},{192,64},{224,... | collective-permute-start | bytes 165896 | tf_op jit(solution)/shard_map/ppermute | solution.py:26

commit v13 on v12

--- a/solution.py
+++ b/solution.py
@@ -16,16 +16,17 @@
     return lax.ppermute(value, axis, [(source, source + steps) for source in range(leading, last)])
 
 
-def reduce_weight_grad(mine, other):
+def reduce_weight_grad(mine, other, tie):
     dp = lax.axis_size("dp")
     cores = lax.axis_size("core")
     mine = mine + lax.ppermute(other, "core", [(i, (i + 1) % cores) for i in range(cores)])
     mine = lax.all_to_all(mine, "chip", 0, 0, tiled=True).sum(axis=0)
+    mine, tie = lax.optimization_barrier((mine, tie))
     step = 1
     while step < dp:
         mine = mine + lax.ppermute(mine, "dp", [(i, i ^ step) for i in range(dp)])
         step *= 2
-    return mine
+    return mine, tie
 
 
 def im2col(frames, offset, hh, ww):
@@ -209,8 +210,10 @@
         [jnp.swapaxes(conv_weight[kt * 9 * cc : (kt + 1) * 9 * cc].reshape(9, cc, cc), 1, 2).reshape(9 * cc, cc) for kt in range(3)],
         axis=0,
     )
-    grad_clips = input_grad_call(later_mask, grad_pre, flipped, hh, ww, nfr).reshape(clips.shape)
-    grad_weight = reduce_weight_grad(mine, other) / jnp.sqrt(jnp.float32(count))
+    grad_clips = input_grad_call(later_mask, grad_pre, flipped, hh, ww, nfr)
+    total, grad_clips = reduce_weight_grad(mine, other, grad_clips)
+    grad_weight = total / jnp.sqrt(jnp.float32(count))
+    grad_clips = grad_clips.reshape(clips.shape)
     return (activated, grad_clips, grad_weight)
 
 

time: 68 us -> 66.7 us (0.981)
  local copies, waits for them, and re-layouts: 6.49 us -> 4.12 us
  waiting for transfers between devices: 21.7 us -> 23.7 us
  other arithmetic: 3.34 us -> 2.38 us
    ppermute x3, waiting for transfers between devices: 4.27 us -> 6.58 us  [reduce_weight_grad(): mine = mine + lax.ppermute(mine, 'dp', [(i, i ^ step) for i in range(dp)])]
    reshape x3, local copies, waits for them, and re-layouts: 2.31 us -> 0.67 us  [per_device(): conv_weight[kt * 9 * cc:(kt + 1) * 9 * cc].reshape(9, cc, cc)]
    concatenate x1, other arithmetic: 1.02 us -> 0.06 us  [per_device(): jnp.concatenate([jnp.swapaxes(conv_weight[kt * 9 * cc:(kt + 1) * 9 * cc]....]
    slice x1, local copies, waits for them, and re-layouts: 0.78 us -> 0.06 us  [per_device(): conv_weight[kt * 9 * cc:(kt + 1) * 9 * cc].reshape(9, cc, cc)]
  transfers between devices with their start and end apart: 7 -> 7, of which waited for: 5 -> 6; matrix products, arithmetic and copies ran while one was open for 7% -> 2% of each run, Pallas kernels for 5% -> 5%
where the time goes in v13:
time: 66.7 us; the launch traced here: 66.4 us
  starting transfers between devices  26.7 us (40%)
  waiting for transfers between devices  23.7 us (36%)
  Pallas kernels  8.68 us (13%)
  local copies, waits for them, and re-layouts  4.12 us (6%)
  other arithmetic  2.38 us (4%)
  between operations  0.78 us (1%)
    ppermute x3, starting transfers between devices, reduce_weight_grad(): mine = mine + lax.ppermute(mine, 'dp', [(i, i ^ step) for i in range(dp)])  13.6 us
    all_to_all x1, waiting for transfers between devices, reduce_weight_grad(): mine = lax.all_to_all(mine, 'chip', 0, 0, tiled=True).sum(axis=0)  10.8 us
    all_to_all x1, starting transfers between devices, reduce_weight_grad(): mine = lax.all_to_all(mine, 'chip', 0, 0, tiled=True).sum(axis=0)  8.76 us
    ppermute x3, waiting for transfers between devices, reduce_weight_grad(): mine = mine + lax.ppermute(mine, 'dp', [(i, i ^ step) for i in range(dp)])  6.58 us
    pallas_call x1, Pallas kernels, forward_call(): pl.pallas_call(functools.partial(forward_kernel, hh, ww, nout, nfr), out_...  5.17 us
    ppermute x2, starting transfers between devices, from_behind(): lax.ppermute(value, axis, [(source, source + steps) for source in range(l...  4.33 us
    ppermute x2, waiting for transfers between devices, from_behind(): lax.ppermute(value, axis, [(source, source + steps) for source in range(l...  4.01 us
    pallas_call x1, Pallas kernels, input_grad_call(): pl.pallas_call(functools.partial(input_grad_kernel, hh, ww, nfr), out_sha...  3.51 us
  transfers between devices with their start and end apart: 7, of which 6 were waited for; matrix products, arithmetic and copies ran while one was open for 2% of the time, Pallas kernels for 5%

profile of v13, /device:TPU:8, one launch (start us, length us, event | category | flops | bytes accessed | tf_op | source)
XLA Modules:
  0.0 66.4 jit_solution(10500468854254748721)
XLA Ops:
  0.6 0.0 copy-start.1
  0.6 0.0 copy-start.3
  0.7 0.0 copy-start
  0.7 1.1 %fusion.1 = (bf16[1,2,16,16,128]{4,3,2,1,0:T(8,128)(2,1)S(1)}, bf16[1,2,16,16,128]{4,3,2,1,0:T(8,128)(2,1)S(1)}) fusion(bf16[1,4,16,16,128]{4,3,2,1,0:T(8,128)(2,1)} %param.4), kind=kLoop, calls=%fused_computation.12 | loop fusion | bytes 524288 | tf_op jit(solution)/shard_map/slice | solution.py:181
  1.7 0.9 %slice.43 = bf16[1,2,16,16,128]{4,3,2,1,0:T(8,128)(2,1)S(1)} slice(bf16[1,4,16,16,128]{4,3,2,1,0:T(8,128)(2,1)} %param.7), slice={[0:1], [0:2], [0:16], [0:16], [0:128]} | slice | bytes 262144 | tf_op jit(solution)/shard_map/slice | solution.py:181
  2.7 1.9 %collective-permute-start.1 = (bf16[1,4,16,16,128]{4,3,2,1,0:T(8,128)(2,1)S(1)}, bf16[1,4,16,16,128]{4,3,2,1,0:T(8,128)(2,1)S(1)}, u32[]{:S(2)}, u32[]{:S(2)}) collective-permute-start(bf16[1,4,16,16,128]{4,3,2,1,0:T(8,128)(2,1)S(1)} %pad_maximum_fusion.1), channel_id=1, source_target_pairs={{1,0},{2,1},{3,2},{4,3},{5,4},{6,5},{7,6},{8,7},{9,8},{10,9},{11,1... | collective-permute-start | bytes 786440 | tf_op jit(solution)/shard_map/ppermute | solution.py:16
  4.6 2.4 %collective-permute-start = (bf16[1,2,16,16,128]{4,3,2,1,0:T(8,128)(2,1)S(1)}, bf16[1,2,16,16,128]{4,3,2,1,0:T(8,128)(2,1)S(1)}, u32[]{:S(2)}, u32[]{:S(2)}) collective-permute-start(bf16[1,2,16,16,128]{4,3,2,1,0:T(8,128)(2,1)S(1)} %get-tuple-element.19), channel_id=1, source_target_pairs={{0,1},{1,2},{2,3},{3,4},{4,5},{5,6},{6,7},{7,8},{8,9},{9,10},{10,1... | collective-permute-start | bytes 393224 | tf_op jit(solution)/shard_map/ppermute | solution.py:16
  7.1 0.0 copy-done.3
  7.1 0.1 pad_add_fusion
  7.2 0.1 dynamic_slice.3
  7.2 0.1 compare_bitcast_fusion.3
  7.3 0.1 pad.10.clone
  7.4 0.1 add_convert_fusion.mask_ref
  7.5 4.0 %collective-permute-done = bf16[1,2,16,16,128]{4,3,2,1,0:T(8,128)(2,1)S(1)} collective-permute-done((bf16[1,2,16,16,128]{4,3,2,1,0:T(8,128)(2,1)S(1)}, bf16[1,2,16,16,128]{4,3,2,1,0:T(8,128)(2,1)S(1)}, u32[]{:S(2)}, u32[]{:S(2)}) %collective-permute-start) | collective-permute-done | bytes 131104 | tf_op jit(solution)/shard_map/ppermute | solution.py:16
  11.5 0.0 collective-permute-done.1
  11.5 0.0 copy-done.1
  11.5 0.0 copy-done
  11.5 0.0 copy-start.2
  11.5 0.9 %copy-done.2 = bf16[1,4,16,16,128]{4,3,2,1,0:T(8,128)(2,1)S(1)} copy-done((bf16[1,4,16,16,128]{4,3,2,1,0:T(8,128)(2,1)S(1)}, bf16[1,4,16,16,128]{4,3,2,1,0:T(8,128)(2,1)}, u32[]{:S(2)}) %copy-start.2) | copy-done | bytes 262168
  12.4 5.2 %shard_map.67 = (bf16[1024,128]{1,0:T(8,128)(2,1)}, bf16[1536,128]{1,0:T(8,128)(2,1)S(1)}, f32[16,108,128]{2,1,0:T(8,128)S(1)}, f32[16,108,128]{2,1,0:T(8,128)S(1)}) custom-call(s32[1]{0:T(128)} %bitcast.core_ref, f32[3,6]{1,0:T(4,128)S(1)} %add_convert_fusion.mask_ref, bf16[512,128]{1,0:T(8,128)(2,1)S(1)} %bitcast.33, bf16[1024,128]{1,0:T(8,128)(2,1)S(1)} %bitcast.30, ...), custom_call_target="tpu_custom_call" | custom-call | flops 2264924160 | bytes 3571712 | tf_op jit(solution)/shard_map/pallas_call | solution.py:103
  17.6 0.3 copy.10
  17.9 0.1 collective-permute-start.2
  18.0 0.1 fusion
  18.1 2.3 %collective-permute-done.2 = f32[16,108,128]{2,0,1:T(8,128)S(1)} collective-permute-done((f32[16,108,128]{2,0,1:T(8,128)S(1)}, f32[16,108,128]{2,0,1:T(8,128)S(1)}, u32[]{:S(2)}, u32[]{:S(2)}) %collective-permute-start.2) | collective-permute-done | bytes 884768 | tf_op jit(solution)/shard_map/ppermute | solution.py:22
  20.4 1.2 %copy_add_fusion = f32[16,108,128]{2,1,0:T(8,128)} fusion(f32[16,108,128]{2,1,0:T(8,128)S(1)} %get-tuple-element.10, f32[16,108,128]{2,0,1:T(8,128)S(1)} %collective-permute-done.2), kind=kLoop, calls=%fused_computation | loop fusion | flops 221184 | bytes 2654208 | tf_op jit(solution)/shard_map/add | solution.py:22
  21.6 8.8 %all-to-all-start = ((f32[16,108,128]{2,1,0:T(8,128)}), f32[16,108,128]{2,1,0:T(8,128)S(1)}, u32[]{:S(2)}, u32[]{:S(2)}) async-start(f32[16,108,128]{2,1,0:T(8,128)} %copy_add_fusion), calls=%async_computation | async-start | bytes 1835008 | tf_op jit(solution)/shard_map/all_to_all | solution.py:23
  30.4 0.1 compare_bitcast_fusion.1
  30.5 0.2 copy.12
  30.7 0.2 copy.13
  30.9 0.2 copy.14
  31.1 0.1 add_convert_fusion.1.mask_ref
  31.2 0.1 pad_maximum_fusion.w_ref
  31.3 3.5 %shard_map.68 = bf16[1024,128]{1,0:T(8,128)(2,1)} custom-call(f32[3,4]{1,0:T(4,128)S(1)} %add_convert_fusion.1.mask_ref, bf16[1536,128]{1,0:T(8,128)(2,1)S(1)} %get-tuple-element.12.gp_ref, bf16[3456,128]{1,0:T(8,128)(2,1)S(1)} %pad_maximum_fusion.w_ref), custom_call_target="tpu_custom_call" | custom-call | flops 905969664 | bytes 1540096 | tf_op jit(solution)/shard_map/pallas_call | solution.py:158
  34.8 10.8 %all-to-all-done = f32[16,108,128]{2,1,0:T(8,128)S(1)} async-done(((f32[16,108,128]{2,1,0:T(8,128)}), f32[16,108,128]{2,1,0:T(8,128)S(1)}, u32[]{:S(2)}, u32[]{:S(2)}) %all-to-all-start) | async-done | bytes 884768 | tf_op jit(solution)/shard_map/all_to_all | solution.py:23
  45.6 0.1 reduce_sum.9
  45.6 2.0 %collective-permute-start.3 = (f32[108,128]{1,0:T(8,128)S(1)}, f32[108,128]{1,0:T(8,128)S(1)}, u32[]{:S(2)}, u32[]{:S(2)}) collective-permute-start(f32[108,128]{1,0:T(8,128)S(1)} %reduce_sum.9), channel_id=1, source_target_pairs={{0,32},{32,0},{64,96},{96,64},{128,160},{160,128},{192,224},{224,1... | collective-permute-start | bytes 165896 | tf_op jit(solution)/shard_map/ppermute | solution.py:27
  47.6 2.3 %collective-permute-done.3 = f32[108,128]{1,0:T(8,128)S(1)} collective-permute-done((f32[108,128]{1,0:T(8,128)S(1)}, f32[108,128]{1,0:T(8,128)S(1)}, u32[]{:S(2)}, u32[]{:S(2)}) %collective-permute-start.3) | collective-permute-done | bytes 55328 | tf_op jit(solution)/shard_map/ppermute | solution.py:27
  49.9 3.7 %collective-permute-start.4 = (f32[108,128]{1,0:T(8,128)S(1)}, f32[108,128]{1,0:T(8,128)S(1)}, u32[]{:S(2)}, u32[]{:S(2)}) collective-permute-start(f32[108,128]{1,0:T(8,128)S(1)} %add.21), channel_id=1, source_target_pairs={{0,64},{32,96},{64,0},{96,32},{128,192},{160,224},{192,128},{224,1... | collective-permute-start | bytes 165896 | tf_op jit(solution)/shard_map/ppermute | solution.py:27
  53.6 2.2 %collective-permute-done.4 = f32[108,128]{1,0:T(8,128)S(1)} collective-permute-done((f32[108,128]{1,0:T(8,128)S(1)}, f32[108,128]{1,0:T(8,128)S(1)}, u32[]{:S(2)}, u32[]{:S(2)}) %collective-permute-start.4) | collective-permute-done | bytes 55328 | tf_op jit(solution)/shard_map/ppermute | solution.py:27
  55.7 7.9 %collective-permute-start.5 = (f32[108,128]{1,0:T(8,128)S(1)}, f32[108,128]{1,0:T(8,128)S(1)}, u32[]{:S(2)}, u32[]{:S(2)}) collective-permute-start(f32[108,128]{1,0:T(8,128)S(1)} %add.22), channel_id=1, source_target_pairs={{0,128},{32,160},{64,192},{96,224},{128,0},{160,32},{192,64},{224,... | collective-permute-start | bytes 165896 | tf_op jit(solution)/shard_map/ppermute | solution.py:27
  63.6 2.2 %collective-permute-done.5 = f32[108,128]{1,0:T(8,128)S(1)} collective-permute-done((f32[108,128]{1,0:T(8,128)S(1)}, f32[108,128]{1,0:T(8,128)S(1)}, u32[]{:S(2)}, u32[]{:S(2)}) %collective-permute-start.5) | collective-permute-done | bytes 55328 | tf_op jit(solution)/shard_map/ppermute | solution.py:27
  65.8 0.6 add_multiply_fusion
  (5 shorter events, 0.0 us)
Async XLA Ops:
  0.6 10.8 %copy-start.1 = (bf16[1,4,16,16,128]{4,3,2,1,0:T(8,128)(2,1)S(1)}, bf16[1,4,16,16,128]{4,3,2,1,0:T(8,128)(2,1)}, u32[]{:S(2)}) copy-start(bf16[1,4,16,16,128]{4,3,2,1,0:T(8,128)(2,1)} %param.4) | copy-start | bytes 786436
  0.6 6.4 %copy-start.3 = (s32[1,128]{1,0:T(1,128)S(1)}, s32[1,128]{1,0:T(1,128)}, u32[]{:S(2)}) copy-start(s32[1,128]{1,0:T(1,128)} %param.5) | copy-start | bytes 1540
  0.7 10.8 %copy-start = (bf16[3456,128]{1,0:T(8,128)(2,1)S(1)}, bf16[3456,128]{1,0:T(8,128)(2,1)}, u32[]{:S(2)}) copy-start(bf16[3456,128]{1,0:T(8,128)(2,1)} %w_ref.1) | copy-start | bytes 2654212
  2.7 8.8 %collective-permute-start.1 = (bf16[1,4,16,16,128]{4,3,2,1,0:T(8,128)(2,1)S(1)}, bf16[1,4,16,16,128]{4,3,2,1,0:T(8,128)(2,1)S(1)}, u32[]{:S(2)}, u32[]{:S(2)}) collective-permute-start(bf16[1,4,16,16,128]{4,3,2,1,0:T(8,128)(2,1)S(1)} %pad_maximum_fusion.1), channel_id=1, source_target_pairs={{1,0},{2,1},{3,2},{4,3},{5,4},{6,5},{7,6},{8,7},{9,8},{10,9},{11,1... | collective-permute-start | bytes 786440 | tf_op jit(solution)/shard_map/ppermute | solution.py:16
  4.6 6.8 %collective-permute-start = (bf16[1,2,16,16,128]{4,3,2,1,0:T(8,128)(2,1)S(1)}, bf16[1,2,16,16,128]{4,3,2,1,0:T(8,128)(2,1)S(1)}, u32[]{:S(2)}, u32[]{:S(2)}) collective-permute-start(bf16[1,2,16,16,128]{4,3,2,1,0:T(8,128)(2,1)S(1)} %get-tuple-element.19), channel_id=1, source_target_pairs={{0,1},{1,2},{2,3},{3,4},{4,5},{5,6},{6,7},{7,8},{8,9},{9,10},{10,1... | collective-permute-start | bytes 393224 | tf_op jit(solution)/shard_map/ppermute | solution.py:16
  11.5 1.0 %copy-start.2 = (bf16[1,4,16,16,128]{4,3,2,1,0:T(8,128)(2,1)S(1)}, bf16[1,4,16,16,128]{4,3,2,1,0:T(8,128)(2,1)}, u32[]{:S(2)}) copy-start(bf16[1,4,16,16,128]{4,3,2,1,0:T(8,128)(2,1)} %param.7) | copy-start | bytes 786436
  17.9 2.5 %collective-permute-start.2 = (f32[16,108,128]{2,0,1:T(8,128)S(1)}, f32[16,108,128]{2,0,1:T(8,128)S(1)}, u32[]{:S(2)}, u32[]{:S(2)}) collective-permute-start(f32[16,108,128]{2,0,1:T(8,128)S(1)} %copy.10), channel_id=1, source_target_pairs={{0,1},{1,0},{2,3},{3,2},{4,5},{5,4},{6,7},{7,6},{8,9},{9,8},{10,11... | collective-permute-start | bytes 2654216 | tf_op jit(solution)/shard_map/ppermute | solution.py:22
  21.6 23.9 %all-to-all-start = ((f32[16,108,128]{2,1,0:T(8,128)}), f32[16,108,128]{2,1,0:T(8,128)S(1)}, u32[]{:S(2)}, u32[]{:S(2)}) async-start(f32[16,108,128]{2,1,0:T(8,128)} %copy_add_fusion), calls=%async_computation | async-start | bytes 1835008 | tf_op jit(solution)/shard_map/all_to_all | solution.py:23
  45.6 4.3 %collective-permute-start.3 = (f32[108,128]{1,0:T(8,128)S(1)}, f32[108,128]{1,0:T(8,128)S(1)}, u32[]{:S(2)}, u32[]{:S(2)}) collective-permute-start(f32[108,128]{1,0:T(8,128)S(1)} %reduce_sum.9), channel_id=1, source_target_pairs={{0,32},{32,0},{64,96},{96,64},{128,160},{160,128},{192,224},{224,1... | collective-permute-start | bytes 165896 | tf_op jit(solution)/shard_map/ppermute | solution.py:27
  49.9 5.8 %collective-permute-start.4 = (f32[108,128]{1,0:T(8,128)S(1)}, f32[108,128]{1,0:T(8,128)S(1)}, u32[]{:S(2)}, u32[]{:S(2)}) collective-permute-start(f32[108,128]{1,0:T(8,128)S(1)} %add.21), channel_id=1, source_target_pairs={{0,64},{32,96},{64,0},{96,32},{128,192},{160,224},{192,128},{224,1... | collective-permute-start | bytes 165896 | tf_op jit(solution)/shard_map/ppermute | solution.py:27
  55.7 10.0 %collective-permute-start.5 = (f32[108,128]{1,0:T(8,128)S(1)}, f32[108,128]{1,0:T(8,128)S(1)}, u32[]{:S(2)}, u32[]{:S(2)}) collective-permute-start(f32[108,128]{1,0:T(8,128)S(1)} %add.22), channel_id=1, source_target_pairs={{0,128},{32,160},{64,192},{96,224},{128,0},{160,32},{192,64},{224,... | collective-permute-start | bytes 165896 | tf_op jit(solution)/shard_map/ppermute | solution.py:27

commit v14 on v13

--- a/solution.py
+++ b/solution.py
@@ -39,7 +39,7 @@
     return jnp.concatenate(pieces, axis=3).reshape(-1, 9 * frames.shape[-1])
 
 
-def forward_kernel(hh, ww, nout, nfr, core_ref, mask_ref, early_ref, own_ref, ahead_ref, cot_ref, w_ref, act_ref, gp_ref, mine_ref, other_ref, col_ref, pad_ref, acc_ref, flat_ref):
+def forward_kernel(hh, ww, nout, nfr, core_ref, mask_ref, early_ref, own_hbm, ahead_ref, cot_hbm, w_ref, act_ref, gp_ref, mine_ref, other_ref, col_ref, pad_ref, acc_ref, flat_ref, cot_ref, cot_sem, own_ref, own_sem):
     frame = hh * ww
     cc = own_ref.shape[1]
     taps = 9 * cc
@@ -47,11 +47,17 @@
     r = lax.broadcasted_iota(jnp.int32, (frame, cc), 0)
     i = r // ww
     j = r % ww
+    own_copy = pltpu.make_async_copy(own_hbm, own_ref, own_sem)
+    own_copy.start()
+    cot_copy = pltpu.make_async_copy(cot_hbm, cot_ref, cot_sem)
+    cot_copy.start()
     pad_ref[...] = jnp.zeros_like(pad_ref)
     for f in range(nout + 2):
         if f < 2:
             source = early_ref[pl.ds(f * frame, frame), :]
         elif f < nfr + 2:
+            if f == 2:
+                own_copy.wait()
             source = own_ref[pl.ds((f - 2) * frame, frame), :]
         else:
             source = ahead_ref[pl.ds((f - nfr - 2) * frame, frame), :]
@@ -63,6 +69,7 @@
                 valid = (i + dy >= 0) & (i + dy < hh) & (j + dx >= 0) & (j + dx < ww)
                 s = jnp.where(valid, s, 0.0)
                 col_ref[f, :, pl.ds((ky * 3 + kx) * cc, cc)] = s.astype(col_ref.dtype)
+    cot_copy.wait()
     for t in range(nout):
         pre = jnp.zeros((frame, cc), jnp.float32)
         for kt in range(3):
@@ -108,13 +115,17 @@
             jax.ShapeDtypeStruct((blocks // 2, krows // blocks, cc), jnp.float32),
             jax.ShapeDtypeStruct((blocks // 2, krows // blocks, cc), jnp.float32),
         ),
-        in_specs=[pl.BlockSpec(memory_space=pltpu.SMEM), pl.BlockSpec(memory_space=pltpu.SMEM), vmem, vmem, vmem, vmem, vmem],
+        in_specs=[pl.BlockSpec(memory_space=pltpu.SMEM), pl.BlockSpec(memory_space=pltpu.SMEM), vmem, pl.BlockSpec(memory_space=pltpu.HBM), vmem, pl.BlockSpec(memory_space=pltpu.HBM), vmem],
         out_specs=(vmem, vmem, vmem, vmem),
         scratch_shapes=[
             pltpu.VMEM((nout + 2, frame, 9 * cc), jnp.bfloat16),
             pltpu.VMEM((frame + 4 * ww, cc), jnp.float32),
             pltpu.VMEM((3, cc, 9 * cc), jnp.float32),
             pltpu.VMEM((krows, cc), jnp.float32),
+            pltpu.VMEM(cot.shape, cot.dtype),
+            pltpu.SemaphoreType.DMA,
+            pltpu.VMEM(own.shape, own.dtype),
+            pltpu.SemaphoreType.DMA,
         ],
         compiler_params=pltpu.CompilerParams(vmem_limit_bytes=48 * 1024 * 1024),
         cost_estimate=pl.CostEstimate(

time: 66.7 us -> 67.4 us (1.010)
  no operation moved by 1% of the time
where the time goes in v14:
time: 67.4 us; the launch traced here: 67.1 us
  starting transfers between devices  26.7 us (40%)
  waiting for transfers between devices  23.7 us (35%)
  Pallas kernels  9.34 us (14%)
  local copies, waits for them, and re-layouts  4.12 us (6%)
  other arithmetic  2.38 us (4%)
  between operations  0.79 us (1%)
    ppermute x3, starting transfers between devices, reduce_weight_grad(): mine = mine + lax.ppermute(mine, 'dp', [(i, i ^ step) for i in range(dp)])  13.6 us
    all_to_all x1, waiting for transfers between devices, reduce_weight_grad(): mine = lax.all_to_all(mine, 'chip', 0, 0, tiled=True).sum(axis=0)  10.8 us
    all_to_all x1, starting transfers between devices, reduce_weight_grad(): mine = lax.all_to_all(mine, 'chip', 0, 0, tiled=True).sum(axis=0)  8.76 us
    ppermute x3, waiting for transfers between devices, reduce_weight_grad(): mine = mine + lax.ppermute(mine, 'dp', [(i, i ^ step) for i in range(dp)])  6.58 us
    pallas_call x1, Pallas kernels, forward_call(): pl.pallas_call(functools.partial(forward_kernel, hh, ww, nout, nfr), out_...  5.83 us
    ppermute x2, starting transfers between devices, from_behind(): lax.ppermute(value, axis, [(source, source + steps) for source in range(l...  4.33 us
    ppermute x2, waiting for transfers between devices, from_behind(): lax.ppermute(value, axis, [(source, source + steps) for source in range(l...  4.01 us
    pallas_call x1, Pallas kernels, input_grad_call(): pl.pallas_call(functools.partial(input_grad_kernel, hh, ww, nfr), out_sha...  3.51 us
  transfers between devices with their start and end apart: 7, of which 6 were waited for; matrix products, arithmetic and copies ran while one was open for 2% of the time, Pallas kernels for 5%

profile of v14, /device:TPU:8, one launch (start us, length us, event | category | flops | bytes accessed | tf_op | source)
XLA Modules:
  0.0 67.1 jit_solution(5964262961578914207)
XLA Ops:
  0.6 0.0 copy-start.1
  0.6 0.0 copy-start.3
  0.7 0.0 copy-start
  0.7 1.1 %fusion.1 = (bf16[1,2,16,16,128]{4,3,2,1,0:T(8,128)(2,1)S(1)}, bf16[1,2,16,16,128]{4,3,2,1,0:T(8,128)(2,1)S(1)}) fusion(bf16[1,4,16,16,128]{4,3,2,1,0:T(8,128)(2,1)} %param.4), kind=kLoop, calls=%fused_computation.12 | loop fusion | bytes 524288 | tf_op jit(solution)/shard_map/slice | solution.py:192
  1.7 0.9 %slice.43 = bf16[1,2,16,16,128]{4,3,2,1,0:T(8,128)(2,1)S(1)} slice(bf16[1,4,16,16,128]{4,3,2,1,0:T(8,128)(2,1)} %param.7), slice={[0:1], [0:2], [0:16], [0:16], [0:128]} | slice | bytes 262144 | tf_op jit(solution)/shard_map/slice | solution.py:192
  2.7 1.9 %collective-permute-start.1 = (bf16[1,4,16,16,128]{4,3,2,1,0:T(8,128)(2,1)S(1)}, bf16[1,4,16,16,128]{4,3,2,1,0:T(8,128)(2,1)S(1)}, u32[]{:S(2)}, u32[]{:S(2)}) collective-permute-start(bf16[1,4,16,16,128]{4,3,2,1,0:T(8,128)(2,1)S(1)} %pad_maximum_fusion.1), channel_id=1, source_target_pairs={{1,0},{2,1},{3,2},{4,3},{5,4},{6,5},{7,6},{8,7},{9,8},{10,9},{11,1... | collective-permute-start | bytes 786440 | tf_op jit(solution)/shard_map/ppermute | solution.py:16
  4.6 2.4 %collective-permute-start = (bf16[1,2,16,16,128]{4,3,2,1,0:T(8,128)(2,1)S(1)}, bf16[1,2,16,16,128]{4,3,2,1,0:T(8,128)(2,1)S(1)}, u32[]{:S(2)}, u32[]{:S(2)}) collective-permute-start(bf16[1,2,16,16,128]{4,3,2,1,0:T(8,128)(2,1)S(1)} %get-tuple-element.19), channel_id=1, source_target_pairs={{0,1},{1,2},{2,3},{3,4},{4,5},{5,6},{6,7},{7,8},{8,9},{9,10},{10,1... | collective-permute-start | bytes 393224 | tf_op jit(solution)/shard_map/ppermute | solution.py:16
  7.1 0.0 copy-done.3
  7.1 0.1 pad_add_fusion
  7.2 0.1 dynamic_slice.3
  7.2 0.1 compare_bitcast_fusion.3
  7.3 0.1 pad.10.clone
  7.4 0.1 add_convert_fusion.mask_ref
  7.5 4.0 %collective-permute-done = bf16[1,2,16,16,128]{4,3,2,1,0:T(8,128)(2,1)S(1)} collective-permute-done((bf16[1,2,16,16,128]{4,3,2,1,0:T(8,128)(2,1)S(1)}, bf16[1,2,16,16,128]{4,3,2,1,0:T(8,128)(2,1)S(1)}, u32[]{:S(2)}, u32[]{:S(2)}) %collective-permute-start) | collective-permute-done | bytes 131104 | tf_op jit(solution)/shard_map/ppermute | solution.py:16
  11.5 0.0 collective-permute-done.1
  11.5 0.0 copy-done.1
  11.5 0.0 copy-done
  11.5 0.0 copy-start.2
  11.5 0.9 %copy-done.2 = bf16[1,4,16,16,128]{4,3,2,1,0:T(8,128)(2,1)S(1)} copy-done((bf16[1,4,16,16,128]{4,3,2,1,0:T(8,128)(2,1)S(1)}, bf16[1,4,16,16,128]{4,3,2,1,0:T(8,128)(2,1)}, u32[]{:S(2)}) %copy-start.2) | copy-done | bytes 262168
  12.4 5.8 %shard_map.67 = (bf16[1024,128]{1,0:T(8,128)(2,1)}, bf16[1536,128]{1,0:T(8,128)(2,1)S(1)}, f32[16,108,128]{2,1,0:T(8,128)S(1)}, f32[16,108,128]{2,1,0:T(8,128)S(1)}) custom-call(s32[1]{0:T(128)} %bitcast.core_ref, f32[3,6]{1,0:T(4,128)S(1)} %add_convert_fusion.mask_ref, bf16[512,128]{1,0:T(8,128)(2,1)S(1)} %bitcast.33, bf16[1024,128]{1,0:T(8,128)(2,1)S(1)} %bitcast.30, ...), custom_call_target="tpu_custom_call" | custom-call | flops 2264924160 | bytes 3571712 | tf_op jit(solution)/shard_map/pallas_call | solution.py:110
  18.3 0.3 copy.10
  18.6 0.1 collective-permute-start.2
  18.7 0.1 fusion
  18.7 2.3 %collective-permute-done.2 = f32[16,108,128]{2,0,1:T(8,128)S(1)} collective-permute-done((f32[16,108,128]{2,0,1:T(8,128)S(1)}, f32[16,108,128]{2,0,1:T(8,128)S(1)}, u32[]{:S(2)}, u32[]{:S(2)}) %collective-permute-start.2) | collective-permute-done | bytes 884768 | tf_op jit(solution)/shard_map/ppermute | solution.py:22
  21.1 1.2 %copy_add_fusion = f32[16,108,128]{2,1,0:T(8,128)} fusion(f32[16,108,128]{2,1,0:T(8,128)S(1)} %get-tuple-element.10, f32[16,108,128]{2,0,1:T(8,128)S(1)} %collective-permute-done.2), kind=kLoop, calls=%fused_computation | loop fusion | flops 221184 | bytes 2654208 | tf_op jit(solution)/shard_map/add | solution.py:22
  22.3 8.8 %all-to-all-start = ((f32[16,108,128]{2,1,0:T(8,128)}), f32[16,108,128]{2,1,0:T(8,128)S(1)}, u32[]{:S(2)}, u32[]{:S(2)}) async-start(f32[16,108,128]{2,1,0:T(8,128)} %copy_add_fusion), calls=%async_computation | async-start | bytes 1835008 | tf_op jit(solution)/shard_map/all_to_all | solution.py:23
  31.1 0.1 compare_bitcast_fusion.1
  31.1 0.2 copy.12
  31.4 0.2 copy.13
  31.6 0.2 copy.14
  31.8 0.1 add_convert_fusion.1.mask_ref
  31.9 0.1 pad_maximum_fusion.w_ref
  31.9 3.5 %shard_map.68 = bf16[1024,128]{1,0:T(8,128)(2,1)} custom-call(f32[3,4]{1,0:T(4,128)S(1)} %add_convert_fusion.1.mask_ref, bf16[1536,128]{1,0:T(8,128)(2,1)S(1)} %get-tuple-element.12.gp_ref, bf16[3456,128]{1,0:T(8,128)(2,1)S(1)} %pad_maximum_fusion.w_ref), custom_call_target="tpu_custom_call" | custom-call | flops 905969664 | bytes 1540096 | tf_op jit(solution)/shard_map/pallas_call | solution.py:169
  35.5 10.8 %all-to-all-done = f32[16,108,128]{2,1,0:T(8,128)S(1)} async-done(((f32[16,108,128]{2,1,0:T(8,128)}), f32[16,108,128]{2,1,0:T(8,128)S(1)}, u32[]{:S(2)}, u32[]{:S(2)}) %all-to-all-start) | async-done | bytes 884768 | tf_op jit(solution)/shard_map/all_to_all | solution.py:23
  46.2 0.1 reduce_sum.9
  46.3 2.0 %collective-permute-start.3 = (f32[108,128]{1,0:T(8,128)S(1)}, f32[108,128]{1,0:T(8,128)S(1)}, u32[]{:S(2)}, u32[]{:S(2)}) collective-permute-start(f32[108,128]{1,0:T(8,128)S(1)} %reduce_sum.9), channel_id=1, source_target_pairs={{0,32},{32,0},{64,96},{96,64},{128,160},{160,128},{192,224},{224,1... | collective-permute-start | bytes 165896 | tf_op jit(solution)/shard_map/ppermute | solution.py:27
  48.3 2.3 %collective-permute-done.3 = f32[108,128]{1,0:T(8,128)S(1)} collective-permute-done((f32[108,128]{1,0:T(8,128)S(1)}, f32[108,128]{1,0:T(8,128)S(1)}, u32[]{:S(2)}, u32[]{:S(2)}) %collective-permute-start.3) | collective-permute-done | bytes 55328 | tf_op jit(solution)/shard_map/ppermute | solution.py:27
  50.6 3.7 %collective-permute-start.4 = (f32[108,128]{1,0:T(8,128)S(1)}, f32[108,128]{1,0:T(8,128)S(1)}, u32[]{:S(2)}, u32[]{:S(2)}) collective-permute-start(f32[108,128]{1,0:T(8,128)S(1)} %add.21), channel_id=1, source_target_pairs={{0,64},{32,96},{64,0},{96,32},{128,192},{160,224},{192,128},{224,1... | collective-permute-start | bytes 165896 | tf_op jit(solution)/shard_map/ppermute | solution.py:27
  54.2 2.2 %collective-permute-done.4 = f32[108,128]{1,0:T(8,128)S(1)} collective-permute-done((f32[108,128]{1,0:T(8,128)S(1)}, f32[108,128]{1,0:T(8,128)S(1)}, u32[]{:S(2)}, u32[]{:S(2)}) %collective-permute-start.4) | collective-permute-done | bytes 55328 | tf_op jit(solution)/shard_map/ppermute | solution.py:27
  56.4 7.9 %collective-permute-start.5 = (f32[108,128]{1,0:T(8,128)S(1)}, f32[108,128]{1,0:T(8,128)S(1)}, u32[]{:S(2)}, u32[]{:S(2)}) collective-permute-start(f32[108,128]{1,0:T(8,128)S(1)} %add.22), channel_id=1, source_target_pairs={{0,128},{32,160},{64,192},{96,224},{128,0},{160,32},{192,64},{224,... | collective-permute-start | bytes 165896 | tf_op jit(solution)/shard_map/ppermute | solution.py:27
  64.3 2.2 %collective-permute-done.5 = f32[108,128]{1,0:T(8,128)S(1)} collective-permute-done((f32[108,128]{1,0:T(8,128)S(1)}, f32[108,128]{1,0:T(8,128)S(1)}, u32[]{:S(2)}, u32[]{:S(2)}) %collective-permute-start.5) | collective-permute-done | bytes 55328 | tf_op jit(solution)/shard_map/ppermute | solution.py:27
  66.4 0.6 add_multiply_fusion
  (5 shorter events, 0.0 us)
Async XLA Ops:
  0.6 10.8 %copy-start.1 = (bf16[1,4,16,16,128]{4,3,2,1,0:T(8,128)(2,1)S(1)}, bf16[1,4,16,16,128]{4,3,2,1,0:T(8,128)(2,1)}, u32[]{:S(2)}) copy-start(bf16[1,4,16,16,128]{4,3,2,1,0:T(8,128)(2,1)} %param.4) | copy-start | bytes 786436
  0.6 6.4 %copy-start.3 = (s32[1,128]{1,0:T(1,128)S(1)}, s32[1,128]{1,0:T(1,128)}, u32[]{:S(2)}) copy-start(s32[1,128]{1,0:T(1,128)} %param.5) | copy-start | bytes 1540
  0.7 10.8 %copy-start = (bf16[3456,128]{1,0:T(8,128)(2,1)S(1)}, bf16[3456,128]{1,0:T(8,128)(2,1)}, u32[]{:S(2)}) copy-start(bf16[3456,128]{1,0:T(8,128)(2,1)} %w_ref.1) | copy-start | bytes 2654212
  2.7 8.8 %collective-permute-start.1 = (bf16[1,4,16,16,128]{4,3,2,1,0:T(8,128)(2,1)S(1)}, bf16[1,4,16,16,128]{4,3,2,1,0:T(8,128)(2,1)S(1)}, u32[]{:S(2)}, u32[]{:S(2)}) collective-permute-start(bf16[1,4,16,16,128]{4,3,2,1,0:T(8,128)(2,1)S(1)} %pad_maximum_fusion.1), channel_id=1, source_target_pairs={{1,0},{2,1},{3,2},{4,3},{5,4},{6,5},{7,6},{8,7},{9,8},{10,9},{11,1... | collective-permute-start | bytes 786440 | tf_op jit(solution)/shard_map/ppermute | solution.py:16
  4.6 6.8 %collective-permute-start = (bf16[1,2,16,16,128]{4,3,2,1,0:T(8,128)(2,1)S(1)}, bf16[1,2,16,16,128]{4,3,2,1,0:T(8,128)(2,1)S(1)}, u32[]{:S(2)}, u32[]{:S(2)}) collective-permute-start(bf16[1,2,16,16,128]{4,3,2,1,0:T(8,128)(2,1)S(1)} %get-tuple-element.19), channel_id=1, source_target_pairs={{0,1},{1,2},{2,3},{3,4},{4,5},{5,6},{6,7},{7,8},{8,9},{9,10},{10,1... | collective-permute-start | bytes 393224 | tf_op jit(solution)/shard_map/ppermute | solution.py:16
  11.5 1.0 %copy-start.2 = (bf16[1,4,16,16,128]{4,3,2,1,0:T(8,128)(2,1)S(1)}, bf16[1,4,16,16,128]{4,3,2,1,0:T(8,128)(2,1)}, u32[]{:S(2)}) copy-start(bf16[1,4,16,16,128]{4,3,2,1,0:T(8,128)(2,1)} %param.7) | copy-start | bytes 786436
  18.6 2.5 %collective-permute-start.2 = (f32[16,108,128]{2,0,1:T(8,128)S(1)}, f32[16,108,128]{2,0,1:T(8,128)S(1)}, u32[]{:S(2)}, u32[]{:S(2)}) collective-permute-start(f32[16,108,128]{2,0,1:T(8,128)S(1)} %copy.10), channel_id=1, source_target_pairs={{0,1},{1,0},{2,3},{3,2},{4,5},{5,4},{6,7},{7,6},{8,9},{9,8},{10,11... | collective-permute-start | bytes 2654216 | tf_op jit(solution)/shard_map/ppermute | solution.py:22
  22.3 23.9 %all-to-all-start = ((f32[16,108,128]{2,1,0:T(8,128)}), f32[16,108,128]{2,1,0:T(8,128)S(1)}, u32[]{:S(2)}, u32[]{:S(2)}) async-start(f32[16,108,128]{2,1,0:T(8,128)} %copy_add_fusion), calls=%async_computation | async-start | bytes 1835008 | tf_op jit(solution)/shard_map/all_to_all | solution.py:23
  46.3 4.3 %collective-permute-start.3 = (f32[108,128]{1,0:T(8,128)S(1)}, f32[108,128]{1,0:T(8,128)S(1)}, u32[]{:S(2)}, u32[]{:S(2)}) collective-permute-start(f32[108,128]{1,0:T(8,128)S(1)} %reduce_sum.9), channel_id=1, source_target_pairs={{0,32},{32,0},{64,96},{96,64},{128,160},{160,128},{192,224},{224,1... | collective-permute-start | bytes 165896 | tf_op jit(solution)/shard_map/ppermute | solution.py:27
  50.6 5.8 %collective-permute-start.4 = (f32[108,128]{1,0:T(8,128)S(1)}, f32[108,128]{1,0:T(8,128)S(1)}, u32[]{:S(2)}, u32[]{:S(2)}) collective-permute-start(f32[108,128]{1,0:T(8,128)S(1)} %add.21), channel_id=1, source_target_pairs={{0,64},{32,96},{64,0},{96,32},{128,192},{160,224},{192,128},{224,1... | collective-permute-start | bytes 165896 | tf_op jit(solution)/shard_map/ppermute | solution.py:27
  56.4 10.0 %collective-permute-start.5 = (f32[108,128]{1,0:T(8,128)S(1)}, f32[108,128]{1,0:T(8,128)S(1)}, u32[]{:S(2)}, u32[]{:S(2)}) collective-permute-start(f32[108,128]{1,0:T(8,128)S(1)} %add.22), channel_id=1, source_target_pairs={{0,128},{32,160},{64,192},{96,224},{128,0},{160,32},{192,64},{224,... | collective-permute-start | bytes 165896 | tf_op jit(solution)/shard_map/ppermute | solution.py:27

commit v15 on v13

--- a/solution.py
+++ b/solution.py
@@ -20,7 +20,9 @@
     dp = lax.axis_size("dp")
     cores = lax.axis_size("core")
     mine = mine + lax.ppermute(other, "core", [(i, (i + 1) % cores) for i in range(cores)])
-    mine = lax.all_to_all(mine, "chip", 0, 0, tiled=True).sum(axis=0)
+    chips = lax.axis_size("chip")
+    mine = lax.all_to_all(mine, "chip", 0, 0, tiled=True)
+    mine = mine.reshape(chips, mine.shape[0] // chips, mine.shape[1]).sum(axis=0)
     mine, tie = lax.optimization_barrier((mine, tie))
     step = 1
     while step < dp:
@@ -39,7 +41,7 @@
     return jnp.concatenate(pieces, axis=3).reshape(-1, 9 * frames.shape[-1])
 
 
-def forward_kernel(hh, ww, nout, nfr, core_ref, mask_ref, early_ref, own_ref, ahead_ref, cot_ref, w_ref, act_ref, gp_ref, mine_ref, other_ref, col_ref, pad_ref, acc_ref, flat_ref):
+def forward_kernel(hh, ww, nout, nfr, blocks_of, core_ref, mask_ref, early_ref, own_ref, ahead_ref, cot_ref, w_ref, act_ref, gp_ref, mine_ref, other_ref, col_ref, pad_ref, acc_ref, flat_ref):
     frame = hh * ww
     cc = own_ref.shape[1]
     taps = 9 * cc
@@ -85,13 +87,13 @@
             acc_ref[kt] = acc_ref[kt] + mask_ref[kt, t] * part
     for kt in range(3):
         flat_ref[pl.ds(kt * taps, taps), :] = jnp.transpose(acc_ref[kt])
-    chips, share = mine_ref.shape[0], mine_ref.shape[1]
+    chips, share = blocks_of, mine_ref.shape[0] // blocks_of
     first = core_ref[0] == 0
     for c in range(chips):
         even = flat_ref[pl.ds(2 * c * share, share), :]
         odd = flat_ref[pl.ds((2 * c + 1) * share, share), :]
-        mine_ref[c] = jnp.where(first, even, odd)
-        other_ref[c] = jnp.where(first, odd, even)
+        mine_ref[pl.ds(c * share, share), :] = jnp.where(first, even, odd)
+        other_ref[pl.ds(c * share, share), :] = jnp.where(first, odd, even)
 
 
 def forward_call(core, mask, early, own, ahead, cot, w, hh, ww, nout, nfr, blocks):
@@ -101,12 +103,12 @@
     vmem = pl.BlockSpec(memory_space=pltpu.VMEM)
     flops = 2 * 3 * frame * 9 * cc * cc * (nout + nfr)
     return pl.pallas_call(
-        functools.partial(forward_kernel, hh, ww, nout, nfr),
+        functools.partial(forward_kernel, hh, ww, nout, nfr, blocks // 2),
         out_shape=(
             jax.ShapeDtypeStruct((nfr * frame, cc), jnp.bfloat16),
             jax.ShapeDtypeStruct((nout * frame, cc), jnp.bfloat16),
-            jax.ShapeDtypeStruct((blocks // 2, krows // blocks, cc), jnp.float32),
-            jax.ShapeDtypeStruct((blocks // 2, krows // blocks, cc), jnp.float32),
+            jax.ShapeDtypeStruct((krows // 2, cc), jnp.float32),
+            jax.ShapeDtypeStruct((krows // 2, cc), jnp.float32),
         ),
         in_specs=[pl.BlockSpec(memory_space=pltpu.SMEM), pl.BlockSpec(memory_space=pltpu.SMEM), vmem, vmem, vmem, vmem, vmem],
         out_specs=(vmem, vmem, vmem, vmem),

time: 66.7 us -> 66.3 us (level)
  other arithmetic: 2.38 us -> 1.25 us
  local copies, waits for them, and re-layouts: 4.12 us -> 4.82 us
    add x1, other arithmetic: 1.22 us -> 0.09 us  [reduce_weight_grad(): mine + lax.ppermute(other, 'core', [(i, (i + 1) % cores) for i in range(c...]
    all_to_all x0 -> x1, local copies, waits for them, and re-layouts: none -> 0.99 us  [reduce_weight_grad(): mine = lax.all_to_all(mine, 'chip', 0, 0, tiled=True)]
where the time goes in v15:
time: 66.3 us; the launch traced here: 66 us
  starting transfers between devices  26.7 us (40%)
  waiting for transfers between devices  23.7 us (36%)
  Pallas kernels  8.68 us (13%)
  local copies, waits for them, and re-layouts  4.82 us (7%)
  other arithmetic  1.25 us (2%)
  between operations  0.78 us (1%)
    ppermute x3, starting transfers between devices, reduce_weight_grad(): mine = mine + lax.ppermute(mine, 'dp', [(i, i ^ step) for i in range(dp)])  13.6 us
    all_to_all x1, waiting for transfers between devices, reduce_weight_grad(): mine = lax.all_to_all(mine, 'chip', 0, 0, tiled=True)  10.8 us
    all_to_all x1, starting transfers between devices, reduce_weight_grad(): mine = lax.all_to_all(mine, 'chip', 0, 0, tiled=True)  8.76 us
    ppermute x3, waiting for transfers between devices, reduce_weight_grad(): mine = mine + lax.ppermute(mine, 'dp', [(i, i ^ step) for i in range(dp)])  6.58 us
    pallas_call x1, Pallas kernels, forward_call(): pl.pallas_call(functools.partial(forward_kernel, hh, ww, nout, nfr, block...  5.17 us
    ppermute x2, starting transfers between devices, from_behind(): lax.ppermute(value, axis, [(source, source + steps) for source in range(l...  4.33 us
    ppermute x2, waiting for transfers between devices, from_behind(): lax.ppermute(value, axis, [(source, source + steps) for source in range(l...  4.01 us
    pallas_call x1, Pallas kernels, input_grad_call(): pl.pallas_call(functools.partial(input_grad_kernel, hh, ww, nfr), out_sha...  3.51 us
  transfers between devices with their start and end apart: 7, of which 6 were waited for; matrix products, arithmetic and copies ran while one was open for 2% of the time, Pallas kernels for 5%

profile of v15, /device:TPU:8, one launch (start us, length us, event | category | flops | bytes accessed | tf_op | source)
XLA Modules:
  0.0 66.0 jit_solution(13504127569566834559)
XLA Ops:
  0.6 0.0 copy-start.1
  0.6 0.0 copy-start.3
  0.7 0.0 copy-start
  0.7 1.1 %fusion.1 = (bf16[1,2,16,16,128]{4,3,2,1,0:T(8,128)(2,1)S(1)}, bf16[1,2,16,16,128]{4,3,2,1,0:T(8,128)(2,1)S(1)}) fusion(bf16[1,4,16,16,128]{4,3,2,1,0:T(8,128)(2,1)} %param.4), kind=kLoop, calls=%fused_computation.11 | loop fusion | bytes 524288 | tf_op jit(solution)/shard_map/slice | solution.py:183
  1.7 0.9 %slice.43 = bf16[1,2,16,16,128]{4,3,2,1,0:T(8,128)(2,1)S(1)} slice(bf16[1,4,16,16,128]{4,3,2,1,0:T(8,128)(2,1)} %param.7), slice={[0:1], [0:2], [0:16], [0:16], [0:128]} | slice | bytes 262144 | tf_op jit(solution)/shard_map/slice | solution.py:183
  2.7 1.9 %collective-permute-start.1 = (bf16[1,4,16,16,128]{4,3,2,1,0:T(8,128)(2,1)S(1)}, bf16[1,4,16,16,128]{4,3,2,1,0:T(8,128)(2,1)S(1)}, u32[]{:S(2)}, u32[]{:S(2)}) collective-permute-start(bf16[1,4,16,16,128]{4,3,2,1,0:T(8,128)(2,1)S(1)} %pad_maximum_fusion.1), channel_id=1, source_target_pairs={{1,0},{2,1},{3,2},{4,3},{5,4},{6,5},{7,6},{8,7},{9,8},{10,9},{11,1... | collective-permute-start | bytes 786440 | tf_op jit(solution)/shard_map/ppermute | solution.py:16
  4.6 2.4 %collective-permute-start = (bf16[1,2,16,16,128]{4,3,2,1,0:T(8,128)(2,1)S(1)}, bf16[1,2,16,16,128]{4,3,2,1,0:T(8,128)(2,1)S(1)}, u32[]{:S(2)}, u32[]{:S(2)}) collective-permute-start(bf16[1,2,16,16,128]{4,3,2,1,0:T(8,128)(2,1)S(1)} %get-tuple-element.19), channel_id=1, source_target_pairs={{0,1},{1,2},{2,3},{3,4},{4,5},{5,6},{6,7},{7,8},{8,9},{9,10},{10,1... | collective-permute-start | bytes 393224 | tf_op jit(solution)/shard_map/ppermute | solution.py:16
  7.1 0.0 copy-done.3
  7.1 0.1 pad_add_fusion
  7.2 0.1 dynamic_slice.3
  7.2 0.1 compare_bitcast_fusion.3
  7.3 0.1 pad.10.clone
  7.4 0.1 add_convert_fusion.mask_ref
  7.5 4.0 %collective-permute-done = bf16[1,2,16,16,128]{4,3,2,1,0:T(8,128)(2,1)S(1)} collective-permute-done((bf16[1,2,16,16,128]{4,3,2,1,0:T(8,128)(2,1)S(1)}, bf16[1,2,16,16,128]{4,3,2,1,0:T(8,128)(2,1)S(1)}, u32[]{:S(2)}, u32[]{:S(2)}) %collective-permute-start) | collective-permute-done | bytes 131104 | tf_op jit(solution)/shard_map/ppermute | solution.py:16
  11.5 0.0 collective-permute-done.1
  11.5 0.0 copy-done.1
  11.5 0.0 copy-done
  11.5 0.0 copy-start.2
  11.5 0.9 %copy-done.2 = bf16[1,4,16,16,128]{4,3,2,1,0:T(8,128)(2,1)S(1)} copy-done((bf16[1,4,16,16,128]{4,3,2,1,0:T(8,128)(2,1)S(1)}, bf16[1,4,16,16,128]{4,3,2,1,0:T(8,128)(2,1)}, u32[]{:S(2)}) %copy-start.2) | copy-done | bytes 262168
  12.4 5.2 %shard_map.67 = (bf16[1024,128]{1,0:T(8,128)(2,1)}, bf16[1536,128]{1,0:T(8,128)(2,1)S(1)}, f32[1728,128]{1,0:T(8,128)S(1)}, f32[1728,128]{1,0:T(8,128)S(1)}) custom-call(s32[1]{0:T(128)} %bitcast.core_ref, f32[3,6]{1,0:T(4,128)S(1)} %add_convert_fusion.mask_ref, bf16[512,128]{1,0:T(8,128)(2,1)S(1)} %bitcast.33, bf16[1024,128]{1,0:T(8,128)(2,1)S(1)} %bitcast.30, ...), custom_call_target="tpu_custom_call" | custom-call | flops 2264924160 | bytes 3571712 | tf_op jit(solution)/shard_map/pallas_call | solution.py:105
  17.6 0.1 collective-permute-start.2
  17.7 0.1 fusion
  17.8 2.3 %collective-permute-done.2 = f32[1728,128]{1,0:T(8,128)S(1)} collective-permute-done((f32[1728,128]{1,0:T(8,128)S(1)}, f32[1728,128]{1,0:T(8,128)S(1)}, u32[]{:S(2)}, u32[]{:S(2)}) %collective-permute-start.2) | collective-permute-done | bytes 884768 | tf_op jit(solution)/shard_map/ppermute | solution.py:22
  20.1 0.1 add.20
  20.2 1.0 %all_to_all.6 = f32[16,108,128]{2,1,0:T(8,128)} reshape(f32[1728,128]{1,0:T(8,128)S(1)} %add.20) | data formatting | bytes 1769472 | tf_op jit(solution)/shard_map/all_to_all | solution.py:24
  21.2 8.8 %all-to-all-start = ((f32[16,108,128]{2,1,0:T(8,128)}), f32[16,108,128]{2,1,0:T(8,128)S(1)}, u32[]{:S(2)}, u32[]{:S(2)}) async-start(f32[16,108,128]{2,1,0:T(8,128)} %all_to_all.6), calls=%async_computation | async-start | bytes 1835008 | tf_op jit(solution)/shard_map/all_to_all | solution.py:24
  30.0 0.1 compare_bitcast_fusion.1
  30.0 0.2 copy.10
  30.3 0.2 copy.11
  30.5 0.2 copy.12
  30.7 0.1 add_convert_fusion.1.mask_ref
  30.8 0.1 pad_maximum_fusion.w_ref
  30.9 3.5 %shard_map.68 = bf16[1024,128]{1,0:T(8,128)(2,1)} custom-call(f32[3,4]{1,0:T(4,128)S(1)} %add_convert_fusion.1.mask_ref, bf16[1536,128]{1,0:T(8,128)(2,1)S(1)} %get-tuple-element.12.gp_ref, bf16[3456,128]{1,0:T(8,128)(2,1)S(1)} %pad_maximum_fusion.w_ref), custom_call_target="tpu_custom_call" | custom-call | flops 905969664 | bytes 1540096 | tf_op jit(solution)/shard_map/pallas_call | solution.py:160
  34.4 10.8 %all-to-all-done = f32[16,108,128]{2,1,0:T(8,128)S(1)} async-done(((f32[16,108,128]{2,1,0:T(8,128)}), f32[16,108,128]{2,1,0:T(8,128)S(1)}, u32[]{:S(2)}, u32[]{:S(2)}) %all-to-all-start) | async-done | bytes 884768 | tf_op jit(solution)/shard_map/all_to_all | solution.py:24
  45.1 0.1 reduce_sum.9
  45.2 2.0 %collective-permute-start.3 = (f32[108,128]{1,0:T(8,128)S(1)}, f32[108,128]{1,0:T(8,128)S(1)}, u32[]{:S(2)}, u32[]{:S(2)}) collective-permute-start(f32[108,128]{1,0:T(8,128)S(1)} %reduce_sum.9), channel_id=1, source_target_pairs={{0,32},{32,0},{64,96},{96,64},{128,160},{160,128},{192,224},{224,1... | collective-permute-start | bytes 165896 | tf_op jit(solution)/shard_map/ppermute | solution.py:29
  47.2 2.3 %collective-permute-done.3 = f32[108,128]{1,0:T(8,128)S(1)} collective-permute-done((f32[108,128]{1,0:T(8,128)S(1)}, f32[108,128]{1,0:T(8,128)S(1)}, u32[]{:S(2)}, u32[]{:S(2)}) %collective-permute-start.3) | collective-permute-done | bytes 55328 | tf_op jit(solution)/shard_map/ppermute | solution.py:29
  49.5 3.7 %collective-permute-start.4 = (f32[108,128]{1,0:T(8,128)S(1)}, f32[108,128]{1,0:T(8,128)S(1)}, u32[]{:S(2)}, u32[]{:S(2)}) collective-permute-start(f32[108,128]{1,0:T(8,128)S(1)} %add.21), channel_id=1, source_target_pairs={{0,64},{32,96},{64,0},{96,32},{128,192},{160,224},{192,128},{224,1... | collective-permute-start | bytes 165896 | tf_op jit(solution)/shard_map/ppermute | solution.py:29
  53.1 2.2 %collective-permute-done.4 = f32[108,128]{1,0:T(8,128)S(1)} collective-permute-done((f32[108,128]{1,0:T(8,128)S(1)}, f32[108,128]{1,0:T(8,128)S(1)}, u32[]{:S(2)}, u32[]{:S(2)}) %collective-permute-start.4) | collective-permute-done | bytes 55328 | tf_op jit(solution)/shard_map/ppermute | solution.py:29
  55.3 7.9 %collective-permute-start.5 = (f32[108,128]{1,0:T(8,128)S(1)}, f32[108,128]{1,0:T(8,128)S(1)}, u32[]{:S(2)}, u32[]{:S(2)}) collective-permute-start(f32[108,128]{1,0:T(8,128)S(1)} %add.22), channel_id=1, source_target_pairs={{0,128},{32,160},{64,192},{96,224},{128,0},{160,32},{192,64},{224,... | collective-permute-start | bytes 165896 | tf_op jit(solution)/shard_map/ppermute | solution.py:29
  63.2 2.2 %collective-permute-done.5 = f32[108,128]{1,0:T(8,128)S(1)} collective-permute-done((f32[108,128]{1,0:T(8,128)S(1)}, f32[108,128]{1,0:T(8,128)S(1)}, u32[]{:S(2)}, u32[]{:S(2)}) %collective-permute-start.5) | collective-permute-done | bytes 55328 | tf_op jit(solution)/shard_map/ppermute | solution.py:29
  65.3 0.6 add_multiply_fusion
  (5 shorter events, 0.0 us)
Async XLA Ops:
  0.6 10.8 %copy-start.1 = (bf16[1,4,16,16,128]{4,3,2,1,0:T(8,128)(2,1)S(1)}, bf16[1,4,16,16,128]{4,3,2,1,0:T(8,128)(2,1)}, u32[]{:S(2)}) copy-start(bf16[1,4,16,16,128]{4,3,2,1,0:T(8,128)(2,1)} %param.4) | copy-start | bytes 786436
  0.6 6.4 %copy-start.3 = (s32[1,128]{1,0:T(1,128)S(1)}, s32[1,128]{1,0:T(1,128)}, u32[]{:S(2)}) copy-start(s32[1,128]{1,0:T(1,128)} %param.5) | copy-start | bytes 1540
  0.7 10.8 %copy-start = (bf16[3456,128]{1,0:T(8,128)(2,1)S(1)}, bf16[3456,128]{1,0:T(8,128)(2,1)}, u32[]{:S(2)}) copy-start(bf16[3456,128]{1,0:T(8,128)(2,1)} %w_ref.1) | copy-start | bytes 2654212
  2.7 8.8 %collective-permute-start.1 = (bf16[1,4,16,16,128]{4,3,2,1,0:T(8,128)(2,1)S(1)}, bf16[1,4,16,16,128]{4,3,2,1,0:T(8,128)(2,1)S(1)}, u32[]{:S(2)}, u32[]{:S(2)}) collective-permute-start(bf16[1,4,16,16,128]{4,3,2,1,0:T(8,128)(2,1)S(1)} %pad_maximum_fusion.1), channel_id=1, source_target_pairs={{1,0},{2,1},{3,2},{4,3},{5,4},{6,5},{7,6},{8,7},{9,8},{10,9},{11,1... | collective-permute-start | bytes 786440 | tf_op jit(solution)/shard_map/ppermute | solution.py:16
  4.6 6.8 %collective-permute-start = (bf16[1,2,16,16,128]{4,3,2,1,0:T(8,128)(2,1)S(1)}, bf16[1,2,16,16,128]{4,3,2,1,0:T(8,128)(2,1)S(1)}, u32[]{:S(2)}, u32[]{:S(2)}) collective-permute-start(bf16[1,2,16,16,128]{4,3,2,1,0:T(8,128)(2,1)S(1)} %get-tuple-element.19), channel_id=1, source_target_pairs={{0,1},{1,2},{2,3},{3,4},{4,5},{5,6},{6,7},{7,8},{8,9},{9,10},{10,1... | collective-permute-start | bytes 393224 | tf_op jit(solution)/shard_map/ppermute | solution.py:16
  11.5 1.0 %copy-start.2 = (bf16[1,4,16,16,128]{4,3,2,1,0:T(8,128)(2,1)S(1)}, bf16[1,4,16,16,128]{4,3,2,1,0:T(8,128)(2,1)}, u32[]{:S(2)}) copy-start(bf16[1,4,16,16,128]{4,3,2,1,0:T(8,128)(2,1)} %param.7) | copy-start | bytes 786436
  17.6 2.5 %collective-permute-start.2 = (f32[1728,128]{1,0:T(8,128)S(1)}, f32[1728,128]{1,0:T(8,128)S(1)}, u32[]{:S(2)}, u32[]{:S(2)}) collective-permute-start(f32[1728,128]{1,0:T(8,128)S(1)} %get-tuple-element.11), channel_id=1, source_target_pairs={{0,1},{1,0},{2,3},{3,2},{4,5},{5,4},{6,7},{7,6},{8,9},{9,8},{10,11... | collective-permute-start | bytes 2654216 | tf_op jit(solution)/shard_map/ppermute | solution.py:22
  21.2 23.9 %all-to-all-start = ((f32[16,108,128]{2,1,0:T(8,128)}), f32[16,108,128]{2,1,0:T(8,128)S(1)}, u32[]{:S(2)}, u32[]{:S(2)}) async-start(f32[16,108,128]{2,1,0:T(8,128)} %all_to_all.6), calls=%async_computation | async-start | bytes 1835008 | tf_op jit(solution)/shard_map/all_to_all | solution.py:24
  45.2 4.3 %collective-permute-start.3 = (f32[108,128]{1,0:T(8,128)S(1)}, f32[108,128]{1,0:T(8,128)S(1)}, u32[]{:S(2)}, u32[]{:S(2)}) collective-permute-start(f32[108,128]{1,0:T(8,128)S(1)} %reduce_sum.9), channel_id=1, source_target_pairs={{0,32},{32,0},{64,96},{96,64},{128,160},{160,128},{192,224},{224,1... | collective-permute-start | bytes 165896 | tf_op jit(solution)/shard_map/ppermute | solution.py:29
  49.5 5.8 %collective-permute-start.4 = (f32[108,128]{1,0:T(8,128)S(1)}, f32[108,128]{1,0:T(8,128)S(1)}, u32[]{:S(2)}, u32[]{:S(2)}) collective-permute-start(f32[108,128]{1,0:T(8,128)S(1)} %add.21), channel_id=1, source_target_pairs={{0,64},{32,96},{64,0},{96,32},{128,192},{160,224},{192,128},{224,1... | collective-permute-start | bytes 165896 | tf_op jit(solution)/shard_map/ppermute | solution.py:29
  55.3 10.0 %collective-permute-start.5 = (f32[108,128]{1,0:T(8,128)S(1)}, f32[108,128]{1,0:T(8,128)S(1)}, u32[]{:S(2)}, u32[]{:S(2)}) collective-permute-start(f32[108,128]{1,0:T(8,128)S(1)} %add.22), channel_id=1, source_target_pairs={{0,128},{32,160},{64,192},{96,224},{128,0},{160,32},{192,64},{224,... | collective-permute-start | bytes 165896 | tf_op jit(solution)/shard_map/ppermute | solution.py:29

commit v16 on v15

--- a/solution.py
+++ b/solution.py
@@ -16,13 +16,13 @@
     return lax.ppermute(value, axis, [(source, source + steps) for source in range(leading, last)])
 
 
-def reduce_weight_grad(mine, other, tie):
+def reduce_weight_grad(mine, other, tie, share):
     dp = lax.axis_size("dp")
     cores = lax.axis_size("core")
     mine = mine + lax.ppermute(other, "core", [(i, (i + 1) % cores) for i in range(cores)])
     chips = lax.axis_size("chip")
     mine = lax.all_to_all(mine, "chip", 0, 0, tiled=True)
-    mine = mine.reshape(chips, mine.shape[0] // chips, mine.shape[1]).sum(axis=0)
+    mine = mine.reshape(chips, mine.shape[0] // chips, mine.shape[1]).sum(axis=0)[:share]
     mine, tie = lax.optimization_barrier((mine, tie))
     step = 1
     while step < dp:
@@ -87,19 +87,22 @@
             acc_ref[kt] = acc_ref[kt] + mask_ref[kt, t] * part
     for kt in range(3):
         flat_ref[pl.ds(kt * taps, taps), :] = jnp.transpose(acc_ref[kt])
-    chips, share = blocks_of, mine_ref.shape[0] // blocks_of
+    chips, slot = blocks_of, mine_ref.shape[0] // blocks_of
+    share = flat_ref.shape[0] // (2 * chips)
     first = core_ref[0] == 0
+    fill = jnp.zeros((slot - share, cc), jnp.float32)
     for c in range(chips):
-        even = flat_ref[pl.ds(2 * c * share, share), :]
-        odd = flat_ref[pl.ds((2 * c + 1) * share, share), :]
-        mine_ref[pl.ds(c * share, share), :] = jnp.where(first, even, odd)
-        other_ref[pl.ds(c * share, share), :] = jnp.where(first, odd, even)
+        even = jnp.concatenate([flat_ref[pl.ds(2 * c * share, share), :], fill], axis=0)
+        odd = jnp.concatenate([flat_ref[pl.ds((2 * c + 1) * share, share), :], fill], axis=0)
+        mine_ref[pl.ds(c * slot, slot), :] = jnp.where(first, even, odd)
+        other_ref[pl.ds(c * slot, slot), :] = jnp.where(first, odd, even)
 
 
 def forward_call(core, mask, early, own, ahead, cot, w, hh, ww, nout, nfr, blocks):
     frame = hh * ww
     cc = own.shape[1]
     krows = w.shape[0]
+    slot = -(-(krows // blocks) // 8) * 8
     vmem = pl.BlockSpec(memory_space=pltpu.VMEM)
     flops = 2 * 3 * frame * 9 * cc * cc * (nout + nfr)
     return pl.pallas_call(
@@ -107,8 +110,8 @@
         out_shape=(
             jax.ShapeDtypeStruct((nfr * frame, cc), jnp.bfloat16),
             jax.ShapeDtypeStruct((nout * frame, cc), jnp.bfloat16),
-            jax.ShapeDtypeStruct((krows // 2, cc), jnp.float32),
-            jax.ShapeDtypeStruct((krows // 2, cc), jnp.float32),
+            jax.ShapeDtypeStruct((blocks // 2 * slot, cc), jnp.float32),
+            jax.ShapeDtypeStruct((blocks // 2 * slot, cc), jnp.float32),
         ),
         in_specs=[pl.BlockSpec(memory_space=pltpu.SMEM), pl.BlockSpec(memory_space=pltpu.SMEM), vmem, vmem, vmem, vmem, vmem],
         out_specs=(vmem, vmem, vmem, vmem),
@@ -213,7 +216,7 @@
         axis=0,
     )
     grad_clips = input_grad_call(later_mask, grad_pre, flipped, hh, ww, nfr)
-    total, grad_clips = reduce_weight_grad(mine, other, grad_clips)
+    total, grad_clips = reduce_weight_grad(mine, other, grad_clips, conv_weight.shape[0] // tm)
     grad_weight = total / jnp.sqrt(jnp.float32(count))
     grad_clips = grad_clips.reshape(clips.shape)
     return (activated, grad_clips, grad_weight)

time: 66.3 us -> 66.2 us (level)
  local copies, waits for them, and re-layouts: 4.82 us -> 3.83 us
  other arithmetic: 1.25 us -> 2.19 us
    all_to_all x1 -> x0, local copies, waits for them, and re-layouts: 0.99 us -> none  [reduce_weight_grad(): mine = lax.all_to_all(mine, 'chip', 0, 0, tiled=True)]
    add x1, other arithmetic: 0.09 us -> 1.02 us  [reduce_weight_grad(): mine + lax.ppermute(other, 'core', [(i, (i + 1) % cores) for i in range(c...]
where the time goes in v16:
time: 66.2 us; the launch traced here: 66 us
  starting transfers between devices  26.7 us (40%)
  waiting for transfers between devices  23.7 us (36%)
  Pallas kernels  8.67 us (13%)
  local copies, waits for them, and re-layouts  3.83 us (6%)
  other arithmetic  2.19 us (3%)
  between operations  0.78 us (1%)
    ppermute x3, starting transfers between devices, reduce_weight_grad(): mine = mine + lax.ppermute(mine, 'dp', [(i, i ^ step) for i in range(dp)])  13.6 us
    all_to_all x1, waiting for transfers between devices, reduce_weight_grad(): mine = lax.all_to_all(mine, 'chip', 0, 0, tiled=True)  10.8 us
    all_to_all x1, starting transfers between devices, reduce_weight_grad(): mine = lax.all_to_all(mine, 'chip', 0, 0, tiled=True)  8.76 us
    ppermute x3, waiting for transfers between devices, reduce_weight_grad(): mine = mine + lax.ppermute(mine, 'dp', [(i, i ^ step) for i in range(dp)])  6.58 us
    pallas_call x1, Pallas kernels, forward_call(): pl.pallas_call(functools.partial(forward_kernel, hh, ww, nout, nfr, block...  5.16 us
    ppermute x2, starting transfers between devices, from_behind(): lax.ppermute(value, axis, [(source, source + steps) for source in range(l...  4.33 us
    ppermute x2, waiting for transfers between devices, from_behind(): lax.ppermute(value, axis, [(source, source + steps) for source in range(l...  4.01 us
    pallas_call x1, Pallas kernels, input_grad_call(): pl.pallas_call(functools.partial(input_grad_kernel, hh, ww, nfr), out_sha...  3.51 us
  transfers between devices with their start and end apart: 7, of which 6 were waited for; matrix products, arithmetic and copies ran while one was open for 2% of the time, Pallas kernels for 5%

profile of v16, /device:TPU:8, one launch (start us, length us, event | category | flops | bytes accessed | tf_op | source)
XLA Modules:
  0.0 66.0 jit_solution(3197874325020081400)
XLA Ops:
  0.6 0.0 copy-start.1
  0.6 0.0 copy-start.3
  0.7 0.0 copy-start
  0.7 1.1 %fusion.1 = (bf16[1,2,16,16,128]{4,3,2,1,0:T(8,128)(2,1)S(1)}, bf16[1,2,16,16,128]{4,3,2,1,0:T(8,128)(2,1)S(1)}) fusion(bf16[1,4,16,16,128]{4,3,2,1,0:T(8,128)(2,1)} %param.4), kind=kLoop, calls=%fused_computation.11 | loop fusion | bytes 524288 | tf_op jit(solution)/shard_map/slice | solution.py:186
  1.7 0.9 %slice.46 = bf16[1,2,16,16,128]{4,3,2,1,0:T(8,128)(2,1)S(1)} slice(bf16[1,4,16,16,128]{4,3,2,1,0:T(8,128)(2,1)} %param.7), slice={[0:1], [0:2], [0:16], [0:16], [0:128]} | slice | bytes 262144 | tf_op jit(solution)/shard_map/slice | solution.py:186
  2.7 1.9 %collective-permute-start.1 = (bf16[1,4,16,16,128]{4,3,2,1,0:T(8,128)(2,1)S(1)}, bf16[1,4,16,16,128]{4,3,2,1,0:T(8,128)(2,1)S(1)}, u32[]{:S(2)}, u32[]{:S(2)}) collective-permute-start(bf16[1,4,16,16,128]{4,3,2,1,0:T(8,128)(2,1)S(1)} %pad_maximum_fusion.1), channel_id=1, source_target_pairs={{1,0},{2,1},{3,2},{4,3},{5,4},{6,5},{7,6},{8,7},{9,8},{10,9},{11,1... | collective-permute-start | bytes 786440 | tf_op jit(solution)/shard_map/ppermute | solution.py:16
  4.6 2.4 %collective-permute-start = (bf16[1,2,16,16,128]{4,3,2,1,0:T(8,128)(2,1)S(1)}, bf16[1,2,16,16,128]{4,3,2,1,0:T(8,128)(2,1)S(1)}, u32[]{:S(2)}, u32[]{:S(2)}) collective-permute-start(bf16[1,2,16,16,128]{4,3,2,1,0:T(8,128)(2,1)S(1)} %get-tuple-element.19), channel_id=1, source_target_pairs={{0,1},{1,2},{2,3},{3,4},{4,5},{5,6},{6,7},{7,8},{8,9},{9,10},{10,1... | collective-permute-start | bytes 393224 | tf_op jit(solution)/shard_map/ppermute | solution.py:16
  7.1 0.0 copy-done.3
  7.1 0.1 pad_add_fusion
  7.2 0.1 dynamic_slice.3
  7.2 0.1 compare_bitcast_fusion.3
  7.3 0.1 pad.10.clone
  7.4 0.1 add_convert_fusion.mask_ref
  7.5 4.0 %collective-permute-done = bf16[1,2,16,16,128]{4,3,2,1,0:T(8,128)(2,1)S(1)} collective-permute-done((bf16[1,2,16,16,128]{4,3,2,1,0:T(8,128)(2,1)S(1)}, bf16[1,2,16,16,128]{4,3,2,1,0:T(8,128)(2,1)S(1)}, u32[]{:S(2)}, u32[]{:S(2)}) %collective-permute-start) | collective-permute-done | bytes 131104 | tf_op jit(solution)/shard_map/ppermute | solution.py:16
  11.5 0.0 collective-permute-done.1
  11.5 0.0 copy-done.1
  11.5 0.0 copy-done
  11.5 0.0 copy-start.2
  11.5 0.9 %copy-done.2 = bf16[1,4,16,16,128]{4,3,2,1,0:T(8,128)(2,1)S(1)} copy-done((bf16[1,4,16,16,128]{4,3,2,1,0:T(8,128)(2,1)S(1)}, bf16[1,4,16,16,128]{4,3,2,1,0:T(8,128)(2,1)}, u32[]{:S(2)}) %copy-start.2) | copy-done | bytes 262168
  12.4 5.2 %shard_map.67 = (bf16[1024,128]{1,0:T(8,128)(2,1)}, bf16[1536,128]{1,0:T(8,128)(2,1)S(1)}, f32[1792,128]{1,0:T(8,128)S(1)}, f32[1792,128]{1,0:T(8,128)S(1)}) custom-call(s32[1]{0:T(128)} %bitcast.core_ref, f32[3,6]{1,0:T(4,128)S(1)} %add_convert_fusion.mask_ref, bf16[512,128]{1,0:T(8,128)(2,1)S(1)} %bitcast.35, bf16[1024,128]{1,0:T(8,128)(2,1)S(1)} %bitcast.32, ...), custom_call_target="tpu_custom_call" | custom-call | flops 2264924160 | bytes 3571712 | tf_op jit(solution)/shard_map/pallas_call | solution.py:108
  17.6 0.1 collective-permute-start.2
  17.7 0.1 fusion
  17.8 2.4 %collective-permute-done.2 = f32[1792,128]{1,0:T(8,128)S(1)} collective-permute-done((f32[1792,128]{1,0:T(8,128)S(1)}, f32[1792,128]{1,0:T(8,128)S(1)}, u32[]{:S(2)}, u32[]{:S(2)}) %collective-permute-start.2) | collective-permute-done | bytes 917536 | tf_op jit(solution)/shard_map/ppermute | solution.py:22
  20.2 1.0 %add.20 = f32[1792,128]{1,0:T(8,128)} add(f32[1792,128]{1,0:T(8,128)S(1)} %get-tuple-element.10, f32[1792,128]{1,0:T(8,128)S(1)} %collective-permute-done.2) | non-fusion elementwise | flops 229376 | bytes 2752512 | tf_op jit(solution)/shard_map/add | solution.py:22
  21.2 8.8 %all-to-all-start = ((f32[16,112,128]{2,1,0:T(8,128)}), f32[16,112,128]{2,1,0:T(8,128)S(1)}, u32[]{:S(2)}, u32[]{:S(2)}) async-start(f32[16,112,128]{2,1,0:T(8,128)} %bitcast.9), calls=%async_computation | async-start | bytes 1835008 | tf_op jit(solution)/shard_map/all_to_all | solution.py:24
  29.9 0.1 compare_bitcast_fusion.1
  30.0 0.2 copy.7
  30.2 0.2 copy.8
  30.5 0.2 copy.9
  30.7 0.1 add_convert_fusion.1.mask_ref
  30.8 0.1 pad_maximum_fusion.w_ref
  30.8 3.5 %shard_map.68 = bf16[1024,128]{1,0:T(8,128)(2,1)} custom-call(f32[3,4]{1,0:T(4,128)S(1)} %add_convert_fusion.1.mask_ref, bf16[1536,128]{1,0:T(8,128)(2,1)S(1)} %get-tuple-element.12.gp_ref, bf16[3456,128]{1,0:T(8,128)(2,1)S(1)} %pad_maximum_fusion.w_ref), custom_call_target="tpu_custom_call" | custom-call | flops 905969664 | bytes 1540096 | tf_op jit(solution)/shard_map/pallas_call | solution.py:163
  34.3 10.8 %all-to-all-done = f32[16,112,128]{2,1,0:T(8,128)S(1)} async-done(((f32[16,112,128]{2,1,0:T(8,128)}), f32[16,112,128]{2,1,0:T(8,128)S(1)}, u32[]{:S(2)}, u32[]{:S(2)}) %all-to-all-start) | async-done | bytes 917536 | tf_op jit(solution)/shard_map/all_to_all | solution.py:24
  45.1 0.1 reduce_sum.9
  45.2 2.0 %collective-permute-start.3 = (f32[108,128]{1,0:T(8,128)S(1)}, f32[108,128]{1,0:T(8,128)S(1)}, u32[]{:S(2)}, u32[]{:S(2)}) collective-permute-start(f32[108,128]{1,0:T(8,128)S(1)} %bitcast.42), channel_id=1, source_target_pairs={{0,32},{32,0},{64,96},{96,64},{128,160},{160,128},{192,224},{224,1... | collective-permute-start | bytes 165896 | tf_op jit(solution)/shard_map/ppermute | solution.py:29
  47.2 2.3 %collective-permute-done.3 = f32[108,128]{1,0:T(8,128)S(1)} collective-permute-done((f32[108,128]{1,0:T(8,128)S(1)}, f32[108,128]{1,0:T(8,128)S(1)}, u32[]{:S(2)}, u32[]{:S(2)}) %collective-permute-start.3) | collective-permute-done | bytes 55328 | tf_op jit(solution)/shard_map/ppermute | solution.py:29
  49.4 3.7 %collective-permute-start.4 = (f32[108,128]{1,0:T(8,128)S(1)}, f32[108,128]{1,0:T(8,128)S(1)}, u32[]{:S(2)}, u32[]{:S(2)}) collective-permute-start(f32[108,128]{1,0:T(8,128)S(1)} %add.21), channel_id=1, source_target_pairs={{0,64},{32,96},{64,0},{96,32},{128,192},{160,224},{192,128},{224,1... | collective-permute-start | bytes 165896 | tf_op jit(solution)/shard_map/ppermute | solution.py:29
  53.1 2.2 %collective-permute-done.4 = f32[108,128]{1,0:T(8,128)S(1)} collective-permute-done((f32[108,128]{1,0:T(8,128)S(1)}, f32[108,128]{1,0:T(8,128)S(1)}, u32[]{:S(2)}, u32[]{:S(2)}) %collective-permute-start.4) | collective-permute-done | bytes 55328 | tf_op jit(solution)/shard_map/ppermute | solution.py:29
  55.3 7.9 %collective-permute-start.5 = (f32[108,128]{1,0:T(8,128)S(1)}, f32[108,128]{1,0:T(8,128)S(1)}, u32[]{:S(2)}, u32[]{:S(2)}) collective-permute-start(f32[108,128]{1,0:T(8,128)S(1)} %add.22), channel_id=1, source_target_pairs={{0,128},{32,160},{64,192},{96,224},{128,0},{160,32},{192,64},{224,... | collective-permute-start | bytes 165896 | tf_op jit(solution)/shard_map/ppermute | solution.py:29
  63.2 2.2 %collective-permute-done.5 = f32[108,128]{1,0:T(8,128)S(1)} collective-permute-done((f32[108,128]{1,0:T(8,128)S(1)}, f32[108,128]{1,0:T(8,128)S(1)}, u32[]{:S(2)}, u32[]{:S(2)}) %collective-permute-start.5) | collective-permute-done | bytes 55328 | tf_op jit(solution)/shard_map/ppermute | solution.py:29
  65.3 0.6 add_multiply_fusion
  (5 shorter events, 0.0 us)
Async XLA Ops:
  0.6 10.8 %copy-start.1 = (bf16[1,4,16,16,128]{4,3,2,1,0:T(8,128)(2,1)S(1)}, bf16[1,4,16,16,128]{4,3,2,1,0:T(8,128)(2,1)}, u32[]{:S(2)}) copy-start(bf16[1,4,16,16,128]{4,3,2,1,0:T(8,128)(2,1)} %param.4) | copy-start | bytes 786436
  0.6 6.4 %copy-start.3 = (s32[1,128]{1,0:T(1,128)S(1)}, s32[1,128]{1,0:T(1,128)}, u32[]{:S(2)}) copy-start(s32[1,128]{1,0:T(1,128)} %param.5) | copy-start | bytes 1540
  0.7 10.8 %copy-start = (bf16[3456,128]{1,0:T(8,128)(2,1)S(1)}, bf16[3456,128]{1,0:T(8,128)(2,1)}, u32[]{:S(2)}) copy-start(bf16[3456,128]{1,0:T(8,128)(2,1)} %w_ref.1) | copy-start | bytes 2654212
  2.7 8.8 %collective-permute-start.1 = (bf16[1,4,16,16,128]{4,3,2,1,0:T(8,128)(2,1)S(1)}, bf16[1,4,16,16,128]{4,3,2,1,0:T(8,128)(2,1)S(1)}, u32[]{:S(2)}, u32[]{:S(2)}) collective-permute-start(bf16[1,4,16,16,128]{4,3,2,1,0:T(8,128)(2,1)S(1)} %pad_maximum_fusion.1), channel_id=1, source_target_pairs={{1,0},{2,1},{3,2},{4,3},{5,4},{6,5},{7,6},{8,7},{9,8},{10,9},{11,1... | collective-permute-start | bytes 786440 | tf_op jit(solution)/shard_map/ppermute | solution.py:16
  4.6 6.8 %collective-permute-start = (bf16[1,2,16,16,128]{4,3,2,1,0:T(8,128)(2,1)S(1)}, bf16[1,2,16,16,128]{4,3,2,1,0:T(8,128)(2,1)S(1)}, u32[]{:S(2)}, u32[]{:S(2)}) collective-permute-start(bf16[1,2,16,16,128]{4,3,2,1,0:T(8,128)(2,1)S(1)} %get-tuple-element.19), channel_id=1, source_target_pairs={{0,1},{1,2},{2,3},{3,4},{4,5},{5,6},{6,7},{7,8},{8,9},{9,10},{10,1... | collective-permute-start | bytes 393224 | tf_op jit(solution)/shard_map/ppermute | solution.py:16
  11.5 1.0 %copy-start.2 = (bf16[1,4,16,16,128]{4,3,2,1,0:T(8,128)(2,1)S(1)}, bf16[1,4,16,16,128]{4,3,2,1,0:T(8,128)(2,1)}, u32[]{:S(2)}) copy-start(bf16[1,4,16,16,128]{4,3,2,1,0:T(8,128)(2,1)} %param.7) | copy-start | bytes 786436
  17.6 2.6 %collective-permute-start.2 = (f32[1792,128]{1,0:T(8,128)S(1)}, f32[1792,128]{1,0:T(8,128)S(1)}, u32[]{:S(2)}, u32[]{:S(2)}) collective-permute-start(f32[1792,128]{1,0:T(8,128)S(1)} %get-tuple-element.11), channel_id=1, source_target_pairs={{0,1},{1,0},{2,3},{3,2},{4,5},{5,4},{6,7},{7,6},{8,9},{9,8},{10,11... | collective-permute-start | bytes 2752520 | tf_op jit(solution)/shard_map/ppermute | solution.py:22
  21.2 23.9 %all-to-all-start = ((f32[16,112,128]{2,1,0:T(8,128)}), f32[16,112,128]{2,1,0:T(8,128)S(1)}, u32[]{:S(2)}, u32[]{:S(2)}) async-start(f32[16,112,128]{2,1,0:T(8,128)} %bitcast.9), calls=%async_computation | async-start | bytes 1835008 | tf_op jit(solution)/shard_map/all_to_all | solution.py:24
  45.2 4.3 %collective-permute-start.3 = (f32[108,128]{1,0:T(8,128)S(1)}, f32[108,128]{1,0:T(8,128)S(1)}, u32[]{:S(2)}, u32[]{:S(2)}) collective-permute-start(f32[108,128]{1,0:T(8,128)S(1)} %bitcast.42), channel_id=1, source_target_pairs={{0,32},{32,0},{64,96},{96,64},{128,160},{160,128},{192,224},{224,1... | collective-permute-start | bytes 165896 | tf_op jit(solution)/shard_map/ppermute | solution.py:29
  49.4 5.8 %collective-permute-start.4 = (f32[108,128]{1,0:T(8,128)S(1)}, f32[108,128]{1,0:T(8,128)S(1)}, u32[]{:S(2)}, u32[]{:S(2)}) collective-permute-start(f32[108,128]{1,0:T(8,128)S(1)} %add.21), channel_id=1, source_target_pairs={{0,64},{32,96},{64,0},{96,32},{128,192},{160,224},{192,128},{224,1... | collective-permute-start | bytes 165896 | tf_op jit(solution)/shard_map/ppermute | solution.py:29
  55.3 10.0 %collective-permute-start.5 = (f32[108,128]{1,0:T(8,128)S(1)}, f32[108,128]{1,0:T(8,128)S(1)}, u32[]{:S(2)}, u32[]{:S(2)}) collective-permute-start(f32[108,128]{1,0:T(8,128)S(1)} %add.22), channel_id=1, source_target_pairs={{0,128},{32,160},{64,192},{96,224},{128,0},{160,32},{192,64},{224,... | collective-permute-start | bytes 165896 | tf_op jit(solution)/shard_map/ppermute | solution.py:29
